TPU v7x, 512 devices: a whole 4x4x16 slice. The times are simulated.
512 devices in a mesh: leaf: 128 (over x_lo, z, y), col: 4 (over x_hi, core).
Axes of the slice: x: 4 (x_hi: 2, x_lo: 2; x = x_hi * 2 + x_lo), y: 4, z: 16, core: 2. Of those that a mesh axis runs over, the one named last changes fastest.
Arguments:
- upper_block: bfloat16 [163840, 1024], P('leaf', 'col'), may hold values from -6 to 6
- lower_block: bfloat16 [131072, 1280], P(('leaf', 'col')), may hold values from -0.15625 to 0.15625
- pivot_inverse: bfloat16 [163840, 1280], P(('leaf', 'col')), may hold values from -1 to 2, as said below
- pivot_perm: int32 [128, 1280], P('leaf'), may hold values from 0 to 1279, each once within a row
- child_rhs: bfloat16 [163840, 128], P('leaf'), may hold values from -6 to 6
- pattern: int32 [128, 4], P('leaf'), may hold values from 0 to 63, as said below
- root_front: bfloat16 [16384, 16384], P(('leaf', 'col')), may hold values from -6 to 6
- root_rhs: bfloat16 [16384, 128], P(('leaf', 'col')), may hold values from -6 to 6
Outputs:
- assembled_front: bfloat16 [16384, 16384], P(('leaf', 'col'))
- assembled_rhs: float32 [16384, 128], P(('leaf', 'col'))
- child_forward: bfloat16 [163840, 128], P(('leaf', 'col'))
Inputs may be any that keep to these rules, and one draw needn't show every extreme that they name: `pattern`: row k equals (k // 2) XOR s_a in column a, for 4 distinct values s_a shared by all rows; siblings 2 j and 2 j + 1 have equal rows. `pivot_inverse`: each block is an invertible matrix.
All inputs are finite; a program needn't handle non-finite values.
Results may differ from a plain program's by a relative error of at most 0.0047.
Values may be sent and summed in bfloat16 or wider, within the bound.
No kernel may reach another device: no remote copies, remote signals or barrier semaphores. Data moves between devices by JAX's collectives and lax.ppermute only.
A program may use at most 64 MiB of HBM per device.

v0:
```python
import jax
import jax.numpy as jnp
from jax import lax
from jax.sharding import PartitionSpec as P


def from_partner(value, axis, stride):
    mask = 2**stride
    pairs = [(source, source ^ mask) for source in range(lax.axis_size(axis))]
    return lax.ppermute(value, axis, pairs)


def body(
    upper_block, lower_block, pivot_inverse, pivot_perm, child_rhs, pattern, root_front, root_rhs
):
    col_count = lax.axis_size("col")
    leaf_count = lax.axis_size("leaf")
    leaf_index = lax.axis_index("leaf")
    col_index = lax.axis_index("col")
    pivot_order = pivot_perm[0]
    shifted_rhs = child_rhs[pivot_order]
    eliminated = jnp.dot(
        pivot_inverse,
        lax.all_gather(upper_block, "col", axis=1, tiled=True)[pivot_order],
        preferred_element_type=jnp.float32,
    ).astype(jnp.bfloat16)
    forward = jnp.dot(pivot_inverse, shifted_rhs, preferred_element_type=jnp.float32).astype(
        jnp.bfloat16
    )
    coupled_width = eliminated.shape[1]
    coupled = jnp.dot(
        lower_block,
        lax.all_gather(eliminated, "col", axis=0, tiled=True),
        preferred_element_type=jnp.float32,
    )
    coupled_rhs = jnp.dot(
        lower_block,
        lax.all_gather(forward, "col", axis=0, tiled=True),
        preferred_element_type=jnp.float32,
    )
    combined = -jnp.concatenate([coupled, coupled_rhs], axis=1)
    column_masks = jnp.bitwise_xor(pattern[0], leaf_index // 2)
    route_mask = 2 * column_masks[col_index]
    level_count = leaf_count.bit_length() - 1
    bit_order = list(range(1, level_count))
    own_side = leaf_index % 2
    half_rows = combined.shape[0] // 2
    own_rows = lax.dynamic_slice_in_dim(combined, own_side * half_rows, half_rows, 0)
    other_rows = lax.dynamic_slice_in_dim(combined, (1 - own_side) * half_rows, half_rows, 0)
    partner_rows = from_partner(other_rows, "leaf", 0)
    moving = (own_rows + partner_rows).astype(jnp.bfloat16)
    for level_bit in bit_order:
        received = from_partner(moving, "leaf", level_bit)
        moving = jnp.where(route_mask // 2**level_bit % 2 == 1, received, moving)
    share_rows = moving.shape[0] // col_count
    spread = lax.all_to_all(
        moving.reshape(col_count, share_rows, moving.shape[1]),
        "col",
        split_axis=0,
        concat_axis=0,
        tiled=True,
    )
    tile_size = coupled_width // col_count
    front_part = spread[:, :, :coupled_width].reshape(col_count, share_rows, col_count, tile_size)
    tile_values = jnp.transpose(front_part, (1, 0, 2, 3)).reshape(
        share_rows, col_count * col_count, tile_size
    )
    target_tiles = jnp.bitwise_xor(
        jnp.bitwise_xor(column_masks[:, None], column_masks[None, :]), leaf_index // 2
    ).reshape(-1)
    front_width = root_front.shape[1]
    assembled = root_front.astype(jnp.float32).reshape(
        share_rows, front_width // tile_size, tile_size
    )
    assembled = assembled.at[:, target_tiles, :].add(tile_values.astype(jnp.float32))
    assembled_front = assembled.reshape(share_rows, front_width).astype(jnp.bfloat16)
    assembled_rhs = root_rhs.astype(jnp.float32) + jnp.sum(
        spread[:, :, coupled_width:].astype(jnp.float32), axis=0
    )
    return (assembled_front, assembled_rhs, forward)


def solution(mesh):
    return jax.shard_map(
        body,
        mesh=mesh,
        in_specs=(
            P("leaf", "col"),
            P(("leaf", "col"), None),
            P(("leaf", "col"), None),
            P("leaf", None),
            P("leaf", None),
            P("leaf", None),
            P(("leaf", "col"), None),
            P(("leaf", "col"), None),
        ),
        out_specs=(P(("leaf", "col"), None), P(("leaf", "col"), None), P(("leaf", "col"), None)),
        check_vma=False,
    )
```

profile of v0, /device:TPU:1, one launch (start us, length us, event | category | flops | bytes accessed | tf_op | source)
XLA Modules:
  0.0 260.7 jit_solution(17440527551047976593)
XLA Ops:
  7.2 0.0 copy-start
  7.2 0.0 all-gather.3.cloned.1.call-start
  7.2 0.7 all-gather.3.cloned.1.call-update
  7.9 0.0 all-gather.5.cloned.1.call-start
  8.0 0.7 fusion.2
  8.7 44.8 %all-gather.3.cloned.1.call-done = bf16[1280,1024]{1,0:T(8,128)(2,1)} async-done(((bf16[1280,256]{1,0:T(8,128)(2,1)}), bf16[1280,1024]{1,0:T(8,128)(2,1)}) %all-gather.3.cloned.1.call-update) | async-done | bytes 2621456 | tf_op jit(solution)/shard_map/all_gather | solution.py:24
  53.5 8.8 %gather_fusion = bf16[1280,1024]{1,0:T(8,128)(2,1)} fusion(bf16[1280,1024]{1,0:T(8,128)(2,1)} %all-gather.3.cloned.1.call-done, s32[2048]{0:T(1024)S(1)} %pad_clamp_fusion), kind=kCustom, calls=%fused_computation | custom fusion | bytes 5248000 | tf_op jit(solution)/shard_map/gather | solution.py:24
  62.2 0.0 copy-done
  62.2 0.0 copy-start.1
  62.2 3.6 %fusion = bf16[320,1024]{1,0:T(8,128)(2,1)} fusion(bf16[320,1280]{1,0:T(8,128)(2,1)S(1)} %copy-done, bf16[1280,1024]{1,0:T(8,128)(2,1)} %gather_fusion), kind=kOutput, calls=%fused_computation.6 | convolution fusion | flops 839188480 | bytes 4096000 | tf_op jit(solution)/shard_map/dot_general | solution.py:22
  65.9 0.0 all-gather.5.cloned.1.call-update
  65.9 0.0 copy-done.1
  65.9 0.0 copy-start.3
  65.9 2.8 %gather_fusion.1 = bf16[1280,128]{1,0:T(8,128)(2,1)S(1)} fusion(bf16[1280,128]{1,0:T(8,128)(2,1)S(1)} %copy-done.1, s32[2048]{0:T(1024)S(1)} %pad_clamp_fusion), kind=kCustom, calls=%fused_computation.1 | custom fusion | bytes 660480 | tf_op jit(solution)/shard_map/gather | solution.py:21
  68.8 0.4 fusion.1
  69.2 0.0 copy-start.4
  69.2 0.6 copy-done.4
  69.8 7.7 %all_gather.11 = bf16[1280,128]{1,0:T(8,128)(2,1)S(1)} all-gather(bf16[320,128]{1,0:T(8,128)(2,1)S(1)} %fusion.1), channel_id=1, replica_groups=mesh['leaf'=128,'col'=4] {'col'}, dimensions={0}, use_global_device_ids=true | all-gather | bytes 409600 | tf_op jit(solution)/shard_map/all_gather | solution.py:38
  77.5 0.0 copy-done.3
  77.5 0.4 convolution_bitcast_fusion.1
  77.9 24.9 %all-gather.5.cloned.1.call-done = bf16[1280,1024]{1,0:T(8,128)(2,1)} async-done(((bf16[320,1024]{1,0:T(8,128)(2,1)}), bf16[1280,1024]{1,0:T(8,128)(2,1)}) %all-gather.5.cloned.1.call-update) | async-done | bytes 2621456 | tf_op jit(solution)/shard_map/all_gather | solution.py:33
  102.8 2.6 %convolution_bitcast_fusion = f32[256,1024]{0,1:T(8,128)S(1)} fusion(bf16[1280,1024]{1,0:T(8,128)(2,1)} %all-gather.5.cloned.1.call-done, bf16[256,1280]{1,0:T(8,128)(2,1)S(1)} %copy-done.3), kind=kOutput, calls=%fused_computation.4 | convolution fusion | flops 671088640 | bytes 4325376 | tf_op jit(solution)/shard_map/dot_general | solution.py:31
  105.5 0.0 copy-start.6
  105.5 0.1 maximum_negate_fusion
  105.6 3.1 %collective-permute-start = (f32[128,1152]{0,1:T(8,128)S(1)}, f32[128,1152]{0,1:T(8,128)S(1)}, u32[]{:S(2)}, u32[]{:S(2)}) collective-permute-start(f32[128,1152]{0,1:T(8,128)S(1)} %constant_dynamic-slice_fusion), channel_id=1, source_target_pairs={{0,4},{4,0},{8,12},{12,8},{16,20},{20,16},{24,28},{28,24},{32,36},... | collective-permute-start | bytes 1769480 | tf_op jit(solution)/shard_map/ppermute | solution.py:10
  108.8 13.4 %collective-permute-done = f32[128,1152]{0,1:T(8,128)S(1)} collective-permute-done((f32[128,1152]{0,1:T(8,128)S(1)}, f32[128,1152]{0,1:T(8,128)S(1)}, u32[]{:S(2)}, u32[]{:S(2)}) %collective-permute-start) | collective-permute-done | bytes 589856 | tf_op jit(solution)/shard_map/ppermute | solution.py:10
  122.2 0.1 add_convert_fusion
  122.2 4.6 %collective-permute-start.1 = (bf16[128,1152]{0,1:T(8,128)(2,1)S(1)}, bf16[128,1152]{0,1:T(8,128)(2,1)S(1)}, u32[]{:S(2)}, u32[]{:S(2)}) collective-permute-start(bf16[128,1152]{0,1:T(8,128)(2,1)S(1)} %add_convert_fusion), channel_id=1, source_target_pairs={{0,8},{4,12},{8,0},{12,4},{16,24},{20,28},{24,16},{28,20},{32,40},... | collective-permute-start | bytes 884744 | tf_op jit(solution)/shard_map/ppermute | solution.py:10
  126.9 0.0 copy-done.6
  126.9 0.6 fusion.4
  130.1 2.9 %collective-permute-done.1 = bf16[128,1152]{0,1:T(8,128)(2,1)S(1)} collective-permute-done((bf16[128,1152]{0,1:T(8,128)(2,1)S(1)}, bf16[128,1152]{0,1:T(8,128)(2,1)S(1)}, u32[]{:S(2)}, u32[]{:S(2)}) %collective-permute-start.1) | collective-permute-done | bytes 294944 | tf_op jit(solution)/shard_map/ppermute | solution.py:10
  133.1 0.0 copy-start.2
  133.1 3.3 %collective-permute-start.2 = (bf16[128,1152]{0,1:T(8,128)(2,1)S(1)}, bf16[128,1152]{0,1:T(8,128)(2,1)S(1)}, u32[]{:S(2)}, u32[]{:S(2)}) collective-permute-start(bf16[128,1152]{0,1:T(8,128)(2,1)S(1)} %broadcast_select_fusion), channel_id=1, source_target_pairs={{0,16},{4,20},{8,24},{12,28},{16,0},{20,4},{24,8},{28,12},{32,48},... | collective-permute-start | bytes 884744 | tf_op jit(solution)/shard_map/ppermute | solution.py:10
  136.5 5.2 %collective-permute-done.2 = bf16[128,1152]{0,1:T(8,128)(2,1)S(1)} collective-permute-done((bf16[128,1152]{0,1:T(8,128)(2,1)S(1)}, bf16[128,1152]{0,1:T(8,128)(2,1)S(1)}, u32[]{:S(2)}, u32[]{:S(2)}) %collective-permute-start.2) | collective-permute-done | bytes 294944 | tf_op jit(solution)/shard_map/ppermute | solution.py:10
  141.7 4.2 %collective-permute-start.3 = (bf16[128,1152]{0,1:T(8,128)(2,1)S(1)}, bf16[128,1152]{0,1:T(8,128)(2,1)S(1)}, u32[]{:S(2)}, u32[]{:S(2)}) collective-permute-start(bf16[128,1152]{0,1:T(8,128)(2,1)S(1)} %broadcast_select_fusion.1), channel_id=1, source_target_pairs={{0,32},{4,36},{8,40},{12,44},{16,48},{20,52},{24,56},{28,60},{32,0... | collective-permute-start | bytes 884744 | tf_op jit(solution)/shard_map/ppermute | solution.py:10
  145.9 12.8 %collective-permute-done.3 = bf16[128,1152]{0,1:T(8,128)(2,1)S(1)} collective-permute-done((bf16[128,1152]{0,1:T(8,128)(2,1)S(1)}, bf16[128,1152]{0,1:T(8,128)(2,1)S(1)}, u32[]{:S(2)}, u32[]{:S(2)}) %collective-permute-start.3) | collective-permute-done | bytes 294944 | tf_op jit(solution)/shard_map/ppermute | solution.py:10
  158.7 7.4 %collective-permute-start.4 = (bf16[128,1152]{0,1:T(8,128)(2,1)S(1)}, bf16[128,1152]{0,1:T(8,128)(2,1)S(1)}, u32[]{:S(2)}, u32[]{:S(2)}) collective-permute-start(bf16[128,1152]{0,1:T(8,128)(2,1)S(1)} %broadcast_select_fusion.2), channel_id=1, source_target_pairs={{0,64},{4,68},{8,72},{12,76},{16,80},{20,84},{24,88},{28,92},{32,9... | collective-permute-start | bytes 884744 | tf_op jit(solution)/shard_map/ppermute | solution.py:10
  166.1 25.4 %collective-permute-done.4 = bf16[128,1152]{0,1:T(8,128)(2,1)S(1)} collective-permute-done((bf16[128,1152]{0,1:T(8,128)(2,1)S(1)}, bf16[128,1152]{0,1:T(8,128)(2,1)S(1)}, u32[]{:S(2)}, u32[]{:S(2)}) %collective-permute-start.4) | collective-permute-done | bytes 294944 | tf_op jit(solution)/shard_map/ppermute | solution.py:10
  191.5 17.5 %collective-permute-start.5 = (bf16[128,1152]{0,1:T(8,128)(2,1)S(1)}, bf16[128,1152]{0,1:T(8,128)(2,1)S(1)}, u32[]{:S(2)}, u32[]{:S(2)}) collective-permute-start(bf16[128,1152]{0,1:T(8,128)(2,1)S(1)} %broadcast_select_fusion.3), channel_id=1, source_target_pairs={{0,128},{4,132},{8,136},{12,140},{16,144},{20,148},{24,152},{28,15... | collective-permute-start | bytes 884744 | tf_op jit(solution)/shard_map/ppermute | solution.py:10
  209.1 14.1 %collective-permute-done.5 = bf16[128,1152]{0,1:T(8,128)(2,1)S(1)} collective-permute-done((bf16[128,1152]{0,1:T(8,128)(2,1)S(1)}, bf16[128,1152]{0,1:T(8,128)(2,1)S(1)}, u32[]{:S(2)}, u32[]{:S(2)}) %collective-permute-start.5) | collective-permute-done | bytes 294944 | tf_op jit(solution)/shard_map/ppermute | solution.py:10
  223.2 2.2 collective-permute-start.6
  225.5 0.1 xor_xor_fusion
  225.6 0.1 xor.61
  225.6 0.0 copy-done.2
  225.6 0.1 reshape.102
  225.8 0.2 copy.23
  226.0 7.2 %collective-permute-done.6 = bf16[128,1152]{0,1:T(8,128)(2,1)} collective-permute-done((bf16[128,1152]{0,1:T(8,128)(2,1)S(1)}, bf16[128,1152]{0,1:T(8,128)(2,1)}, u32[]{:S(2)}, u32[]{:S(2)}) %collective-permute-start.6) | collective-permute-done | bytes 294944 | tf_op jit(solution)/shard_map/ppermute | solution.py:10
  233.3 1.0 broadcast_select_fusion.5
  234.3 0.9 copy.16
  235.2 4.5 %all-to-all-start = ((bf16[4,32,1152]{2,1,0:T(8,128)(2,1)}), bf16[4,32,1152]{2,1,0:T(8,128)(2,1)}, u32[]{:S(2)}, u32[]{:S(2)}) async-start(bf16[4,32,1152]{2,1,0:T(8,128)(2,1)} %bitcast.8), calls=%async_computation | async-start | bytes 589824 | tf_op jit(solution)/shard_map/all_to_all | solution.py:56
  239.6 7.1 %all-to-all-done = bf16[4,32,1152]{2,1,0:T(8,128)(2,1)} async-done(((bf16[4,32,1152]{2,1,0:T(8,128)(2,1)}), bf16[4,32,1152]{2,1,0:T(8,128)(2,1)}, u32[]{:S(2)}, u32[]{:S(2)}) %all-to-all-start) | async-done | bytes 294944 | tf_op jit(solution)/shard_map/all_to_all | solution.py:56
  246.8 1.0 slice_convert_fusion
  247.8 1.0 reshape.105
  248.8 1.1 copy.17
  249.9 1.3 scatter_fusion
  251.3 0.0 copy-start.5
  251.3 0.2 convert_bitcast_fusion
  251.5 1.0 copy.21
  252.5 0.8 convert_reduce_fusion
  253.3 0.0 copy-done.5
  253.3 0.6 convert_add_fusion
  (10 shorter events, 0.2 us)
Async XLA Ops:
  7.2 55.1 %copy-start = (bf16[320,1280]{1,0:T(8,128)(2,1)S(1)}, bf16[320,1280]{1,0:T(8,128)(2,1)}, u32[]{:S(2)}) copy-start(bf16[320,1280]{1,0:T(8,128)(2,1)} %param.10) | copy-start | bytes 2457604
  7.2 46.3 %all-gather.3.cloned.1.call-start = ((), (), s32[]{:S(2)}) async-start(), calls=%async_computation.1 | async-start | bytes 3276800 | tf_op jit(solution)/shard_map/all_gather | solution.py:24
  7.9 94.9 %all-gather.5.cloned.1.call-start = ((), (), s32[]{:S(2)}) async-start(), calls=%async_computation.2 | async-start | bytes 3276800 | tf_op jit(solution)/shard_map/all_gather | solution.py:33
  62.2 3.7 %copy-start.1 = (bf16[1280,128]{1,0:T(8,128)(2,1)S(1)}, bf16[1280,128]{1,0:T(8,128)(2,1)}, u32[]{:S(2)}) copy-start(bf16[1280,128]{1,0:T(8,128)(2,1)} %param.12) | copy-start | bytes 983044
  65.9 11.6 %copy-start.3 = (bf16[256,1280]{1,0:T(8,128)(2,1)S(1)}, bf16[256,1280]{1,0:T(8,128)(2,1)}, u32[]{:S(2)}) copy-start(bf16[256,1280]{1,0:T(8,128)(2,1)} %param.9) | copy-start | bytes 1966084
  69.2 0.6 copy-start.4
  105.5 21.4 %copy-start.6 = (s32[1,4]{1,0:T(1,128)S(1)}, s32[1,4]{1,0:T(1,128)}, u32[]{:S(2)}) copy-start(s32[1,4]{1,0:T(1,128)} %param.13) | copy-start | bytes 52
  105.6 16.6 %collective-permute-start = (f32[128,1152]{0,1:T(8,128)S(1)}, f32[128,1152]{0,1:T(8,128)S(1)}, u32[]{:S(2)}, u32[]{:S(2)}) collective-permute-start(f32[128,1152]{0,1:T(8,128)S(1)} %constant_dynamic-slice_fusion), channel_id=1, source_target_pairs={{0,4},{4,0},{8,12},{12,8},{16,20},{20,16},{24,28},{28,24},{32,36},... | collective-permute-start | bytes 1769480 | tf_op jit(solution)/shard_map/ppermute | solution.py:10
  122.2 10.8 %collective-permute-start.1 = (bf16[128,1152]{0,1:T(8,128)(2,1)S(1)}, bf16[128,1152]{0,1:T(8,128)(2,1)S(1)}, u32[]{:S(2)}, u32[]{:S(2)}) collective-permute-start(bf16[128,1152]{0,1:T(8,128)(2,1)S(1)} %add_convert_fusion), channel_id=1, source_target_pairs={{0,8},{4,12},{8,0},{12,4},{16,24},{20,28},{24,16},{28,20},{32,40},... | collective-permute-start | bytes 884744 | tf_op jit(solution)/shard_map/ppermute | solution.py:10
  133.1 92.6 %copy-start.2 = (bf16[32,16384]{1,0:T(8,128)(2,1)S(1)}, bf16[32,16384]{1,0:T(8,128)(2,1)}, u32[]{:S(2)}) copy-start(bf16[32,16384]{1,0:T(8,128)(2,1)} %param.14) | copy-start | bytes 3145732
  133.1 8.5 %collective-permute-start.2 = (bf16[128,1152]{0,1:T(8,128)(2,1)S(1)}, bf16[128,1152]{0,1:T(8,128)(2,1)S(1)}, u32[]{:S(2)}, u32[]{:S(2)}) collective-permute-start(bf16[128,1152]{0,1:T(8,128)(2,1)S(1)} %broadcast_select_fusion), channel_id=1, source_target_pairs={{0,16},{4,20},{8,24},{12,28},{16,0},{20,4},{24,8},{28,12},{32,48},... | collective-permute-start | bytes 884744 | tf_op jit(solution)/shard_map/ppermute | solution.py:10
  141.7 17.0 %collective-permute-start.3 = (bf16[128,1152]{0,1:T(8,128)(2,1)S(1)}, bf16[128,1152]{0,1:T(8,128)(2,1)S(1)}, u32[]{:S(2)}, u32[]{:S(2)}) collective-permute-start(bf16[128,1152]{0,1:T(8,128)(2,1)S(1)} %broadcast_select_fusion.1), channel_id=1, source_target_pairs={{0,32},{4,36},{8,40},{12,44},{16,48},{20,52},{24,56},{28,60},{32,0... | collective-permute-start | bytes 884744 | tf_op jit(solution)/shard_map/ppermute | solution.py:10
  158.7 32.8 %collective-permute-start.4 = (bf16[128,1152]{0,1:T(8,128)(2,1)S(1)}, bf16[128,1152]{0,1:T(8,128)(2,1)S(1)}, u32[]{:S(2)}, u32[]{:S(2)}) collective-permute-start(bf16[128,1152]{0,1:T(8,128)(2,1)S(1)} %broadcast_select_fusion.2), channel_id=1, source_target_pairs={{0,64},{4,68},{8,72},{12,76},{16,80},{20,84},{24,88},{28,92},{32,9... | collective-permute-start | bytes 884744 | tf_op jit(solution)/shard_map/ppermute | solution.py:10
  191.5 31.7 %collective-permute-start.5 = (bf16[128,1152]{0,1:T(8,128)(2,1)S(1)}, bf16[128,1152]{0,1:T(8,128)(2,1)S(1)}, u32[]{:S(2)}, u32[]{:S(2)}) collective-permute-start(bf16[128,1152]{0,1:T(8,128)(2,1)S(1)} %broadcast_select_fusion.3), channel_id=1, source_target_pairs={{0,128},{4,132},{8,136},{12,140},{16,144},{20,148},{24,152},{28,15... | collective-permute-start | bytes 884744 | tf_op jit(solution)/shard_map/ppermute | solution.py:10
  223.2 10.1 %collective-permute-start.6 = (bf16[128,1152]{0,1:T(8,128)(2,1)S(1)}, bf16[128,1152]{0,1:T(8,128)(2,1)}, u32[]{:S(2)}, u32[]{:S(2)}) collective-permute-start(bf16[128,1152]{0,1:T(8,128)(2,1)S(1)} %broadcast_select_fusion.4), channel_id=1, source_target_pairs={{0,256},{4,260},{8,264},{12,268},{16,272},{20,276},{24,280},{28,28... | collective-permute-start | bytes 884744 | tf_op jit(solution)/shard_map/ppermute | solution.py:10
  235.2 11.6 %all-to-all-start = ((bf16[4,32,1152]{2,1,0:T(8,128)(2,1)}), bf16[4,32,1152]{2,1,0:T(8,128)(2,1)}, u32[]{:S(2)}, u32[]{:S(2)}) async-start(bf16[4,32,1152]{2,1,0:T(8,128)(2,1)} %bitcast.8), calls=%async_computation | async-start | bytes 589824 | tf_op jit(solution)/shard_map/all_to_all | solution.py:56
  251.3 2.0 copy-start.5
Sparse Core Ops, SparseCore 0:
  10.1 43.3 all-gather.2
  66.0 36.7 all-gather.4
where the time goes:
time: 261 us
  waiting for transfers between devices  159 us (61%)
  starting transfers between devices  46.9 us (18%)
  between operations  17.2 us (7%)
  local copies, waits for them, and re-layouts  16.7 us (6%)
  blocking collectives  7.71 us (3%)
  matrix products  7.04 us (3%)
  other arithmetic  6.69 us (3%)
    ppermute x7, waiting for transfers between devices, from_partner(): return lax.ppermute(value, axis, pairs)  81 us
    all_gather x1, waiting for transfers between devices, body(): lax.all_gather(upper_block, 'col', axis=1, tiled=True)[pivot_order]  44.8 us
    ppermute x7, starting transfers between devices, from_partner(): return lax.ppermute(value, axis, pairs)  42.3 us
    all_gather x1, waiting for transfers between devices, body(): lax.all_gather(eliminated, 'col', axis=0, tiled=True)  24.9 us
    gather x1, local copies, waits for them, and re-layouts, body(): lax.all_gather(upper_block, 'col', axis=1, tiled=True)[pivot_order]  8.77 us
    all_gather x1, blocking collectives, body(): lax.all_gather(forward, 'col', axis=0, tiled=True)  7.71 us
    all_to_all x1, waiting for transfers between devices, body(): lax.all_to_all(moving.reshape(col_count, share_rows, moving.shape[1]), 'c...  7.13 us
  transfers between devices with their start and end apart: 10, of which 10 were waited for; matrix products, arithmetic and copies ran while one was open for 2% of the time, Pallas kernels for 0%

commit v1 on v0

v1 whole, which is shorter than its diff:
```python
import jax
import jax.numpy as jnp
from jax import lax
from jax.sharding import Mesh
from jax.sharding import PartitionSpec as P

LEAF = "leaf"
COLS = ("xh", "core")


def xor_route(value, mask_count):
    leaf_count = lax.axis_size(LEAF)

    def branch(mask):
        if mask == 0:
            return lambda x: x
        pairs = [(source, source ^ mask) for source in range(leaf_count)]
        return lambda x: lax.ppermute(x, LEAF, pairs)

    return [branch(2 * step) for step in range(mask_count)]


def body(
    upper_block, lower_block, pivot_inverse, pivot_perm, child_rhs, pattern, root_front, root_rhs
):
    leaf_count = lax.axis_size(LEAF)
    leaf_index = lax.axis_index(LEAF)
    piv = pivot_inverse.shape[1]
    share = pivot_inverse.shape[0]
    upper_x = lax.all_gather(upper_block, "xh", axis=0)
    upper_all = lax.all_gather(upper_x, "core", axis=0)
    order = pivot_perm[0]
    selector = (order[:, None] == lax.broadcasted_iota(jnp.int32, (piv, piv), 1)).astype(
        pivot_inverse.dtype
    )
    inverse_perm = jnp.dot(pivot_inverse, selector, preferred_element_type=jnp.float32).astype(
        pivot_inverse.dtype
    )
    forward = jnp.dot(inverse_perm, child_rhs, preferred_element_type=jnp.float32).astype(
        jnp.bfloat16
    )
    eliminated = jnp.einsum(
        "ip,cxpn->ixcn", inverse_perm, upper_all, preferred_element_type=jnp.float32
    ).astype(jnp.bfloat16)
    coupled_width = eliminated.shape[1] * eliminated.shape[2] * eliminated.shape[3]
    rows_out = jnp.concatenate([eliminated.reshape(share, coupled_width), forward], axis=1)
    rows_x = lax.all_gather(rows_out, "xh", axis=0)
    rows_all = lax.all_gather(rows_x, "core", axis=0)
    lower_rows = lower_block.shape[0]
    combined = -jnp.einsum(
        "rxcp,cxpn->rn",
        lower_block.reshape(lower_rows, 2, 2, share),
        rows_all,
        preferred_element_type=jnp.float32,
    )
    own_side = leaf_index % 2
    half_rows = lower_rows // 2
    own_rows = lax.dynamic_slice_in_dim(combined, own_side * half_rows, half_rows, 0)
    other_rows = lax.dynamic_slice_in_dim(combined, (1 - own_side) * half_rows, half_rows, 0)
    partner_rows = lax.ppermute(other_rows, LEAF, [(s, s ^ 1) for s in range(leaf_count)])
    moving = (own_rows + partner_rows).astype(jnp.bfloat16)
    col_count = 4
    share_rows = half_rows // col_count
    spread = lax.all_to_all(
        moving.reshape(col_count, share_rows, moving.shape[1]),
        COLS,
        split_axis=0,
        concat_axis=0,
        tiled=True,
    )
    column_masks = jnp.bitwise_xor(pattern[0], leaf_index // 2)
    branches = xor_route(None, leaf_count // 2)

    def route_piece(a, routed):
        piece = lax.dynamic_index_in_dim(spread, a, 0, keepdims=False)
        sent = lax.switch(column_masks[a], branches, piece)
        return lax.dynamic_update_index_in_dim(routed, sent, a, 0)

    routed = lax.fori_loop(0, col_count, route_piece, jnp.zeros_like(spread))
    tile_size = coupled_width // col_count
    front_part = routed[:, :, :coupled_width].reshape(col_count, share_rows, col_count, tile_size)
    tile_values = jnp.transpose(front_part, (1, 0, 2, 3)).reshape(
        share_rows, col_count * col_count, tile_size
    )
    target_tiles = jnp.bitwise_xor(
        jnp.bitwise_xor(column_masks[:, None], column_masks[None, :]), leaf_index // 2
    ).reshape(-1)
    front_width = root_front.shape[1]
    assembled = root_front.astype(jnp.float32).reshape(
        share_rows, front_width // tile_size, tile_size
    )
    assembled = assembled.at[:, target_tiles, :].add(tile_values.astype(jnp.float32))
    assembled_front = assembled.reshape(share_rows, front_width).astype(jnp.bfloat16)
    assembled_rhs = root_rhs.astype(jnp.float32) + jnp.sum(
        routed[:, :, coupled_width:].astype(jnp.float32), axis=0
    )
    return (assembled_front, assembled_rhs, forward)


def solution(mesh):
    leaf_count, col_count = mesh.devices.shape
    fine = Mesh(mesh.devices.reshape(leaf_count, 2, col_count // 2), (LEAF,) + COLS)
    rows = P((LEAF,) + COLS, None)
    return jax.shard_map(
        body,
        mesh=fine,
        in_specs=(
            P(LEAF, COLS),
            rows,
            rows,
            P(LEAF, None),
            P(LEAF, None),
            P(LEAF, None),
            rows,
            rows,
        ),
        out_specs=(rows, rows, rows),
        check_vma=False,
    )
```

time: 261 us -> 271 us (1.038)
  the two profiles are of different devices: /device:TPU:1 before, /device:TPU:64 now
where the time goes in v1:
time: 271 us; the launch traced here: 270 us
  waiting for transfers between devices  192 us (71%)
  starting transfers between devices  30.6 us (11%)
  local copies, waits for them, and re-layouts  14.6 us (5%)
  between operations  14 us (5%)
  matrix products  7.79 us (3%)
  other arithmetic  7.64 us (3%)
  loops' own time  2.93 us (1%)
    ppermute x4, waiting for transfers between devices, branch(): return lambda x: lax.ppermute(x, LEAF, pairs)  45.5 us
    all_gather x1, waiting for transfers between devices, body(): upper_x = lax.all_gather(upper_block, 'xh', axis=0)  41.9 us
    all_gather x1, waiting for transfers between devices, body(): rows_x = lax.all_gather(rows_out, 'xh', axis=0)  39.3 us
    ppermute x4, starting transfers between devices, branch(): return lambda x: lax.ppermute(x, LEAF, pairs)  22.8 us
    all_gather x1, waiting for transfers between devices, body(): rows_all = lax.all_gather(rows_x, 'core', axis=0)  22.7 us
    all_gather x1, waiting for transfers between devices, body(): upper_all = lax.all_gather(upper_x, 'core', axis=0)  20.7 us
    ppermute x1, waiting for transfers between devices, body(): lax.ppermute(other_rows, LEAF, [(s, s ^ 1) for s in range(leaf_count)])  13.7 us
    all_to_all x1, waiting for transfers between devices, body(): lax.all_to_all(moving.reshape(col_count, share_rows, moving.shape[1]), CO...  7.89 us
  transfers between devices with their start and end apart: 10, of which 10 were waited for; matrix products, arithmetic and copies ran while one was open for 2% of the time, Pallas kernels for 0%

profile of v1, /device:TPU:64, one launch (start us, length us, event | category | flops | bytes accessed | tf_op | source)
XLA Modules:
  0.0 269.9 jit_solution(16081020735650656002)
XLA Ops:
  7.2 0.0 copy-start
  7.2 0.0 all-gather.9.cloned.1.call-start
  7.2 0.7 all-gather.9.cloned.1.call-update
  7.9 0.0 all-gather.11.cloned.1.call-start
  8.0 41.9 %all-gather.9.cloned.1.call-done = bf16[2560,256]{1,0:T(8,128)(2,1)} async-done(((bf16[1280,256]{1,0:T(8,128)(2,1)}), bf16[2560,256]{1,0:T(8,128)(2,1)}) %all-gather.9.cloned.1.call-update) | async-done | bytes 1310736 | tf_op jit(solution)/shard_map/all_gather | solution.py:30
  49.8 0.0 all-gather.11.cloned.1.call-update
  49.9 0.0 all-gather.13.cloned.1.call-start
  49.9 0.7 reduce
  50.6 0.0 copy-start.5
  50.7 1.5 fusion.3
  52.2 0.4 convolution_convert_fusion.1
  52.6 0.0 copy-start.4
  52.6 20.7 %all-gather.11.cloned.1.call-done = bf16[4,1280,256]{2,1,0:T(8,128)(2,1)} async-done(((bf16[2,1280,256]{2,1,0:T(8,128)(2,1)}), bf16[4,1280,256]{2,1,0:T(8,128)(2,1)}) %all-gather.11.cloned.1.call-update) | async-done | bytes 2621456 | tf_op jit(solution)/shard_map/all_gather | solution.py:31
  73.3 2.7 %fusion.4 = bf16[320,2,2,256]{3,0,1,2:T(8,128)(2,1)S(1)} fusion(bf16[2,2,1280,256]{3,2,1,0:T(8,128)(2,1)} %bitcast.246, bf16[1280,320]{0,1:T(8,128)(2,1)S(1)} %fusion.3), kind=kOutput, calls=%fused_computation.74 | convolution fusion | flops 839188480 | bytes 4096000 | tf_op jit(solution)/shard_map/ip,cxpn->ixcn/dot_general | solution.py:42
  76.1 0.7 copy.19
  76.7 0.5 reshape.78
  77.2 0.0 copy-start.3
  77.2 0.9 pad_maximum_fusion
  78.1 0.0 all-gather.13.cloned.1.call-update
  78.2 0.0 all-gather.15.cloned.1.call-start
  78.2 39.3 %all-gather.13.cloned.1.call-done = bf16[640,1152]{1,0:T(8,128)(2,1)} async-done(((bf16[320,1152]{1,0:T(8,128)(2,1)}), bf16[640,1152]{1,0:T(8,128)(2,1)}) %all-gather.13.cloned.1.call-update) | async-done | bytes 1474576 | tf_op jit(solution)/shard_map/all_gather | solution.py:47
  117.5 0.0 all-gather.15.cloned.1.call-update
  117.5 1.1 copy.20
  118.6 22.7 %all-gather.15.cloned.1.call-done = bf16[4,320,1152]{2,1,0:T(8,128)(2,1)} async-done(((bf16[2,320,1152]{2,1,0:T(8,128)(2,1)}), bf16[4,320,1152]{2,1,0:T(8,128)(2,1)}) %all-gather.15.cloned.1.call-update) | async-done | bytes 2949136 | tf_op jit(solution)/shard_map/all_gather | solution.py:48
  141.3 3.1 %fusion.2 = f32[1152,256]{0,1:T(8,128)S(1)} fusion(bf16[2,2,320,1152]{3,2,1,0:T(8,128)(2,1)} %bitcast.245, bf16[256,2,2,320]{0,3,2,1:T(8,128)(2,1)} %bitcast.244), kind=kOutput, calls=%fused_computation.70 | convolution fusion | flops 755269632 | bytes 4784128 | tf_op jit(solution)/shard_map/rxcp,cxpn->rn/dot_general | solution.py:50
  144.4 0.9 dynamic-slice_bitcast_fusion.63
  145.4 3.4 %collective-permute-start.63 = (f32[128,1152]{1,0:T(8,128)}, f32[128,1152]{1,0:T(8,128)}, u32[]{:S(2)}, u32[]{:S(2)}) collective-permute-start(f32[128,1152]{1,0:T(8,128)} %dynamic-slice_bitcast_fusion.63), channel_id=1, source_target_pairs={{0,4},{4,0},{8,12},{12,8},{16,20},{20,16},{24,28},{28,24},{32,36},... | collective-permute-start | bytes 1769480 | tf_op jit(solution)/shard_map/ppermute | solution.py:60
  148.8 0.1 xor_xor_fusion
  148.9 0.1 xor.61
  149.0 0.1 reshape.81
  149.1 0.2 copy.32
  149.4 13.7 %collective-permute-done.63 = f32[128,1152]{1,0:T(8,128)} collective-permute-done((f32[128,1152]{1,0:T(8,128)}, f32[128,1152]{1,0:T(8,128)}, u32[]{:S(2)}, u32[]{:S(2)}) %collective-permute-start.63) | collective-permute-done | bytes 589856 | tf_op jit(solution)/shard_map/ppermute | solution.py:60
  163.1 2.0 fusion.7
  165.1 4.2 %all-to-all-start = ((bf16[4,32,1152]{2,1,0:T(8,128)(2,1)}), bf16[4,32,1152]{2,1,0:T(8,128)(2,1)S(1)}, u32[]{:S(2)}, u32[]{:S(2)}) async-start(bf16[4,32,1152]{2,1,0:T(8,128)(2,1)} %bitcast.141), calls=%async_computation | async-start | bytes 589824 | tf_op jit(solution)/shard_map/all_to_all | solution.py:64
  169.4 7.9 %all-to-all-done = bf16[4,32,1152]{2,1,0:T(8,128)(2,1)S(1)} async-done(((bf16[4,32,1152]{2,1,0:T(8,128)(2,1)}), bf16[4,32,1152]{2,1,0:T(8,128)(2,1)S(1)}, u32[]{:S(2)}, u32[]{:S(2)}) %all-to-all-start) | async-done | bytes 294944 | tf_op jit(solution)/shard_map/all_to_all | solution.py:64
  177.2 77.3 %while.13 = (s32[]{:T(128)}, bf16[4,32,1152]{2,1,0:T(8,128)(2,1)S(1)}, s32[4]{0:T(128)S(1)}, bf16[4,32,1152]{2,1,0:T(8,128)(2,1)S(1)}, s32[]{:T(128)}, /*index=5*/s32[1]{0:T(128)}, s32[1]{0:T(128)}) while((s32[]{:T(128)}, bf16[4,32,1152]{2,1,0:T(8,128)(2,1)S(1)}, s32[4]{0:T(128)S(1)}, bf16[4,32,1152]{2,1,0:T(8,128)(2,1)S(1)}, s32[]{:T(128)}, ...), condition=%wide.region_65.66_spmd, body=%wide.region_0.65_spmd.sunk | while | flops 3 | bytes 590001 | solution.py:79
  177.2 0.6 dynamic_slice.342
  178.5 33.9 %conditional.2 = (bf16[1,32,1152]{2,1,0:T(8,128)(2,1)}) conditional(s32[]{:T(128)} %bitcast.236, (bf16[4,32,1152]{2,1,0:T(8,128)(2,1)S(1)}, s32[]{:T(128)}) %tuple.357, (bf16[4,32,1152]{2,1,0:T(8,128)(2,1)S(1)}, s32[]{:T(128)}) %tuple.357, (bf16[4,32,1152]{2,1,0:T(8,128)(2,1)S(1)}, s32[]{:T(128)}) %tuple.357, ...), branch_computations={%region_1.1_spmd, %region_2.2_spmd, %region_3.3_spmd, %region_4.4_... | conditional | bytes 442420 | solution.py:76
  178.6 15.5 %collective-permute-start.51 = (bf16[32,1152]{1,0:T(8,128)(2,1)S(1)}, bf16[32,1152]{1,0:T(8,128)(2,1)}, u32[]{:S(2)}, u32[]{:S(2)}) collective-permute-start(bf16[32,1152]{1,0:T(8,128)(2,1)S(1)} %dynamic-slice_bitcast_fusion.51), channel_id=1, source_target_pairs={{0,416},{4,420},{8,424},{12,428},{16,432},{20,436},{24,440},{28,44... | collective-permute-start | bytes 221192 | tf_op jit(solution)/shard_map/while/body/eval_jaxpr/cond/branch_52_fun/ppermute | solution.py:18
  194.1 18.3 %collective-permute-done.51 = bf16[32,1152]{1,0:T(8,128)(2,1)} collective-permute-done((bf16[32,1152]{1,0:T(8,128)(2,1)S(1)}, bf16[32,1152]{1,0:T(8,128)(2,1)}, u32[]{:S(2)}, u32[]{:S(2)}) %collective-permute-start.51) | collective-permute-done | bytes 73760 | tf_op jit(solution)/shard_map/while/body/eval_jaxpr/cond/branch_52_fun/ppermute | solution.py:18
  212.4 0.9 constant_dynamic-update-slice_fusion.2
  213.3 0.6 dynamic_slice.342
  214.5 6.4 %conditional.2 = (bf16[1,32,1152]{2,1,0:T(8,128)(2,1)}) conditional(s32[]{:T(128)} %bitcast.236, (bf16[4,32,1152]{2,1,0:T(8,128)(2,1)S(1)}, s32[]{:T(128)}) %tuple.357, (bf16[4,32,1152]{2,1,0:T(8,128)(2,1)S(1)}, s32[]{:T(128)}) %tuple.357, (bf16[4,32,1152]{2,1,0:T(8,128)(2,1)S(1)}, s32[]{:T(128)}) %tuple.357, ...), branch_computations={%region_1.1_spmd, %region_2.2_spmd, %region_3.3_spmd, %region_4.4_... | conditional | bytes 442420 | solution.py:76
  214.6 1.9 collective-permute-start.1
  216.5 4.4 %collective-permute-done.1 = bf16[32,1152]{1,0:T(8,128)(2,1)} collective-permute-done((bf16[32,1152]{1,0:T(8,128)(2,1)S(1)}, bf16[32,1152]{1,0:T(8,128)(2,1)}, u32[]{:S(2)}, u32[]{:S(2)}) %collective-permute-start.1) | collective-permute-done | bytes 73760 | tf_op jit(solution)/shard_map/while/body/eval_jaxpr/cond/branch_2_fun/ppermute | solution.py:18
  220.9 0.9 constant_dynamic-update-slice_fusion.2
  221.9 0.6 dynamic_slice.342
  223.1 10.6 %conditional.2 = (bf16[1,32,1152]{2,1,0:T(8,128)(2,1)}) conditional(s32[]{:T(128)} %bitcast.236, (bf16[4,32,1152]{2,1,0:T(8,128)(2,1)S(1)}, s32[]{:T(128)}) %tuple.357, (bf16[4,32,1152]{2,1,0:T(8,128)(2,1)S(1)}, s32[]{:T(128)}) %tuple.357, (bf16[4,32,1152]{2,1,0:T(8,128)(2,1)S(1)}, s32[]{:T(128)}) %tuple.357, ...), branch_computations={%region_1.1_spmd, %region_2.2_spmd, %region_3.3_spmd, %region_4.4_... | conditional | bytes 442420 | solution.py:76
  223.2 1.9 collective-permute-start.7
  225.1 8.6 %collective-permute-done.7 = bf16[32,1152]{1,0:T(8,128)(2,1)} collective-permute-done((bf16[32,1152]{1,0:T(8,128)(2,1)S(1)}, bf16[32,1152]{1,0:T(8,128)(2,1)}, u32[]{:S(2)}, u32[]{:S(2)}) %collective-permute-start.7) | collective-permute-done | bytes 73760 | tf_op jit(solution)/shard_map/while/body/eval_jaxpr/cond/branch_8_fun/ppermute | solution.py:18
  233.7 0.9 constant_dynamic-update-slice_fusion.2
  234.6 0.6 dynamic_slice.342
  235.8 17.8 %conditional.2 = (bf16[1,32,1152]{2,1,0:T(8,128)(2,1)}) conditional(s32[]{:T(128)} %bitcast.236, (bf16[4,32,1152]{2,1,0:T(8,128)(2,1)S(1)}, s32[]{:T(128)}) %tuple.357, (bf16[4,32,1152]{2,1,0:T(8,128)(2,1)S(1)}, s32[]{:T(128)}) %tuple.357, (bf16[4,32,1152]{2,1,0:T(8,128)(2,1)S(1)}, s32[]{:T(128)}) %tuple.357, ...), branch_computations={%region_1.1_spmd, %region_2.2_spmd, %region_3.3_spmd, %region_4.4_... | conditional | bytes 442420 | solution.py:76
  235.9 3.5 %collective-permute-start.22 = (bf16[32,1152]{1,0:T(8,128)(2,1)S(1)}, bf16[32,1152]{1,0:T(8,128)(2,1)}, u32[]{:S(2)}, u32[]{:S(2)}) collective-permute-start(bf16[32,1152]{1,0:T(8,128)(2,1)S(1)} %dynamic-slice_bitcast_fusion.22), channel_id=1, source_target_pairs={{0,184},{4,188},{8,176},{12,180},{16,168},{20,172},{24,160},{28,16... | collective-permute-start | bytes 221192 | tf_op jit(solution)/shard_map/while/body/eval_jaxpr/cond/branch_23_fun/ppermute | solution.py:18
  239.4 14.2 %collective-permute-done.22 = bf16[32,1152]{1,0:T(8,128)(2,1)} collective-permute-done((bf16[32,1152]{1,0:T(8,128)(2,1)S(1)}, bf16[32,1152]{1,0:T(8,128)(2,1)}, u32[]{:S(2)}, u32[]{:S(2)}) %collective-permute-start.22) | collective-permute-done | bytes 73760 | tf_op jit(solution)/shard_map/while/body/eval_jaxpr/cond/branch_23_fun/ppermute | solution.py:18
  253.6 0.9 constant_dynamic-update-slice_fusion.2
  254.5 0.8 slice_convert_fusion
  255.4 2.1 reshape.84
  257.5 1.9 copy.22
  259.4 2.2 scatter_fusion
  261.6 0.0 copy-start.6
  261.6 0.2 convert_bitcast_fusion
  261.8 1.0 copy.28
  262.8 0.6 convert_add_fusion
  (19 shorter events, 0.1 us)
Async XLA Ops:
  7.2 43.5 %copy-start = (bf16[320,1280]{1,0:T(8,128)(2,1)S(1)}, bf16[320,1280]{1,0:T(8,128)(2,1)}, u32[]{:S(2)}) copy-start(bf16[320,1280]{1,0:T(8,128)(2,1)} %param.76) | copy-start | bytes 2457604
  7.2 42.7 %all-gather.9.cloned.1.call-start = ((), (), s32[]{:S(2)}) async-start(), calls=%async_computation.1 | async-start | bytes 1966080 | tf_op jit(solution)/shard_map/all_gather | solution.py:30
  7.9 65.4 %all-gather.11.cloned.1.call-start = ((), (), s32[]{:S(2)}) async-start(), calls=%async_computation.2 | async-start | bytes 3932160 | tf_op jit(solution)/shard_map/all_gather | solution.py:31
  49.9 67.6 %all-gather.13.cloned.1.call-start = ((), (), s32[]{:S(2)}) async-start(), calls=%async_computation.3 | async-start | bytes 2211840 | tf_op jit(solution)/shard_map/all_gather | solution.py:47
  50.6 1.6 copy-start.5
  52.6 24.6 %copy-start.4 = (bf16[320,128]{1,0:T(8,128)(2,1)}, bf16[320,128]{1,0:T(8,128)(2,1)S(1)}, u32[]{:S(2)}) copy-start(bf16[320,128]{1,0:T(8,128)(2,1)S(1)} %convolution_convert_fusion.1) | copy-start | bytes 245764
  77.2 40.3 %copy-start.3 = (bf16[256,1280]{1,0:T(8,128)(2,1)S(1)}, bf16[256,1280]{1,0:T(8,128)(2,1)}, u32[]{:S(2)}) copy-start(bf16[256,1280]{1,0:T(8,128)(2,1)} %param.75) | copy-start | bytes 1966084
  78.2 63.1 %all-gather.15.cloned.1.call-start = ((), (), s32[]{:S(2)}) async-start(), calls=%async_computation.4 | async-start | bytes 4423680 | tf_op jit(solution)/shard_map/all_gather | solution.py:48
  141.3 7.5 %copy-start.7 = (s32[1,4]{1,0:T(1,128)S(1)}, s32[1,4]{1,0:T(1,128)}, u32[]{:S(2)}) copy-start(s32[1,4]{1,0:T(1,128)} %param.79) | copy-start | bytes 52
  141.3 7.7 %copy-start.2 = (bf16[32,16384]{1,0:T(8,128)(2,1)S(1)}, bf16[32,16384]{1,0:T(8,128)(2,1)}, u32[]{:S(2)}) copy-start(bf16[32,16384]{1,0:T(8,128)(2,1)} %param.80) | copy-start | bytes 3145732
  144.4 4.7 %copy-start.1 = (f32[1152,256]{0,1:T(8,128)}, f32[1152,256]{0,1:T(8,128)S(1)}, u32[]{:S(2)}) copy-start(f32[1152,256]{0,1:T(8,128)S(1)} %fusion.2) | copy-start | bytes 3538948
  145.4 17.7 %collective-permute-start.63 = (f32[128,1152]{1,0:T(8,128)}, f32[128,1152]{1,0:T(8,128)}, u32[]{:S(2)}, u32[]{:S(2)}) collective-permute-start(f32[128,1152]{1,0:T(8,128)} %dynamic-slice_bitcast_fusion.63), channel_id=1, source_target_pairs={{0,4},{4,0},{8,12},{12,8},{16,20},{20,16},{24,28},{28,24},{32,36},... | collective-permute-start | bytes 1769480 | tf_op jit(solution)/shard_map/ppermute | solution.py:60
  165.1 12.1 %all-to-all-start = ((bf16[4,32,1152]{2,1,0:T(8,128)(2,1)}), bf16[4,32,1152]{2,1,0:T(8,128)(2,1)S(1)}, u32[]{:S(2)}, u32[]{:S(2)}) async-start(bf16[4,32,1152]{2,1,0:T(8,128)(2,1)} %bitcast.141), calls=%async_computation | async-start | bytes 589824 | tf_op jit(solution)/shard_map/all_to_all | solution.py:64
  178.6 33.8 %collective-permute-start.51 = (bf16[32,1152]{1,0:T(8,128)(2,1)S(1)}, bf16[32,1152]{1,0:T(8,128)(2,1)}, u32[]{:S(2)}, u32[]{:S(2)}) collective-permute-start(bf16[32,1152]{1,0:T(8,128)(2,1)S(1)} %dynamic-slice_bitcast_fusion.51), channel_id=1, source_target_pairs={{0,416},{4,420},{8,424},{12,428},{16,432},{20,436},{24,440},{28,44... | collective-permute-start | bytes 221192 | tf_op jit(solution)/shard_map/while/body/eval_jaxpr/cond/branch_52_fun/ppermute | solution.py:18
  214.6 6.4 %collective-permute-start.1 = (bf16[32,1152]{1,0:T(8,128)(2,1)S(1)}, bf16[32,1152]{1,0:T(8,128)(2,1)}, u32[]{:S(2)}, u32[]{:S(2)}) collective-permute-start(bf16[32,1152]{1,0:T(8,128)(2,1)S(1)} %dynamic-slice_bitcast_fusion.1), channel_id=1, source_target_pairs={{0,16},{4,20},{8,24},{12,28},{16,0},{20,4},{24,8},{28,12},{32,48},... | collective-permute-start | bytes 221192 | tf_op jit(solution)/shard_map/while/body/eval_jaxpr/cond/branch_2_fun/ppermute | solution.py:18
  223.2 10.5 %collective-permute-start.7 = (bf16[32,1152]{1,0:T(8,128)(2,1)S(1)}, bf16[32,1152]{1,0:T(8,128)(2,1)}, u32[]{:S(2)}, u32[]{:S(2)}) collective-permute-start(bf16[32,1152]{1,0:T(8,128)(2,1)S(1)} %dynamic-slice_bitcast_fusion.7), channel_id=1, source_target_pairs={{0,64},{4,68},{8,72},{12,76},{16,80},{20,84},{24,88},{28,92},{32,9... | collective-permute-start | bytes 221192 | tf_op jit(solution)/shard_map/while/body/eval_jaxpr/cond/branch_8_fun/ppermute | solution.py:18
  235.9 17.7 %collective-permute-start.22 = (bf16[32,1152]{1,0:T(8,128)(2,1)S(1)}, bf16[32,1152]{1,0:T(8,128)(2,1)}, u32[]{:S(2)}, u32[]{:S(2)}) collective-permute-start(bf16[32,1152]{1,0:T(8,128)(2,1)S(1)} %dynamic-slice_bitcast_fusion.22), channel_id=1, source_target_pairs={{0,184},{4,188},{8,176},{12,180},{16,168},{20,172},{24,160},{28,16... | collective-permute-start | bytes 221192 | tf_op jit(solution)/shard_map/while/body/eval_jaxpr/cond/branch_23_fun/ppermute | solution.py:18
  261.6 1.2 copy-start.6
Sparse Core Ops, SparseCore 0:
  10.1 39.6 all-gather.8
  51.9 21.3 all-gather.10
  78.3 39.1 all-gather.12
  119.4 21.8 all-gather.14

commit v2 on v1

--- a/solution.py
+++ b/solution.py
@@ -27,8 +27,7 @@
     leaf_index = lax.axis_index(LEAF)
     piv = pivot_inverse.shape[1]
     share = pivot_inverse.shape[0]
-    upper_x = lax.all_gather(upper_block, "xh", axis=0)
-    upper_all = lax.all_gather(upper_x, "core", axis=0)
+    upper_all = lax.all_gather(upper_block, COLS, axis=0)
     order = pivot_perm[0]
     selector = (order[:, None] == lax.broadcasted_iota(jnp.int32, (piv, piv), 1)).astype(
         pivot_inverse.dtype
@@ -40,16 +39,15 @@
         jnp.bfloat16
     )
     eliminated = jnp.einsum(
-        "ip,cxpn->ixcn", inverse_perm, upper_all, preferred_element_type=jnp.float32
+        "ip,kpn->ikn", inverse_perm, upper_all, preferred_element_type=jnp.float32
     ).astype(jnp.bfloat16)
-    coupled_width = eliminated.shape[1] * eliminated.shape[2] * eliminated.shape[3]
+    coupled_width = eliminated.shape[1] * eliminated.shape[2]
     rows_out = jnp.concatenate([eliminated.reshape(share, coupled_width), forward], axis=1)
-    rows_x = lax.all_gather(rows_out, "xh", axis=0)
-    rows_all = lax.all_gather(rows_x, "core", axis=0)
+    rows_all = lax.all_gather(rows_out, COLS, axis=0)
     lower_rows = lower_block.shape[0]
     combined = -jnp.einsum(
-        "rxcp,cxpn->rn",
-        lower_block.reshape(lower_rows, 2, 2, share),
+        "rkp,kpn->rn",
+        lower_block.reshape(lower_rows, 4, share),
         rows_all,
         preferred_element_type=jnp.float32,
     )

time: 271 us -> 226 us (0.83)
  the two profiles are of different devices: /device:TPU:64 before, /device:TPU:1 now
where the time goes in v2:
time: 226 us; the launch traced here: 225 us
  waiting for transfers between devices  132 us (58%)
  starting transfers between devices  46.8 us (21%)
  between operations  14.3 us (6%)
  local copies, waits for them, and re-layouts  13.6 us (6%)
  matrix products  7.79 us (3%)
  other arithmetic  7.64 us (3%)
  loops' own time  2.96 us (1%)
    all_gather x1, waiting for transfers between devices, body(): upper_all = lax.all_gather(upper_block, COLS, axis=0)  42.5 us
    ppermute x4, starting transfers between devices, branch(): return lambda x: lax.ppermute(x, LEAF, pairs)  39.2 us
    all_gather x1, waiting for transfers between devices, body(): rows_all = lax.all_gather(rows_out, COLS, axis=0)  37.6 us
    ppermute x4, waiting for transfers between devices, branch(): return lambda x: lax.ppermute(x, LEAF, pairs)  31.4 us
    ppermute x1, waiting for transfers between devices, body(): lax.ppermute(other_rows, LEAF, [(s, s ^ 1) for s in range(leaf_count)])  13.1 us
    all_to_all x1, waiting for transfers between devices, body(): lax.all_to_all(moving.reshape(col_count, share_rows, moving.shape[1]), CO...  7.02 us
  transfers between devices with their start and end apart: 8, of which 8 were waited for; matrix products, arithmetic and copies ran while one was open for 2% of the time, Pallas kernels for 0%

profile of v2, /device:TPU:1, one launch (start us, length us, event | category | flops | bytes accessed | tf_op | source)
XLA Modules:
  0.0 225.4 jit_solution(9312667150855500014)
XLA Ops:
  7.2 0.0 copy-start
  7.2 0.0 all-gather.5.cloned.1.call-start
  7.2 0.7 all-gather.5.cloned.1.call-update
  7.9 0.0 all-gather.7.cloned.1.call-start
  8.0 0.7 reduce
  8.7 0.0 copy-done
  8.7 0.0 copy-start.5
  8.7 1.5 fusion.3
  10.2 0.0 copy-done.5
  10.3 0.4 convolution_convert_fusion.1
  10.6 0.0 copy-start.4
  10.7 42.5 %all-gather.5.cloned.1.call-done = bf16[5120,256]{1,0:T(8,128)(2,1)} async-done(((bf16[1280,256]{1,0:T(8,128)(2,1)}), bf16[5120,256]{1,0:T(8,128)(2,1)}) %all-gather.5.cloned.1.call-update) | async-done | bytes 2621456 | tf_op jit(solution)/shard_map/all_gather | solution.py:30
  53.1 2.7 %fusion.4 = bf16[4,40,8,256]{3,2,1,0:T(8,128)(2,1)S(1)} fusion(bf16[4,1280,256]{2,1,0:T(8,128)(2,1)} %bitcast.241, bf16[1280,320]{0,1:T(8,128)(2,1)S(1)} %fusion.3), kind=kOutput, calls=%fused_computation.74 | convolution fusion | flops 839188480 | bytes 4096000 | tf_op jit(solution)/shard_map/ip,kpn->ikn/dot_general | solution.py:41
  55.9 0.0 copy-start.3
  55.9 0.1 copy.19
  56.0 0.0 copy-done.4
  56.0 0.9 pad_maximum_fusion
  56.9 0.0 all-gather.7.cloned.1.call-update
  56.9 0.1 copy-done.3
  57.0 1.1 copy.14
  58.1 37.6 %all-gather.7.cloned.1.call-done = bf16[1280,1152]{1,0:T(8,128)(2,1)} async-done(((bf16[320,1152]{1,0:T(8,128)(2,1)}), bf16[1280,1152]{1,0:T(8,128)(2,1)}) %all-gather.7.cloned.1.call-update) | async-done | bytes 2949136 | tf_op jit(solution)/shard_map/all_gather | solution.py:46
  95.7 3.1 %fusion.2 = f32[1152,256]{0,1:T(8,128)S(1)} fusion(bf16[4,320,1152]{2,1,0:T(8,128)(2,1)} %bitcast.240, bf16[256,4,320]{0,2,1:T(8,128)(2,1)} %bitcast.239), kind=kOutput, calls=%fused_computation.70 | convolution fusion | flops 755269632 | bytes 4784128 | tf_op jit(solution)/shard_map/rkp,kpn->rn/dot_general | solution.py:48
  98.9 0.0 copy-start.1
  98.9 1.0 dynamic-slice_bitcast_fusion.63
  99.8 3.1 %collective-permute-start.63 = (f32[128,1152]{1,0:T(8,128)}, f32[128,1152]{1,0:T(8,128)}, u32[]{:S(2)}, u32[]{:S(2)}) collective-permute-start(f32[128,1152]{1,0:T(8,128)} %dynamic-slice_bitcast_fusion.63), channel_id=1, source_target_pairs={{0,4},{4,0},{8,12},{12,8},{16,20},{20,16},{24,28},{28,24},{32,36},... | collective-permute-start | bytes 1769480 | tf_op jit(solution)/shard_map/ppermute | solution.py:58
  103.0 0.0 copy-done.7
  103.0 0.1 xor_xor_fusion
  103.1 0.1 xor.61
  103.2 0.1 reshape.81
  103.3 0.0 copy-done.1
  103.3 0.2 copy.22
  103.6 13.1 %collective-permute-done.63 = f32[128,1152]{1,0:T(8,128)} collective-permute-done((f32[128,1152]{1,0:T(8,128)}, f32[128,1152]{1,0:T(8,128)}, u32[]{:S(2)}, u32[]{:S(2)}) %collective-permute-start.63) | collective-permute-done | bytes 589856 | tf_op jit(solution)/shard_map/ppermute | solution.py:58
  116.7 2.0 fusion.6
  118.7 4.5 %all-to-all-start = ((bf16[4,32,1152]{2,1,0:T(8,128)(2,1)}), bf16[4,32,1152]{2,1,0:T(8,128)(2,1)S(1)}, u32[]{:S(2)}, u32[]{:S(2)}) async-start(bf16[4,32,1152]{2,1,0:T(8,128)(2,1)} %bitcast.136), calls=%async_computation | async-start | bytes 589824 | tf_op jit(solution)/shard_map/all_to_all | solution.py:62
  123.2 7.0 %all-to-all-done = bf16[4,32,1152]{2,1,0:T(8,128)(2,1)S(1)} async-done(((bf16[4,32,1152]{2,1,0:T(8,128)(2,1)}), bf16[4,32,1152]{2,1,0:T(8,128)(2,1)S(1)}, u32[]{:S(2)}, u32[]{:S(2)}) %all-to-all-start) | async-done | bytes 294944 | tf_op jit(solution)/shard_map/all_to_all | solution.py:62
  130.2 79.5 %while.13 = (s32[]{:T(128)}, bf16[4,32,1152]{2,1,0:T(8,128)(2,1)S(1)}, s32[4]{0:T(128)S(1)}, bf16[4,32,1152]{2,1,0:T(8,128)(2,1)S(1)}, s32[]{:T(128)}, /*index=5*/s32[1]{0:T(128)}, s32[1]{0:T(128)}) while((s32[]{:T(128)}, bf16[4,32,1152]{2,1,0:T(8,128)(2,1)S(1)}, s32[4]{0:T(128)S(1)}, bf16[4,32,1152]{2,1,0:T(8,128)(2,1)S(1)}, s32[]{:T(128)}, ...), condition=%wide.region_65.66_spmd, body=%wide.region_0.65_spmd.sunk | while | flops 3 | bytes 590001 | solution.py:77
  130.2 0.6 dynamic_slice.342
  131.5 12.3 %conditional.2 = (bf16[1,32,1152]{2,1,0:T(8,128)(2,1)}) conditional(s32[]{:T(128)} %bitcast.232, (bf16[4,32,1152]{2,1,0:T(8,128)(2,1)S(1)}, s32[]{:T(128)}) %tuple.357, (bf16[4,32,1152]{2,1,0:T(8,128)(2,1)S(1)}, s32[]{:T(128)}) %tuple.357, (bf16[4,32,1152]{2,1,0:T(8,128)(2,1)S(1)}, s32[]{:T(128)}) %tuple.357, ...), branch_computations={%region_1.1_spmd, %region_2.2_spmd, %region_3.3_spmd, %region_4.4_... | conditional | bytes 442420 | solution.py:74
  131.6 10.1 %collective-permute-start.21 = (bf16[32,1152]{1,0:T(8,128)(2,1)S(1)}, bf16[32,1152]{1,0:T(8,128)(2,1)}, u32[]{:S(2)}, u32[]{:S(2)}) collective-permute-start(bf16[32,1152]{1,0:T(8,128)(2,1)S(1)} %dynamic-slice_bitcast_fusion.21), channel_id=1, source_target_pairs={{0,176},{4,180},{8,184},{12,188},{16,160},{20,164},{24,168},{28,17... | collective-permute-start | bytes 221192 | tf_op jit(solution)/shard_map/while/body/eval_jaxpr/cond/branch_22_fun/ppermute | solution.py:18
  141.7 2.1 collective-permute-done.21
  143.8 0.9 constant_dynamic-update-slice_fusion.2
  144.7 0.6 dynamic_slice.342
  145.9 20.4 %conditional.2 = (bf16[1,32,1152]{2,1,0:T(8,128)(2,1)}) conditional(s32[]{:T(128)} %bitcast.232, (bf16[4,32,1152]{2,1,0:T(8,128)(2,1)S(1)}, s32[]{:T(128)}) %tuple.357, (bf16[4,32,1152]{2,1,0:T(8,128)(2,1)S(1)}, s32[]{:T(128)}) %tuple.357, (bf16[4,32,1152]{2,1,0:T(8,128)(2,1)S(1)}, s32[]{:T(128)}) %tuple.357, ...), branch_computations={%region_1.1_spmd, %region_2.2_spmd, %region_3.3_spmd, %region_4.4_... | conditional | bytes 442420 | solution.py:74
  146.0 14.1 %collective-permute-start.8 = (bf16[32,1152]{1,0:T(8,128)(2,1)S(1)}, bf16[32,1152]{1,0:T(8,128)(2,1)}, u32[]{:S(2)}, u32[]{:S(2)}) collective-permute-start(bf16[32,1152]{1,0:T(8,128)(2,1)S(1)} %dynamic-slice_bitcast_fusion.8), channel_id=1, source_target_pairs={{0,72},{4,76},{8,64},{12,68},{16,88},{20,92},{24,80},{28,84},{32,1... | collective-permute-start | bytes 221192 | tf_op jit(solution)/shard_map/while/body/eval_jaxpr/cond/branch_9_fun/ppermute | solution.py:18
  160.1 6.2 %collective-permute-done.8 = bf16[32,1152]{1,0:T(8,128)(2,1)} collective-permute-done((bf16[32,1152]{1,0:T(8,128)(2,1)S(1)}, bf16[32,1152]{1,0:T(8,128)(2,1)}, u32[]{:S(2)}, u32[]{:S(2)}) %collective-permute-start.8) | collective-permute-done | bytes 73760 | tf_op jit(solution)/shard_map/while/body/eval_jaxpr/cond/branch_9_fun/ppermute | solution.py:18
  166.3 0.9 constant_dynamic-update-slice_fusion.2
  167.2 0.6 dynamic_slice.342
  168.4 30.0 %conditional.2 = (bf16[1,32,1152]{2,1,0:T(8,128)(2,1)}) conditional(s32[]{:T(128)} %bitcast.232, (bf16[4,32,1152]{2,1,0:T(8,128)(2,1)S(1)}, s32[]{:T(128)}) %tuple.357, (bf16[4,32,1152]{2,1,0:T(8,128)(2,1)S(1)}, s32[]{:T(128)}) %tuple.357, (bf16[4,32,1152]{2,1,0:T(8,128)(2,1)S(1)}, s32[]{:T(128)}) %tuple.357, ...), branch_computations={%region_1.1_spmd, %region_2.2_spmd, %region_3.3_spmd, %region_4.4_... | conditional | bytes 442420 | solution.py:74
  168.5 12.8 %collective-permute-start.62 = (bf16[32,1152]{1,0:T(8,128)(2,1)S(1)}, bf16[32,1152]{1,0:T(8,128)(2,1)}, u32[]{:S(2)}, u32[]{:S(2)}) collective-permute-start(bf16[32,1152]{1,0:T(8,128)(2,1)S(1)} %dynamic-slice_bitcast_fusion.62), channel_id=1, source_target_pairs={{0,504},{4,508},{8,496},{12,500},{16,488},{20,492},{24,480},{28,48... | collective-permute-start | bytes 221192 | tf_op jit(solution)/shard_map/while/body/eval_jaxpr/cond/branch_63_fun/ppermute | solution.py:18
  181.3 17.1 %collective-permute-done.62 = bf16[32,1152]{1,0:T(8,128)(2,1)} collective-permute-done((bf16[32,1152]{1,0:T(8,128)(2,1)S(1)}, bf16[32,1152]{1,0:T(8,128)(2,1)}, u32[]{:S(2)}, u32[]{:S(2)}) %collective-permute-start.62) | collective-permute-done | bytes 73760 | tf_op jit(solution)/shard_map/while/body/eval_jaxpr/cond/branch_63_fun/ppermute | solution.py:18
  198.4 0.9 constant_dynamic-update-slice_fusion.2
  199.3 0.6 dynamic_slice.342
  200.6 8.2 %conditional.2 = (bf16[1,32,1152]{2,1,0:T(8,128)(2,1)}) conditional(s32[]{:T(128)} %bitcast.232, (bf16[4,32,1152]{2,1,0:T(8,128)(2,1)S(1)}, s32[]{:T(128)}) %tuple.357, (bf16[4,32,1152]{2,1,0:T(8,128)(2,1)S(1)}, s32[]{:T(128)}) %tuple.357, (bf16[4,32,1152]{2,1,0:T(8,128)(2,1)S(1)}, s32[]{:T(128)}) %tuple.357, ...), branch_computations={%region_1.1_spmd, %region_2.2_spmd, %region_3.3_spmd, %region_4.4_... | conditional | bytes 442420 | solution.py:74
  200.6 2.2 collective-permute-start.3
  202.8 6.0 %collective-permute-done.3 = bf16[32,1152]{1,0:T(8,128)(2,1)} collective-permute-done((bf16[32,1152]{1,0:T(8,128)(2,1)S(1)}, bf16[32,1152]{1,0:T(8,128)(2,1)}, u32[]{:S(2)}, u32[]{:S(2)}) %collective-permute-start.3) | collective-permute-done | bytes 73760 | tf_op jit(solution)/shard_map/while/body/eval_jaxpr/cond/branch_4_fun/ppermute | solution.py:18
  208.8 0.9 constant_dynamic-update-slice_fusion.2
  209.7 0.8 slice_convert_fusion
  210.6 2.1 reshape.84
  212.7 1.9 copy.15
  214.6 2.2 scatter_fusion
  216.8 0.0 copy-start.6
  216.8 0.2 convert_bitcast_fusion
  217.0 1.0 copy.20
  218.0 0.6 convert_add_fusion
  (12 shorter events, 0.1 us)
Async XLA Ops:
  7.2 1.5 copy-start
  7.2 45.9 %all-gather.5.cloned.1.call-start = ((), (), s32[]{:S(2)}) async-start(), calls=%async_computation.1 | async-start | bytes 3276800 | tf_op jit(solution)/shard_map/all_gather | solution.py:30
  7.9 87.8 %all-gather.7.cloned.1.call-start = ((), (), s32[]{:S(2)}) async-start(), calls=%async_computation.2 | async-start | bytes 3686400 | tf_op jit(solution)/shard_map/all_gather | solution.py:46
  8.7 1.6 copy-start.5
  10.6 45.3 %copy-start.4 = (bf16[320,128]{1,0:T(8,128)(2,1)}, bf16[320,128]{1,0:T(8,128)(2,1)S(1)}, u32[]{:S(2)}) copy-start(bf16[320,128]{1,0:T(8,128)(2,1)S(1)} %convolution_convert_fusion.1) | copy-start | bytes 245764
  55.9 1.1 copy-start.3
  95.7 7.3 %copy-start.7 = (s32[1,4]{1,0:T(1,128)S(1)}, s32[1,4]{1,0:T(1,128)}, u32[]{:S(2)}) copy-start(s32[1,4]{1,0:T(1,128)} %param.79) | copy-start | bytes 52
  95.7 7.4 %copy-start.2 = (bf16[32,16384]{1,0:T(8,128)(2,1)S(1)}, bf16[32,16384]{1,0:T(8,128)(2,1)}, u32[]{:S(2)}) copy-start(bf16[32,16384]{1,0:T(8,128)(2,1)} %param.80) | copy-start | bytes 3145732
  98.9 4.5 %copy-start.1 = (f32[1152,256]{0,1:T(8,128)}, f32[1152,256]{0,1:T(8,128)S(1)}, u32[]{:S(2)}) copy-start(f32[1152,256]{0,1:T(8,128)S(1)} %fusion.2) | copy-start | bytes 3538948
  99.8 16.9 %collective-permute-start.63 = (f32[128,1152]{1,0:T(8,128)}, f32[128,1152]{1,0:T(8,128)}, u32[]{:S(2)}, u32[]{:S(2)}) collective-permute-start(f32[128,1152]{1,0:T(8,128)} %dynamic-slice_bitcast_fusion.63), channel_id=1, source_target_pairs={{0,4},{4,0},{8,12},{12,8},{16,20},{20,16},{24,28},{28,24},{32,36},... | collective-permute-start | bytes 1769480 | tf_op jit(solution)/shard_map/ppermute | solution.py:58
  118.7 11.5 %all-to-all-start = ((bf16[4,32,1152]{2,1,0:T(8,128)(2,1)}), bf16[4,32,1152]{2,1,0:T(8,128)(2,1)S(1)}, u32[]{:S(2)}, u32[]{:S(2)}) async-start(bf16[4,32,1152]{2,1,0:T(8,128)(2,1)} %bitcast.136), calls=%async_computation | async-start | bytes 589824 | tf_op jit(solution)/shard_map/all_to_all | solution.py:62
  131.6 12.2 %collective-permute-start.21 = (bf16[32,1152]{1,0:T(8,128)(2,1)S(1)}, bf16[32,1152]{1,0:T(8,128)(2,1)}, u32[]{:S(2)}, u32[]{:S(2)}) collective-permute-start(bf16[32,1152]{1,0:T(8,128)(2,1)S(1)} %dynamic-slice_bitcast_fusion.21), channel_id=1, source_target_pairs={{0,176},{4,180},{8,184},{12,188},{16,160},{20,164},{24,168},{28,17... | collective-permute-start | bytes 221192 | tf_op jit(solution)/shard_map/while/body/eval_jaxpr/cond/branch_22_fun/ppermute | solution.py:18
  146.0 20.3 %collective-permute-start.8 = (bf16[32,1152]{1,0:T(8,128)(2,1)S(1)}, bf16[32,1152]{1,0:T(8,128)(2,1)}, u32[]{:S(2)}, u32[]{:S(2)}) collective-permute-start(bf16[32,1152]{1,0:T(8,128)(2,1)S(1)} %dynamic-slice_bitcast_fusion.8), channel_id=1, source_target_pairs={{0,72},{4,76},{8,64},{12,68},{16,88},{20,92},{24,80},{28,84},{32,1... | collective-permute-start | bytes 221192 | tf_op jit(solution)/shard_map/while/body/eval_jaxpr/cond/branch_9_fun/ppermute | solution.py:18
  168.5 29.9 %collective-permute-start.62 = (bf16[32,1152]{1,0:T(8,128)(2,1)S(1)}, bf16[32,1152]{1,0:T(8,128)(2,1)}, u32[]{:S(2)}, u32[]{:S(2)}) collective-permute-start(bf16[32,1152]{1,0:T(8,128)(2,1)S(1)} %dynamic-slice_bitcast_fusion.62), channel_id=1, source_target_pairs={{0,504},{4,508},{8,496},{12,500},{16,488},{20,492},{24,480},{28,48... | collective-permute-start | bytes 221192 | tf_op jit(solution)/shard_map/while/body/eval_jaxpr/cond/branch_63_fun/ppermute | solution.py:18
  200.6 8.2 %collective-permute-start.3 = (bf16[32,1152]{1,0:T(8,128)(2,1)S(1)}, bf16[32,1152]{1,0:T(8,128)(2,1)}, u32[]{:S(2)}, u32[]{:S(2)}) collective-permute-start(bf16[32,1152]{1,0:T(8,128)(2,1)S(1)} %dynamic-slice_bitcast_fusion.3), channel_id=1, source_target_pairs={{0,32},{4,36},{8,40},{12,44},{16,48},{20,52},{24,56},{28,60},{32,0... | collective-permute-start | bytes 221192 | tf_op jit(solution)/shard_map/while/body/eval_jaxpr/cond/branch_4_fun/ppermute | solution.py:18
  216.8 1.2 copy-start.6
Sparse Core Ops, SparseCore 0:
  10.1 42.9 all-gather.4
  57.0 38.6 all-gather.6

commit v3 on v2

--- a/solution.py
+++ b/solution.py
@@ -20,6 +20,18 @@
     return [branch(2 * step) for step in range(mask_count)]
 
 
+def col_gather(block):
+    remote = lax.ppermute(block, COLS, [(c, c ^ 2) for c in range(4)])
+    chip = jnp.stack([block, remote])
+    partner = lax.ppermute(chip, COLS, [(c, c ^ 1) for c in range(4)])
+    return jnp.concatenate([chip, partner])
+
+
+def relative_order(col_index):
+    flipped = jnp.bitwise_xor(jnp.arange(4, dtype=jnp.int32), col_index)
+    return (flipped % 2) * 2 + flipped // 2
+
+
 def body(
     upper_block, lower_block, pivot_inverse, pivot_perm, child_rhs, pattern, root_front, root_rhs
 ):
@@ -27,7 +39,8 @@
     leaf_index = lax.axis_index(LEAF)
     piv = pivot_inverse.shape[1]
     share = pivot_inverse.shape[0]
-    upper_all = lax.all_gather(upper_block, COLS, axis=0)
+    col_index = lax.axis_index(COLS)
+    upper_all = col_gather(upper_block)
     order = pivot_perm[0]
     selector = (order[:, None] == lax.broadcasted_iota(jnp.int32, (piv, piv), 1)).astype(
         pivot_inverse.dtype
@@ -38,12 +51,14 @@
     forward = jnp.dot(inverse_perm, child_rhs, preferred_element_type=jnp.float32).astype(
         jnp.bfloat16
     )
+    canonical = relative_order(col_index)
     eliminated = jnp.einsum(
-        "ip,kpn->ikn", inverse_perm, upper_all, preferred_element_type=jnp.float32
+        "ip,kpn->ikn", inverse_perm, jnp.take(upper_all, canonical, axis=0),
+        preferred_element_type=jnp.float32,
     ).astype(jnp.bfloat16)
     coupled_width = eliminated.shape[1] * eliminated.shape[2]
     rows_out = jnp.concatenate([eliminated.reshape(share, coupled_width), forward], axis=1)
-    rows_all = lax.all_gather(rows_out, COLS, axis=0)
+    rows_all = jnp.take(col_gather(rows_out), canonical, axis=0)
     lower_rows = lower_block.shape[0]
     combined = -jnp.einsum(
         "rkp,kpn->rn",

time: 226 us -> 206 us (0.912); the launches traced: 225 us -> 202 us
  waiting for transfers between devices: 132 us -> 82.3 us
  starting transfers between devices: 46.8 us -> 71.4 us
  between operations: 14.3 us -> 0.98 us
  local copies, waits for them, and re-layouts: 13.6 us -> 23 us
  other arithmetic: 7.64 us -> 13.4 us
    all_gather x2 -> x0, waiting for transfers between devices: 80.1 us -> none  [the longest x1 42.5 us: body(): upper_all = lax.all_gather(upper_block, COLS, axis=0)]
    ppermute x0 -> x4, waiting for transfers between devices: none -> 29.8 us  [the longest x2 27.5 us: col_gather(): remote = lax.ppermute(block, COLS, [(c, c ^ 2) for c in range(4)])]
    ppermute x0 -> x4, starting transfers between devices: none -> 20.2 us  [the longest x2 10.6 us: col_gather(): remote = lax.ppermute(block, COLS, [(c, c ^ 2) for c in range(4)])]
    gather x0 -> x2, local copies, waits for them, and re-layouts: none -> 6.58 us  [the longest x1 4.39 us: body(): rows_all = jnp.take(col_gather(rows_out), canonical, axis=0)]
    concatenate x1 -> x2, other arithmetic: 0.92 us -> 4.87 us  [col_gather(): return jnp.concatenate([chip, partner])]
    ppermute x4, starting transfers between devices: 39.2 us -> 42.2 us  [branch(): return lambda x: lax.ppermute(x, LEAF, pairs)]
    another operation x0 -> x3, other arithmetic: none -> 2.6 us  [col_gather(): chip = jnp.stack([block, remote])]
    dynamic_update_slice x4, local copies, waits for them, and re-layouts: 3.59 us -> 6.06 us  [route_piece(): return lax.dynamic_update_index_in_dim(routed, sent, a, 0)]
  transfers between devices with their start and end apart: 8 -> 10, of which waited for: 8 -> 10; matrix products, arithmetic and copies ran while one was open for 2% -> 2% of each run, Pallas kernels for 0% -> 0%
where the time goes in v3:
time: 206 us; the launch traced here: 202 us
  waiting for transfers between devices  82.3 us (40%)
  starting transfers between devices  71.4 us (35%)
  local copies, waits for them, and re-layouts  23 us (11%)
  other arithmetic  13.4 us (7%)
  matrix products  8.05 us (4%)
  loops' own time  2.91 us (1%)
    ppermute x4, starting transfers between devices, branch(): return lambda x: lax.ppermute(x, LEAF, pairs)  42.2 us
    ppermute x4, waiting for transfers between devices, branch(): return lambda x: lax.ppermute(x, LEAF, pairs)  32.8 us
    ppermute x2, waiting for transfers between devices, col_gather(): remote = lax.ppermute(block, COLS, [(c, c ^ 2) for c in range(4)])  27.5 us
    ppermute x1, waiting for transfers between devices, body(): lax.ppermute(other_rows, LEAF, [(s, s ^ 1) for s in range(leaf_count)])  12.7 us
    ppermute x2, starting transfers between devices, col_gather(): remote = lax.ppermute(block, COLS, [(c, c ^ 2) for c in range(4)])  10.6 us
    ppermute x2, starting transfers between devices, col_gather(): partner = lax.ppermute(chip, COLS, [(c, c ^ 1) for c in range(4)])  9.61 us
    all_to_all x1, waiting for transfers between devices, body(): lax.all_to_all(moving.reshape(col_count, share_rows, moving.shape[1]), CO...  7.02 us
    dynamic_update_slice x4, local copies, waits for them, and re-layouts, route_piece(): return lax.dynamic_update_index_in_dim(routed, sent, a, 0)  6.06 us
  transfers between devices with their start and end apart: 10, of which 10 were waited for; matrix products, arithmetic and copies ran while one was open for 2% of the time, Pallas kernels for 0%

profile of v3, /device:TPU:1, one launch (start us, length us, event | category | flops | bytes accessed | tf_op | source)
XLA Modules:
  0.0 202.1 jit_solution(811740655721610279)
XLA Ops:
  0.6 0.0 copy-start
  0.7 5.6 %collective-permute-start.63 = (bf16[1280,256]{1,0:T(8,128)(2,1)}, bf16[1280,256]{1,0:T(8,128)(2,1)S(1)}, u32[]{:S(2)}, u32[]{:S(2)}) collective-permute-start(bf16[1280,256]{1,0:T(8,128)(2,1)} %param.74), channel_id=1, source_target_pairs={{0,2},{1,3},{2,0},{3,1},{4,6},{5,7},{6,4},{7,5},{8,10},{9,11},{10,... | collective-permute-start | bytes 1966088 | tf_op jit(solution)/shard_map/ppermute | solution.py:24
  6.3 11.3 %collective-permute-done.63 = bf16[1280,256]{1,0:T(8,128)(2,1)S(1)} collective-permute-done((bf16[1280,256]{1,0:T(8,128)(2,1)}, bf16[1280,256]{1,0:T(8,128)(2,1)S(1)}, u32[]{:S(2)}, u32[]{:S(2)}) %collective-permute-start.63) | collective-permute-done | bytes 655392 | tf_op jit(solution)/shard_map/ppermute | solution.py:24
  17.6 0.8 copy-done.2
  18.4 1.2 pad_maximum_fusion.3
  19.6 6.5 %collective-permute-start.64 = (bf16[2,1280,256]{2,1,0:T(8,128)(2,1)S(1)}, bf16[2,1280,256]{2,1,0:T(8,128)(2,1)}, u32[]{:S(2)}, u32[]{:S(2)}) collective-permute-start(bf16[2,1280,256]{2,1,0:T(8,128)(2,1)S(1)} %pad_maximum_fusion.3), channel_id=1, source_target_pairs={{0,1},{1,0},{2,3},{3,2},{4,5},{5,4},{6,7},{7,6},{8,9},{9,8},{10,11... | collective-permute-start | bytes 3932168 | tf_op jit(solution)/shard_map/ppermute | solution.py:26
  26.3 1.5 fusion.8
  27.8 0.4 convolution_convert_fusion
  28.2 0.5 copy-done.6
  28.7 0.2 collective-permute-done.64
  28.9 1.6 pad_maximum_fusion.1
  30.5 2.2 %gather_fusion = bf16[4,1280,256]{2,1,0:T(8,128)(2,1)} fusion(bf16[4,1280,256]{2,1,0:T(8,128)(2,1)S(1)} %pad_maximum_fusion.1, s32[1024]{0:T(1024)S(1)} %pad_clamp_fusion), kind=kCustom, calls=%fused_computation | custom fusion | bytes 5242896 | tf_op jit(solution)/shard_map/jit(_take)/gather | solution.py:56
  32.7 3.1 %fusion.20 = bf16[4,40,8,256]{3,2,1,0:T(8,128)(2,1)S(1)} fusion(bf16[4,1280,256]{2,1,0:T(8,128)(2,1)} %gather_fusion, pred[4]{0:T(512)(128)(4,1)S(1)} %compare_and_fusion, bf16[1280,320]{0,1:T(8,128)(2,1)} %copy-done.6), kind=kOutput, calls=%fused_computation.88 | convolution fusion | flops 840499200 | bytes 4096004 | tf_op jit(solution)/shard_map/ip,kpn->ikn/dot_general | solution.py:55
  35.8 0.1 copy.19
  35.9 0.1 fusion.33
  36.0 5.0 %collective-permute-start.65 = (bf16[320,1152]{1,0:T(8,128)(2,1)S(1)}, bf16[320,1152]{1,0:T(8,128)(2,1)S(1)}, u32[]{:S(2)}, u32[]{:S(2)}) collective-permute-start(bf16[320,1152]{1,0:T(8,128)(2,1)S(1)} %get-tuple-element.739), channel_id=1, source_target_pairs={{0,2},{1,3},{2,0},{3,1},{4,6},{5,7},{6,4},{7,5},{8,10},{9,11},{10,... | collective-permute-start | bytes 2211848 | tf_op jit(solution)/shard_map/ppermute | solution.py:24
  41.0 16.2 %collective-permute-done.65 = bf16[320,1152]{1,0:T(8,128)(2,1)S(1)} collective-permute-done((bf16[320,1152]{1,0:T(8,128)(2,1)S(1)}, bf16[320,1152]{1,0:T(8,128)(2,1)S(1)}, u32[]{:S(2)}, u32[]{:S(2)}) %collective-permute-start.65) | collective-permute-done | bytes 737312 | tf_op jit(solution)/shard_map/ppermute | solution.py:24
  57.2 1.3 pad_maximum_fusion.2
  58.5 3.1 %collective-permute-start.66 = (bf16[2,320,1152]{2,1,0:T(8,128)(2,1)}, bf16[2,320,1152]{2,1,0:T(8,128)(2,1)}, u32[]{:S(2)}, u32[]{:S(2)}) collective-permute-start(bf16[2,320,1152]{2,1,0:T(8,128)(2,1)} %pad_maximum_fusion.2), channel_id=1, source_target_pairs={{0,1},{1,0},{2,3},{3,2},{4,5},{5,4},{6,7},{7,6},{8,9},{9,8},{10,11... | collective-permute-start | bytes 4423688 | tf_op jit(solution)/shard_map/ppermute | solution.py:26
  61.7 1.1 copy.14
  62.7 2.1 %collective-permute-done.66 = bf16[2,320,1152]{2,1,0:T(8,128)(2,1)} collective-permute-done((bf16[2,320,1152]{2,1,0:T(8,128)(2,1)}, bf16[2,320,1152]{2,1,0:T(8,128)(2,1)}, u32[]{:S(2)}, u32[]{:S(2)}) %collective-permute-start.66) | collective-permute-done | bytes 1474592 | tf_op jit(solution)/shard_map/ppermute | solution.py:26
  64.9 3.3 %pad_maximum_fusion = bf16[4,320,1152]{2,1,0:T(8,128)(2,1)} fusion(bf16[2,320,1152]{2,1,0:T(8,128)(2,1)} %collective-permute-done.66, bf16[1,320,1152]{2,1,0:T(8,128)(2,1)S(1)} %bitcast.239, bf16[1,320,1152]{2,1,0:T(8,128)(2,1)S(1)} %get-tuple-element.738), kind=kLoop, calls=%fused_computation.71 | loop fusion | flops 2949120 | bytes 5898240 | tf_op jit(solution)/shard_map/concatenate | solution.py:27
  68.2 4.4 %gather_fusion.1 = bf16[4,320,1152]{2,1,0:T(8,128)(2,1)} fusion(bf16[4,320,1152]{2,1,0:T(8,128)(2,1)} %pad_maximum_fusion, s32[1024]{0:T(1024)S(1)} %pad_clamp_fusion), kind=kCustom, calls=%fused_computation.1 | custom fusion | bytes 5898256 | tf_op jit(solution)/shard_map/jit(_take)/gather | solution.py:61
  72.5 3.0 %fusion.9 = f32[1152,256]{0,1:T(8,128)S(1)} fusion(bf16[256,4,320]{0,2,1:T(8,128)(2,1)S(1)} %bitcast.248, bf16[4,320,1152]{2,1,0:T(8,128)(2,1)} %gather_fusion.1, pred[4]{0:T(512)(128)(4,1)S(1)} %compare_and_fusion), kind=kOutput, calls=%fused_computation.77 | convolution fusion | flops 756744192 | bytes 4784132 | tf_op jit(solution)/shard_map/rkp,kpn->rn/dot_general | solution.py:63
  75.6 1.0 copy-done.4
  76.6 0.9 dynamic-slice_bitcast_fusion.63
  77.5 3.4 %collective-permute-start.67 = (f32[128,1152]{1,0:T(8,128)}, f32[128,1152]{1,0:T(8,128)S(1)}, u32[]{:S(2)}, u32[]{:S(2)}) collective-permute-start(f32[128,1152]{1,0:T(8,128)} %dynamic-slice_bitcast_fusion.63), channel_id=1, source_target_pairs={{0,4},{4,0},{8,12},{12,8},{16,20},{20,16},{24,28},{28,24},{32,36},... | collective-permute-start | bytes 1769480 | tf_op jit(solution)/shard_map/ppermute | solution.py:73
  80.9 0.1 xor_xor_fusion
  81.0 0.1 xor.80
  81.1 0.1 reshape.172
  81.2 0.2 copy.22
  81.5 12.7 %collective-permute-done.67 = f32[128,1152]{1,0:T(8,128)S(1)} collective-permute-done((f32[128,1152]{1,0:T(8,128)}, f32[128,1152]{1,0:T(8,128)S(1)}, u32[]{:S(2)}, u32[]{:S(2)}) %collective-permute-start.67) | collective-permute-done | bytes 589856 | tf_op jit(solution)/shard_map/ppermute | solution.py:73
  94.2 1.8 fusion.24
  96.0 5.6 %all-to-all-start = ((bf16[4,32,1152]{2,1,0:T(8,128)(2,1)}), bf16[4,32,1152]{2,1,0:T(8,128)(2,1)S(1)}, u32[]{:S(2)}, u32[]{:S(2)}) async-start(bf16[4,32,1152]{2,1,0:T(8,128)(2,1)} %bitcast.139), calls=%async_computation | async-start | bytes 589824 | tf_op jit(solution)/shard_map/all_to_all | solution.py:77
  101.6 7.0 %all-to-all-done = bf16[4,32,1152]{2,1,0:T(8,128)(2,1)S(1)} async-done(((bf16[4,32,1152]{2,1,0:T(8,128)(2,1)}), bf16[4,32,1152]{2,1,0:T(8,128)(2,1)S(1)}, u32[]{:S(2)}, u32[]{:S(2)}) %all-to-all-start) | async-done | bytes 294944 | tf_op jit(solution)/shard_map/all_to_all | solution.py:77
  108.7 86.3 %while.13 = (s32[]{:T(128)}, bf16[4,32,1152]{2,1,0:T(8,128)(2,1)}, s32[4]{0:T(128)S(1)}, bf16[4,32,1152]{2,1,0:T(8,128)(2,1)S(1)}, s32[]{:T(128)}, /*index=5*/s32[1]{0:T(128)}, s32[1]{0:T(128)}) while((s32[]{:T(128)}, bf16[4,32,1152]{2,1,0:T(8,128)(2,1)}, s32[4]{0:T(128)S(1)}, bf16[4,32,1152]{2,1,0:T(8,128)(2,1)S(1)}, s32[]{:T(128)}, ...), condition=%wide.region_65.66_spmd, body=%wide.region_0.65_spmd.sunk | while | flops 3 | bytes 590509 | solution.py:92
  108.7 0.6 dynamic_slice.342
  109.9 23.6 %conditional.2 = (bf16[1,32,1152]{2,1,0:T(8,128)(2,1)}) conditional(s32[]{:T(128)} %bitcast.235, (bf16[4,32,1152]{2,1,0:T(8,128)(2,1)S(1)}, s32[]{:T(128)}) %tuple.358, (bf16[4,32,1152]{2,1,0:T(8,128)(2,1)S(1)}, s32[]{:T(128)}) %tuple.358, (bf16[4,32,1152]{2,1,0:T(8,128)(2,1)S(1)}, s32[]{:T(128)}) %tuple.358, ...), branch_computations={%region_1.1_spmd, %region_2.2_spmd, %region_3.3_spmd, %region_4.4_... | conditional | bytes 442420 | solution.py:89
  110.0 18.7 %collective-permute-start.33 = (bf16[32,1152]{1,0:T(8,128)(2,1)S(1)}, bf16[32,1152]{1,0:T(8,128)(2,1)}, u32[]{:S(2)}, u32[]{:S(2)}) collective-permute-start(bf16[32,1152]{1,0:T(8,128)(2,1)S(1)} %dynamic-slice_bitcast_fusion.33), channel_id=1, source_target_pairs={{0,272},{4,276},{8,280},{12,284},{16,256},{20,260},{24,264},{28,26... | collective-permute-start | bytes 221192 | tf_op jit(solution)/shard_map/while/body/eval_jaxpr/cond/branch_34_fun/ppermute | solution.py:18
  128.6 4.8 %collective-permute-done.33 = bf16[32,1152]{1,0:T(8,128)(2,1)} collective-permute-done((bf16[32,1152]{1,0:T(8,128)(2,1)S(1)}, bf16[32,1152]{1,0:T(8,128)(2,1)}, u32[]{:S(2)}, u32[]{:S(2)}) %collective-permute-start.33) | collective-permute-done | bytes 73760 | tf_op jit(solution)/shard_map/while/body/eval_jaxpr/cond/branch_34_fun/ppermute | solution.py:18
  133.5 1.5 constant_dynamic-update-slice_fusion.2
  135.0 0.6 dynamic_slice.342
  136.2 5.3 %conditional.2 = (bf16[1,32,1152]{2,1,0:T(8,128)(2,1)}) conditional(s32[]{:T(128)} %bitcast.235, (bf16[4,32,1152]{2,1,0:T(8,128)(2,1)S(1)}, s32[]{:T(128)}) %tuple.358, (bf16[4,32,1152]{2,1,0:T(8,128)(2,1)S(1)}, s32[]{:T(128)}) %tuple.358, (bf16[4,32,1152]{2,1,0:T(8,128)(2,1)S(1)}, s32[]{:T(128)}) %tuple.358, ...), branch_computations={%region_1.1_spmd, %region_2.2_spmd, %region_3.3_spmd, %region_4.4_... | conditional | bytes 442420 | solution.py:89
  136.3 2.2 %collective-permute-start.31 = (bf16[32,1152]{1,0:T(8,128)(2,1)S(1)}, bf16[32,1152]{1,0:T(8,128)(2,1)}, u32[]{:S(2)}, u32[]{:S(2)}) collective-permute-start(bf16[32,1152]{1,0:T(8,128)(2,1)S(1)} %dynamic-slice_bitcast_fusion.31), channel_id=1, source_target_pairs={{0,256},{4,260},{8,264},{12,268},{16,272},{20,276},{24,280},{28,28... | collective-permute-start | bytes 221192 | tf_op jit(solution)/shard_map/while/body/eval_jaxpr/cond/branch_32_fun/ppermute | solution.py:18
  138.5 3.0 %collective-permute-done.31 = bf16[32,1152]{1,0:T(8,128)(2,1)} collective-permute-done((bf16[32,1152]{1,0:T(8,128)(2,1)S(1)}, bf16[32,1152]{1,0:T(8,128)(2,1)}, u32[]{:S(2)}, u32[]{:S(2)}) %collective-permute-start.31) | collective-permute-done | bytes 73760 | tf_op jit(solution)/shard_map/while/body/eval_jaxpr/cond/branch_32_fun/ppermute | solution.py:18
  141.5 1.5 constant_dynamic-update-slice_fusion.2
  143.0 0.6 dynamic_slice.342
  144.3 34.8 %conditional.2 = (bf16[1,32,1152]{2,1,0:T(8,128)(2,1)}) conditional(s32[]{:T(128)} %bitcast.235, (bf16[4,32,1152]{2,1,0:T(8,128)(2,1)S(1)}, s32[]{:T(128)}) %tuple.358, (bf16[4,32,1152]{2,1,0:T(8,128)(2,1)S(1)}, s32[]{:T(128)}) %tuple.358, (bf16[4,32,1152]{2,1,0:T(8,128)(2,1)S(1)}, s32[]{:T(128)}) %tuple.358, ...), branch_computations={%region_1.1_spmd, %region_2.2_spmd, %region_3.3_spmd, %region_4.4_... | conditional | bytes 442420 | solution.py:89
  144.3 19.4 %collective-permute-start.58 = (bf16[32,1152]{1,0:T(8,128)(2,1)S(1)}, bf16[32,1152]{1,0:T(8,128)(2,1)}, u32[]{:S(2)}, u32[]{:S(2)}) collective-permute-start(bf16[32,1152]{1,0:T(8,128)(2,1)S(1)} %dynamic-slice_bitcast_fusion.58), channel_id=1, source_target_pairs={{0,472},{4,476},{8,464},{12,468},{16,456},{20,460},{24,448},{28,45... | collective-permute-start | bytes 221192 | tf_op jit(solution)/shard_map/while/body/eval_jaxpr/cond/branch_59_fun/ppermute | solution.py:18
  163.8 15.3 %collective-permute-done.58 = bf16[32,1152]{1,0:T(8,128)(2,1)} collective-permute-done((bf16[32,1152]{1,0:T(8,128)(2,1)S(1)}, bf16[32,1152]{1,0:T(8,128)(2,1)}, u32[]{:S(2)}, u32[]{:S(2)}) %collective-permute-start.58) | collective-permute-done | bytes 73760 | tf_op jit(solution)/shard_map/while/body/eval_jaxpr/cond/branch_59_fun/ppermute | solution.py:18
  179.1 1.5 constant_dynamic-update-slice_fusion.2
  180.6 0.6 dynamic_slice.342
  181.8 11.6 %conditional.2 = (bf16[1,32,1152]{2,1,0:T(8,128)(2,1)}) conditional(s32[]{:T(128)} %bitcast.235, (bf16[4,32,1152]{2,1,0:T(8,128)(2,1)S(1)}, s32[]{:T(128)}) %tuple.358, (bf16[4,32,1152]{2,1,0:T(8,128)(2,1)S(1)}, s32[]{:T(128)}) %tuple.358, (bf16[4,32,1152]{2,1,0:T(8,128)(2,1)S(1)}, s32[]{:T(128)}) %tuple.358, ...), branch_computations={%region_1.1_spmd, %region_2.2_spmd, %region_3.3_spmd, %region_4.4_... | conditional | bytes 442420 | solution.py:89
  181.9 1.9 collective-permute-start.24
  183.8 9.6 %collective-permute-done.24 = bf16[32,1152]{1,0:T(8,128)(2,1)} collective-permute-done((bf16[32,1152]{1,0:T(8,128)(2,1)S(1)}, bf16[32,1152]{1,0:T(8,128)(2,1)}, u32[]{:S(2)}, u32[]{:S(2)}) %collective-permute-start.24) | collective-permute-done | bytes 73760 | tf_op jit(solution)/shard_map/while/body/eval_jaxpr/cond/branch_25_fun/ppermute | solution.py:18
  193.4 1.5 constant_dynamic-update-slice_fusion.2
  195.0 1.0 slice_convert_fusion
  196.0 0.8 convert_reduce_fusion
  196.7 1.0 reshape.175
  197.8 1.1 copy.15
  198.9 1.3 scatter_fusion
  200.3 0.2 convert_bitcast_fusion
  200.4 1.0 copy.20
  201.5 0.6 convert_add_fusion
  (35 shorter events, 0.2 us)
Async XLA Ops:
  0.6 25.6 %copy-start = (bf16[320,1280]{1,0:T(8,128)(2,1)S(1)}, bf16[320,1280]{1,0:T(8,128)(2,1)}, u32[]{:S(2)}) copy-start(bf16[320,1280]{1,0:T(8,128)(2,1)} %param.76) | copy-start | bytes 2457604
  0.6 25.5 %copy-start.12 = (s32[1,1280]{1,0:T(1,128)S(1)}, s32[1,1280]{1,0:T(1,128)}, u32[]{:S(2)}) copy-start(s32[1,1280]{1,0:T(1,128)} %param.77) | copy-start | bytes 15364
  0.7 16.9 %collective-permute-start.63 = (bf16[1280,256]{1,0:T(8,128)(2,1)}, bf16[1280,256]{1,0:T(8,128)(2,1)S(1)}, u32[]{:S(2)}, u32[]{:S(2)}) collective-permute-start(bf16[1280,256]{1,0:T(8,128)(2,1)} %param.74), channel_id=1, source_target_pairs={{0,2},{1,3},{2,0},{3,1},{4,6},{5,7},{6,4},{7,5},{8,10},{9,11},{10,... | collective-permute-start | bytes 1966088 | tf_op jit(solution)/shard_map/ppermute | solution.py:24
  17.6 0.8 copy-start.2
  19.6 9.3 %collective-permute-start.64 = (bf16[2,1280,256]{2,1,0:T(8,128)(2,1)S(1)}, bf16[2,1280,256]{2,1,0:T(8,128)(2,1)}, u32[]{:S(2)}, u32[]{:S(2)}) collective-permute-start(bf16[2,1280,256]{2,1,0:T(8,128)(2,1)S(1)} %pad_maximum_fusion.3), channel_id=1, source_target_pairs={{0,1},{1,0},{2,3},{3,2},{4,5},{5,4},{6,7},{7,6},{8,9},{9,8},{10,11... | collective-permute-start | bytes 3932168 | tf_op jit(solution)/shard_map/ppermute | solution.py:26
  26.2 1.6 copy-start.10
  26.3 2.7 %copy-start.1 = (bf16[1280,256]{1,0:T(8,128)(2,1)S(1)}, bf16[1280,256]{1,0:T(8,128)(2,1)}, u32[]{:S(2)}) copy-start(bf16[1280,256]{1,0:T(8,128)(2,1)} %param.74) | copy-start | bytes 1966084
  26.3 2.6 %copy-start.3 = (bf16[1280,256]{1,0:T(8,128)(2,1)S(1)}, bf16[1280,256]{1,0:T(8,128)(2,1)}, u32[]{:S(2)}) copy-start(bf16[1280,256]{1,0:T(8,128)(2,1)} %copy-done.2) | copy-start | bytes 1966084
  27.8 0.9 copy-start.6
  28.7 7.2 %copy-start.9 = (bf16[320,128]{1,0:T(8,128)(2,1)}, bf16[320,128]{1,0:T(8,128)(2,1)S(1)}, u32[]{:S(2)}) copy-start(bf16[320,128]{1,0:T(8,128)(2,1)S(1)} %convolution_convert_fusion) | copy-start | bytes 245764
  35.9 25.8 %copy-start.7 = (bf16[256,1280]{1,0:T(8,128)(2,1)S(1)}, bf16[256,1280]{1,0:T(8,128)(2,1)}, u32[]{:S(2)}) copy-start(bf16[256,1280]{1,0:T(8,128)(2,1)} %param.75) | copy-start | bytes 1966084
  36.0 21.2 %collective-permute-start.65 = (bf16[320,1152]{1,0:T(8,128)(2,1)S(1)}, bf16[320,1152]{1,0:T(8,128)(2,1)S(1)}, u32[]{:S(2)}, u32[]{:S(2)}) collective-permute-start(bf16[320,1152]{1,0:T(8,128)(2,1)S(1)} %get-tuple-element.739), channel_id=1, source_target_pairs={{0,2},{1,3},{2,0},{3,1},{4,6},{5,7},{6,4},{7,5},{8,10},{9,11},{10,... | collective-permute-start | bytes 2211848 | tf_op jit(solution)/shard_map/ppermute | solution.py:24
  58.5 6.3 %collective-permute-start.66 = (bf16[2,320,1152]{2,1,0:T(8,128)(2,1)}, bf16[2,320,1152]{2,1,0:T(8,128)(2,1)}, u32[]{:S(2)}, u32[]{:S(2)}) collective-permute-start(bf16[2,320,1152]{2,1,0:T(8,128)(2,1)} %pad_maximum_fusion.2), channel_id=1, source_target_pairs={{0,1},{1,0},{2,3},{3,2},{4,5},{5,4},{6,7},{7,6},{8,9},{9,8},{10,11... | collective-permute-start | bytes 4423688 | tf_op jit(solution)/shard_map/ppermute | solution.py:26
  68.1 4.4 %copy-start.8 = (bf16[256,1280]{0,1:T(8,128)(2,1)S(1)}, bf16[256,1280]{0,1:T(8,128)(2,1)}, u32[]{:S(2)}) copy-start(bf16[256,1280]{0,1:T(8,128)(2,1)} %copy.14) | copy-start | bytes 1966084
  72.5 8.4 %copy-start.13 = (s32[1,4]{1,0:T(1,128)S(1)}, s32[1,4]{1,0:T(1,128)}, u32[]{:S(2)}) copy-start(s32[1,4]{1,0:T(1,128)} %param.79) | copy-start | bytes 52
  72.5 8.5 %copy-start.5 = (bf16[32,16384]{1,0:T(8,128)(2,1)S(1)}, bf16[32,16384]{1,0:T(8,128)(2,1)}, u32[]{:S(2)}) copy-start(bf16[32,16384]{1,0:T(8,128)(2,1)} %param.80) | copy-start | bytes 3145732
  75.6 1.0 copy-start.4
  77.5 16.7 %collective-permute-start.67 = (f32[128,1152]{1,0:T(8,128)}, f32[128,1152]{1,0:T(8,128)S(1)}, u32[]{:S(2)}, u32[]{:S(2)}) collective-permute-start(f32[128,1152]{1,0:T(8,128)} %dynamic-slice_bitcast_fusion.63), channel_id=1, source_target_pairs={{0,4},{4,0},{8,12},{12,8},{16,20},{20,16},{24,28},{28,24},{32,36},... | collective-permute-start | bytes 1769480 | tf_op jit(solution)/shard_map/ppermute | solution.py:73
  96.0 12.6 %all-to-all-start = ((bf16[4,32,1152]{2,1,0:T(8,128)(2,1)}), bf16[4,32,1152]{2,1,0:T(8,128)(2,1)S(1)}, u32[]{:S(2)}, u32[]{:S(2)}) async-start(bf16[4,32,1152]{2,1,0:T(8,128)(2,1)} %bitcast.139), calls=%async_computation | async-start | bytes 589824 | tf_op jit(solution)/shard_map/all_to_all | solution.py:77
  110.0 23.5 %collective-permute-start.33 = (bf16[32,1152]{1,0:T(8,128)(2,1)S(1)}, bf16[32,1152]{1,0:T(8,128)(2,1)}, u32[]{:S(2)}, u32[]{:S(2)}) collective-permute-start(bf16[32,1152]{1,0:T(8,128)(2,1)S(1)} %dynamic-slice_bitcast_fusion.33), channel_id=1, source_target_pairs={{0,272},{4,276},{8,280},{12,284},{16,256},{20,260},{24,264},{28,26... | collective-permute-start | bytes 221192 | tf_op jit(solution)/shard_map/while/body/eval_jaxpr/cond/branch_34_fun/ppermute | solution.py:18
  136.3 5.2 %collective-permute-start.31 = (bf16[32,1152]{1,0:T(8,128)(2,1)S(1)}, bf16[32,1152]{1,0:T(8,128)(2,1)}, u32[]{:S(2)}, u32[]{:S(2)}) collective-permute-start(bf16[32,1152]{1,0:T(8,128)(2,1)S(1)} %dynamic-slice_bitcast_fusion.31), channel_id=1, source_target_pairs={{0,256},{4,260},{8,264},{12,268},{16,272},{20,276},{24,280},{28,28... | collective-permute-start | bytes 221192 | tf_op jit(solution)/shard_map/while/body/eval_jaxpr/cond/branch_32_fun/ppermute | solution.py:18
  144.3 34.7 %collective-permute-start.58 = (bf16[32,1152]{1,0:T(8,128)(2,1)S(1)}, bf16[32,1152]{1,0:T(8,128)(2,1)}, u32[]{:S(2)}, u32[]{:S(2)}) collective-permute-start(bf16[32,1152]{1,0:T(8,128)(2,1)S(1)} %dynamic-slice_bitcast_fusion.58), channel_id=1, source_target_pairs={{0,472},{4,476},{8,464},{12,468},{16,456},{20,460},{24,448},{28,45... | collective-permute-start | bytes 221192 | tf_op jit(solution)/shard_map/while/body/eval_jaxpr/cond/branch_59_fun/ppermute | solution.py:18
  181.9 11.5 %collective-permute-start.24 = (bf16[32,1152]{1,0:T(8,128)(2,1)S(1)}, bf16[32,1152]{1,0:T(8,128)(2,1)}, u32[]{:S(2)}, u32[]{:S(2)}) collective-permute-start(bf16[32,1152]{1,0:T(8,128)(2,1)S(1)} %dynamic-slice_bitcast_fusion.24), channel_id=1, source_target_pairs={{0,200},{4,204},{8,192},{12,196},{16,216},{20,220},{24,208},{28,21... | collective-permute-start | bytes 221192 | tf_op jit(solution)/shard_map/while/body/eval_jaxpr/cond/branch_25_fun/ppermute | solution.py:18
  200.2 1.2 copy-start.11

commit v4 on v3

--- a/solution.py
+++ b/solution.py
@@ -52,17 +52,19 @@
         jnp.bfloat16
     )
     canonical = relative_order(col_index)
-    eliminated = jnp.einsum(
-        "ip,kpn->ikn", inverse_perm, jnp.take(upper_all, canonical, axis=0),
-        preferred_element_type=jnp.float32,
+    eliminated = jnp.take(
+        jnp.einsum("ip,kpn->ikn", inverse_perm, upper_all, preferred_element_type=jnp.float32),
+        canonical,
+        axis=1,
     ).astype(jnp.bfloat16)
     coupled_width = eliminated.shape[1] * eliminated.shape[2]
     rows_out = jnp.concatenate([eliminated.reshape(share, coupled_width), forward], axis=1)
-    rows_all = jnp.take(col_gather(rows_out), canonical, axis=0)
+    rows_all = col_gather(rows_out)
     lower_rows = lower_block.shape[0]
+    source_blocks = jnp.bitwise_xor(jnp.array([0, 2, 1, 3], jnp.int32), col_index)
     combined = -jnp.einsum(
         "rkp,kpn->rn",
-        lower_block.reshape(lower_rows, 4, share),
+        jnp.take(lower_block.reshape(lower_rows, 4, share), source_blocks, axis=1),
         rows_all,
         preferred_element_type=jnp.float32,
     )
@@ -70,8 +72,10 @@
     half_rows = lower_rows // 2
     own_rows = lax.dynamic_slice_in_dim(combined, own_side * half_rows, half_rows, 0)
     other_rows = lax.dynamic_slice_in_dim(combined, (1 - own_side) * half_rows, half_rows, 0)
-    partner_rows = lax.ppermute(other_rows, LEAF, [(s, s ^ 1) for s in range(leaf_count)])
-    moving = (own_rows + partner_rows).astype(jnp.bfloat16)
+    partner_rows = lax.ppermute(
+        other_rows.astype(jnp.bfloat16), LEAF, [(s, s ^ 1) for s in range(leaf_count)]
+    )
+    moving = (own_rows + partner_rows.astype(jnp.float32)).astype(jnp.bfloat16)
     col_count = 4
     share_rows = half_rows // col_count
     spread = lax.all_to_all(

time: 206 us -> 218 us (1.058)
  the two profiles are of different devices: /device:TPU:1 before, /device:TPU:8 now
where the time goes in v4:
time: 218 us; the launch traced here: 217 us
  waiting for transfers between devices  97.1 us (45%)
  starting transfers between devices  84.5 us (39%)
  local copies, waits for them, and re-layouts  14.9 us (7%)
  other arithmetic  9.09 us (4%)
  matrix products  7.23 us (3%)
  loops' own time  2.95 us (1%)
    ppermute x4, starting transfers between devices, branch(): return lambda x: lax.ppermute(x, LEAF, pairs)  64.1 us
    ppermute x4, waiting for transfers between devices, branch(): return lambda x: lax.ppermute(x, LEAF, pairs)  46 us
    ppermute x2, waiting for transfers between devices, col_gather(): remote = lax.ppermute(block, COLS, [(c, c ^ 2) for c in range(4)])  32.1 us
    ppermute x2, starting transfers between devices, col_gather(): remote = lax.ppermute(block, COLS, [(c, c ^ 2) for c in range(4)])  10.1 us
    ppermute x1, waiting for transfers between devices, body(): lax.ppermute(other_rows.astype(jnp.bfloat16), LEAF, [(s, s ^ 1) for s in...  8.3 us
    all_to_all x1, waiting for transfers between devices, body(): lax.all_to_all(moving.reshape(col_count, share_rows, moving.shape[1]), CO...  7.89 us
  transfers between devices with their start and end apart: 10, of which 10 were waited for; matrix products, arithmetic and copies ran while one was open for 2% of the time, Pallas kernels for 0%

profile of v4, /device:TPU:8, one launch (start us, length us, event | category | flops | bytes accessed | tf_op | source)
XLA Modules:
  0.0 216.8 jit_solution(14635645356783576855)
XLA Ops:
  0.6 0.0 copy-start
  0.7 5.1 %collective-permute-start.63 = (bf16[1280,256]{1,0:T(8,128)(2,1)}, bf16[1280,256]{1,0:T(8,128)(2,1)S(1)}, u32[]{:S(2)}, u32[]{:S(2)}) collective-permute-start(bf16[1280,256]{1,0:T(8,128)(2,1)} %param.75), channel_id=1, source_target_pairs={{0,2},{1,3},{2,0},{3,1},{4,6},{5,7},{6,4},{7,5},{8,10},{9,11},{10,... | collective-permute-start | bytes 1966088 | tf_op jit(solution)/shard_map/ppermute | solution.py:24
  5.7 15.1 %collective-permute-done.63 = bf16[1280,256]{1,0:T(8,128)(2,1)S(1)} collective-permute-done((bf16[1280,256]{1,0:T(8,128)(2,1)}, bf16[1280,256]{1,0:T(8,128)(2,1)S(1)}, u32[]{:S(2)}, u32[]{:S(2)}) %collective-permute-start.63) | collective-permute-done | bytes 655392 | tf_op jit(solution)/shard_map/ppermute | solution.py:24
  20.9 1.4 pad_maximum_fusion.1
  22.3 1.9 collective-permute-start.64
  24.3 0.1 broadcast_in_dim.232
  24.4 0.0 copy-start.9
  24.5 1.5 fusion.11
  26.0 0.4 convolution_convert_fusion
  26.4 0.0 copy-start.8
  26.4 0.9 collective-permute-done.64
  27.4 2.3 %fusion.15 = bf16[320,4,256]{2,0,1:T(8,128)(2,1)S(1)} fusion(bf16[2,1280,256]{2,1,0:T(8,128)(2,1)} %collective-permute-done.64, bf16[1,1280,256]{2,1,0:T(8,128)(2,1)S(1)} %bitcast.245, bf16[1,1280,256]{2,1,0:T(8,128)(2,1)S(1)} %bitcast.243, bf16[1280,320]{0,1:T(8,128)(2,1)S(1)} %fusion.11), kind=kOutput, calls=%fused_computation.80 | convolution fusion | flops 846725120 | bytes 4096000 | tf_op jit(solution)/shard_map/ip,kpn->ikn/dot_general | solution.py:56
  29.7 0.6 gather_fusion.1
  30.3 0.1 copy.19
  30.4 0.2 select_convert_fusion
  30.6 0.1 fusion.35
  30.7 0.0 copy-start.7
  30.7 5.1 %collective-permute-start.65 = (bf16[320,1152]{1,0:T(8,128)(2,1)S(1)}, bf16[320,1152]{1,0:T(8,128)(2,1)S(1)}, u32[]{:S(2)}, u32[]{:S(2)}) collective-permute-start(bf16[320,1152]{1,0:T(8,128)(2,1)S(1)} %get-tuple-element.741), channel_id=1, source_target_pairs={{0,2},{1,3},{2,0},{3,1},{4,6},{5,7},{6,4},{7,5},{8,10},{9,11},{10,... | collective-permute-start | bytes 2211848 | tf_op jit(solution)/shard_map/ppermute | solution.py:24
  35.8 17.0 %collective-permute-done.65 = bf16[320,1152]{1,0:T(8,128)(2,1)S(1)} collective-permute-done((bf16[320,1152]{1,0:T(8,128)(2,1)S(1)}, bf16[320,1152]{1,0:T(8,128)(2,1)S(1)}, u32[]{:S(2)}, u32[]{:S(2)}) %collective-permute-start.65) | collective-permute-done | bytes 737312 | tf_op jit(solution)/shard_map/ppermute | solution.py:24
  52.8 1.4 pad_maximum_fusion
  54.2 1.9 collective-permute-start.66
  56.1 0.2 copy.13
  56.4 1.4 gather_fusion
  57.8 1.8 collective-permute-done.66
  59.7 3.0 %fusion.12 = f32[256,1152]{1,0:T(8,128)S(1)} fusion(bf16[2,320,1152]{2,1,0:T(8,128)(2,1)} %collective-permute-done.66, bf16[1,320,1152]{2,1,0:T(8,128)(2,1)} %bitcast.241, bf16[1,320,1152]{2,1,0:T(8,128)(2,1)S(1)} %get-tuple-element.740, bf16[4,256,320]{1,2,0:T(8,128)(2,1)} %gather_fusion, pred[4]{0:T(512)(128)(4,1)S(1)} %get-tuple-element.738), kind=kOutput, calls=%fused_computation.79 | convolution fusion | flops 758546432 | bytes 4784132 | tf_op jit(solution)/shard_map/rkp,kpn->rn/dot_general | solution.py:65
  62.6 1.0 copy-done.3
  63.7 2.1 collective-permute-start.67
  65.9 0.1 xor_xor_fusion
  66.0 0.1 xor.84
  66.1 0.1 reshape.176
  66.2 0.2 copy.22
  66.5 8.3 %collective-permute-done.67 = bf16[128,1152]{1,0:T(8,128)(2,1)} collective-permute-done((bf16[128,1152]{1,0:T(8,128)(2,1)S(1)}, bf16[128,1152]{1,0:T(8,128)(2,1)}, u32[]{:S(2)}, u32[]{:S(2)}) %collective-permute-start.67) | collective-permute-done | bytes 294944 | tf_op jit(solution)/shard_map/ppermute | solution.py:75
  74.8 1.9 add_convert_fusion
  76.7 4.3 %all-to-all-start = ((bf16[4,32,1152]{2,1,0:T(8,128)(2,1)}), bf16[4,32,1152]{2,1,0:T(8,128)(2,1)S(1)}, u32[]{:S(2)}, u32[]{:S(2)}) async-start(bf16[4,32,1152]{2,1,0:T(8,128)(2,1)} %bitcast.139), calls=%async_computation | async-start | bytes 589824 | tf_op jit(solution)/shard_map/all_to_all | solution.py:81
  81.0 7.9 %all-to-all-done = bf16[4,32,1152]{2,1,0:T(8,128)(2,1)S(1)} async-done(((bf16[4,32,1152]{2,1,0:T(8,128)(2,1)}), bf16[4,32,1152]{2,1,0:T(8,128)(2,1)S(1)}, u32[]{:S(2)}, u32[]{:S(2)}) %all-to-all-start) | async-done | bytes 294944 | tf_op jit(solution)/shard_map/all_to_all | solution.py:81
  88.9 119.1 %while.13 = (s32[]{:T(128)}, bf16[4,32,1152]{2,1,0:T(8,128)(2,1)S(1)}, s32[4]{0:T(128)S(1)}, bf16[4,32,1152]{2,1,0:T(8,128)(2,1)S(1)}, s32[]{:T(128)}, /*index=5*/s32[1]{0:T(128)}, s32[1]{0:T(128)}) while((s32[]{:T(128)}, bf16[4,32,1152]{2,1,0:T(8,128)(2,1)S(1)}, s32[4]{0:T(128)S(1)}, bf16[4,32,1152]{2,1,0:T(8,128)(2,1)S(1)}, s32[]{:T(128)}, ...), condition=%wide.region_65.66_spmd, body=%wide.region_0.65_spmd.sunk | while | flops 3 | bytes 590001 | solution.py:96
  88.9 0.6 dynamic_slice.344
  90.1 24.0 %conditional.2 = (bf16[1,32,1152]{2,1,0:T(8,128)(2,1)}) conditional(s32[]{:T(128)} %bitcast.231, (bf16[4,32,1152]{2,1,0:T(8,128)(2,1)S(1)}, s32[]{:T(128)}) %tuple.359, (bf16[4,32,1152]{2,1,0:T(8,128)(2,1)S(1)}, s32[]{:T(128)}) %tuple.359, (bf16[4,32,1152]{2,1,0:T(8,128)(2,1)S(1)}, s32[]{:T(128)}) %tuple.359, ...), branch_computations={%region_1.1_spmd, %region_2.2_spmd, %region_3.3_spmd, %region_4.4_... | conditional | bytes 442420 | solution.py:93
  90.2 18.2 %collective-permute-start.32 = (bf16[32,1152]{1,0:T(8,128)(2,1)S(1)}, bf16[32,1152]{1,0:T(8,128)(2,1)}, u32[]{:S(2)}, u32[]{:S(2)}) collective-permute-start(bf16[32,1152]{1,0:T(8,128)(2,1)S(1)} %dynamic-slice_bitcast_fusion.32), channel_id=1, source_target_pairs={{0,264},{4,268},{8,256},{12,260},{16,280},{20,284},{24,272},{28,27... | collective-permute-start | bytes 221192 | tf_op jit(solution)/shard_map/while/body/eval_jaxpr/cond/branch_33_fun/ppermute | solution.py:18
  108.4 5.7 %collective-permute-done.32 = bf16[32,1152]{1,0:T(8,128)(2,1)} collective-permute-done((bf16[32,1152]{1,0:T(8,128)(2,1)S(1)}, bf16[32,1152]{1,0:T(8,128)(2,1)}, u32[]{:S(2)}, u32[]{:S(2)}) %collective-permute-start.32) | collective-permute-done | bytes 73760 | tf_op jit(solution)/shard_map/while/body/eval_jaxpr/cond/branch_33_fun/ppermute | solution.py:18
  114.1 0.9 constant_dynamic-update-slice_fusion.2
  115.0 0.6 dynamic_slice.344
  116.3 27.1 %conditional.2 = (bf16[1,32,1152]{2,1,0:T(8,128)(2,1)}) conditional(s32[]{:T(128)} %bitcast.231, (bf16[4,32,1152]{2,1,0:T(8,128)(2,1)S(1)}, s32[]{:T(128)}) %tuple.359, (bf16[4,32,1152]{2,1,0:T(8,128)(2,1)S(1)}, s32[]{:T(128)}) %tuple.359, (bf16[4,32,1152]{2,1,0:T(8,128)(2,1)S(1)}, s32[]{:T(128)}) %tuple.359, ...), branch_computations={%region_1.1_spmd, %region_2.2_spmd, %region_3.3_spmd, %region_4.4_... | conditional | bytes 442420 | solution.py:93
  116.4 17.7 %collective-permute-start.38 = (bf16[32,1152]{1,0:T(8,128)(2,1)S(1)}, bf16[32,1152]{1,0:T(8,128)(2,1)}, u32[]{:S(2)}, u32[]{:S(2)}) collective-permute-start(bf16[32,1152]{1,0:T(8,128)(2,1)S(1)} %dynamic-slice_bitcast_fusion.38), channel_id=1, source_target_pairs={{0,312},{4,316},{8,304},{12,308},{16,296},{20,300},{24,288},{28,29... | collective-permute-start | bytes 221192 | tf_op jit(solution)/shard_map/while/body/eval_jaxpr/cond/branch_39_fun/ppermute | solution.py:18
  134.1 9.3 %collective-permute-done.38 = bf16[32,1152]{1,0:T(8,128)(2,1)} collective-permute-done((bf16[32,1152]{1,0:T(8,128)(2,1)S(1)}, bf16[32,1152]{1,0:T(8,128)(2,1)}, u32[]{:S(2)}, u32[]{:S(2)}) %collective-permute-start.38) | collective-permute-done | bytes 73760 | tf_op jit(solution)/shard_map/while/body/eval_jaxpr/cond/branch_39_fun/ppermute | solution.py:18
  143.4 0.9 constant_dynamic-update-slice_fusion.2
  144.3 0.6 dynamic_slice.344
  145.5 31.7 %conditional.2 = (bf16[1,32,1152]{2,1,0:T(8,128)(2,1)}) conditional(s32[]{:T(128)} %bitcast.231, (bf16[4,32,1152]{2,1,0:T(8,128)(2,1)S(1)}, s32[]{:T(128)}) %tuple.359, (bf16[4,32,1152]{2,1,0:T(8,128)(2,1)S(1)}, s32[]{:T(128)}) %tuple.359, (bf16[4,32,1152]{2,1,0:T(8,128)(2,1)S(1)}, s32[]{:T(128)}) %tuple.359, ...), branch_computations={%region_1.1_spmd, %region_2.2_spmd, %region_3.3_spmd, %region_4.4_... | conditional | bytes 442420 | solution.py:93
  145.6 15.3 %collective-permute-start.40 = (bf16[32,1152]{1,0:T(8,128)(2,1)S(1)}, bf16[32,1152]{1,0:T(8,128)(2,1)}, u32[]{:S(2)}, u32[]{:S(2)}) collective-permute-start(bf16[32,1152]{1,0:T(8,128)(2,1)S(1)} %dynamic-slice_bitcast_fusion.40), channel_id=1, source_target_pairs={{0,328},{4,332},{8,320},{12,324},{16,344},{20,348},{24,336},{28,34... | collective-permute-start | bytes 221192 | tf_op jit(solution)/shard_map/while/body/eval_jaxpr/cond/branch_41_fun/ppermute | solution.py:18
  160.9 16.3 %collective-permute-done.40 = bf16[32,1152]{1,0:T(8,128)(2,1)} collective-permute-done((bf16[32,1152]{1,0:T(8,128)(2,1)S(1)}, bf16[32,1152]{1,0:T(8,128)(2,1)}, u32[]{:S(2)}, u32[]{:S(2)}) %collective-permute-start.40) | collective-permute-done | bytes 73760 | tf_op jit(solution)/shard_map/while/body/eval_jaxpr/cond/branch_41_fun/ppermute | solution.py:18
  177.2 0.9 constant_dynamic-update-slice_fusion.2
  178.2 0.6 dynamic_slice.344
  179.4 27.6 %conditional.2 = (bf16[1,32,1152]{2,1,0:T(8,128)(2,1)}) conditional(s32[]{:T(128)} %bitcast.231, (bf16[4,32,1152]{2,1,0:T(8,128)(2,1)S(1)}, s32[]{:T(128)}) %tuple.359, (bf16[4,32,1152]{2,1,0:T(8,128)(2,1)S(1)}, s32[]{:T(128)}) %tuple.359, (bf16[4,32,1152]{2,1,0:T(8,128)(2,1)S(1)}, s32[]{:T(128)}) %tuple.359, ...), branch_computations={%region_1.1_spmd, %region_2.2_spmd, %region_3.3_spmd, %region_4.4_... | conditional | bytes 442420 | solution.py:93
  179.5 12.9 %collective-permute-start.39 = (bf16[32,1152]{1,0:T(8,128)(2,1)S(1)}, bf16[32,1152]{1,0:T(8,128)(2,1)}, u32[]{:S(2)}, u32[]{:S(2)}) collective-permute-start(bf16[32,1152]{1,0:T(8,128)(2,1)S(1)} %dynamic-slice_bitcast_fusion.39), channel_id=1, source_target_pairs={{0,320},{4,324},{8,328},{12,332},{16,336},{20,340},{24,344},{28,34... | collective-permute-start | bytes 221192 | tf_op jit(solution)/shard_map/while/body/eval_jaxpr/cond/branch_40_fun/ppermute | solution.py:18
  192.4 14.7 %collective-permute-done.39 = bf16[32,1152]{1,0:T(8,128)(2,1)} collective-permute-done((bf16[32,1152]{1,0:T(8,128)(2,1)S(1)}, bf16[32,1152]{1,0:T(8,128)(2,1)}, u32[]{:S(2)}, u32[]{:S(2)}) %collective-permute-start.39) | collective-permute-done | bytes 73760 | tf_op jit(solution)/shard_map/while/body/eval_jaxpr/cond/branch_40_fun/ppermute | solution.py:18
  207.0 0.9 constant_dynamic-update-slice_fusion.2
  207.9 0.8 slice_convert_fusion
  208.8 2.1 reshape.179
  210.9 1.9 copy.15
  212.8 2.2 scatter_fusion
  215.0 0.2 convert_bitcast_fusion
  215.2 0.0 copy-start.10
  215.2 1.0 copy.20
  216.2 0.6 convert_add_fusion
  (38 shorter events, 0.3 us)
Async XLA Ops:
  0.6 23.8 %copy-start = (bf16[320,1280]{1,0:T(8,128)(2,1)S(1)}, bf16[320,1280]{1,0:T(8,128)(2,1)}, u32[]{:S(2)}) copy-start(bf16[320,1280]{1,0:T(8,128)(2,1)} %param.77) | copy-start | bytes 2457604
  0.6 23.7 %copy-start.11 = (s32[1,1280]{1,0:T(1,128)S(1)}, s32[1,1280]{1,0:T(1,128)}, u32[]{:S(2)}) copy-start(s32[1,1280]{1,0:T(1,128)} %param.78) | copy-start | bytes 15364
  0.7 20.2 %collective-permute-start.63 = (bf16[1280,256]{1,0:T(8,128)(2,1)}, bf16[1280,256]{1,0:T(8,128)(2,1)S(1)}, u32[]{:S(2)}, u32[]{:S(2)}) collective-permute-start(bf16[1280,256]{1,0:T(8,128)(2,1)} %param.75), channel_id=1, source_target_pairs={{0,2},{1,3},{2,0},{3,1},{4,6},{5,7},{6,4},{7,5},{8,10},{9,11},{10,... | collective-permute-start | bytes 1966088 | tf_op jit(solution)/shard_map/ppermute | solution.py:24
  20.9 3.5 %copy-start.5 = (bf16[1280,256]{1,0:T(8,128)(2,1)}, bf16[1280,256]{1,0:T(8,128)(2,1)S(1)}, u32[]{:S(2)}) copy-start(bf16[1280,256]{1,0:T(8,128)(2,1)S(1)} %collective-permute-done.63) | copy-start | bytes 1966084
  22.3 5.1 %collective-permute-start.64 = (bf16[2,1280,256]{2,1,0:T(8,128)(2,1)S(1)}, bf16[2,1280,256]{2,1,0:T(8,128)(2,1)}, u32[]{:S(2)}, u32[]{:S(2)}) collective-permute-start(bf16[2,1280,256]{2,1,0:T(8,128)(2,1)S(1)} %pad_maximum_fusion.1), channel_id=1, source_target_pairs={{0,1},{1,0},{2,3},{3,2},{4,5},{5,4},{6,7},{7,6},{8,9},{9,8},{10,11... | collective-permute-start | bytes 3932168 | tf_op jit(solution)/shard_map/ppermute | solution.py:26
  24.4 1.6 copy-start.9
  24.5 2.9 %copy-start.4 = (bf16[1280,256]{1,0:T(8,128)(2,1)S(1)}, bf16[1280,256]{1,0:T(8,128)(2,1)}, u32[]{:S(2)}) copy-start(bf16[1280,256]{1,0:T(8,128)(2,1)} %param.75) | copy-start | bytes 1966084
  24.5 2.9 %copy-start.6 = (bf16[1280,256]{1,0:T(8,128)(2,1)S(1)}, bf16[1280,256]{1,0:T(8,128)(2,1)}, u32[]{:S(2)}) copy-start(bf16[1280,256]{1,0:T(8,128)(2,1)} %copy-done.5) | copy-start | bytes 1966084
  26.4 4.1 %copy-start.8 = (bf16[320,128]{1,0:T(8,128)(2,1)}, bf16[320,128]{1,0:T(8,128)(2,1)S(1)}, u32[]{:S(2)}) copy-start(bf16[320,128]{1,0:T(8,128)(2,1)S(1)} %convolution_convert_fusion) | copy-start | bytes 245764
  30.7 25.4 %copy-start.7 = (bf16[256,1280]{1,0:T(8,128)(2,1)S(1)}, bf16[256,1280]{1,0:T(8,128)(2,1)}, u32[]{:S(2)}) copy-start(bf16[256,1280]{1,0:T(8,128)(2,1)} %param.76) | copy-start | bytes 1966084
  30.7 22.1 %collective-permute-start.65 = (bf16[320,1152]{1,0:T(8,128)(2,1)S(1)}, bf16[320,1152]{1,0:T(8,128)(2,1)S(1)}, u32[]{:S(2)}, u32[]{:S(2)}) collective-permute-start(bf16[320,1152]{1,0:T(8,128)(2,1)S(1)} %get-tuple-element.741), channel_id=1, source_target_pairs={{0,2},{1,3},{2,0},{3,1},{4,6},{5,7},{6,4},{7,5},{8,10},{9,11},{10,... | collective-permute-start | bytes 2211848 | tf_op jit(solution)/shard_map/ppermute | solution.py:24
  52.8 3.3 %copy-start.2 = (bf16[320,1152]{1,0:T(8,128)(2,1)}, bf16[320,1152]{1,0:T(8,128)(2,1)S(1)}, u32[]{:S(2)}) copy-start(bf16[320,1152]{1,0:T(8,128)(2,1)S(1)} %collective-permute-done.65) | copy-start | bytes 2211844
  52.8 3.6 %copy-start.12 = (s32[4]{0:T(128)S(1)}, s32[4]{0:T(128)}, u32[]{:S(2)}) copy-start(s32[4]{0:T(128)} %constant.268.clone) | copy-start | bytes 52
  54.2 5.5 %collective-permute-start.66 = (bf16[2,320,1152]{2,1,0:T(8,128)(2,1)}, bf16[2,320,1152]{2,1,0:T(8,128)(2,1)}, u32[]{:S(2)}, u32[]{:S(2)}) collective-permute-start(bf16[2,320,1152]{2,1,0:T(8,128)(2,1)} %pad_maximum_fusion), channel_id=1, source_target_pairs={{0,1},{1,0},{2,3},{3,2},{4,5},{5,4},{6,7},{7,6},{8,9},{9,8},{10,11... | collective-permute-start | bytes 4423688 | tf_op jit(solution)/shard_map/ppermute | solution.py:26
  59.7 6.2 %copy-start.13 = (s32[1,4]{1,0:T(1,128)S(1)}, s32[1,4]{1,0:T(1,128)}, u32[]{:S(2)}) copy-start(s32[1,4]{1,0:T(1,128)} %param.80) | copy-start | bytes 52
  59.7 6.4 %copy-start.1 = (bf16[32,16384]{1,0:T(8,128)(2,1)S(1)}, bf16[32,16384]{1,0:T(8,128)(2,1)}, u32[]{:S(2)}) copy-start(bf16[32,16384]{1,0:T(8,128)(2,1)} %param.81) | copy-start | bytes 3145732
  62.6 1.0 copy-start.3
  63.7 11.1 %collective-permute-start.67 = (bf16[128,1152]{1,0:T(8,128)(2,1)S(1)}, bf16[128,1152]{1,0:T(8,128)(2,1)}, u32[]{:S(2)}, u32[]{:S(2)}) collective-permute-start(bf16[128,1152]{1,0:T(8,128)(2,1)S(1)} %dynamic-slice_convert_fusion), channel_id=1, source_target_pairs={{0,4},{4,0},{8,12},{12,8},{16,20},{20,16},{24,28},{28,24},{32,36},... | collective-permute-start | bytes 884744 | tf_op jit(solution)/shard_map/ppermute | solution.py:75
  76.7 12.2 %all-to-all-start = ((bf16[4,32,1152]{2,1,0:T(8,128)(2,1)}), bf16[4,32,1152]{2,1,0:T(8,128)(2,1)S(1)}, u32[]{:S(2)}, u32[]{:S(2)}) async-start(bf16[4,32,1152]{2,1,0:T(8,128)(2,1)} %bitcast.139), calls=%async_computation | async-start | bytes 589824 | tf_op jit(solution)/shard_map/all_to_all | solution.py:81
  90.2 23.9 %collective-permute-start.32 = (bf16[32,1152]{1,0:T(8,128)(2,1)S(1)}, bf16[32,1152]{1,0:T(8,128)(2,1)}, u32[]{:S(2)}, u32[]{:S(2)}) collective-permute-start(bf16[32,1152]{1,0:T(8,128)(2,1)S(1)} %dynamic-slice_bitcast_fusion.32), channel_id=1, source_target_pairs={{0,264},{4,268},{8,256},{12,260},{16,280},{20,284},{24,272},{28,27... | collective-permute-start | bytes 221192 | tf_op jit(solution)/shard_map/while/body/eval_jaxpr/cond/branch_33_fun/ppermute | solution.py:18
  116.4 27.0 %collective-permute-start.38 = (bf16[32,1152]{1,0:T(8,128)(2,1)S(1)}, bf16[32,1152]{1,0:T(8,128)(2,1)}, u32[]{:S(2)}, u32[]{:S(2)}) collective-permute-start(bf16[32,1152]{1,0:T(8,128)(2,1)S(1)} %dynamic-slice_bitcast_fusion.38), channel_id=1, source_target_pairs={{0,312},{4,316},{8,304},{12,308},{16,296},{20,300},{24,288},{28,29... | collective-permute-start | bytes 221192 | tf_op jit(solution)/shard_map/while/body/eval_jaxpr/cond/branch_39_fun/ppermute | solution.py:18
  145.6 31.6 %collective-permute-start.40 = (bf16[32,1152]{1,0:T(8,128)(2,1)S(1)}, bf16[32,1152]{1,0:T(8,128)(2,1)}, u32[]{:S(2)}, u32[]{:S(2)}) collective-permute-start(bf16[32,1152]{1,0:T(8,128)(2,1)S(1)} %dynamic-slice_bitcast_fusion.40), channel_id=1, source_target_pairs={{0,328},{4,332},{8,320},{12,324},{16,344},{20,348},{24,336},{28,34... | collective-permute-start | bytes 221192 | tf_op jit(solution)/shard_map/while/body/eval_jaxpr/cond/branch_41_fun/ppermute | solution.py:18
  179.5 27.6 %collective-permute-start.39 = (bf16[32,1152]{1,0:T(8,128)(2,1)S(1)}, bf16[32,1152]{1,0:T(8,128)(2,1)}, u32[]{:S(2)}, u32[]{:S(2)}) collective-permute-start(bf16[32,1152]{1,0:T(8,128)(2,1)S(1)} %dynamic-slice_bitcast_fusion.39), channel_id=1, source_target_pairs={{0,320},{4,324},{8,328},{12,332},{16,336},{20,340},{24,344},{28,34... | collective-permute-start | bytes 221192 | tf_op jit(solution)/shard_map/while/body/eval_jaxpr/cond/branch_40_fun/ppermute | solution.py:18
  215.2 1.1 copy-start.10

commit v5 on v4

--- a/solution.py
+++ b/solution.py
@@ -78,12 +78,19 @@
     moving = (own_rows + partner_rows.astype(jnp.float32)).astype(jnp.bfloat16)
     col_count = 4
     share_rows = half_rows // col_count
-    spread = lax.all_to_all(
-        moving.reshape(col_count, share_rows, moving.shape[1]),
-        COLS,
-        split_axis=0,
-        concat_axis=0,
-        tiled=True,
+    quarters = moving.reshape(col_count, share_rows, moving.shape[1])
+    by_distance = [lax.dynamic_index_in_dim(quarters, col_index, 0, keepdims=False)]
+    for distance in range(1, col_count):
+        outgoing = lax.dynamic_index_in_dim(
+            quarters, jnp.bitwise_xor(col_index, distance), 0, keepdims=False
+        )
+        by_distance.append(
+            lax.ppermute(outgoing, COLS, [(c, c ^ distance) for c in range(col_count)])
+        )
+    spread = jnp.take(
+        jnp.stack(by_distance),
+        jnp.bitwise_xor(jnp.arange(col_count, dtype=jnp.int32), col_index),
+        axis=0,
     )
     column_masks = jnp.bitwise_xor(pattern[0], leaf_index // 2)
     branches = xor_route(None, leaf_count // 2)

time: 218 us -> 180 us (0.83)
  the two profiles are of different devices: /device:TPU:8 before, /device:TPU:1 now
where the time goes in v5:
time: 180 us; the launch traced here: 177 us
  starting transfers between devices  83.7 us (46%)
  waiting for transfers between devices  52.1 us (29%)
  local copies, waits for them, and re-layouts  21.3 us (12%)
  other arithmetic  8.97 us (5%)
  matrix products  7.37 us (4%)
  loops' own time  2.9 us (2%)
    ppermute x4, starting transfers between devices, branch(): return lambda x: lax.ppermute(x, LEAF, pairs)  50.4 us
    ppermute x2, waiting for transfers between devices, col_gather(): remote = lax.ppermute(block, COLS, [(c, c ^ 2) for c in range(4)])  27.5 us
    ppermute x4, waiting for transfers between devices, branch(): return lambda x: lax.ppermute(x, LEAF, pairs)  11.6 us
    ppermute x2, starting transfers between devices, col_gather(): remote = lax.ppermute(block, COLS, [(c, c ^ 2) for c in range(4)])  10.5 us
    ppermute x3, starting transfers between devices, body(): lax.ppermute(outgoing, COLS, [(c, c ^ distance) for c in range(col_count)])  9.78 us
    ppermute x2, starting transfers between devices, col_gather(): partner = lax.ppermute(chip, COLS, [(c, c ^ 1) for c in range(4)])  9.62 us
    ppermute x1, waiting for transfers between devices, body(): lax.ppermute(other_rows.astype(jnp.bfloat16), LEAF, [(s, s ^ 1) for s in...  7.19 us
    dynamic_update_slice x4, local copies, waits for them, and re-layouts, route_piece(): return lax.dynamic_update_index_in_dim(routed, sent, a, 0)  6.07 us
  transfers between devices with their start and end apart: 12, of which 10 were waited for; matrix products, arithmetic and copies ran while one was open for 4% of the time, Pallas kernels for 0%

profile of v5, /device:TPU:1, one launch (start us, length us, event | category | flops | bytes accessed | tf_op | source)
XLA Modules:
  0.0 177.4 jit_solution(9018601271868210112)
XLA Ops:
  0.7 5.6 %collective-permute-start.63 = (bf16[1280,256]{1,0:T(8,128)(2,1)}, bf16[1280,256]{1,0:T(8,128)(2,1)S(1)}, u32[]{:S(2)}, u32[]{:S(2)}) collective-permute-start(bf16[1280,256]{1,0:T(8,128)(2,1)} %param.75), channel_id=1, source_target_pairs={{0,2},{1,3},{2,0},{3,1},{4,6},{5,7},{6,4},{7,5},{8,10},{9,11},{10,... | collective-permute-start | bytes 1966088 | tf_op jit(solution)/shard_map/ppermute | solution.py:24
  6.3 11.3 %collective-permute-done.63 = bf16[1280,256]{1,0:T(8,128)(2,1)S(1)} collective-permute-done((bf16[1280,256]{1,0:T(8,128)(2,1)}, bf16[1280,256]{1,0:T(8,128)(2,1)S(1)}, u32[]{:S(2)}, u32[]{:S(2)}) %collective-permute-start.63) | collective-permute-done | bytes 655392 | tf_op jit(solution)/shard_map/ppermute | solution.py:24
  17.6 1.4 pad_maximum_fusion.1
  19.0 6.5 %collective-permute-start.64 = (bf16[2,1280,256]{2,1,0:T(8,128)(2,1)S(1)}, bf16[2,1280,256]{2,1,0:T(8,128)(2,1)}, u32[]{:S(2)}, u32[]{:S(2)}) collective-permute-start(bf16[2,1280,256]{2,1,0:T(8,128)(2,1)S(1)} %pad_maximum_fusion.1), channel_id=1, source_target_pairs={{0,1},{1,0},{2,3},{3,2},{4,5},{5,4},{6,7},{7,6},{8,9},{9,8},{10,11... | collective-permute-start | bytes 3932168 | tf_op jit(solution)/shard_map/ppermute | solution.py:26
  25.6 0.1 broadcast_in_dim.243
  25.8 1.5 fusion.11
  27.3 0.4 convolution_convert_fusion
  27.7 0.6 collective-permute-done.64
  28.3 2.3 %fusion.15 = bf16[320,4,256]{2,0,1:T(8,128)(2,1)S(1)} fusion(bf16[2,1280,256]{2,1,0:T(8,128)(2,1)} %collective-permute-done.64, bf16[1,1280,256]{2,1,0:T(8,128)(2,1)S(1)} %bitcast.257, bf16[1,1280,256]{2,1,0:T(8,128)(2,1)S(1)} %bitcast.255, bf16[1280,320]{0,1:T(8,128)(2,1)S(1)} %fusion.11), kind=kOutput, calls=%fused_computation.81 | convolution fusion | flops 846725120 | bytes 4096000 | tf_op jit(solution)/shard_map/ip,kpn->ikn/dot_general | solution.py:56
  30.6 0.6 gather_fusion.1
  31.2 0.1 copy.19
  31.3 0.2 select_convert_fusion
  31.5 0.1 fusion.36
  31.6 4.9 %collective-permute-start.65 = (bf16[320,1152]{1,0:T(8,128)(2,1)S(1)}, bf16[320,1152]{1,0:T(8,128)(2,1)S(1)}, u32[]{:S(2)}, u32[]{:S(2)}) collective-permute-start(bf16[320,1152]{1,0:T(8,128)(2,1)S(1)} %get-tuple-element.741), channel_id=1, source_target_pairs={{0,2},{1,3},{2,0},{3,1},{4,6},{5,7},{6,4},{7,5},{8,10},{9,11},{10,... | collective-permute-start | bytes 2211848 | tf_op jit(solution)/shard_map/ppermute | solution.py:24
  36.5 16.2 %collective-permute-done.65 = bf16[320,1152]{1,0:T(8,128)(2,1)S(1)} collective-permute-done((bf16[320,1152]{1,0:T(8,128)(2,1)S(1)}, bf16[320,1152]{1,0:T(8,128)(2,1)S(1)}, u32[]{:S(2)}, u32[]{:S(2)}) %collective-permute-start.65) | collective-permute-done | bytes 737312 | tf_op jit(solution)/shard_map/ppermute | solution.py:24
  52.7 0.9 copy-done.3
  53.6 1.3 pad_maximum_fusion
  54.9 3.1 %collective-permute-start.66 = (bf16[2,320,1152]{2,1,0:T(8,128)(2,1)}, bf16[2,320,1152]{2,1,0:T(8,128)(2,1)}, u32[]{:S(2)}, u32[]{:S(2)}) collective-permute-start(bf16[2,320,1152]{2,1,0:T(8,128)(2,1)} %pad_maximum_fusion), channel_id=1, source_target_pairs={{0,1},{1,0},{2,3},{3,2},{4,5},{5,4},{6,7},{7,6},{8,9},{9,8},{10,11... | collective-permute-start | bytes 4423688 | tf_op jit(solution)/shard_map/ppermute | solution.py:26
  58.0 2.2 %copy.13 = bf16[256,1280]{0,1:T(8,128)(2,1)} copy(bf16[256,1280]{1,0:T(8,128)(2,1)} %param.76) | data formatting | bytes 1310720 | tf_op args[1]
  60.2 0.1 xor_xor_fusion
  60.3 0.1 xor.101
  60.4 0.1 reshape.188
  60.5 0.2 copy.22
  60.8 0.4 copy-done.11
  61.2 2.5 %gather_fusion = bf16[4,256,320]{1,2,0:T(8,128)(2,1)} fusion(bf16[256,4,320]{0,2,1:T(8,128)(2,1)} %bitcast.245, s32[1024]{0:T(1024)S(1)} %pad_clamp_fusion.2), kind=kCustom, calls=%fused_computation | custom fusion | bytes 1310736 | tf_op jit(solution)/shard_map/jit(_take)/gather | solution.py:67
  63.7 3.1 %fusion.12 = f32[256,1152]{1,0:T(8,128)S(1)} fusion(bf16[2,320,1152]{2,1,0:T(8,128)(2,1)} %collective-permute-done.66, bf16[1,320,1152]{2,1,0:T(8,128)(2,1)} %bitcast.253, bf16[1,320,1152]{2,1,0:T(8,128)(2,1)} %copy-done.1, bf16[4,256,320]{1,2,0:T(8,128)(2,1)} %gather_fusion, pred[4]{0:T(512)(128)(4,1)S(1)} %get-tuple-element.738), kind=kOutput, calls=%fused_computation.80 | convolution fusion | flops 758546432 | bytes 4784132 | tf_op jit(solution)/shard_map/rkp,kpn->rn/dot_general | solution.py:65
  66.9 3.4 %collective-permute-start.67 = (bf16[128,1152]{1,0:T(8,128)(2,1)S(1)}, bf16[128,1152]{1,0:T(8,128)(2,1)S(1)}, u32[]{:S(2)}, u32[]{:S(2)}) collective-permute-start(bf16[128,1152]{1,0:T(8,128)(2,1)S(1)} %dynamic-slice_convert_fusion), channel_id=1, source_target_pairs={{0,4},{4,0},{8,12},{12,8},{16,20},{20,16},{24,28},{28,24},{32,36},... | collective-permute-start | bytes 884744 | tf_op jit(solution)/shard_map/ppermute | solution.py:75
  70.3 7.2 %collective-permute-done.67 = bf16[128,1152]{1,0:T(8,128)(2,1)S(1)} collective-permute-done((bf16[128,1152]{1,0:T(8,128)(2,1)S(1)}, bf16[128,1152]{1,0:T(8,128)(2,1)S(1)}, u32[]{:S(2)}, u32[]{:S(2)}) %collective-permute-start.67) | collective-permute-done | bytes 294944 | tf_op jit(solution)/shard_map/ppermute | solution.py:75
  77.6 2.6 %collective-permute-start.68 = (bf16[32,1152]{1,0:T(8,128)(2,1)S(1)}, bf16[32,1152]{1,0:T(8,128)(2,1)S(1)}, u32[]{:S(2)}, u32[]{:S(2)}) collective-permute-start(bf16[32,1152]{1,0:T(8,128)(2,1)S(1)} %get-tuple-element.745), channel_id=1, source_target_pairs={{0,1},{1,0},{2,3},{3,2},{4,5},{5,4},{6,7},{7,6},{8,9},{9,8},{10,11... | collective-permute-start | bytes 221192 | tf_op jit(solution)/shard_map/ppermute | solution.py:88
  80.3 4.8 %collective-permute-start.69 = (bf16[32,1152]{1,0:T(8,128)(2,1)S(1)}, bf16[32,1152]{1,0:T(8,128)(2,1)S(1)}, u32[]{:S(2)}, u32[]{:S(2)}) collective-permute-start(bf16[32,1152]{1,0:T(8,128)(2,1)S(1)} %get-tuple-element.744), channel_id=1, source_target_pairs={{0,2},{1,3},{2,0},{3,1},{4,6},{5,7},{6,4},{7,5},{8,10},{9,11},{10,... | collective-permute-start | bytes 221192 | tf_op jit(solution)/shard_map/ppermute | solution.py:88
  85.1 2.3 %collective-permute-start.70 = (bf16[32,1152]{1,0:T(8,128)(2,1)S(1)}, bf16[32,1152]{1,0:T(8,128)(2,1)S(1)}, u32[]{:S(2)}, u32[]{:S(2)}) collective-permute-start(bf16[32,1152]{1,0:T(8,128)(2,1)S(1)} %get-tuple-element.743), channel_id=1, source_target_pairs={{0,3},{1,2},{2,1},{3,0},{4,7},{5,6},{6,5},{7,4},{8,11},{9,10},{10,... | collective-permute-start | bytes 221192 | tf_op jit(solution)/shard_map/ppermute | solution.py:88
  87.5 0.1 collective-permute-done.69
  87.6 5.1 %collective-permute-done.70 = bf16[32,1152]{1,0:T(8,128)(2,1)S(1)} collective-permute-done((bf16[32,1152]{1,0:T(8,128)(2,1)S(1)}, bf16[32,1152]{1,0:T(8,128)(2,1)S(1)}, u32[]{:S(2)}, u32[]{:S(2)}) %collective-permute-start.70) | collective-permute-done | bytes 73760 | tf_op jit(solution)/shard_map/ppermute | solution.py:88
  92.7 0.6 gather_fusion.2
  93.3 0.1 broadcast_select_fusion
  93.4 73.4 %while.13 = (s32[]{:T(128)}, bf16[4,32,1152]{2,1,0:T(8,128)(2,1)}, s32[4]{0:T(128)S(1)}, bf16[4,32,1152]{2,1,0:T(8,128)(2,1)S(1)}, s32[]{:T(128)}, /*index=5*/s32[1]{0:T(128)}, s32[1]{0:T(128)}) while((s32[]{:T(128)}, bf16[4,32,1152]{2,1,0:T(8,128)(2,1)}, s32[4]{0:T(128)S(1)}, bf16[4,32,1152]{2,1,0:T(8,128)(2,1)S(1)}, s32[]{:T(128)}, ...), condition=%wide.region_65.66_spmd, body=%wide.region_0.65_spmd.sunk | while | flops 3 | bytes 590509 | solution.py:103
  93.4 0.6 dynamic_slice.365
  94.7 24.8 %conditional.2 = (bf16[1,32,1152]{2,1,0:T(8,128)(2,1)}) conditional(s32[]{:T(128)} %bitcast.242, (bf16[4,32,1152]{2,1,0:T(8,128)(2,1)S(1)}, s32[]{:T(128)}) %tuple.363, (bf16[4,32,1152]{2,1,0:T(8,128)(2,1)S(1)}, s32[]{:T(128)}) %tuple.363, (bf16[4,32,1152]{2,1,0:T(8,128)(2,1)S(1)}, s32[]{:T(128)}) %tuple.363, ...), branch_computations={%region_1.1_spmd, %region_2.2_spmd, %region_3.3_spmd, %region_4.4_... | conditional | bytes 442420 | solution.py:100
  94.7 18.7 %collective-permute-start.35 = (bf16[32,1152]{1,0:T(8,128)(2,1)S(1)}, bf16[32,1152]{1,0:T(8,128)(2,1)}, u32[]{:S(2)}, u32[]{:S(2)}) collective-permute-start(bf16[32,1152]{1,0:T(8,128)(2,1)S(1)} %dynamic-slice_bitcast_fusion.35), channel_id=1, source_target_pairs={{0,288},{4,292},{8,296},{12,300},{16,304},{20,308},{24,312},{28,31... | collective-permute-start | bytes 221192 | tf_op jit(solution)/shard_map/while/body/eval_jaxpr/cond/branch_36_fun/ppermute | solution.py:18
  113.4 6.0 %collective-permute-done.35 = bf16[32,1152]{1,0:T(8,128)(2,1)} collective-permute-done((bf16[32,1152]{1,0:T(8,128)(2,1)S(1)}, bf16[32,1152]{1,0:T(8,128)(2,1)}, u32[]{:S(2)}, u32[]{:S(2)}) %collective-permute-start.35) | collective-permute-done | bytes 73760 | tf_op jit(solution)/shard_map/while/body/eval_jaxpr/cond/branch_36_fun/ppermute | solution.py:18
  119.5 1.5 constant_dynamic-update-slice_fusion.2
  121.0 0.6 dynamic_slice.365
  122.2 12.5 %conditional.2 = (bf16[1,32,1152]{2,1,0:T(8,128)(2,1)}) conditional(s32[]{:T(128)} %bitcast.242, (bf16[4,32,1152]{2,1,0:T(8,128)(2,1)S(1)}, s32[]{:T(128)}) %tuple.363, (bf16[4,32,1152]{2,1,0:T(8,128)(2,1)S(1)}, s32[]{:T(128)}) %tuple.363, (bf16[4,32,1152]{2,1,0:T(8,128)(2,1)S(1)}, s32[]{:T(128)}) %tuple.363, ...), branch_computations={%region_1.1_spmd, %region_2.2_spmd, %region_3.3_spmd, %region_4.4_... | conditional | bytes 442420 | solution.py:100
  122.3 10.4 %collective-permute-start.13 = (bf16[32,1152]{1,0:T(8,128)(2,1)S(1)}, bf16[32,1152]{1,0:T(8,128)(2,1)}, u32[]{:S(2)}, u32[]{:S(2)}) collective-permute-start(bf16[32,1152]{1,0:T(8,128)(2,1)S(1)} %dynamic-slice_bitcast_fusion.13), channel_id=1, source_target_pairs={{0,112},{4,116},{8,120},{12,124},{16,96},{20,100},{24,104},{28,108... | collective-permute-start | bytes 221192 | tf_op jit(solution)/shard_map/while/body/eval_jaxpr/cond/branch_14_fun/ppermute | solution.py:18
  132.7 1.9 %collective-permute-done.13 = bf16[32,1152]{1,0:T(8,128)(2,1)} collective-permute-done((bf16[32,1152]{1,0:T(8,128)(2,1)S(1)}, bf16[32,1152]{1,0:T(8,128)(2,1)}, u32[]{:S(2)}, u32[]{:S(2)}) %collective-permute-start.13) | collective-permute-done | bytes 73760 | tf_op jit(solution)/shard_map/while/body/eval_jaxpr/cond/branch_14_fun/ppermute | solution.py:18
  134.7 1.5 constant_dynamic-update-slice_fusion.2
  136.2 0.6 dynamic_slice.365
  137.4 8.6 %conditional.2 = (bf16[1,32,1152]{2,1,0:T(8,128)(2,1)}) conditional(s32[]{:T(128)} %bitcast.242, (bf16[4,32,1152]{2,1,0:T(8,128)(2,1)S(1)}, s32[]{:T(128)}) %tuple.363, (bf16[4,32,1152]{2,1,0:T(8,128)(2,1)S(1)}, s32[]{:T(128)}) %tuple.363, (bf16[4,32,1152]{2,1,0:T(8,128)(2,1)S(1)}, s32[]{:T(128)}) %tuple.363, ...), branch_computations={%region_1.1_spmd, %region_2.2_spmd, %region_3.3_spmd, %region_4.4_... | conditional | bytes 442420 | solution.py:100
  137.5 6.7 %collective-permute-start.4 = (bf16[32,1152]{1,0:T(8,128)(2,1)S(1)}, bf16[32,1152]{1,0:T(8,128)(2,1)}, u32[]{:S(2)}, u32[]{:S(2)}) collective-permute-start(bf16[32,1152]{1,0:T(8,128)(2,1)S(1)} %dynamic-slice_bitcast_fusion.4), channel_id=1, source_target_pairs={{0,40},{4,44},{8,32},{12,36},{16,56},{20,60},{24,48},{28,52},{32,8... | collective-permute-start | bytes 221192 | tf_op jit(solution)/shard_map/while/body/eval_jaxpr/cond/branch_5_fun/ppermute | solution.py:18
  144.2 1.8 %collective-permute-done.4 = bf16[32,1152]{1,0:T(8,128)(2,1)} collective-permute-done((bf16[32,1152]{1,0:T(8,128)(2,1)S(1)}, bf16[32,1152]{1,0:T(8,128)(2,1)}, u32[]{:S(2)}, u32[]{:S(2)}) %collective-permute-start.4) | collective-permute-done | bytes 73760 | tf_op jit(solution)/shard_map/while/body/eval_jaxpr/cond/branch_5_fun/ppermute | solution.py:18
  146.0 1.5 constant_dynamic-update-slice_fusion.2
  147.5 0.6 dynamic_slice.365
  148.8 16.6 %conditional.2 = (bf16[1,32,1152]{2,1,0:T(8,128)(2,1)}) conditional(s32[]{:T(128)} %bitcast.242, (bf16[4,32,1152]{2,1,0:T(8,128)(2,1)S(1)}, s32[]{:T(128)}) %tuple.363, (bf16[4,32,1152]{2,1,0:T(8,128)(2,1)S(1)}, s32[]{:T(128)}) %tuple.363, (bf16[4,32,1152]{2,1,0:T(8,128)(2,1)S(1)}, s32[]{:T(128)}) %tuple.363, ...), branch_computations={%region_1.1_spmd, %region_2.2_spmd, %region_3.3_spmd, %region_4.4_... | conditional | bytes 442420 | solution.py:100
  148.8 14.7 %collective-permute-start.15 = (bf16[32,1152]{1,0:T(8,128)(2,1)S(1)}, bf16[32,1152]{1,0:T(8,128)(2,1)}, u32[]{:S(2)}, u32[]{:S(2)}) collective-permute-start(bf16[32,1152]{1,0:T(8,128)(2,1)S(1)} %dynamic-slice_bitcast_fusion.15), channel_id=1, source_target_pairs={{0,128},{4,132},{8,136},{12,140},{16,144},{20,148},{24,152},{28,15... | collective-permute-start | bytes 221192 | tf_op jit(solution)/shard_map/while/body/eval_jaxpr/cond/branch_16_fun/ppermute | solution.py:18
  163.5 1.8 %collective-permute-done.15 = bf16[32,1152]{1,0:T(8,128)(2,1)} collective-permute-done((bf16[32,1152]{1,0:T(8,128)(2,1)S(1)}, bf16[32,1152]{1,0:T(8,128)(2,1)}, u32[]{:S(2)}, u32[]{:S(2)}) %collective-permute-start.15) | collective-permute-done | bytes 73760 | tf_op jit(solution)/shard_map/while/body/eval_jaxpr/cond/branch_16_fun/ppermute | solution.py:18
  165.3 1.5 constant_dynamic-update-slice_fusion.2
  166.8 1.8 %slice_convert_fusion = f32[4,32,1024]{2,1,0:T(8,128)} fusion(bf16[4,32,1152]{2,1,0:T(8,128)(2,1)} %get-tuple-element.729), kind=kLoop, calls=%fused_computation.103 | loop fusion | flops 131072 | bytes 786432 | tf_op jit(solution)/shard_map/convert_element_type | solution.py:116
  168.6 0.8 convert_reduce_fusion
  169.4 2.1 %reshape.191 = f32[4,32,4,256]{3,2,1,0:T(4,128)} reshape(f32[4,32,1024]{2,1,0:T(8,128)} %slice_convert_fusion) | data formatting | bytes 1048576 | tf_op jit(solution)/shard_map/convert_element_type | solution.py:116
  171.5 1.9 %copy.15 = f32[32,4,4,256]{3,0,2,1:T(8,128)} copy(f32[32,4,4,256]{3,2,0,1:T(4,128)} %bitcast.249) | data formatting | bytes 1048576 | tf_op jit(solution)/shard_map/convert_element_type | solution.py:116
  173.4 2.2 %scatter_fusion = f32[32,64,256]{2,0,1:T(8,128)S(1)} fusion(f32[32,64,256]{2,0,1:T(8,128)S(1)} %bitcast.243, s32[16]{0:T(128)S(1)} %fusion.31, f32[16,32,256]{2,1,0:T(8,128)} %bitcast.248), kind=kCustom, calls=%fused_computation.3 | custom fusion | flops 131072 | bytes 1572928 | tf_op jit(solution)/shard_map/scatter-add | solution.py:116
  175.6 0.2 convert_bitcast_fusion
  175.8 1.0 copy.20
  176.8 0.6 convert_add_fusion
  (46 shorter events, 0.4 us)
Async XLA Ops:
  0.6 25.1 %copy-start = (bf16[320,1280]{1,0:T(8,128)(2,1)S(1)}, bf16[320,1280]{1,0:T(8,128)(2,1)}, u32[]{:S(2)}) copy-start(bf16[320,1280]{1,0:T(8,128)(2,1)} %param.77) | copy-start | bytes 2457604
  0.6 25.0 %copy-start.10 = (s32[1,1280]{1,0:T(1,128)S(1)}, s32[1,1280]{1,0:T(1,128)}, u32[]{:S(2)}) copy-start(s32[1,1280]{1,0:T(1,128)} %param.78) | copy-start | bytes 15364
  0.7 16.9 %collective-permute-start.63 = (bf16[1280,256]{1,0:T(8,128)(2,1)}, bf16[1280,256]{1,0:T(8,128)(2,1)S(1)}, u32[]{:S(2)}, u32[]{:S(2)}) collective-permute-start(bf16[1280,256]{1,0:T(8,128)(2,1)} %param.75), channel_id=1, source_target_pairs={{0,2},{1,3},{2,0},{3,1},{4,6},{5,7},{6,4},{7,5},{8,10},{9,11},{10,... | collective-permute-start | bytes 1966088 | tf_op jit(solution)/shard_map/ppermute | solution.py:24
  17.6 8.1 %copy-start.5 = (bf16[1280,256]{1,0:T(8,128)(2,1)}, bf16[1280,256]{1,0:T(8,128)(2,1)S(1)}, u32[]{:S(2)}) copy-start(bf16[1280,256]{1,0:T(8,128)(2,1)S(1)} %collective-permute-done.63) | copy-start | bytes 1966084
  19.0 9.3 %collective-permute-start.64 = (bf16[2,1280,256]{2,1,0:T(8,128)(2,1)S(1)}, bf16[2,1280,256]{2,1,0:T(8,128)(2,1)}, u32[]{:S(2)}, u32[]{:S(2)}) collective-permute-start(bf16[2,1280,256]{2,1,0:T(8,128)(2,1)S(1)} %pad_maximum_fusion.1), channel_id=1, source_target_pairs={{0,1},{1,0},{2,3},{3,2},{4,5},{5,4},{6,7},{7,6},{8,9},{9,8},{10,11... | collective-permute-start | bytes 3932168 | tf_op jit(solution)/shard_map/ppermute | solution.py:26
  25.7 1.6 copy-start.8
  25.7 2.6 %copy-start.4 = (bf16[1280,256]{1,0:T(8,128)(2,1)S(1)}, bf16[1280,256]{1,0:T(8,128)(2,1)}, u32[]{:S(2)}) copy-start(bf16[1280,256]{1,0:T(8,128)(2,1)} %param.75) | copy-start | bytes 1966084
  25.7 2.6 %copy-start.6 = (bf16[1280,256]{1,0:T(8,128)(2,1)S(1)}, bf16[1280,256]{1,0:T(8,128)(2,1)}, u32[]{:S(2)}) copy-start(bf16[1280,256]{1,0:T(8,128)(2,1)} %copy-done.5) | copy-start | bytes 1966084
  27.7 3.8 %copy-start.7 = (bf16[320,128]{1,0:T(8,128)(2,1)}, bf16[320,128]{1,0:T(8,128)(2,1)S(1)}, u32[]{:S(2)}) copy-start(bf16[320,128]{1,0:T(8,128)(2,1)S(1)} %convolution_convert_fusion) | copy-start | bytes 245764
  31.6 28.6 %copy-start.1 = (bf16[1,320,1152]{2,1,0:T(8,128)(2,1)}, bf16[1,320,1152]{2,1,0:T(8,128)(2,1)S(1)}, u32[]{:S(2)}) copy-start(bf16[1,320,1152]{2,1,0:T(8,128)(2,1)S(1)} %get-tuple-element.740) | copy-start | bytes 2211844
  31.6 21.1 %collective-permute-start.65 = (bf16[320,1152]{1,0:T(8,128)(2,1)S(1)}, bf16[320,1152]{1,0:T(8,128)(2,1)S(1)}, u32[]{:S(2)}, u32[]{:S(2)}) collective-permute-start(bf16[320,1152]{1,0:T(8,128)(2,1)S(1)} %get-tuple-element.741), channel_id=1, source_target_pairs={{0,2},{1,3},{2,0},{3,1},{4,6},{5,7},{6,4},{7,5},{8,10},{9,11},{10,... | collective-permute-start | bytes 2211848 | tf_op jit(solution)/shard_map/ppermute | solution.py:24
  52.7 0.9 copy-start.3
  53.6 6.6 %copy-start.12 = (s32[1,4]{1,0:T(1,128)S(1)}, s32[1,4]{1,0:T(1,128)}, u32[]{:S(2)}) copy-start(s32[1,4]{1,0:T(1,128)} %param.80) | copy-start | bytes 52
  53.6 6.8 %copy-start.2 = (bf16[32,16384]{1,0:T(8,128)(2,1)S(1)}, bf16[32,16384]{1,0:T(8,128)(2,1)}, u32[]{:S(2)}) copy-start(bf16[32,16384]{1,0:T(8,128)(2,1)} %param.81) | copy-start | bytes 3145732
  54.9 8.9 %collective-permute-start.66 = (bf16[2,320,1152]{2,1,0:T(8,128)(2,1)}, bf16[2,320,1152]{2,1,0:T(8,128)(2,1)}, u32[]{:S(2)}, u32[]{:S(2)}) collective-permute-start(bf16[2,320,1152]{2,1,0:T(8,128)(2,1)} %pad_maximum_fusion), channel_id=1, source_target_pairs={{0,1},{1,0},{2,3},{3,2},{4,5},{5,4},{6,7},{7,6},{8,9},{9,8},{10,11... | collective-permute-start | bytes 4423688 | tf_op jit(solution)/shard_map/ppermute | solution.py:26
  60.5 0.7 copy-start.11
  66.9 10.6 %collective-permute-start.67 = (bf16[128,1152]{1,0:T(8,128)(2,1)S(1)}, bf16[128,1152]{1,0:T(8,128)(2,1)S(1)}, u32[]{:S(2)}, u32[]{:S(2)}) collective-permute-start(bf16[128,1152]{1,0:T(8,128)(2,1)S(1)} %dynamic-slice_convert_fusion), channel_id=1, source_target_pairs={{0,4},{4,0},{8,12},{12,8},{16,20},{20,16},{24,28},{28,24},{32,36},... | collective-permute-start | bytes 884744 | tf_op jit(solution)/shard_map/ppermute | solution.py:75
  77.6 9.8 %collective-permute-start.68 = (bf16[32,1152]{1,0:T(8,128)(2,1)S(1)}, bf16[32,1152]{1,0:T(8,128)(2,1)S(1)}, u32[]{:S(2)}, u32[]{:S(2)}) collective-permute-start(bf16[32,1152]{1,0:T(8,128)(2,1)S(1)} %get-tuple-element.745), channel_id=1, source_target_pairs={{0,1},{1,0},{2,3},{3,2},{4,5},{5,4},{6,7},{7,6},{8,9},{9,8},{10,11... | collective-permute-start | bytes 221192 | tf_op jit(solution)/shard_map/ppermute | solution.py:88
  80.3 7.3 %collective-permute-start.69 = (bf16[32,1152]{1,0:T(8,128)(2,1)S(1)}, bf16[32,1152]{1,0:T(8,128)(2,1)S(1)}, u32[]{:S(2)}, u32[]{:S(2)}) collective-permute-start(bf16[32,1152]{1,0:T(8,128)(2,1)S(1)} %get-tuple-element.744), channel_id=1, source_target_pairs={{0,2},{1,3},{2,0},{3,1},{4,6},{5,7},{6,4},{7,5},{8,10},{9,11},{10,... | collective-permute-start | bytes 221192 | tf_op jit(solution)/shard_map/ppermute | solution.py:88
  85.1 7.6 %collective-permute-start.70 = (bf16[32,1152]{1,0:T(8,128)(2,1)S(1)}, bf16[32,1152]{1,0:T(8,128)(2,1)S(1)}, u32[]{:S(2)}, u32[]{:S(2)}) collective-permute-start(bf16[32,1152]{1,0:T(8,128)(2,1)S(1)} %get-tuple-element.743), channel_id=1, source_target_pairs={{0,3},{1,2},{2,1},{3,0},{4,7},{5,6},{6,5},{7,4},{8,11},{9,10},{10,... | collective-permute-start | bytes 221192 | tf_op jit(solution)/shard_map/ppermute | solution.py:88
  94.7 24.7 %collective-permute-start.35 = (bf16[32,1152]{1,0:T(8,128)(2,1)S(1)}, bf16[32,1152]{1,0:T(8,128)(2,1)}, u32[]{:S(2)}, u32[]{:S(2)}) collective-permute-start(bf16[32,1152]{1,0:T(8,128)(2,1)S(1)} %dynamic-slice_bitcast_fusion.35), channel_id=1, source_target_pairs={{0,288},{4,292},{8,296},{12,300},{16,304},{20,308},{24,312},{28,31... | collective-permute-start | bytes 221192 | tf_op jit(solution)/shard_map/while/body/eval_jaxpr/cond/branch_36_fun/ppermute | solution.py:18
  122.3 12.4 %collective-permute-start.13 = (bf16[32,1152]{1,0:T(8,128)(2,1)S(1)}, bf16[32,1152]{1,0:T(8,128)(2,1)}, u32[]{:S(2)}, u32[]{:S(2)}) collective-permute-start(bf16[32,1152]{1,0:T(8,128)(2,1)S(1)} %dynamic-slice_bitcast_fusion.13), channel_id=1, source_target_pairs={{0,112},{4,116},{8,120},{12,124},{16,96},{20,100},{24,104},{28,108... | collective-permute-start | bytes 221192 | tf_op jit(solution)/shard_map/while/body/eval_jaxpr/cond/branch_14_fun/ppermute | solution.py:18
  137.5 8.5 %collective-permute-start.4 = (bf16[32,1152]{1,0:T(8,128)(2,1)S(1)}, bf16[32,1152]{1,0:T(8,128)(2,1)}, u32[]{:S(2)}, u32[]{:S(2)}) collective-permute-start(bf16[32,1152]{1,0:T(8,128)(2,1)S(1)} %dynamic-slice_bitcast_fusion.4), channel_id=1, source_target_pairs={{0,40},{4,44},{8,32},{12,36},{16,56},{20,60},{24,48},{28,52},{32,8... | collective-permute-start | bytes 221192 | tf_op jit(solution)/shard_map/while/body/eval_jaxpr/cond/branch_5_fun/ppermute | solution.py:18
  148.8 16.5 %collective-permute-start.15 = (bf16[32,1152]{1,0:T(8,128)(2,1)S(1)}, bf16[32,1152]{1,0:T(8,128)(2,1)}, u32[]{:S(2)}, u32[]{:S(2)}) collective-permute-start(bf16[32,1152]{1,0:T(8,128)(2,1)S(1)} %dynamic-slice_bitcast_fusion.15), channel_id=1, source_target_pairs={{0,128},{4,132},{8,136},{12,140},{16,144},{20,148},{24,152},{28,15... | collective-permute-start | bytes 221192 | tf_op jit(solution)/shard_map/while/body/eval_jaxpr/cond/branch_16_fun/ppermute | solution.py:18
  175.8 1.1 copy-start.9

commit v6 on v5

--- a/solution.py
+++ b/solution.py
@@ -103,18 +103,22 @@
     routed = lax.fori_loop(0, col_count, route_piece, jnp.zeros_like(spread))
     tile_size = coupled_width // col_count
     front_part = routed[:, :, :coupled_width].reshape(col_count, share_rows, col_count, tile_size)
-    tile_values = jnp.transpose(front_part, (1, 0, 2, 3)).reshape(
-        share_rows, col_count * col_count, tile_size
-    )
     target_tiles = jnp.bitwise_xor(
         jnp.bitwise_xor(column_masks[:, None], column_masks[None, :]), leaf_index // 2
-    ).reshape(-1)
+    )
     front_width = root_front.shape[1]
-    assembled = root_front.astype(jnp.float32).reshape(
-        share_rows, front_width // tile_size, tile_size
-    )
-    assembled = assembled.at[:, target_tiles, :].add(tile_values.astype(jnp.float32))
-    assembled_front = assembled.reshape(share_rows, front_width).astype(jnp.bfloat16)
+    placement = (
+        target_tiles[:, :, None]
+        == lax.broadcasted_iota(jnp.int32, (col_count, col_count, front_width // tile_size), 2)
+    ).astype(front_part.dtype)
+    by_row = jnp.transpose(front_part, (1, 0, 2, 3))
+    update = lax.dot_general(
+        jnp.broadcast_to(placement, (share_rows,) + placement.shape),
+        by_row,
+        (((1, 2), (1, 2)), ((0,), (0,))),
+        preferred_element_type=jnp.float32,
+    ).reshape(share_rows, front_width)
+    assembled_front = (root_front.astype(jnp.float32) + update).astype(jnp.bfloat16)
     assembled_rhs = root_rhs.astype(jnp.float32) + jnp.sum(
         routed[:, :, coupled_width:].astype(jnp.float32), axis=0
     )

time: 180 us -> 185 us (1.028)
  waiting for transfers between devices: 52.1 us -> 80.2 us
  local copies, waits for them, and re-layouts: 21.3 us -> 11.2 us
  starting transfers between devices: 83.7 us -> 75.6 us
  other arithmetic: 8.97 us -> 4.96 us
    ppermute x4 -> x3, waiting for transfers between devices: 11.6 us -> 38 us  [branch(): return lambda x: lax.ppermute(x, LEAF, pairs)]
    ppermute x4 -> x3, starting transfers between devices: 50.4 us -> 41.6 us  [branch(): return lambda x: lax.ppermute(x, LEAF, pairs)]
    convert_element_type x3 -> x0, local copies, waits for them, and re-layouts: 5.06 us -> none  [the longest x2 4.03 us: body(): tile_values.astype(jnp.float32)]
    dynamic_update_slice x4, local copies, waits for them, and re-layouts: 6.07 us -> 3.59 us  [route_piece(): return lax.dynamic_update_index_in_dim(routed, sent, a, 0)]
    scatter-add x1 -> x0, other arithmetic: 2.16 us -> none  [body(): assembled.at[:, target_tiles, :].add(tile_values.astype(jnp.float32))]
    ppermute x2, waiting for transfers between devices: 0.58 us -> 2.74 us  [col_gather(): partner = lax.ppermute(chip, COLS, [(c, c ^ 1) for c in range(4)])]
    gather x1, local copies, waits for them, and re-layouts: 2.53 us -> 0.59 us  [body(): jnp.take(lower_block.reshape(lower_rows, 4, share), source_blocks, axis=1)]
  transfers between devices with their start and end apart: 12 -> 11, of which waited for: 10 -> 10; matrix products, arithmetic and copies ran while one was open for 4% -> 2% of each run, Pallas kernels for 0% -> 0%
where the time goes in v6:
time: 185 us; the launch traced here: 184 us
  waiting for transfers between devices  80.2 us (43%)
  starting transfers between devices  75.6 us (41%)
  local copies, waits for them, and re-layouts  11.2 us (6%)
  matrix products  7.5 us (4%)
  other arithmetic  4.96 us (3%)
  loops' own time  2.94 us (2%)
    ppermute x3, starting transfers between devices, branch(): return lambda x: lax.ppermute(x, LEAF, pairs)  41.6 us
    ppermute x3, waiting for transfers between devices, branch(): return lambda x: lax.ppermute(x, LEAF, pairs)  38 us
    ppermute x2, waiting for transfers between devices, col_gather(): remote = lax.ppermute(block, COLS, [(c, c ^ 2) for c in range(4)])  27.5 us
    ppermute x2, starting transfers between devices, col_gather(): remote = lax.ppermute(block, COLS, [(c, c ^ 2) for c in range(4)])  10.6 us
    ppermute x3, starting transfers between devices, body(): lax.ppermute(outgoing, COLS, [(c, c ^ distance) for c in range(col_count)])  10.2 us
    ppermute x2, starting transfers between devices, col_gather(): partner = lax.ppermute(chip, COLS, [(c, c ^ 1) for c in range(4)])  9.74 us
    ppermute x1, waiting for transfers between devices, body(): lax.ppermute(other_rows.astype(jnp.bfloat16), LEAF, [(s, s ^ 1) for s in...  6.72 us
    ppermute x3, waiting for transfers between devices, body(): lax.ppermute(outgoing, COLS, [(c, c ^ distance) for c in range(col_count)])  5.2 us
  transfers between devices with their start and end apart: 11, of which 10 were waited for; matrix products, arithmetic and copies ran while one was open for 2% of the time, Pallas kernels for 0%

profile of v6, /device:TPU:1, one launch (start us, length us, event | category | flops | bytes accessed | tf_op | source)
XLA Modules:
  0.0 183.5 jit_solution(9185943102467635814)
XLA Ops:
  0.6 0.0 copy-start
  0.7 5.6 %collective-permute-start.63 = (bf16[1280,256]{1,0:T(8,128)(2,1)}, bf16[1280,256]{1,0:T(8,128)(2,1)S(1)}, u32[]{:S(2)}, u32[]{:S(2)}) collective-permute-start(bf16[1280,256]{1,0:T(8,128)(2,1)} %param.75), channel_id=1, source_target_pairs={{0,2},{1,3},{2,0},{3,1},{4,6},{5,7},{6,4},{7,5},{8,10},{9,11},{10,... | collective-permute-start | bytes 1966088 | tf_op jit(solution)/shard_map/ppermute | solution.py:24
  6.3 11.3 %collective-permute-done.63 = bf16[1280,256]{1,0:T(8,128)(2,1)S(1)} collective-permute-done((bf16[1280,256]{1,0:T(8,128)(2,1)}, bf16[1280,256]{1,0:T(8,128)(2,1)S(1)}, u32[]{:S(2)}, u32[]{:S(2)}) %collective-permute-start.63) | collective-permute-done | bytes 655392 | tf_op jit(solution)/shard_map/ppermute | solution.py:24
  17.6 1.2 pad_maximum_fusion.1
  18.8 6.5 %collective-permute-start.64 = (bf16[2,1280,256]{2,1,0:T(8,128)(2,1)S(1)}, bf16[2,1280,256]{2,1,0:T(8,128)(2,1)}, u32[]{:S(2)}, u32[]{:S(2)}) collective-permute-start(bf16[2,1280,256]{2,1,0:T(8,128)(2,1)S(1)} %pad_maximum_fusion.1), channel_id=1, source_target_pairs={{0,1},{1,0},{2,3},{3,2},{4,5},{5,4},{6,7},{7,6},{8,9},{9,8},{10,11... | collective-permute-start | bytes 3932168 | tf_op jit(solution)/shard_map/ppermute | solution.py:26
  25.3 0.1 broadcast_in_dim.247
  25.5 0.0 copy-start.6
  25.5 0.0 copy-start.3
  25.5 1.5 fusion.11
  27.1 0.4 convolution_convert_fusion
  27.4 0.0 copy-start.5
  27.5 0.6 collective-permute-done.64
  28.1 2.3 %fusion.15 = bf16[320,4,256]{2,0,1:T(8,128)(2,1)S(1)} fusion(bf16[2,1280,256]{2,1,0:T(8,128)(2,1)} %collective-permute-done.64, bf16[1,1280,256]{2,1,0:T(8,128)(2,1)S(1)} %bitcast.248, bf16[1,1280,256]{2,1,0:T(8,128)(2,1)S(1)} %bitcast.246, bf16[1280,320]{0,1:T(8,128)(2,1)S(1)} %fusion.11), kind=kOutput, calls=%fused_computation.80 | convolution fusion | flops 846725120 | bytes 4096000 | tf_op jit(solution)/shard_map/ip,kpn->ikn/dot_general | solution.py:56
  30.4 0.6 gather_fusion.1
  31.0 0.1 copy.18
  31.1 0.2 select_convert_fusion
  31.3 0.1 fusion.40
  31.4 5.0 %collective-permute-start.65 = (bf16[320,1152]{1,0:T(8,128)(2,1)S(1)}, bf16[320,1152]{1,0:T(8,128)(2,1)S(1)}, u32[]{:S(2)}, u32[]{:S(2)}) collective-permute-start(bf16[320,1152]{1,0:T(8,128)(2,1)S(1)} %get-tuple-element.741), channel_id=1, source_target_pairs={{0,2},{1,3},{2,0},{3,1},{4,6},{5,7},{6,4},{7,5},{8,10},{9,11},{10,... | collective-permute-start | bytes 2211848 | tf_op jit(solution)/shard_map/ppermute | solution.py:24
  36.4 16.2 %collective-permute-done.65 = bf16[320,1152]{1,0:T(8,128)(2,1)S(1)} collective-permute-done((bf16[320,1152]{1,0:T(8,128)(2,1)S(1)}, bf16[320,1152]{1,0:T(8,128)(2,1)S(1)}, u32[]{:S(2)}, u32[]{:S(2)}) %collective-permute-start.65) | collective-permute-done | bytes 737312 | tf_op jit(solution)/shard_map/ppermute | solution.py:24
  52.6 0.9 copy-done.2
  53.5 1.3 pad_maximum_fusion
  54.8 3.2 %collective-permute-start.66 = (bf16[2,320,1152]{2,1,0:T(8,128)(2,1)}, bf16[2,320,1152]{2,1,0:T(8,128)(2,1)}, u32[]{:S(2)}, u32[]{:S(2)}) collective-permute-start(bf16[2,320,1152]{2,1,0:T(8,128)(2,1)} %pad_maximum_fusion), channel_id=1, source_target_pairs={{0,1},{1,0},{2,3},{3,2},{4,5},{5,4},{6,7},{7,6},{8,9},{9,8},{10,11... | collective-permute-start | bytes 4423688 | tf_op jit(solution)/shard_map/ppermute | solution.py:26
  58.1 0.2 copy.13
  58.4 0.6 gather_fusion
  59.0 0.1 xor_xor_fusion
  59.1 2.1 %collective-permute-done.66 = bf16[2,320,1152]{2,1,0:T(8,128)(2,1)} collective-permute-done((bf16[2,320,1152]{2,1,0:T(8,128)(2,1)}, bf16[2,320,1152]{2,1,0:T(8,128)(2,1)}, u32[]{:S(2)}, u32[]{:S(2)}) %collective-permute-start.66) | collective-permute-done | bytes 1474592 | tf_op jit(solution)/shard_map/ppermute | solution.py:26
  61.2 2.7 %fusion.12 = f32[256,1152]{1,0:T(8,128)S(1)} fusion(bf16[2,320,1152]{2,1,0:T(8,128)(2,1)} %collective-permute-done.66, bf16[1,320,1152]{2,1,0:T(8,128)(2,1)} %bitcast.244, bf16[1,320,1152]{2,1,0:T(8,128)(2,1)S(1)} %get-tuple-element.740, bf16[4,256,320]{1,2,0:T(8,128)(2,1)S(1)} %gather_fusion, pred[4]{0:T(512)(128)(4,1)S(1)} %get-tuple-element.738), kind=kOutput, calls=%fused_computation.79 | convolution fusion | flops 758546432 | bytes 4784132 | tf_op jit(solution)/shard_map/rkp,kpn->rn/dot_general | solution.py:65
  64.0 3.4 %collective-permute-start.67 = (bf16[128,1152]{1,0:T(8,128)(2,1)S(1)}, bf16[128,1152]{1,0:T(8,128)(2,1)S(1)}, u32[]{:S(2)}, u32[]{:S(2)}) collective-permute-start(bf16[128,1152]{1,0:T(8,128)(2,1)S(1)} %dynamic-slice_convert_fusion), channel_id=1, source_target_pairs={{0,4},{4,0},{8,12},{12,8},{16,20},{20,16},{24,28},{28,24},{32,36},... | collective-permute-start | bytes 884744 | tf_op jit(solution)/shard_map/ppermute | solution.py:75
  67.4 0.1 fusion.30
  67.5 6.7 %collective-permute-done.67 = bf16[128,1152]{1,0:T(8,128)(2,1)S(1)} collective-permute-done((bf16[128,1152]{1,0:T(8,128)(2,1)S(1)}, bf16[128,1152]{1,0:T(8,128)(2,1)S(1)}, u32[]{:S(2)}, u32[]{:S(2)}) %collective-permute-start.67) | collective-permute-done | bytes 294944 | tf_op jit(solution)/shard_map/ppermute | solution.py:75
  74.2 0.1 add_convert_fusion.1
  74.3 3.0 %collective-permute-start.68 = (bf16[32,1152]{1,0:T(8,128)(2,1)S(1)}, bf16[32,1152]{1,0:T(8,128)(2,1)S(1)}, u32[]{:S(2)}, u32[]{:S(2)}) collective-permute-start(bf16[32,1152]{1,0:T(8,128)(2,1)S(1)} %get-tuple-element.745), channel_id=1, source_target_pairs={{0,1},{1,0},{2,3},{3,2},{4,5},{5,4},{6,7},{7,6},{8,9},{9,8},{10,11... | collective-permute-start | bytes 221192 | tf_op jit(solution)/shard_map/ppermute | solution.py:88
  77.4 4.8 %collective-permute-start.69 = (bf16[32,1152]{1,0:T(8,128)(2,1)S(1)}, bf16[32,1152]{1,0:T(8,128)(2,1)S(1)}, u32[]{:S(2)}, u32[]{:S(2)}) collective-permute-start(bf16[32,1152]{1,0:T(8,128)(2,1)S(1)} %get-tuple-element.744), channel_id=1, source_target_pairs={{0,2},{1,3},{2,0},{3,1},{4,6},{5,7},{6,4},{7,5},{8,10},{9,11},{10,... | collective-permute-start | bytes 221192 | tf_op jit(solution)/shard_map/ppermute | solution.py:88
  82.2 2.3 %collective-permute-start.70 = (bf16[32,1152]{1,0:T(8,128)(2,1)S(1)}, bf16[32,1152]{1,0:T(8,128)(2,1)S(1)}, u32[]{:S(2)}, u32[]{:S(2)}) collective-permute-start(bf16[32,1152]{1,0:T(8,128)(2,1)S(1)} %get-tuple-element.743), channel_id=1, source_target_pairs={{0,3},{1,2},{2,1},{3,0},{4,7},{5,6},{6,5},{7,4},{8,11},{9,10},{10,... | collective-permute-start | bytes 221192 | tf_op jit(solution)/shard_map/ppermute | solution.py:88
  84.6 0.1 collective-permute-done.69
  84.7 5.1 %collective-permute-done.70 = bf16[32,1152]{1,0:T(8,128)(2,1)S(1)} collective-permute-done((bf16[32,1152]{1,0:T(8,128)(2,1)S(1)}, bf16[32,1152]{1,0:T(8,128)(2,1)S(1)}, u32[]{:S(2)}, u32[]{:S(2)}) %collective-permute-start.70) | collective-permute-done | bytes 73760 | tf_op jit(solution)/shard_map/ppermute | solution.py:88
  89.8 0.6 gather_fusion.2
  90.4 0.1 broadcast_select_fusion
  90.5 89.2 %while.13 = (s32[]{:T(128)}, bf16[4,32,1152]{2,1,0:T(8,128)(2,1)S(1)}, s32[4]{0:T(128)S(1)}, bf16[4,32,1152]{2,1,0:T(8,128)(2,1)S(1)}, s32[]{:T(128)}, /*index=5*/s32[1]{0:T(128)}, s32[1]{0:T(128)}) while((s32[]{:T(128)}, bf16[4,32,1152]{2,1,0:T(8,128)(2,1)S(1)}, s32[4]{0:T(128)S(1)}, bf16[4,32,1152]{2,1,0:T(8,128)(2,1)S(1)}, s32[]{:T(128)}, ...), condition=%wide.region_65.66_spmd, body=%wide.region_0.65_spmd.sunk | while | flops 3 | bytes 590001 | solution.py:103
  90.5 0.6 dynamic_slice.365
  91.8 0.7 conditional.2
  91.8 0.6 constant_dynamic-slice_fusion
  92.4 0.9 constant_dynamic-update-slice_fusion.2
  93.3 0.6 dynamic_slice.365
  94.6 16.2 %conditional.2 = (bf16[1,32,1152]{2,1,0:T(8,128)(2,1)}) conditional(s32[]{:T(128)} %bitcast.236, (bf16[4,32,1152]{2,1,0:T(8,128)(2,1)S(1)}, s32[]{:T(128)}) %tuple.363, (bf16[4,32,1152]{2,1,0:T(8,128)(2,1)S(1)}, s32[]{:T(128)}) %tuple.363, (bf16[4,32,1152]{2,1,0:T(8,128)(2,1)S(1)}, s32[]{:T(128)}) %tuple.363, ...), branch_computations={%region_1.1_spmd, %region_2.2_spmd, %region_3.3_spmd, %region_4.4_... | conditional | bytes 442420 | solution.py:100
  94.7 12.0 %collective-permute-start.25 = (bf16[32,1152]{1,0:T(8,128)(2,1)S(1)}, bf16[32,1152]{1,0:T(8,128)(2,1)}, u32[]{:S(2)}, u32[]{:S(2)}) collective-permute-start(bf16[32,1152]{1,0:T(8,128)(2,1)S(1)} %dynamic-slice_bitcast_fusion.25), channel_id=1, source_target_pairs={{0,208},{4,212},{8,216},{12,220},{16,192},{20,196},{24,200},{28,20... | collective-permute-start | bytes 221192 | tf_op jit(solution)/shard_map/while/body/eval_jaxpr/cond/branch_26_fun/ppermute | solution.py:18
  106.7 4.1 %collective-permute-done.25 = bf16[32,1152]{1,0:T(8,128)(2,1)} collective-permute-done((bf16[32,1152]{1,0:T(8,128)(2,1)S(1)}, bf16[32,1152]{1,0:T(8,128)(2,1)}, u32[]{:S(2)}, u32[]{:S(2)}) %collective-permute-start.25) | collective-permute-done | bytes 73760 | tf_op jit(solution)/shard_map/while/body/eval_jaxpr/cond/branch_26_fun/ppermute | solution.py:18
  110.8 0.9 constant_dynamic-update-slice_fusion.2
  111.7 0.6 dynamic_slice.365
  113.0 30.2 %conditional.2 = (bf16[1,32,1152]{2,1,0:T(8,128)(2,1)}) conditional(s32[]{:T(128)} %bitcast.236, (bf16[4,32,1152]{2,1,0:T(8,128)(2,1)S(1)}, s32[]{:T(128)}) %tuple.363, (bf16[4,32,1152]{2,1,0:T(8,128)(2,1)S(1)}, s32[]{:T(128)}) %tuple.363, (bf16[4,32,1152]{2,1,0:T(8,128)(2,1)S(1)}, s32[]{:T(128)}) %tuple.363, ...), branch_computations={%region_1.1_spmd, %region_2.2_spmd, %region_3.3_spmd, %region_4.4_... | conditional | bytes 442420 | solution.py:100
  113.0 15.8 %collective-permute-start.56 = (bf16[32,1152]{1,0:T(8,128)(2,1)S(1)}, bf16[32,1152]{1,0:T(8,128)(2,1)}, u32[]{:S(2)}, u32[]{:S(2)}) collective-permute-start(bf16[32,1152]{1,0:T(8,128)(2,1)S(1)} %dynamic-slice_bitcast_fusion.56), channel_id=1, source_target_pairs={{0,456},{4,460},{8,448},{12,452},{16,472},{20,476},{24,464},{28,46... | collective-permute-start | bytes 221192 | tf_op jit(solution)/shard_map/while/body/eval_jaxpr/cond/branch_57_fun/ppermute | solution.py:18
  128.8 14.3 %collective-permute-done.56 = bf16[32,1152]{1,0:T(8,128)(2,1)} collective-permute-done((bf16[32,1152]{1,0:T(8,128)(2,1)S(1)}, bf16[32,1152]{1,0:T(8,128)(2,1)}, u32[]{:S(2)}, u32[]{:S(2)}) %collective-permute-start.56) | collective-permute-done | bytes 73760 | tf_op jit(solution)/shard_map/while/body/eval_jaxpr/cond/branch_57_fun/ppermute | solution.py:18
  143.1 0.9 constant_dynamic-update-slice_fusion.2
  144.0 0.6 dynamic_slice.365
  145.3 33.5 %conditional.2 = (bf16[1,32,1152]{2,1,0:T(8,128)(2,1)}) conditional(s32[]{:T(128)} %bitcast.236, (bf16[4,32,1152]{2,1,0:T(8,128)(2,1)S(1)}, s32[]{:T(128)}) %tuple.363, (bf16[4,32,1152]{2,1,0:T(8,128)(2,1)S(1)}, s32[]{:T(128)}) %tuple.363, (bf16[4,32,1152]{2,1,0:T(8,128)(2,1)S(1)}, s32[]{:T(128)}) %tuple.363, ...), branch_computations={%region_1.1_spmd, %region_2.2_spmd, %region_3.3_spmd, %region_4.4_... | conditional | bytes 442420 | solution.py:100
  145.3 13.8 %collective-permute-start.49 = (bf16[32,1152]{1,0:T(8,128)(2,1)S(1)}, bf16[32,1152]{1,0:T(8,128)(2,1)}, u32[]{:S(2)}, u32[]{:S(2)}) collective-permute-start(bf16[32,1152]{1,0:T(8,128)(2,1)S(1)} %dynamic-slice_bitcast_fusion.49), channel_id=1, source_target_pairs={{0,400},{4,404},{8,408},{12,412},{16,384},{20,388},{24,392},{28,39... | collective-permute-start | bytes 221192 | tf_op jit(solution)/shard_map/while/body/eval_jaxpr/cond/branch_50_fun/ppermute | solution.py:18
  159.2 19.6 %collective-permute-done.49 = bf16[32,1152]{1,0:T(8,128)(2,1)} collective-permute-done((bf16[32,1152]{1,0:T(8,128)(2,1)S(1)}, bf16[32,1152]{1,0:T(8,128)(2,1)}, u32[]{:S(2)}, u32[]{:S(2)}) %collective-permute-start.49) | collective-permute-done | bytes 73760 | tf_op jit(solution)/shard_map/while/body/eval_jaxpr/cond/branch_50_fun/ppermute | solution.py:18
  178.8 0.9 constant_dynamic-update-slice_fusion.2
  179.7 0.2 reshape.202
  179.9 0.6 fusion.26
  180.5 1.2 copy.19
  181.7 0.0 copy-start.7
  181.7 1.1 add_convert_fusion
  182.9 0.6 convert_add_fusion
  (36 shorter events, 0.3 us)
Async XLA Ops:
  0.6 24.8 %copy-start = (bf16[320,1280]{1,0:T(8,128)(2,1)S(1)}, bf16[320,1280]{1,0:T(8,128)(2,1)}, u32[]{:S(2)}) copy-start(bf16[320,1280]{1,0:T(8,128)(2,1)} %param.77) | copy-start | bytes 2457604
  0.6 24.8 %copy-start.8 = (s32[1,1280]{1,0:T(1,128)S(1)}, s32[1,1280]{1,0:T(1,128)}, u32[]{:S(2)}) copy-start(s32[1,1280]{1,0:T(1,128)} %param.78) | copy-start | bytes 15364
  0.7 16.9 %collective-permute-start.63 = (bf16[1280,256]{1,0:T(8,128)(2,1)}, bf16[1280,256]{1,0:T(8,128)(2,1)S(1)}, u32[]{:S(2)}, u32[]{:S(2)}) collective-permute-start(bf16[1280,256]{1,0:T(8,128)(2,1)} %param.75), channel_id=1, source_target_pairs={{0,2},{1,3},{2,0},{3,1},{4,6},{5,7},{6,4},{7,5},{8,10},{9,11},{10,... | collective-permute-start | bytes 1966088 | tf_op jit(solution)/shard_map/ppermute | solution.py:24
  18.8 9.3 %collective-permute-start.64 = (bf16[2,1280,256]{2,1,0:T(8,128)(2,1)S(1)}, bf16[2,1280,256]{2,1,0:T(8,128)(2,1)}, u32[]{:S(2)}, u32[]{:S(2)}) collective-permute-start(bf16[2,1280,256]{2,1,0:T(8,128)(2,1)S(1)} %pad_maximum_fusion.1), channel_id=1, source_target_pairs={{0,1},{1,0},{2,3},{3,2},{4,5},{5,4},{6,7},{7,6},{8,9},{9,8},{10,11... | collective-permute-start | bytes 3932168 | tf_op jit(solution)/shard_map/ppermute | solution.py:26
  25.5 1.6 copy-start.6
  25.5 2.6 %copy-start.3 = (bf16[1280,256]{1,0:T(8,128)(2,1)S(1)}, bf16[1280,256]{1,0:T(8,128)(2,1)}, u32[]{:S(2)}) copy-start(bf16[1280,256]{1,0:T(8,128)(2,1)} %param.75) | copy-start | bytes 1966084
  27.4 3.8 %copy-start.5 = (bf16[320,128]{1,0:T(8,128)(2,1)}, bf16[320,128]{1,0:T(8,128)(2,1)S(1)}, u32[]{:S(2)}) copy-start(bf16[320,128]{1,0:T(8,128)(2,1)S(1)} %convolution_convert_fusion) | copy-start | bytes 245764
  31.4 26.7 %copy-start.4 = (bf16[256,1280]{1,0:T(8,128)(2,1)S(1)}, bf16[256,1280]{1,0:T(8,128)(2,1)}, u32[]{:S(2)}) copy-start(bf16[256,1280]{1,0:T(8,128)(2,1)} %param.76) | copy-start | bytes 1966084
  31.4 21.2 %collective-permute-start.65 = (bf16[320,1152]{1,0:T(8,128)(2,1)S(1)}, bf16[320,1152]{1,0:T(8,128)(2,1)S(1)}, u32[]{:S(2)}, u32[]{:S(2)}) collective-permute-start(bf16[320,1152]{1,0:T(8,128)(2,1)S(1)} %get-tuple-element.741), channel_id=1, source_target_pairs={{0,2},{1,3},{2,0},{3,1},{4,6},{5,7},{6,4},{7,5},{8,10},{9,11},{10,... | collective-permute-start | bytes 2211848 | tf_op jit(solution)/shard_map/ppermute | solution.py:24
  52.6 0.9 copy-start.2
  53.5 4.8 %copy-start.9 = (s32[4]{0:T(128)S(1)}, s32[4]{0:T(128)}, u32[]{:S(2)}) copy-start(s32[4]{0:T(128)} %constant.288.clone) | copy-start | bytes 52
  54.8 4.2 %copy-start.10 = (s32[1,4]{1,0:T(1,128)S(1)}, s32[1,4]{1,0:T(1,128)}, u32[]{:S(2)}) copy-start(s32[1,4]{1,0:T(1,128)} %param.80) | copy-start | bytes 52
  54.8 6.5 %collective-permute-start.66 = (bf16[2,320,1152]{2,1,0:T(8,128)(2,1)}, bf16[2,320,1152]{2,1,0:T(8,128)(2,1)}, u32[]{:S(2)}, u32[]{:S(2)}) collective-permute-start(bf16[2,320,1152]{2,1,0:T(8,128)(2,1)} %pad_maximum_fusion), channel_id=1, source_target_pairs={{0,1},{1,0},{2,3},{3,2},{4,5},{5,4},{6,7},{7,6},{8,9},{9,8},{10,11... | collective-permute-start | bytes 4423688 | tf_op jit(solution)/shard_map/ppermute | solution.py:26
  64.0 10.2 %collective-permute-start.67 = (bf16[128,1152]{1,0:T(8,128)(2,1)S(1)}, bf16[128,1152]{1,0:T(8,128)(2,1)S(1)}, u32[]{:S(2)}, u32[]{:S(2)}) collective-permute-start(bf16[128,1152]{1,0:T(8,128)(2,1)S(1)} %dynamic-slice_convert_fusion), channel_id=1, source_target_pairs={{0,4},{4,0},{8,12},{12,8},{16,20},{20,16},{24,28},{28,24},{32,36},... | collective-permute-start | bytes 884744 | tf_op jit(solution)/shard_map/ppermute | solution.py:75
  74.3 10.2 %collective-permute-start.68 = (bf16[32,1152]{1,0:T(8,128)(2,1)S(1)}, bf16[32,1152]{1,0:T(8,128)(2,1)S(1)}, u32[]{:S(2)}, u32[]{:S(2)}) collective-permute-start(bf16[32,1152]{1,0:T(8,128)(2,1)S(1)} %get-tuple-element.745), channel_id=1, source_target_pairs={{0,1},{1,0},{2,3},{3,2},{4,5},{5,4},{6,7},{7,6},{8,9},{9,8},{10,11... | collective-permute-start | bytes 221192 | tf_op jit(solution)/shard_map/ppermute | solution.py:88
  77.4 7.3 %collective-permute-start.69 = (bf16[32,1152]{1,0:T(8,128)(2,1)S(1)}, bf16[32,1152]{1,0:T(8,128)(2,1)S(1)}, u32[]{:S(2)}, u32[]{:S(2)}) collective-permute-start(bf16[32,1152]{1,0:T(8,128)(2,1)S(1)} %get-tuple-element.744), channel_id=1, source_target_pairs={{0,2},{1,3},{2,0},{3,1},{4,6},{5,7},{6,4},{7,5},{8,10},{9,11},{10,... | collective-permute-start | bytes 221192 | tf_op jit(solution)/shard_map/ppermute | solution.py:88
  82.2 7.6 %collective-permute-start.70 = (bf16[32,1152]{1,0:T(8,128)(2,1)S(1)}, bf16[32,1152]{1,0:T(8,128)(2,1)S(1)}, u32[]{:S(2)}, u32[]{:S(2)}) collective-permute-start(bf16[32,1152]{1,0:T(8,128)(2,1)S(1)} %get-tuple-element.743), channel_id=1, source_target_pairs={{0,3},{1,2},{2,1},{3,0},{4,7},{5,6},{6,5},{7,4},{8,11},{9,10},{10,... | collective-permute-start | bytes 221192 | tf_op jit(solution)/shard_map/ppermute | solution.py:88
  94.7 16.1 %collective-permute-start.25 = (bf16[32,1152]{1,0:T(8,128)(2,1)S(1)}, bf16[32,1152]{1,0:T(8,128)(2,1)}, u32[]{:S(2)}, u32[]{:S(2)}) collective-permute-start(bf16[32,1152]{1,0:T(8,128)(2,1)S(1)} %dynamic-slice_bitcast_fusion.25), channel_id=1, source_target_pairs={{0,208},{4,212},{8,216},{12,220},{16,192},{20,196},{24,200},{28,20... | collective-permute-start | bytes 221192 | tf_op jit(solution)/shard_map/while/body/eval_jaxpr/cond/branch_26_fun/ppermute | solution.py:18
  113.0 30.1 %collective-permute-start.56 = (bf16[32,1152]{1,0:T(8,128)(2,1)S(1)}, bf16[32,1152]{1,0:T(8,128)(2,1)}, u32[]{:S(2)}, u32[]{:S(2)}) collective-permute-start(bf16[32,1152]{1,0:T(8,128)(2,1)S(1)} %dynamic-slice_bitcast_fusion.56), channel_id=1, source_target_pairs={{0,456},{4,460},{8,448},{12,452},{16,472},{20,476},{24,464},{28,46... | collective-permute-start | bytes 221192 | tf_op jit(solution)/shard_map/while/body/eval_jaxpr/cond/branch_57_fun/ppermute | solution.py:18
  145.3 33.4 %collective-permute-start.49 = (bf16[32,1152]{1,0:T(8,128)(2,1)S(1)}, bf16[32,1152]{1,0:T(8,128)(2,1)}, u32[]{:S(2)}, u32[]{:S(2)}) collective-permute-start(bf16[32,1152]{1,0:T(8,128)(2,1)S(1)} %dynamic-slice_bitcast_fusion.49), channel_id=1, source_target_pairs={{0,400},{4,404},{8,408},{12,412},{16,384},{20,388},{24,392},{28,39... | collective-permute-start | bytes 221192 | tf_op jit(solution)/shard_map/while/body/eval_jaxpr/cond/branch_50_fun/ppermute | solution.py:18
  180.5 1.2 copy-start.1
  181.7 1.2 copy-start.7

commit v7 on v6

--- a/solution.py
+++ b/solution.py
@@ -20,10 +20,14 @@
     return [branch(2 * step) for step in range(mask_count)]
 
 
-def col_gather(block):
+def col_gather(block, beside=None):
     remote = lax.ppermute(block, COLS, [(c, c ^ 2) for c in range(4)])
+    if beside is not None:
+        remote, beside = lax.optimization_barrier((remote, beside))
     chip = jnp.stack([block, remote])
     partner = lax.ppermute(chip, COLS, [(c, c ^ 1) for c in range(4)])
+    if beside is not None:
+        return jnp.concatenate([chip, partner]), beside
     return jnp.concatenate([chip, partner])
 
 
@@ -40,7 +44,6 @@
     piv = pivot_inverse.shape[1]
     share = pivot_inverse.shape[0]
     col_index = lax.axis_index(COLS)
-    upper_all = col_gather(upper_block)
     order = pivot_perm[0]
     selector = (order[:, None] == lax.broadcasted_iota(jnp.int32, (piv, piv), 1)).astype(
         pivot_inverse.dtype
@@ -51,6 +54,7 @@
     forward = jnp.dot(inverse_perm, child_rhs, preferred_element_type=jnp.float32).astype(
         jnp.bfloat16
     )
+    upper_all, (inverse_perm, forward) = col_gather(upper_block, (inverse_perm, forward))
     canonical = relative_order(col_index)
     eliminated = jnp.take(
         jnp.einsum("ip,kpn->ikn", inverse_perm, upper_all, preferred_element_type=jnp.float32),

time: 185 us -> 185 us (level)
  the two profiles are of different devices: /device:TPU:1 before, /device:TPU:96 now
where the time goes in v7:
time: 185 us; the launch traced here: 184 us
  waiting for transfers between devices  95.7 us (52%)
  starting transfers between devices  59.3 us (32%)
  local copies, waits for them, and re-layouts  11.4 us (6%)
  matrix products  7.85 us (4%)
  other arithmetic  5.65 us (3%)
  loops' own time  2.99 us (2%)
    ppermute x4, waiting for transfers between devices, branch(): return lambda x: lax.ppermute(x, LEAF, pairs)  48.3 us
    ppermute x4, starting transfers between devices, branch(): return lambda x: lax.ppermute(x, LEAF, pairs)  32.5 us
    ppermute x2, waiting for transfers between devices, col_gather(): remote = lax.ppermute(block, COLS, [(c, c ^ 2) for c in range(4)])  29.4 us
    ppermute x2, starting transfers between devices, col_gather(): remote = lax.ppermute(block, COLS, [(c, c ^ 2) for c in range(4)])  10.1 us
    ppermute x3, starting transfers between devices, body(): lax.ppermute(outgoing, COLS, [(c, c ^ distance) for c in range(col_count)])  9.27 us
    ppermute x1, waiting for transfers between devices, body(): lax.ppermute(other_rows.astype(jnp.bfloat16), LEAF, [(s, s ^ 1) for s in...  7.36 us
    ppermute x2, waiting for transfers between devices, col_gather(): partner = lax.ppermute(chip, COLS, [(c, c ^ 1) for c in range(4)])  5.48 us
    ppermute x3, waiting for transfers between devices, body(): lax.ppermute(outgoing, COLS, [(c, c ^ distance) for c in range(col_count)])  5.21 us
  transfers between devices with their start and end apart: 12, of which 11 were waited for; matrix products, arithmetic and copies ran while one was open for 2% of the time, Pallas kernels for 0%

profile of v7, /device:TPU:96, one launch (start us, length us, event | category | flops | bytes accessed | tf_op | source)
XLA Modules:
  0.0 184.1 jit_solution(15978671384369798471)
XLA Ops:
  0.6 0.0 copy-start
  0.6 5.1 %collective-permute-start.63 = (bf16[1280,256]{1,0:T(8,128)(2,1)}, bf16[1280,256]{1,0:T(8,128)(2,1)S(1)}, u32[]{:S(2)}, u32[]{:S(2)}) collective-permute-start(bf16[1280,256]{1,0:T(8,128)(2,1)} %param.75), channel_id=1, source_target_pairs={{0,2},{1,3},{2,0},{3,1},{4,6},{5,7},{6,4},{7,5},{8,10},{9,11},{10,... | collective-permute-start | bytes 1966088 | tf_op jit(solution)/shard_map/ppermute | solution.py:24
  5.7 0.7 reduce
  6.5 1.5 fusion.11
  8.0 0.4 convolution_convert_fusion
  8.4 0.0 copy-start.6
  8.4 12.4 %collective-permute-done.63 = bf16[1280,256]{1,0:T(8,128)(2,1)S(1)} collective-permute-done((bf16[1280,256]{1,0:T(8,128)(2,1)}, bf16[1280,256]{1,0:T(8,128)(2,1)S(1)}, u32[]{:S(2)}, u32[]{:S(2)}) %collective-permute-start.63) | collective-permute-done | bytes 655392 | tf_op jit(solution)/shard_map/ppermute | solution.py:24
  20.9 0.8 copy-done.4
  21.7 1.2 pad_maximum_fusion.1
  22.9 1.9 %collective-permute-start.64 = (bf16[2,1280,256]{2,1,0:T(8,128)(2,1)S(1)}, bf16[2,1280,256]{2,1,0:T(8,128)(2,1)}, u32[]{:S(2)}, u32[]{:S(2)}) collective-permute-start(bf16[2,1280,256]{2,1,0:T(8,128)(2,1)S(1)} %pad_maximum_fusion.1), channel_id=1, source_target_pairs={{0,1},{1,0},{2,3},{3,2},{4,5},{5,4},{6,7},{7,6},{8,9},{9,8},{10,11... | collective-permute-start | bytes 3932168 | tf_op jit(solution)/shard_map/ppermute | solution.py:28
  24.9 0.1 broadcast_in_dim.247
  25.0 3.0 %collective-permute-done.64 = bf16[2,1280,256]{2,1,0:T(8,128)(2,1)} collective-permute-done((bf16[2,1280,256]{2,1,0:T(8,128)(2,1)S(1)}, bf16[2,1280,256]{2,1,0:T(8,128)(2,1)}, u32[]{:S(2)}, u32[]{:S(2)}) %collective-permute-start.64) | collective-permute-done | bytes 1310752 | tf_op jit(solution)/shard_map/ppermute | solution.py:28
  28.0 2.7 %fusion.15 = bf16[320,4,256]{2,0,1:T(8,128)(2,1)S(1)} fusion(bf16[2,1280,256]{2,1,0:T(8,128)(2,1)} %collective-permute-done.64, bf16[1,1280,256]{2,1,0:T(8,128)(2,1)} %bitcast.250, bf16[1,1280,256]{2,1,0:T(8,128)(2,1)} %bitcast.247, bf16[320,1280]{1,0:T(8,128)(2,1)S(1)} %bitcast.244), kind=kOutput, calls=%fused_computation.80 | convolution fusion | flops 846725120 | bytes 4096000 | tf_op jit(solution)/shard_map/ip,kpn->ikn/dot_general | solution.py:60
  30.7 0.6 gather_fusion.1
  31.3 0.1 copy.18
  31.3 0.2 select_convert_fusion
  31.5 0.1 fusion.40
  31.6 5.1 %collective-permute-start.65 = (bf16[320,1152]{1,0:T(8,128)(2,1)S(1)}, bf16[320,1152]{1,0:T(8,128)(2,1)S(1)}, u32[]{:S(2)}, u32[]{:S(2)}) collective-permute-start(bf16[320,1152]{1,0:T(8,128)(2,1)S(1)} %get-tuple-element.747), channel_id=1, source_target_pairs={{0,2},{1,3},{2,0},{3,1},{4,6},{5,7},{6,4},{7,5},{8,10},{9,11},{10,... | collective-permute-start | bytes 2211848 | tf_op jit(solution)/shard_map/ppermute | solution.py:24
  36.7 17.0 %collective-permute-done.65 = bf16[320,1152]{1,0:T(8,128)(2,1)S(1)} collective-permute-done((bf16[320,1152]{1,0:T(8,128)(2,1)S(1)}, bf16[320,1152]{1,0:T(8,128)(2,1)S(1)}, u32[]{:S(2)}, u32[]{:S(2)}) %collective-permute-start.65) | collective-permute-done | bytes 737312 | tf_op jit(solution)/shard_map/ppermute | solution.py:24
  53.7 0.9 copy-done.2
  54.6 1.3 pad_maximum_fusion
  55.9 2.0 %collective-permute-start.66 = (bf16[2,320,1152]{2,1,0:T(8,128)(2,1)}, bf16[2,320,1152]{2,1,0:T(8,128)(2,1)}, u32[]{:S(2)}, u32[]{:S(2)}) collective-permute-start(bf16[2,320,1152]{2,1,0:T(8,128)(2,1)} %pad_maximum_fusion), channel_id=1, source_target_pairs={{0,1},{1,0},{2,3},{3,2},{4,5},{5,4},{6,7},{7,6},{8,9},{9,8},{10,11... | collective-permute-start | bytes 4423688 | tf_op jit(solution)/shard_map/ppermute | solution.py:28
  58.0 0.2 copy.13
  58.3 0.6 gather_fusion
  58.9 0.1 xor_xor_fusion
  59.0 2.5 %collective-permute-done.66 = bf16[2,320,1152]{2,1,0:T(8,128)(2,1)} collective-permute-done((bf16[2,320,1152]{2,1,0:T(8,128)(2,1)}, bf16[2,320,1152]{2,1,0:T(8,128)(2,1)}, u32[]{:S(2)}, u32[]{:S(2)}) %collective-permute-start.66) | collective-permute-done | bytes 1474592 | tf_op jit(solution)/shard_map/ppermute | solution.py:28
  61.5 2.7 %fusion.12 = f32[256,1152]{1,0:T(8,128)S(1)} fusion(bf16[2,320,1152]{2,1,0:T(8,128)(2,1)} %collective-permute-done.66, bf16[1,320,1152]{2,1,0:T(8,128)(2,1)} %bitcast.246, bf16[1,320,1152]{2,1,0:T(8,128)(2,1)S(1)} %get-tuple-element.746, bf16[4,256,320]{1,2,0:T(8,128)(2,1)S(1)} %gather_fusion, pred[4]{0:T(512)(128)(4,1)S(1)} %get-tuple-element.744), kind=kOutput, calls=%fused_computation.79 | convolution fusion | flops 758546432 | bytes 4784132 | tf_op jit(solution)/shard_map/rkp,kpn->rn/dot_general | solution.py:69
  64.2 3.5 %collective-permute-start.67 = (bf16[128,1152]{1,0:T(8,128)(2,1)S(1)}, bf16[128,1152]{1,0:T(8,128)(2,1)S(1)}, u32[]{:S(2)}, u32[]{:S(2)}) collective-permute-start(bf16[128,1152]{1,0:T(8,128)(2,1)S(1)} %dynamic-slice_convert_fusion), channel_id=1, source_target_pairs={{0,4},{4,0},{8,12},{12,8},{16,20},{20,16},{24,28},{28,24},{32,36},... | collective-permute-start | bytes 884744 | tf_op jit(solution)/shard_map/ppermute | solution.py:79
  67.7 0.1 fusion.30
  67.8 7.4 %collective-permute-done.67 = bf16[128,1152]{1,0:T(8,128)(2,1)S(1)} collective-permute-done((bf16[128,1152]{1,0:T(8,128)(2,1)S(1)}, bf16[128,1152]{1,0:T(8,128)(2,1)S(1)}, u32[]{:S(2)}, u32[]{:S(2)}) %collective-permute-start.67) | collective-permute-done | bytes 294944 | tf_op jit(solution)/shard_map/ppermute | solution.py:79
  75.2 0.1 add_convert_fusion.1
  75.3 1.9 %collective-permute-start.68 = (bf16[32,1152]{1,0:T(8,128)(2,1)S(1)}, bf16[32,1152]{1,0:T(8,128)(2,1)S(1)}, u32[]{:S(2)}, u32[]{:S(2)}) collective-permute-start(bf16[32,1152]{1,0:T(8,128)(2,1)S(1)} %get-tuple-element.751), channel_id=1, source_target_pairs={{0,1},{1,0},{2,3},{3,2},{4,5},{5,4},{6,7},{7,6},{8,9},{9,8},{10,11... | collective-permute-start | bytes 221192 | tf_op jit(solution)/shard_map/ppermute | solution.py:92
  77.2 4.9 %collective-permute-start.69 = (bf16[32,1152]{1,0:T(8,128)(2,1)S(1)}, bf16[32,1152]{1,0:T(8,128)(2,1)S(1)}, u32[]{:S(2)}, u32[]{:S(2)}) collective-permute-start(bf16[32,1152]{1,0:T(8,128)(2,1)S(1)} %get-tuple-element.750), channel_id=1, source_target_pairs={{0,2},{1,3},{2,0},{3,1},{4,6},{5,7},{6,4},{7,5},{8,10},{9,11},{10,... | collective-permute-start | bytes 221192 | tf_op jit(solution)/shard_map/ppermute | solution.py:92
  82.1 2.4 %collective-permute-start.70 = (bf16[32,1152]{1,0:T(8,128)(2,1)S(1)}, bf16[32,1152]{1,0:T(8,128)(2,1)S(1)}, u32[]{:S(2)}, u32[]{:S(2)}) collective-permute-start(bf16[32,1152]{1,0:T(8,128)(2,1)S(1)} %get-tuple-element.749), channel_id=1, source_target_pairs={{0,3},{1,2},{2,1},{3,0},{4,7},{5,6},{6,5},{7,4},{8,11},{9,10},{10,... | collective-permute-start | bytes 221192 | tf_op jit(solution)/shard_map/ppermute | solution.py:92
  84.6 0.7 collective-permute-done.69
  85.3 4.5 %collective-permute-done.70 = bf16[32,1152]{1,0:T(8,128)(2,1)S(1)} collective-permute-done((bf16[32,1152]{1,0:T(8,128)(2,1)S(1)}, bf16[32,1152]{1,0:T(8,128)(2,1)S(1)}, u32[]{:S(2)}, u32[]{:S(2)}) %collective-permute-start.70) | collective-permute-done | bytes 73760 | tf_op jit(solution)/shard_map/ppermute | solution.py:92
  89.8 0.6 gather_fusion.2
  90.5 0.1 broadcast_select_fusion
  90.6 89.7 %while.13 = (s32[]{:T(128)}, bf16[4,32,1152]{2,1,0:T(8,128)(2,1)S(1)}, s32[4]{0:T(128)S(1)}, bf16[4,32,1152]{2,1,0:T(8,128)(2,1)S(1)}, s32[]{:T(128)}, /*index=5*/s32[1]{0:T(128)}, s32[1]{0:T(128)}) while((s32[]{:T(128)}, bf16[4,32,1152]{2,1,0:T(8,128)(2,1)S(1)}, s32[4]{0:T(128)S(1)}, bf16[4,32,1152]{2,1,0:T(8,128)(2,1)S(1)}, s32[]{:T(128)}, ...), condition=%wide.region_65.66_spmd, body=%wide.region_0.65_spmd.sunk | while | flops 3 | bytes 590001 | solution.py:107
  90.6 0.6 dynamic_slice.365
  91.8 19.1 %conditional.2 = (bf16[1,32,1152]{2,1,0:T(8,128)(2,1)}) conditional(s32[]{:T(128)} %bitcast.237, (bf16[4,32,1152]{2,1,0:T(8,128)(2,1)S(1)}, s32[]{:T(128)}) %tuple.365, (bf16[4,32,1152]{2,1,0:T(8,128)(2,1)S(1)}, s32[]{:T(128)}) %tuple.365, (bf16[4,32,1152]{2,1,0:T(8,128)(2,1)S(1)}, s32[]{:T(128)}) %tuple.365, ...), branch_computations={%region_1.1_spmd, %region_2.2_spmd, %region_3.3_spmd, %region_4.4_... | conditional | bytes 442420 | solution.py:104
  91.9 13.1 %collective-permute-start.26 = (bf16[32,1152]{1,0:T(8,128)(2,1)S(1)}, bf16[32,1152]{1,0:T(8,128)(2,1)}, u32[]{:S(2)}, u32[]{:S(2)}) collective-permute-start(bf16[32,1152]{1,0:T(8,128)(2,1)S(1)} %dynamic-slice_bitcast_fusion.26), channel_id=1, source_target_pairs={{0,216},{4,220},{8,208},{12,212},{16,200},{20,204},{24,192},{28,19... | collective-permute-start | bytes 221192 | tf_op jit(solution)/shard_map/while/body/eval_jaxpr/cond/branch_27_fun/ppermute | solution.py:18
  105.0 5.9 %collective-permute-done.26 = bf16[32,1152]{1,0:T(8,128)(2,1)} collective-permute-done((bf16[32,1152]{1,0:T(8,128)(2,1)S(1)}, bf16[32,1152]{1,0:T(8,128)(2,1)}, u32[]{:S(2)}, u32[]{:S(2)}) %collective-permute-start.26) | collective-permute-done | bytes 73760 | tf_op jit(solution)/shard_map/while/body/eval_jaxpr/cond/branch_27_fun/ppermute | solution.py:18
  110.9 0.9 constant_dynamic-update-slice_fusion.2
  111.8 0.6 dynamic_slice.365
  113.1 31.6 %conditional.2 = (bf16[1,32,1152]{2,1,0:T(8,128)(2,1)}) conditional(s32[]{:T(128)} %bitcast.237, (bf16[4,32,1152]{2,1,0:T(8,128)(2,1)S(1)}, s32[]{:T(128)}) %tuple.365, (bf16[4,32,1152]{2,1,0:T(8,128)(2,1)S(1)}, s32[]{:T(128)}) %tuple.365, (bf16[4,32,1152]{2,1,0:T(8,128)(2,1)S(1)}, s32[]{:T(128)}) %tuple.365, ...), branch_computations={%region_1.1_spmd, %region_2.2_spmd, %region_3.3_spmd, %region_4.4_... | conditional | bytes 442420 | solution.py:104
  113.2 14.7 %collective-permute-start.56 = (bf16[32,1152]{1,0:T(8,128)(2,1)S(1)}, bf16[32,1152]{1,0:T(8,128)(2,1)}, u32[]{:S(2)}, u32[]{:S(2)}) collective-permute-start(bf16[32,1152]{1,0:T(8,128)(2,1)S(1)} %dynamic-slice_bitcast_fusion.56), channel_id=1, source_target_pairs={{0,456},{4,460},{8,448},{12,452},{16,472},{20,476},{24,464},{28,46... | collective-permute-start | bytes 221192 | tf_op jit(solution)/shard_map/while/body/eval_jaxpr/cond/branch_57_fun/ppermute | solution.py:18
  127.9 16.8 %collective-permute-done.56 = bf16[32,1152]{1,0:T(8,128)(2,1)} collective-permute-done((bf16[32,1152]{1,0:T(8,128)(2,1)S(1)}, bf16[32,1152]{1,0:T(8,128)(2,1)}, u32[]{:S(2)}, u32[]{:S(2)}) %collective-permute-start.56) | collective-permute-done | bytes 73760 | tf_op jit(solution)/shard_map/while/body/eval_jaxpr/cond/branch_57_fun/ppermute | solution.py:18
  144.7 0.9 constant_dynamic-update-slice_fusion.2
  145.6 0.6 dynamic_slice.365
  146.8 13.0 %conditional.2 = (bf16[1,32,1152]{2,1,0:T(8,128)(2,1)}) conditional(s32[]{:T(128)} %bitcast.237, (bf16[4,32,1152]{2,1,0:T(8,128)(2,1)S(1)}, s32[]{:T(128)}) %tuple.365, (bf16[4,32,1152]{2,1,0:T(8,128)(2,1)S(1)}, s32[]{:T(128)}) %tuple.365, (bf16[4,32,1152]{2,1,0:T(8,128)(2,1)S(1)}, s32[]{:T(128)}) %tuple.365, ...), branch_computations={%region_1.1_spmd, %region_2.2_spmd, %region_3.3_spmd, %region_4.4_... | conditional | bytes 442420 | solution.py:104
  146.9 1.9 %collective-permute-start.29 = (bf16[32,1152]{1,0:T(8,128)(2,1)S(1)}, bf16[32,1152]{1,0:T(8,128)(2,1)}, u32[]{:S(2)}, u32[]{:S(2)}) collective-permute-start(bf16[32,1152]{1,0:T(8,128)(2,1)S(1)} %dynamic-slice_bitcast_fusion.29), channel_id=1, source_target_pairs={{0,240},{4,244},{8,248},{12,252},{16,224},{20,228},{24,232},{28,23... | collective-permute-start | bytes 221192 | tf_op jit(solution)/shard_map/while/body/eval_jaxpr/cond/branch_30_fun/ppermute | solution.py:18
  148.9 11.0 %collective-permute-done.29 = bf16[32,1152]{1,0:T(8,128)(2,1)} collective-permute-done((bf16[32,1152]{1,0:T(8,128)(2,1)S(1)}, bf16[32,1152]{1,0:T(8,128)(2,1)}, u32[]{:S(2)}, u32[]{:S(2)}) %collective-permute-start.29) | collective-permute-done | bytes 73760 | tf_op jit(solution)/shard_map/while/body/eval_jaxpr/cond/branch_30_fun/ppermute | solution.py:18
  159.9 0.9 constant_dynamic-update-slice_fusion.2
  160.8 0.6 dynamic_slice.365
  162.0 17.4 %conditional.2 = (bf16[1,32,1152]{2,1,0:T(8,128)(2,1)}) conditional(s32[]{:T(128)} %bitcast.237, (bf16[4,32,1152]{2,1,0:T(8,128)(2,1)S(1)}, s32[]{:T(128)}) %tuple.365, (bf16[4,32,1152]{2,1,0:T(8,128)(2,1)S(1)}, s32[]{:T(128)}) %tuple.365, (bf16[4,32,1152]{2,1,0:T(8,128)(2,1)S(1)}, s32[]{:T(128)}) %tuple.365, ...), branch_computations={%region_1.1_spmd, %region_2.2_spmd, %region_3.3_spmd, %region_4.4_... | conditional | bytes 442420 | solution.py:104
  162.1 2.7 %collective-permute-start.18 = (bf16[32,1152]{1,0:T(8,128)(2,1)S(1)}, bf16[32,1152]{1,0:T(8,128)(2,1)}, u32[]{:S(2)}, u32[]{:S(2)}) collective-permute-start(bf16[32,1152]{1,0:T(8,128)(2,1)S(1)} %dynamic-slice_bitcast_fusion.18), channel_id=1, source_target_pairs={{0,152},{4,156},{8,144},{12,148},{16,136},{20,140},{24,128},{28,13... | collective-permute-start | bytes 221192 | tf_op jit(solution)/shard_map/while/body/eval_jaxpr/cond/branch_19_fun/ppermute | solution.py:18
  164.8 14.6 %collective-permute-done.18 = bf16[32,1152]{1,0:T(8,128)(2,1)} collective-permute-done((bf16[32,1152]{1,0:T(8,128)(2,1)S(1)}, bf16[32,1152]{1,0:T(8,128)(2,1)}, u32[]{:S(2)}, u32[]{:S(2)}) %collective-permute-start.18) | collective-permute-done | bytes 73760 | tf_op jit(solution)/shard_map/while/body/eval_jaxpr/cond/branch_19_fun/ppermute | solution.py:18
  179.4 0.9 constant_dynamic-update-slice_fusion.2
  180.3 0.2 reshape.202
  180.5 0.6 fusion.26
  181.1 1.2 copy.19
  182.3 1.1 add_convert_fusion
  183.5 0.6 convert_add_fusion
  (38 shorter events, 0.4 us)
Async XLA Ops:
  0.6 5.8 %copy-start = (bf16[320,1280]{1,0:T(8,128)(2,1)S(1)}, bf16[320,1280]{1,0:T(8,128)(2,1)}, u32[]{:S(2)}) copy-start(bf16[320,1280]{1,0:T(8,128)(2,1)} %param.77) | copy-start | bytes 2457604
  0.6 20.2 %collective-permute-start.63 = (bf16[1280,256]{1,0:T(8,128)(2,1)}, bf16[1280,256]{1,0:T(8,128)(2,1)S(1)}, u32[]{:S(2)}, u32[]{:S(2)}) collective-permute-start(bf16[1280,256]{1,0:T(8,128)(2,1)} %param.75), channel_id=1, source_target_pairs={{0,2},{1,3},{2,0},{3,1},{4,6},{5,7},{6,4},{7,5},{8,10},{9,11},{10,... | collective-permute-start | bytes 1966088 | tf_op jit(solution)/shard_map/ppermute | solution.py:24
  6.4 1.6 copy-start.7
  8.0 13.7 %copy-start.3 = (bf16[1280,256]{1,0:T(8,128)(2,1)S(1)}, bf16[1280,256]{1,0:T(8,128)(2,1)}, u32[]{:S(2)}) copy-start(bf16[1280,256]{1,0:T(8,128)(2,1)} %param.75) | copy-start | bytes 1966084
  8.4 23.1 %copy-start.6 = (bf16[320,128]{1,0:T(8,128)(2,1)}, bf16[320,128]{1,0:T(8,128)(2,1)S(1)}, u32[]{:S(2)}) copy-start(bf16[320,128]{1,0:T(8,128)(2,1)S(1)} %convolution_convert_fusion) | copy-start | bytes 245764
  20.9 0.8 copy-start.4
  22.9 5.1 %collective-permute-start.64 = (bf16[2,1280,256]{2,1,0:T(8,128)(2,1)S(1)}, bf16[2,1280,256]{2,1,0:T(8,128)(2,1)}, u32[]{:S(2)}, u32[]{:S(2)}) collective-permute-start(bf16[2,1280,256]{2,1,0:T(8,128)(2,1)S(1)} %pad_maximum_fusion.1), channel_id=1, source_target_pairs={{0,1},{1,0},{2,3},{3,2},{4,5},{5,4},{6,7},{7,6},{8,9},{9,8},{10,11... | collective-permute-start | bytes 3932168 | tf_op jit(solution)/shard_map/ppermute | solution.py:28
  31.6 26.3 %copy-start.5 = (bf16[256,1280]{1,0:T(8,128)(2,1)S(1)}, bf16[256,1280]{1,0:T(8,128)(2,1)}, u32[]{:S(2)}) copy-start(bf16[256,1280]{1,0:T(8,128)(2,1)} %param.76) | copy-start | bytes 1966084
  31.6 22.1 %collective-permute-start.65 = (bf16[320,1152]{1,0:T(8,128)(2,1)S(1)}, bf16[320,1152]{1,0:T(8,128)(2,1)S(1)}, u32[]{:S(2)}, u32[]{:S(2)}) collective-permute-start(bf16[320,1152]{1,0:T(8,128)(2,1)S(1)} %get-tuple-element.747), channel_id=1, source_target_pairs={{0,2},{1,3},{2,0},{3,1},{4,6},{5,7},{6,4},{7,5},{8,10},{9,11},{10,... | collective-permute-start | bytes 2211848 | tf_op jit(solution)/shard_map/ppermute | solution.py:24
  53.7 0.9 copy-start.2
  54.6 3.6 %copy-start.9 = (s32[4]{0:T(128)S(1)}, s32[4]{0:T(128)}, u32[]{:S(2)}) copy-start(s32[4]{0:T(128)} %constant.288.clone) | copy-start | bytes 52
  55.9 3.0 %copy-start.10 = (s32[1,4]{1,0:T(1,128)S(1)}, s32[1,4]{1,0:T(1,128)}, u32[]{:S(2)}) copy-start(s32[1,4]{1,0:T(1,128)} %param.80) | copy-start | bytes 52
  55.9 5.6 %collective-permute-start.66 = (bf16[2,320,1152]{2,1,0:T(8,128)(2,1)}, bf16[2,320,1152]{2,1,0:T(8,128)(2,1)}, u32[]{:S(2)}, u32[]{:S(2)}) collective-permute-start(bf16[2,320,1152]{2,1,0:T(8,128)(2,1)} %pad_maximum_fusion), channel_id=1, source_target_pairs={{0,1},{1,0},{2,3},{3,2},{4,5},{5,4},{6,7},{7,6},{8,9},{9,8},{10,11... | collective-permute-start | bytes 4423688 | tf_op jit(solution)/shard_map/ppermute | solution.py:28
  64.2 10.9 %collective-permute-start.67 = (bf16[128,1152]{1,0:T(8,128)(2,1)S(1)}, bf16[128,1152]{1,0:T(8,128)(2,1)S(1)}, u32[]{:S(2)}, u32[]{:S(2)}) collective-permute-start(bf16[128,1152]{1,0:T(8,128)(2,1)S(1)} %dynamic-slice_convert_fusion), channel_id=1, source_target_pairs={{0,4},{4,0},{8,12},{12,8},{16,20},{20,16},{24,28},{28,24},{32,36},... | collective-permute-start | bytes 884744 | tf_op jit(solution)/shard_map/ppermute | solution.py:79
  75.3 9.3 %collective-permute-start.68 = (bf16[32,1152]{1,0:T(8,128)(2,1)S(1)}, bf16[32,1152]{1,0:T(8,128)(2,1)S(1)}, u32[]{:S(2)}, u32[]{:S(2)}) collective-permute-start(bf16[32,1152]{1,0:T(8,128)(2,1)S(1)} %get-tuple-element.751), channel_id=1, source_target_pairs={{0,1},{1,0},{2,3},{3,2},{4,5},{5,4},{6,7},{7,6},{8,9},{9,8},{10,11... | collective-permute-start | bytes 221192 | tf_op jit(solution)/shard_map/ppermute | solution.py:92
  77.2 8.1 %collective-permute-start.69 = (bf16[32,1152]{1,0:T(8,128)(2,1)S(1)}, bf16[32,1152]{1,0:T(8,128)(2,1)S(1)}, u32[]{:S(2)}, u32[]{:S(2)}) collective-permute-start(bf16[32,1152]{1,0:T(8,128)(2,1)S(1)} %get-tuple-element.750), channel_id=1, source_target_pairs={{0,2},{1,3},{2,0},{3,1},{4,6},{5,7},{6,4},{7,5},{8,10},{9,11},{10,... | collective-permute-start | bytes 221192 | tf_op jit(solution)/shard_map/ppermute | solution.py:92
  82.1 7.7 %collective-permute-start.70 = (bf16[32,1152]{1,0:T(8,128)(2,1)S(1)}, bf16[32,1152]{1,0:T(8,128)(2,1)S(1)}, u32[]{:S(2)}, u32[]{:S(2)}) collective-permute-start(bf16[32,1152]{1,0:T(8,128)(2,1)S(1)} %get-tuple-element.749), channel_id=1, source_target_pairs={{0,3},{1,2},{2,1},{3,0},{4,7},{5,6},{6,5},{7,4},{8,11},{9,10},{10,... | collective-permute-start | bytes 221192 | tf_op jit(solution)/shard_map/ppermute | solution.py:92
  91.9 19.0 %collective-permute-start.26 = (bf16[32,1152]{1,0:T(8,128)(2,1)S(1)}, bf16[32,1152]{1,0:T(8,128)(2,1)}, u32[]{:S(2)}, u32[]{:S(2)}) collective-permute-start(bf16[32,1152]{1,0:T(8,128)(2,1)S(1)} %dynamic-slice_bitcast_fusion.26), channel_id=1, source_target_pairs={{0,216},{4,220},{8,208},{12,212},{16,200},{20,204},{24,192},{28,19... | collective-permute-start | bytes 221192 | tf_op jit(solution)/shard_map/while/body/eval_jaxpr/cond/branch_27_fun/ppermute | solution.py:18
  113.2 31.5 %collective-permute-start.56 = (bf16[32,1152]{1,0:T(8,128)(2,1)S(1)}, bf16[32,1152]{1,0:T(8,128)(2,1)}, u32[]{:S(2)}, u32[]{:S(2)}) collective-permute-start(bf16[32,1152]{1,0:T(8,128)(2,1)S(1)} %dynamic-slice_bitcast_fusion.56), channel_id=1, source_target_pairs={{0,456},{4,460},{8,448},{12,452},{16,472},{20,476},{24,464},{28,46... | collective-permute-start | bytes 221192 | tf_op jit(solution)/shard_map/while/body/eval_jaxpr/cond/branch_57_fun/ppermute | solution.py:18
  146.9 13.0 %collective-permute-start.29 = (bf16[32,1152]{1,0:T(8,128)(2,1)S(1)}, bf16[32,1152]{1,0:T(8,128)(2,1)}, u32[]{:S(2)}, u32[]{:S(2)}) collective-permute-start(bf16[32,1152]{1,0:T(8,128)(2,1)S(1)} %dynamic-slice_bitcast_fusion.29), channel_id=1, source_target_pairs={{0,240},{4,244},{8,248},{12,252},{16,224},{20,228},{24,232},{28,23... | collective-permute-start | bytes 221192 | tf_op jit(solution)/shard_map/while/body/eval_jaxpr/cond/branch_30_fun/ppermute | solution.py:18
  162.1 17.3 %collective-permute-start.18 = (bf16[32,1152]{1,0:T(8,128)(2,1)S(1)}, bf16[32,1152]{1,0:T(8,128)(2,1)}, u32[]{:S(2)}, u32[]{:S(2)}) collective-permute-start(bf16[32,1152]{1,0:T(8,128)(2,1)S(1)} %dynamic-slice_bitcast_fusion.18), channel_id=1, source_target_pairs={{0,152},{4,156},{8,144},{12,148},{16,136},{20,140},{24,128},{28,13... | collective-permute-start | bytes 221192 | tf_op jit(solution)/shard_map/while/body/eval_jaxpr/cond/branch_19_fun/ppermute | solution.py:18
  181.1 1.2 copy-start.1
  182.3 1.2 copy-start.8

commit v8 on v6

--- a/solution.py
+++ b/solution.py
@@ -72,21 +72,26 @@
     half_rows = lower_rows // 2
     own_rows = lax.dynamic_slice_in_dim(combined, own_side * half_rows, half_rows, 0)
     other_rows = lax.dynamic_slice_in_dim(combined, (1 - own_side) * half_rows, half_rows, 0)
-    partner_rows = lax.ppermute(
-        other_rows.astype(jnp.bfloat16), LEAF, [(s, s ^ 1) for s in range(leaf_count)]
-    )
-    moving = (own_rows + partner_rows.astype(jnp.float32)).astype(jnp.bfloat16)
     col_count = 4
     share_rows = half_rows // col_count
-    quarters = moving.reshape(col_count, share_rows, moving.shape[1])
-    by_distance = [lax.dynamic_index_in_dim(quarters, col_index, 0, keepdims=False)]
-    for distance in range(1, col_count):
-        outgoing = lax.dynamic_index_in_dim(
-            quarters, jnp.bitwise_xor(col_index, distance), 0, keepdims=False
+    width = combined.shape[1]
+    device_count = leaf_count * col_count
+    everyone = (LEAF,) + COLS
+    own_quarters = own_rows.reshape(col_count, share_rows, width)
+    other_quarters = other_rows.astype(jnp.bfloat16).reshape(col_count, share_rows, width)
+    by_distance = []
+    for distance in range(col_count):
+        target_quarter = jnp.bitwise_xor(col_index, distance)
+        sibling_mask = col_count + distance
+        from_sibling = lax.ppermute(
+            lax.dynamic_index_in_dim(other_quarters, target_quarter, 0, keepdims=False),
+            everyone,
+            [(d, d ^ sibling_mask) for d in range(device_count)],
         )
-        by_distance.append(
-            lax.ppermute(outgoing, COLS, [(c, c ^ distance) for c in range(col_count)])
-        )
+        own = lax.dynamic_index_in_dim(own_quarters, target_quarter, 0, keepdims=False)
+        if distance:
+            own = lax.ppermute(own, everyone, [(d, d ^ distance) for d in range(device_count)])
+        by_distance.append((own + from_sibling.astype(jnp.float32)).astype(jnp.bfloat16))
     spread = jnp.take(
         jnp.stack(by_distance),
         jnp.bitwise_xor(jnp.arange(col_count, dtype=jnp.int32), col_index),

time: 185 us -> 197 us (1.065)
  starting transfers between devices: 75.6 us -> 95.8 us
  waiting for transfers between devices: 80.2 us -> 73.4 us
    ppermute x3 -> x4, starting transfers between devices: 41.6 us -> 52 us  [branch(): return lambda x: lax.ppermute(x, LEAF, pairs)]
    ppermute x4 -> x7, starting transfers between devices: 13.6 us -> 23.5 us  [the longest x3 12.9 us: body(): lax.ppermute(own, everyone, [(d, d ^ distance) for d in range(device_coun...]
    ppermute x4 -> x7, waiting for transfers between devices: 11.9 us -> 5.9 us  [the longest x4 5.89 us: body(): lax.ppermute(lax.dynamic_index_in_dim(other_quarters, target_quarter, 0,...]
    ppermute x3 -> x4, waiting for transfers between devices: 38 us -> 37.3 us  [branch(): return lambda x: lax.ppermute(x, LEAF, pairs)]
  transfers between devices with their start and end apart: 11 -> 15, of which waited for: 10 -> 9; matrix products, arithmetic and copies ran while one was open for 2% -> 2% of each run, Pallas kernels for 0% -> 0%
where the time goes in v8:
time: 197 us
  starting transfers between devices  95.8 us (49%)
  waiting for transfers between devices  73.4 us (37%)
  local copies, waits for them, and re-layouts  10.7 us (5%)
  matrix products  7.5 us (4%)
  other arithmetic  4.99 us (3%)
  loops' own time  3 us (2%)
    ppermute x4, starting transfers between devices, branch(): return lambda x: lax.ppermute(x, LEAF, pairs)  52 us
    ppermute x4, waiting for transfers between devices, branch(): return lambda x: lax.ppermute(x, LEAF, pairs)  37.3 us
    ppermute x2, waiting for transfers between devices, col_gather(): remote = lax.ppermute(block, COLS, [(c, c ^ 2) for c in range(4)])  27.5 us
    ppermute x3, starting transfers between devices, body(): lax.ppermute(own, everyone, [(d, d ^ distance) for d in range(device_coun...  12.9 us
    ppermute x2, starting transfers between devices, col_gather(): remote = lax.ppermute(block, COLS, [(c, c ^ 2) for c in range(4)])  10.6 us
    ppermute x4, starting transfers between devices, body(): lax.ppermute(lax.dynamic_index_in_dim(other_quarters, target_quarter, 0,...  10.6 us
    ppermute x2, starting transfers between devices, col_gather(): partner = lax.ppermute(chip, COLS, [(c, c ^ 1) for c in range(4)])  9.74 us
    ppermute x4, waiting for transfers between devices, body(): lax.ppermute(lax.dynamic_index_in_dim(other_quarters, target_quarter, 0,...  5.89 us
  transfers between devices with their start and end apart: 15, of which 9 were waited for; matrix products, arithmetic and copies ran while one was open for 2% of the time, Pallas kernels for 0%

profile of v8, /device:TPU:1, one launch (start us, length us, event | category | flops | bytes accessed | tf_op | source)
XLA Modules:
  0.0 196.5 jit_solution(12369275676486142094)
XLA Ops:
  0.6 0.0 copy-start
  0.7 5.6 %collective-permute-start.63 = (bf16[1280,256]{1,0:T(8,128)(2,1)}, bf16[1280,256]{1,0:T(8,128)(2,1)S(1)}, u32[]{:S(2)}, u32[]{:S(2)}) collective-permute-start(bf16[1280,256]{1,0:T(8,128)(2,1)} %param.75), channel_id=1, source_target_pairs={{0,2},{1,3},{2,0},{3,1},{4,6},{5,7},{6,4},{7,5},{8,10},{9,11},{10,... | collective-permute-start | bytes 1966088 | tf_op jit(solution)/shard_map/ppermute | solution.py:24
  6.3 11.3 %collective-permute-done.63 = bf16[1280,256]{1,0:T(8,128)(2,1)S(1)} collective-permute-done((bf16[1280,256]{1,0:T(8,128)(2,1)}, bf16[1280,256]{1,0:T(8,128)(2,1)S(1)}, u32[]{:S(2)}, u32[]{:S(2)}) %collective-permute-start.63) | collective-permute-done | bytes 655392 | tf_op jit(solution)/shard_map/ppermute | solution.py:24
  17.6 1.2 pad_maximum_fusion.1
  18.8 6.5 %collective-permute-start.64 = (bf16[2,1280,256]{2,1,0:T(8,128)(2,1)S(1)}, bf16[2,1280,256]{2,1,0:T(8,128)(2,1)}, u32[]{:S(2)}, u32[]{:S(2)}) collective-permute-start(bf16[2,1280,256]{2,1,0:T(8,128)(2,1)S(1)} %pad_maximum_fusion.1), channel_id=1, source_target_pairs={{0,1},{1,0},{2,3},{3,2},{4,5},{5,4},{6,7},{7,6},{8,9},{9,8},{10,11... | collective-permute-start | bytes 3932168 | tf_op jit(solution)/shard_map/ppermute | solution.py:26
  25.3 0.1 broadcast_in_dim.247
  25.5 0.0 copy-start.6
  25.5 0.0 copy-start.3
  25.5 1.5 fusion.11
  27.1 0.4 convolution_convert_fusion
  27.4 0.0 copy-start.5
  27.5 0.6 collective-permute-done.64
  28.1 2.3 %fusion.15 = bf16[320,4,256]{2,0,1:T(8,128)(2,1)S(1)} fusion(bf16[2,1280,256]{2,1,0:T(8,128)(2,1)} %collective-permute-done.64, bf16[1,1280,256]{2,1,0:T(8,128)(2,1)S(1)} %bitcast.270, bf16[1,1280,256]{2,1,0:T(8,128)(2,1)S(1)} %bitcast.268, bf16[1280,320]{0,1:T(8,128)(2,1)S(1)} %fusion.11), kind=kOutput, calls=%fused_computation.80 | convolution fusion | flops 846725120 | bytes 4096000 | tf_op jit(solution)/shard_map/ip,kpn->ikn/dot_general | solution.py:56
  30.4 0.6 gather_fusion.1
  31.0 0.1 copy.18
  31.1 0.2 select_convert_fusion
  31.3 0.1 fusion.45
  31.4 5.0 %collective-permute-start.65 = (bf16[320,1152]{1,0:T(8,128)(2,1)S(1)}, bf16[320,1152]{1,0:T(8,128)(2,1)S(1)}, u32[]{:S(2)}, u32[]{:S(2)}) collective-permute-start(bf16[320,1152]{1,0:T(8,128)(2,1)S(1)} %get-tuple-element.741), channel_id=1, source_target_pairs={{0,2},{1,3},{2,0},{3,1},{4,6},{5,7},{6,4},{7,5},{8,10},{9,11},{10,... | collective-permute-start | bytes 2211848 | tf_op jit(solution)/shard_map/ppermute | solution.py:24
  36.4 16.2 %collective-permute-done.65 = bf16[320,1152]{1,0:T(8,128)(2,1)S(1)} collective-permute-done((bf16[320,1152]{1,0:T(8,128)(2,1)S(1)}, bf16[320,1152]{1,0:T(8,128)(2,1)S(1)}, u32[]{:S(2)}, u32[]{:S(2)}) %collective-permute-start.65) | collective-permute-done | bytes 737312 | tf_op jit(solution)/shard_map/ppermute | solution.py:24
  52.6 0.9 copy-done.2
  53.5 1.3 pad_maximum_fusion
  54.8 3.2 %collective-permute-start.66 = (bf16[2,320,1152]{2,1,0:T(8,128)(2,1)}, bf16[2,320,1152]{2,1,0:T(8,128)(2,1)}, u32[]{:S(2)}, u32[]{:S(2)}) collective-permute-start(bf16[2,320,1152]{2,1,0:T(8,128)(2,1)} %pad_maximum_fusion), channel_id=1, source_target_pairs={{0,1},{1,0},{2,3},{3,2},{4,5},{5,4},{6,7},{7,6},{8,9},{9,8},{10,11... | collective-permute-start | bytes 4423688 | tf_op jit(solution)/shard_map/ppermute | solution.py:26
  58.1 0.2 copy.13
  58.4 0.6 gather_fusion
  59.0 0.1 xor_xor_fusion
  59.1 0.1 fusion.35
  59.2 2.0 %collective-permute-done.66 = bf16[2,320,1152]{2,1,0:T(8,128)(2,1)} collective-permute-done((bf16[2,320,1152]{2,1,0:T(8,128)(2,1)}, bf16[2,320,1152]{2,1,0:T(8,128)(2,1)}, u32[]{:S(2)}, u32[]{:S(2)}) %collective-permute-start.66) | collective-permute-done | bytes 1474592 | tf_op jit(solution)/shard_map/ppermute | solution.py:26
  61.2 2.7 %fusion.12 = f32[256,1152]{1,0:T(8,128)S(1)} fusion(bf16[2,320,1152]{2,1,0:T(8,128)(2,1)} %collective-permute-done.66, bf16[1,320,1152]{2,1,0:T(8,128)(2,1)} %bitcast.266, bf16[1,320,1152]{2,1,0:T(8,128)(2,1)S(1)} %get-tuple-element.740, bf16[4,256,320]{1,2,0:T(8,128)(2,1)S(1)} %gather_fusion, pred[4]{0:T(512)(128)(4,1)S(1)} %get-tuple-element.738), kind=kOutput, calls=%fused_computation.79 | convolution fusion | flops 758546432 | bytes 4784132 | tf_op jit(solution)/shard_map/rkp,kpn->rn/dot_general | solution.py:65
  64.0 3.4 %collective-permute-start.67 = (bf16[32,1152]{1,0:T(8,128)(2,1)S(1)}, bf16[32,1152]{1,0:T(8,128)(2,1)S(1)}, u32[]{:S(2)}, u32[]{:S(2)}) collective-permute-start(bf16[32,1152]{1,0:T(8,128)(2,1)S(1)} %get-tuple-element.745), channel_id=1, source_target_pairs={{0,4},{1,5},{2,6},{3,7},{4,0},{5,1},{6,2},{7,3},{8,12},{9,13},{10,... | collective-permute-start | bytes 221192 | tf_op jit(solution)/shard_map/ppermute | solution.py:86
  67.5 2.6 %collective-permute-start.68 = (f32[32,1152]{1,0:T(8,128)S(1)}, f32[32,1152]{1,0:T(8,128)S(1)}, u32[]{:S(2)}, u32[]{:S(2)}) collective-permute-start(f32[32,1152]{1,0:T(8,128)S(1)} %get-tuple-element.742), channel_id=1, source_target_pairs={{0,1},{1,0},{2,3},{3,2},{4,5},{5,4},{6,7},{7,6},{8,9},{9,8},{10,11... | collective-permute-start | bytes 442376 | tf_op jit(solution)/shard_map/ppermute | solution.py:93
  70.1 1.9 collective-permute-start.69
  72.0 4.7 %collective-permute-start.70 = (f32[32,1152]{1,0:T(8,128)S(1)}, f32[32,1152]{1,0:T(8,128)S(1)}, u32[]{:S(2)}, u32[]{:S(2)}) collective-permute-start(f32[32,1152]{1,0:T(8,128)S(1)} %get-tuple-element.744), channel_id=1, source_target_pairs={{0,2},{1,3},{2,0},{3,1},{4,6},{5,7},{6,4},{7,5},{8,10},{9,11},{10,... | collective-permute-start | bytes 442376 | tf_op jit(solution)/shard_map/ppermute | solution.py:93
  76.8 3.1 %collective-permute-start.71 = (bf16[32,1152]{1,0:T(8,128)(2,1)S(1)}, bf16[32,1152]{1,0:T(8,128)(2,1)S(1)}, u32[]{:S(2)}, u32[]{:S(2)}) collective-permute-start(bf16[32,1152]{1,0:T(8,128)(2,1)S(1)} %get-tuple-element.747), channel_id=1, source_target_pairs={{0,6},{1,7},{2,4},{3,5},{4,2},{5,3},{6,0},{7,1},{8,14},{9,15},{10,... | collective-permute-start | bytes 221192 | tf_op jit(solution)/shard_map/ppermute | solution.py:86
  79.9 5.6 %collective-permute-start.72 = (f32[32,1152]{1,0:T(8,128)S(1)}, f32[32,1152]{1,0:T(8,128)S(1)}, u32[]{:S(2)}, u32[]{:S(2)}) collective-permute-start(f32[32,1152]{1,0:T(8,128)S(1)} %get-tuple-element.743), channel_id=1, source_target_pairs={{0,3},{1,2},{2,1},{3,0},{4,7},{5,6},{6,5},{7,4},{8,11},{9,10},{10,... | collective-permute-start | bytes 442376 | tf_op jit(solution)/shard_map/ppermute | solution.py:93
  85.6 2.1 %collective-permute-start.73 = (bf16[32,1152]{1,0:T(8,128)(2,1)S(1)}, bf16[32,1152]{1,0:T(8,128)(2,1)S(1)}, u32[]{:S(2)}, u32[]{:S(2)}) collective-permute-start(bf16[32,1152]{1,0:T(8,128)(2,1)S(1)} %get-tuple-element.746), channel_id=1, source_target_pairs={{0,7},{1,6},{2,5},{3,4},{4,3},{5,2},{6,1},{7,0},{8,15},{9,14},{10,... | collective-permute-start | bytes 221192 | tf_op jit(solution)/shard_map/ppermute | solution.py:86
  87.8 5.9 %collective-permute-done.73 = bf16[32,1152]{1,0:T(8,128)(2,1)S(1)} collective-permute-done((bf16[32,1152]{1,0:T(8,128)(2,1)S(1)}, bf16[32,1152]{1,0:T(8,128)(2,1)S(1)}, u32[]{:S(2)}, u32[]{:S(2)}) %collective-permute-start.73) | collective-permute-done | bytes 73760 | tf_op jit(solution)/shard_map/ppermute | solution.py:86
  93.7 0.6 gather_fusion.2
  94.3 0.1 broadcast_select_fusion
  94.4 98.3 %while.13 = (s32[]{:T(128)}, bf16[4,32,1152]{2,1,0:T(8,128)(2,1)S(1)}, s32[4]{0:T(128)S(1)}, bf16[4,32,1152]{2,1,0:T(8,128)(2,1)S(1)}, s32[]{:T(128)}, /*index=5*/s32[1]{0:T(128)}, s32[1]{0:T(128)}) while((s32[]{:T(128)}, bf16[4,32,1152]{2,1,0:T(8,128)(2,1)S(1)}, s32[4]{0:T(128)S(1)}, bf16[4,32,1152]{2,1,0:T(8,128)(2,1)S(1)}, s32[]{:T(128)}, ...), condition=%wide.region_65.66_spmd, body=%wide.region_0.65_spmd.sunk | while | flops 3 | bytes 590001 | solution.py:108
  94.4 0.6 dynamic_slice.388
  95.7 15.4 %conditional.2 = (bf16[1,32,1152]{2,1,0:T(8,128)(2,1)}) conditional(s32[]{:T(128)} %bitcast.256, (bf16[4,32,1152]{2,1,0:T(8,128)(2,1)S(1)}, s32[]{:T(128)}) %tuple.365, (bf16[4,32,1152]{2,1,0:T(8,128)(2,1)S(1)}, s32[]{:T(128)}) %tuple.365, (bf16[4,32,1152]{2,1,0:T(8,128)(2,1)S(1)}, s32[]{:T(128)}) %tuple.365, ...), branch_computations={%region_1.1_spmd, %region_2.2_spmd, %region_3.3_spmd, %region_4.4_... | conditional | bytes 442420 | solution.py:105
  95.8 12.9 %collective-permute-start.13 = (bf16[32,1152]{1,0:T(8,128)(2,1)S(1)}, bf16[32,1152]{1,0:T(8,128)(2,1)}, u32[]{:S(2)}, u32[]{:S(2)}) collective-permute-start(bf16[32,1152]{1,0:T(8,128)(2,1)S(1)} %dynamic-slice_bitcast_fusion.13), channel_id=1, source_target_pairs={{0,112},{4,116},{8,120},{12,124},{16,96},{20,100},{24,104},{28,108... | collective-permute-start | bytes 221192 | tf_op jit(solution)/shard_map/while/body/eval_jaxpr/cond/branch_14_fun/ppermute | solution.py:18
  108.7 2.5 %collective-permute-done.13 = bf16[32,1152]{1,0:T(8,128)(2,1)} collective-permute-done((bf16[32,1152]{1,0:T(8,128)(2,1)S(1)}, bf16[32,1152]{1,0:T(8,128)(2,1)}, u32[]{:S(2)}, u32[]{:S(2)}) %collective-permute-start.13) | collective-permute-done | bytes 73760 | tf_op jit(solution)/shard_map/while/body/eval_jaxpr/cond/branch_14_fun/ppermute | solution.py:18
  111.1 0.9 constant_dynamic-update-slice_fusion.2
  112.0 0.6 dynamic_slice.388
  113.3 11.7 %conditional.2 = (bf16[1,32,1152]{2,1,0:T(8,128)(2,1)}) conditional(s32[]{:T(128)} %bitcast.256, (bf16[4,32,1152]{2,1,0:T(8,128)(2,1)S(1)}, s32[]{:T(128)}) %tuple.365, (bf16[4,32,1152]{2,1,0:T(8,128)(2,1)S(1)}, s32[]{:T(128)}) %tuple.365, (bf16[4,32,1152]{2,1,0:T(8,128)(2,1)S(1)}, s32[]{:T(128)}) %tuple.365, ...), branch_computations={%region_1.1_spmd, %region_2.2_spmd, %region_3.3_spmd, %region_4.4_... | conditional | bytes 442420 | solution.py:105
  113.3 9.2 %collective-permute-start.23 = (bf16[32,1152]{1,0:T(8,128)(2,1)S(1)}, bf16[32,1152]{1,0:T(8,128)(2,1)}, u32[]{:S(2)}, u32[]{:S(2)}) collective-permute-start(bf16[32,1152]{1,0:T(8,128)(2,1)S(1)} %dynamic-slice_bitcast_fusion.23), channel_id=1, source_target_pairs={{0,192},{4,196},{8,200},{12,204},{16,208},{20,212},{24,216},{28,22... | collective-permute-start | bytes 221192 | tf_op jit(solution)/shard_map/while/body/eval_jaxpr/cond/branch_24_fun/ppermute | solution.py:18
  122.5 2.5 %collective-permute-done.23 = bf16[32,1152]{1,0:T(8,128)(2,1)} collective-permute-done((bf16[32,1152]{1,0:T(8,128)(2,1)S(1)}, bf16[32,1152]{1,0:T(8,128)(2,1)}, u32[]{:S(2)}, u32[]{:S(2)}) %collective-permute-start.23) | collective-permute-done | bytes 73760 | tf_op jit(solution)/shard_map/while/body/eval_jaxpr/cond/branch_24_fun/ppermute | solution.py:18
  125.0 0.9 constant_dynamic-update-slice_fusion.2
  125.9 0.6 dynamic_slice.388
  127.1 32.5 %conditional.2 = (bf16[1,32,1152]{2,1,0:T(8,128)(2,1)}) conditional(s32[]{:T(128)} %bitcast.256, (bf16[4,32,1152]{2,1,0:T(8,128)(2,1)S(1)}, s32[]{:T(128)}) %tuple.365, (bf16[4,32,1152]{2,1,0:T(8,128)(2,1)S(1)}, s32[]{:T(128)}) %tuple.365, (bf16[4,32,1152]{2,1,0:T(8,128)(2,1)S(1)}, s32[]{:T(128)}) %tuple.365, ...), branch_computations={%region_1.1_spmd, %region_2.2_spmd, %region_3.3_spmd, %region_4.4_... | conditional | bytes 442420 | solution.py:105
  127.2 17.1 %collective-permute-start.58 = (bf16[32,1152]{1,0:T(8,128)(2,1)S(1)}, bf16[32,1152]{1,0:T(8,128)(2,1)}, u32[]{:S(2)}, u32[]{:S(2)}) collective-permute-start(bf16[32,1152]{1,0:T(8,128)(2,1)S(1)} %dynamic-slice_bitcast_fusion.58), channel_id=1, source_target_pairs={{0,472},{4,476},{8,464},{12,468},{16,456},{20,460},{24,448},{28,45... | collective-permute-start | bytes 221192 | tf_op jit(solution)/shard_map/while/body/eval_jaxpr/cond/branch_59_fun/ppermute | solution.py:18
  144.3 15.3 %collective-permute-done.58 = bf16[32,1152]{1,0:T(8,128)(2,1)} collective-permute-done((bf16[32,1152]{1,0:T(8,128)(2,1)S(1)}, bf16[32,1152]{1,0:T(8,128)(2,1)}, u32[]{:S(2)}, u32[]{:S(2)}) %collective-permute-start.58) | collective-permute-done | bytes 73760 | tf_op jit(solution)/shard_map/while/body/eval_jaxpr/cond/branch_59_fun/ppermute | solution.py:18
  159.6 0.9 constant_dynamic-update-slice_fusion.2
  160.5 0.6 dynamic_slice.388
  161.8 30.1 %conditional.2 = (bf16[1,32,1152]{2,1,0:T(8,128)(2,1)}) conditional(s32[]{:T(128)} %bitcast.256, (bf16[4,32,1152]{2,1,0:T(8,128)(2,1)S(1)}, s32[]{:T(128)}) %tuple.365, (bf16[4,32,1152]{2,1,0:T(8,128)(2,1)S(1)}, s32[]{:T(128)}) %tuple.365, (bf16[4,32,1152]{2,1,0:T(8,128)(2,1)S(1)}, s32[]{:T(128)}) %tuple.365, ...), branch_computations={%region_1.1_spmd, %region_2.2_spmd, %region_3.3_spmd, %region_4.4_... | conditional | bytes 442420 | solution.py:105
  161.9 12.8 %collective-permute-start.62 = (bf16[32,1152]{1,0:T(8,128)(2,1)S(1)}, bf16[32,1152]{1,0:T(8,128)(2,1)}, u32[]{:S(2)}, u32[]{:S(2)}) collective-permute-start(bf16[32,1152]{1,0:T(8,128)(2,1)S(1)} %dynamic-slice_bitcast_fusion.62), channel_id=1, source_target_pairs={{0,504},{4,508},{8,496},{12,500},{16,488},{20,492},{24,480},{28,48... | collective-permute-start | bytes 221192 | tf_op jit(solution)/shard_map/while/body/eval_jaxpr/cond/branch_63_fun/ppermute | solution.py:18
  174.7 17.1 %collective-permute-done.62 = bf16[32,1152]{1,0:T(8,128)(2,1)} collective-permute-done((bf16[32,1152]{1,0:T(8,128)(2,1)S(1)}, bf16[32,1152]{1,0:T(8,128)(2,1)}, u32[]{:S(2)}, u32[]{:S(2)}) %collective-permute-start.62) | collective-permute-done | bytes 73760 | tf_op jit(solution)/shard_map/while/body/eval_jaxpr/cond/branch_63_fun/ppermute | solution.py:18
  191.8 0.9 constant_dynamic-update-slice_fusion.2
  192.8 0.2 reshape.206
  193.0 0.6 fusion.26
  193.5 1.2 copy.19
  194.8 1.1 add_convert_fusion
  195.9 0.6 convert_add_fusion
  (49 shorter events, 0.6 us)
Async XLA Ops:
  0.6 24.8 %copy-start = (bf16[320,1280]{1,0:T(8,128)(2,1)S(1)}, bf16[320,1280]{1,0:T(8,128)(2,1)}, u32[]{:S(2)}) copy-start(bf16[320,1280]{1,0:T(8,128)(2,1)} %param.77) | copy-start | bytes 2457604
  0.6 24.8 %copy-start.8 = (s32[1,1280]{1,0:T(1,128)S(1)}, s32[1,1280]{1,0:T(1,128)}, u32[]{:S(2)}) copy-start(s32[1,1280]{1,0:T(1,128)} %param.78) | copy-start | bytes 15364
  0.7 16.9 %collective-permute-start.63 = (bf16[1280,256]{1,0:T(8,128)(2,1)}, bf16[1280,256]{1,0:T(8,128)(2,1)S(1)}, u32[]{:S(2)}, u32[]{:S(2)}) collective-permute-start(bf16[1280,256]{1,0:T(8,128)(2,1)} %param.75), channel_id=1, source_target_pairs={{0,2},{1,3},{2,0},{3,1},{4,6},{5,7},{6,4},{7,5},{8,10},{9,11},{10,... | collective-permute-start | bytes 1966088 | tf_op jit(solution)/shard_map/ppermute | solution.py:24
  18.8 9.3 %collective-permute-start.64 = (bf16[2,1280,256]{2,1,0:T(8,128)(2,1)S(1)}, bf16[2,1280,256]{2,1,0:T(8,128)(2,1)}, u32[]{:S(2)}, u32[]{:S(2)}) collective-permute-start(bf16[2,1280,256]{2,1,0:T(8,128)(2,1)S(1)} %pad_maximum_fusion.1), channel_id=1, source_target_pairs={{0,1},{1,0},{2,3},{3,2},{4,5},{5,4},{6,7},{7,6},{8,9},{9,8},{10,11... | collective-permute-start | bytes 3932168 | tf_op jit(solution)/shard_map/ppermute | solution.py:26
  25.5 1.6 copy-start.6
  25.5 2.6 %copy-start.3 = (bf16[1280,256]{1,0:T(8,128)(2,1)S(1)}, bf16[1280,256]{1,0:T(8,128)(2,1)}, u32[]{:S(2)}) copy-start(bf16[1280,256]{1,0:T(8,128)(2,1)} %param.75) | copy-start | bytes 1966084
  27.4 3.8 %copy-start.5 = (bf16[320,128]{1,0:T(8,128)(2,1)}, bf16[320,128]{1,0:T(8,128)(2,1)S(1)}, u32[]{:S(2)}) copy-start(bf16[320,128]{1,0:T(8,128)(2,1)S(1)} %convolution_convert_fusion) | copy-start | bytes 245764
  31.4 26.7 %copy-start.4 = (bf16[256,1280]{1,0:T(8,128)(2,1)S(1)}, bf16[256,1280]{1,0:T(8,128)(2,1)}, u32[]{:S(2)}) copy-start(bf16[256,1280]{1,0:T(8,128)(2,1)} %param.76) | copy-start | bytes 1966084
  31.4 21.2 %collective-permute-start.65 = (bf16[320,1152]{1,0:T(8,128)(2,1)S(1)}, bf16[320,1152]{1,0:T(8,128)(2,1)S(1)}, u32[]{:S(2)}, u32[]{:S(2)}) collective-permute-start(bf16[320,1152]{1,0:T(8,128)(2,1)S(1)} %get-tuple-element.741), channel_id=1, source_target_pairs={{0,2},{1,3},{2,0},{3,1},{4,6},{5,7},{6,4},{7,5},{8,10},{9,11},{10,... | collective-permute-start | bytes 2211848 | tf_op jit(solution)/shard_map/ppermute | solution.py:24
  52.6 0.9 copy-start.2
  53.5 4.8 %copy-start.9 = (s32[4]{0:T(128)S(1)}, s32[4]{0:T(128)}, u32[]{:S(2)}) copy-start(s32[4]{0:T(128)} %constant.298.clone) | copy-start | bytes 52
  54.8 4.3 %copy-start.10 = (s32[1,4]{1,0:T(1,128)S(1)}, s32[1,4]{1,0:T(1,128)}, u32[]{:S(2)}) copy-start(s32[1,4]{1,0:T(1,128)} %param.80) | copy-start | bytes 52
  54.8 6.5 %collective-permute-start.66 = (bf16[2,320,1152]{2,1,0:T(8,128)(2,1)}, bf16[2,320,1152]{2,1,0:T(8,128)(2,1)}, u32[]{:S(2)}, u32[]{:S(2)}) collective-permute-start(bf16[2,320,1152]{2,1,0:T(8,128)(2,1)} %pad_maximum_fusion), channel_id=1, source_target_pairs={{0,1},{1,0},{2,3},{3,2},{4,5},{5,4},{6,7},{7,6},{8,9},{9,8},{10,11... | collective-permute-start | bytes 4423688 | tf_op jit(solution)/shard_map/ppermute | solution.py:26
  64.0 15.9 %collective-permute-start.67 = (bf16[32,1152]{1,0:T(8,128)(2,1)S(1)}, bf16[32,1152]{1,0:T(8,128)(2,1)S(1)}, u32[]{:S(2)}, u32[]{:S(2)}) collective-permute-start(bf16[32,1152]{1,0:T(8,128)(2,1)S(1)} %get-tuple-element.745), channel_id=1, source_target_pairs={{0,4},{1,5},{2,6},{3,7},{4,0},{5,1},{6,2},{7,3},{8,12},{9,13},{10,... | collective-permute-start | bytes 221192 | tf_op jit(solution)/shard_map/ppermute | solution.py:86
  67.5 20.1 %collective-permute-start.68 = (f32[32,1152]{1,0:T(8,128)S(1)}, f32[32,1152]{1,0:T(8,128)S(1)}, u32[]{:S(2)}, u32[]{:S(2)}) collective-permute-start(f32[32,1152]{1,0:T(8,128)S(1)} %get-tuple-element.742), channel_id=1, source_target_pairs={{0,1},{1,0},{2,3},{3,2},{4,5},{5,4},{6,7},{7,6},{8,9},{9,8},{10,11... | collective-permute-start | bytes 442376 | tf_op jit(solution)/shard_map/ppermute | solution.py:93
  70.1 15.4 %collective-permute-start.69 = (bf16[32,1152]{1,0:T(8,128)(2,1)S(1)}, bf16[32,1152]{1,0:T(8,128)(2,1)S(1)}, u32[]{:S(2)}, u32[]{:S(2)}) collective-permute-start(bf16[32,1152]{1,0:T(8,128)(2,1)S(1)} %get-tuple-element.748), channel_id=1, source_target_pairs={{0,5},{1,4},{2,7},{3,6},{4,1},{5,0},{6,3},{7,2},{8,13},{9,12},{10,... | collective-permute-start | bytes 221192 | tf_op jit(solution)/shard_map/ppermute | solution.py:86
  72.0 15.7 %collective-permute-start.70 = (f32[32,1152]{1,0:T(8,128)S(1)}, f32[32,1152]{1,0:T(8,128)S(1)}, u32[]{:S(2)}, u32[]{:S(2)}) collective-permute-start(f32[32,1152]{1,0:T(8,128)S(1)} %get-tuple-element.744), channel_id=1, source_target_pairs={{0,2},{1,3},{2,0},{3,1},{4,6},{5,7},{6,4},{7,5},{8,10},{9,11},{10,... | collective-permute-start | bytes 442376 | tf_op jit(solution)/shard_map/ppermute | solution.py:93
  76.8 11.0 %collective-permute-start.71 = (bf16[32,1152]{1,0:T(8,128)(2,1)S(1)}, bf16[32,1152]{1,0:T(8,128)(2,1)S(1)}, u32[]{:S(2)}, u32[]{:S(2)}) collective-permute-start(bf16[32,1152]{1,0:T(8,128)(2,1)S(1)} %get-tuple-element.747), channel_id=1, source_target_pairs={{0,6},{1,7},{2,4},{3,5},{4,2},{5,3},{6,0},{7,1},{8,14},{9,15},{10,... | collective-permute-start | bytes 221192 | tf_op jit(solution)/shard_map/ppermute | solution.py:86
  79.9 13.7 %collective-permute-start.72 = (f32[32,1152]{1,0:T(8,128)S(1)}, f32[32,1152]{1,0:T(8,128)S(1)}, u32[]{:S(2)}, u32[]{:S(2)}) collective-permute-start(f32[32,1152]{1,0:T(8,128)S(1)} %get-tuple-element.743), channel_id=1, source_target_pairs={{0,3},{1,2},{2,1},{3,0},{4,7},{5,6},{6,5},{7,4},{8,11},{9,10},{10,... | collective-permute-start | bytes 442376 | tf_op jit(solution)/shard_map/ppermute | solution.py:93
  85.6 8.1 %collective-permute-start.73 = (bf16[32,1152]{1,0:T(8,128)(2,1)S(1)}, bf16[32,1152]{1,0:T(8,128)(2,1)S(1)}, u32[]{:S(2)}, u32[]{:S(2)}) collective-permute-start(bf16[32,1152]{1,0:T(8,128)(2,1)S(1)} %get-tuple-element.746), channel_id=1, source_target_pairs={{0,7},{1,6},{2,5},{3,4},{4,3},{5,2},{6,1},{7,0},{8,15},{9,14},{10,... | collective-permute-start | bytes 221192 | tf_op jit(solution)/shard_map/ppermute | solution.py:86
  95.8 15.4 %collective-permute-start.13 = (bf16[32,1152]{1,0:T(8,128)(2,1)S(1)}, bf16[32,1152]{1,0:T(8,128)(2,1)}, u32[]{:S(2)}, u32[]{:S(2)}) collective-permute-start(bf16[32,1152]{1,0:T(8,128)(2,1)S(1)} %dynamic-slice_bitcast_fusion.13), channel_id=1, source_target_pairs={{0,112},{4,116},{8,120},{12,124},{16,96},{20,100},{24,104},{28,108... | collective-permute-start | bytes 221192 | tf_op jit(solution)/shard_map/while/body/eval_jaxpr/cond/branch_14_fun/ppermute | solution.py:18
  113.3 11.6 %collective-permute-start.23 = (bf16[32,1152]{1,0:T(8,128)(2,1)S(1)}, bf16[32,1152]{1,0:T(8,128)(2,1)}, u32[]{:S(2)}, u32[]{:S(2)}) collective-permute-start(bf16[32,1152]{1,0:T(8,128)(2,1)S(1)} %dynamic-slice_bitcast_fusion.23), channel_id=1, source_target_pairs={{0,192},{4,196},{8,200},{12,204},{16,208},{20,212},{24,216},{28,22... | collective-permute-start | bytes 221192 | tf_op jit(solution)/shard_map/while/body/eval_jaxpr/cond/branch_24_fun/ppermute | solution.py:18
  127.2 32.4 %collective-permute-start.58 = (bf16[32,1152]{1,0:T(8,128)(2,1)S(1)}, bf16[32,1152]{1,0:T(8,128)(2,1)}, u32[]{:S(2)}, u32[]{:S(2)}) collective-permute-start(bf16[32,1152]{1,0:T(8,128)(2,1)S(1)} %dynamic-slice_bitcast_fusion.58), channel_id=1, source_target_pairs={{0,472},{4,476},{8,464},{12,468},{16,456},{20,460},{24,448},{28,45... | collective-permute-start | bytes 221192 | tf_op jit(solution)/shard_map/while/body/eval_jaxpr/cond/branch_59_fun/ppermute | solution.py:18
  161.9 29.9 %collective-permute-start.62 = (bf16[32,1152]{1,0:T(8,128)(2,1)S(1)}, bf16[32,1152]{1,0:T(8,128)(2,1)}, u32[]{:S(2)}, u32[]{:S(2)}) collective-permute-start(bf16[32,1152]{1,0:T(8,128)(2,1)S(1)} %dynamic-slice_bitcast_fusion.62), channel_id=1, source_target_pairs={{0,504},{4,508},{8,496},{12,500},{16,488},{20,492},{24,480},{28,48... | collective-permute-start | bytes 221192 | tf_op jit(solution)/shard_map/while/body/eval_jaxpr/cond/branch_63_fun/ppermute | solution.py:18
  193.5 1.2 copy-start.1
  194.8 1.2 copy-start.7

commit v9 on v6

--- a/solution.py
+++ b/solution.py
@@ -78,19 +78,12 @@
     moving = (own_rows + partner_rows.astype(jnp.float32)).astype(jnp.bfloat16)
     col_count = 4
     share_rows = half_rows // col_count
-    quarters = moving.reshape(col_count, share_rows, moving.shape[1])
-    by_distance = [lax.dynamic_index_in_dim(quarters, col_index, 0, keepdims=False)]
-    for distance in range(1, col_count):
-        outgoing = lax.dynamic_index_in_dim(
-            quarters, jnp.bitwise_xor(col_index, distance), 0, keepdims=False
-        )
-        by_distance.append(
-            lax.ppermute(outgoing, COLS, [(c, c ^ distance) for c in range(col_count)])
-        )
-    spread = jnp.take(
-        jnp.stack(by_distance),
-        jnp.bitwise_xor(jnp.arange(col_count, dtype=jnp.int32), col_index),
-        axis=0,
+    spread = lax.all_to_all(
+        moving.reshape(col_count, share_rows, moving.shape[1]),
+        COLS,
+        split_axis=0,
+        concat_axis=0,
+        tiled=True,
     )
     column_masks = jnp.bitwise_xor(pattern[0], leaf_index // 2)
     branches = xor_route(None, leaf_count // 2)

time: 185 us -> 195 us (1.054)
  starting transfers between devices: 75.6 us -> 84.9 us
    ppermute x3 -> x4, starting transfers between devices: 41.6 us -> 55.7 us  [branch(): return lambda x: lax.ppermute(x, LEAF, pairs)]
    ppermute x3 -> x0, starting transfers between devices: 10.2 us -> none  [body(): lax.ppermute(outgoing, COLS, [(c, c ^ distance) for c in range(col_count)])]
    all_to_all x0 -> x1, waiting for transfers between devices: none -> 6.95 us  [body(): lax.all_to_all(moving.reshape(col_count, share_rows, moving.shape[1]), CO...]
    all_to_all x0 -> x1, starting transfers between devices: none -> 5.59 us  [body(): lax.all_to_all(moving.reshape(col_count, share_rows, moving.shape[1]), CO...]
    ppermute x3 -> x0, waiting for transfers between devices: 5.2 us -> none  [body(): lax.ppermute(outgoing, COLS, [(c, c ^ distance) for c in range(col_count)])]
    ppermute x3 -> x4, waiting for transfers between devices: 38 us -> 36.3 us  [branch(): return lambda x: lax.ppermute(x, LEAF, pairs)]
  transfers between devices with their start and end apart: 11 -> 10, of which waited for: 10 -> 10; matrix products, arithmetic and copies ran while one was open for 2% -> 2% of each run, Pallas kernels for 0% -> 0%
where the time goes in v9:
time: 195 us; the launch traced here: 194 us
  starting transfers between devices  84.9 us (44%)
  waiting for transfers between devices  80.4 us (41%)
  local copies, waits for them, and re-layouts  11 us (6%)
  matrix products  7.52 us (4%)
  other arithmetic  6.58 us (3%)
  loops' own time  2.99 us (2%)
    ppermute x4, starting transfers between devices, branch(): return lambda x: lax.ppermute(x, LEAF, pairs)  55.7 us
    ppermute x4, waiting for transfers between devices, branch(): return lambda x: lax.ppermute(x, LEAF, pairs)  36.3 us
    ppermute x2, waiting for transfers between devices, col_gather(): remote = lax.ppermute(block, COLS, [(c, c ^ 2) for c in range(4)])  27.5 us
    ppermute x2, starting transfers between devices, col_gather(): remote = lax.ppermute(block, COLS, [(c, c ^ 2) for c in range(4)])  10.6 us
    ppermute x2, starting transfers between devices, col_gather(): partner = lax.ppermute(chip, COLS, [(c, c ^ 1) for c in range(4)])  9.61 us
    all_to_all x1, waiting for transfers between devices, body(): lax.all_to_all(moving.reshape(col_count, share_rows, moving.shape[1]), CO...  6.95 us
    ppermute x1, waiting for transfers between devices, body(): lax.ppermute(other_rows.astype(jnp.bfloat16), LEAF, [(s, s ^ 1) for s in...  6.69 us
    all_to_all x1, starting transfers between devices, body(): lax.all_to_all(moving.reshape(col_count, share_rows, moving.shape[1]), CO...  5.59 us
  transfers between devices with their start and end apart: 10, of which 10 were waited for; matrix products, arithmetic and copies ran while one was open for 2% of the time, Pallas kernels for 0%

profile of v9, /device:TPU:1, one launch (start us, length us, event | category | flops | bytes accessed | tf_op | source)
XLA Modules:
  0.0 194.3 jit_solution(13816841714860769144)
XLA Ops:
  0.6 0.0 copy-start
  0.7 5.6 %collective-permute-start.63 = (bf16[1280,256]{1,0:T(8,128)(2,1)}, bf16[1280,256]{1,0:T(8,128)(2,1)S(1)}, u32[]{:S(2)}, u32[]{:S(2)}) collective-permute-start(bf16[1280,256]{1,0:T(8,128)(2,1)} %param.75), channel_id=1, source_target_pairs={{0,2},{1,3},{2,0},{3,1},{4,6},{5,7},{6,4},{7,5},{8,10},{9,11},{10,... | collective-permute-start | bytes 1966088 | tf_op jit(solution)/shard_map/ppermute | solution.py:24
  6.3 11.3 %collective-permute-done.63 = bf16[1280,256]{1,0:T(8,128)(2,1)S(1)} collective-permute-done((bf16[1280,256]{1,0:T(8,128)(2,1)}, bf16[1280,256]{1,0:T(8,128)(2,1)S(1)}, u32[]{:S(2)}, u32[]{:S(2)}) %collective-permute-start.63) | collective-permute-done | bytes 655392 | tf_op jit(solution)/shard_map/ppermute | solution.py:24
  17.6 1.2 pad_maximum_fusion.1
  18.8 6.5 %collective-permute-start.64 = (bf16[2,1280,256]{2,1,0:T(8,128)(2,1)S(1)}, bf16[2,1280,256]{2,1,0:T(8,128)(2,1)}, u32[]{:S(2)}, u32[]{:S(2)}) collective-permute-start(bf16[2,1280,256]{2,1,0:T(8,128)(2,1)S(1)} %pad_maximum_fusion.1), channel_id=1, source_target_pairs={{0,1},{1,0},{2,3},{3,2},{4,5},{5,4},{6,7},{7,6},{8,9},{9,8},{10,11... | collective-permute-start | bytes 3932168 | tf_op jit(solution)/shard_map/ppermute | solution.py:26
  25.3 0.1 broadcast_in_dim.236
  25.5 0.0 copy-done
  25.5 0.0 copy-start.7
  25.5 0.0 copy-start.4
  25.5 1.5 fusion.11
  27.1 0.4 convolution_convert_fusion
  27.4 0.0 copy-start.6
  27.5 0.6 collective-permute-done.64
  28.1 2.3 %fusion.15 = bf16[320,4,256]{2,0,1:T(8,128)(2,1)S(1)} fusion(bf16[2,1280,256]{2,1,0:T(8,128)(2,1)} %collective-permute-done.64, bf16[1,1280,256]{2,1,0:T(8,128)(2,1)S(1)} %bitcast.236, bf16[1,1280,256]{2,1,0:T(8,128)(2,1)S(1)} %bitcast.234, bf16[1280,320]{0,1:T(8,128)(2,1)S(1)} %fusion.11), kind=kOutput, calls=%fused_computation.79 | convolution fusion | flops 846725120 | bytes 4096000 | tf_op jit(solution)/shard_map/ip,kpn->ikn/dot_general | solution.py:56
  30.4 0.6 gather_fusion.1
  31.0 0.1 copy.18
  31.1 0.2 select_convert_fusion
  31.3 0.1 fusion.39
  31.4 0.0 copy-start.5
  31.4 5.0 %collective-permute-start.65 = (bf16[320,1152]{1,0:T(8,128)(2,1)S(1)}, bf16[320,1152]{1,0:T(8,128)(2,1)S(1)}, u32[]{:S(2)}, u32[]{:S(2)}) collective-permute-start(bf16[320,1152]{1,0:T(8,128)(2,1)S(1)} %get-tuple-element.741), channel_id=1, source_target_pairs={{0,2},{1,3},{2,0},{3,1},{4,6},{5,7},{6,4},{7,5},{8,10},{9,11},{10,... | collective-permute-start | bytes 2211848 | tf_op jit(solution)/shard_map/ppermute | solution.py:24
  36.4 16.2 %collective-permute-done.65 = bf16[320,1152]{1,0:T(8,128)(2,1)S(1)} collective-permute-done((bf16[320,1152]{1,0:T(8,128)(2,1)S(1)}, bf16[320,1152]{1,0:T(8,128)(2,1)S(1)}, u32[]{:S(2)}, u32[]{:S(2)}) %collective-permute-start.65) | collective-permute-done | bytes 737312 | tf_op jit(solution)/shard_map/ppermute | solution.py:24
  52.6 0.9 copy-done.2
  53.5 1.3 pad_maximum_fusion
  54.8 3.1 %collective-permute-start.66 = (bf16[2,320,1152]{2,1,0:T(8,128)(2,1)}, bf16[2,320,1152]{2,1,0:T(8,128)(2,1)}, u32[]{:S(2)}, u32[]{:S(2)}) collective-permute-start(bf16[2,320,1152]{2,1,0:T(8,128)(2,1)} %pad_maximum_fusion), channel_id=1, source_target_pairs={{0,1},{1,0},{2,3},{3,2},{4,5},{5,4},{6,7},{7,6},{8,9},{9,8},{10,11... | collective-permute-start | bytes 4423688 | tf_op jit(solution)/shard_map/ppermute | solution.py:26
  57.9 0.2 copy.13
  58.2 0.6 gather_fusion
  58.8 2.3 %collective-permute-done.66 = bf16[2,320,1152]{2,1,0:T(8,128)(2,1)} collective-permute-done((bf16[2,320,1152]{2,1,0:T(8,128)(2,1)}, bf16[2,320,1152]{2,1,0:T(8,128)(2,1)}, u32[]{:S(2)}, u32[]{:S(2)}) %collective-permute-start.66) | collective-permute-done | bytes 1474592 | tf_op jit(solution)/shard_map/ppermute | solution.py:26
  61.1 2.7 %fusion.12 = f32[256,1152]{1,0:T(8,128)S(1)} fusion(bf16[2,320,1152]{2,1,0:T(8,128)(2,1)} %collective-permute-done.66, bf16[1,320,1152]{2,1,0:T(8,128)(2,1)} %bitcast.232, bf16[1,320,1152]{2,1,0:T(8,128)(2,1)S(1)} %get-tuple-element.740, bf16[4,256,320]{1,2,0:T(8,128)(2,1)S(1)} %gather_fusion, pred[4]{0:T(512)(128)(4,1)S(1)} %get-tuple-element.738), kind=kOutput, calls=%fused_computation.78 | convolution fusion | flops 758546432 | bytes 4784132 | tf_op jit(solution)/shard_map/rkp,kpn->rn/dot_general | solution.py:65
  63.8 1.0 copy-done.3
  64.9 3.4 %collective-permute-start.67 = (bf16[128,1152]{1,0:T(8,128)(2,1)S(1)}, bf16[128,1152]{1,0:T(8,128)(2,1)S(1)}, u32[]{:S(2)}, u32[]{:S(2)}) collective-permute-start(bf16[128,1152]{1,0:T(8,128)(2,1)S(1)} %dynamic-slice_convert_fusion), channel_id=1, source_target_pairs={{0,4},{4,0},{8,12},{12,8},{16,20},{20,16},{24,28},{28,24},{32,36},... | collective-permute-start | bytes 884744 | tf_op jit(solution)/shard_map/ppermute | solution.py:75
  68.4 0.1 xor_xor_fusion
  68.4 6.7 %collective-permute-done.67 = bf16[128,1152]{1,0:T(8,128)(2,1)S(1)} collective-permute-done((bf16[128,1152]{1,0:T(8,128)(2,1)S(1)}, bf16[128,1152]{1,0:T(8,128)(2,1)S(1)}, u32[]{:S(2)}, u32[]{:S(2)}) %collective-permute-start.67) | collective-permute-done | bytes 294944 | tf_op jit(solution)/shard_map/ppermute | solution.py:75
  75.1 1.8 add_convert_fusion.1
  77.0 5.6 %all-to-all-start = ((bf16[4,32,1152]{2,1,0:T(8,128)(2,1)}), bf16[4,32,1152]{2,1,0:T(8,128)(2,1)S(1)}, u32[]{:S(2)}, u32[]{:S(2)}) async-start(bf16[4,32,1152]{2,1,0:T(8,128)(2,1)} %bitcast.138), calls=%async_computation | async-start | bytes 589824 | tf_op jit(solution)/shard_map/all_to_all | solution.py:81
  82.5 0.1 fusion.30
  82.6 7.0 %all-to-all-done = bf16[4,32,1152]{2,1,0:T(8,128)(2,1)S(1)} async-done(((bf16[4,32,1152]{2,1,0:T(8,128)(2,1)}), bf16[4,32,1152]{2,1,0:T(8,128)(2,1)S(1)}, u32[]{:S(2)}, u32[]{:S(2)}) %all-to-all-start) | async-done | bytes 294944 | tf_op jit(solution)/shard_map/all_to_all | solution.py:81
  89.6 101.0 %while.13 = (s32[]{:T(128)}, bf16[4,32,1152]{2,1,0:T(8,128)(2,1)S(1)}, s32[4]{0:T(128)S(1)}, bf16[4,32,1152]{2,1,0:T(8,128)(2,1)S(1)}, s32[]{:T(128)}, /*index=5*/s32[1]{0:T(128)}, s32[1]{0:T(128)}) while((s32[]{:T(128)}, bf16[4,32,1152]{2,1,0:T(8,128)(2,1)S(1)}, s32[4]{0:T(128)S(1)}, bf16[4,32,1152]{2,1,0:T(8,128)(2,1)S(1)}, s32[]{:T(128)}, ...), condition=%wide.region_65.66_spmd, body=%wide.region_0.65_spmd.sunk | while | flops 3 | bytes 590001 | solution.py:96
  89.6 0.6 dynamic_slice.344
  90.8 18.8 %conditional.2 = (bf16[1,32,1152]{2,1,0:T(8,128)(2,1)}) conditional(s32[]{:T(128)} %bitcast.225, (bf16[4,32,1152]{2,1,0:T(8,128)(2,1)S(1)}, s32[]{:T(128)}) %tuple.359, (bf16[4,32,1152]{2,1,0:T(8,128)(2,1)S(1)}, s32[]{:T(128)}) %tuple.359, (bf16[4,32,1152]{2,1,0:T(8,128)(2,1)S(1)}, s32[]{:T(128)}) %tuple.359, ...), branch_computations={%region_1.1_spmd, %region_2.2_spmd, %region_3.3_spmd, %region_4.4_... | conditional | bytes 442420 | solution.py:93
  90.9 14.6 %collective-permute-start.26 = (bf16[32,1152]{1,0:T(8,128)(2,1)S(1)}, bf16[32,1152]{1,0:T(8,128)(2,1)}, u32[]{:S(2)}, u32[]{:S(2)}) collective-permute-start(bf16[32,1152]{1,0:T(8,128)(2,1)S(1)} %dynamic-slice_bitcast_fusion.26), channel_id=1, source_target_pairs={{0,216},{4,220},{8,208},{12,212},{16,200},{20,204},{24,192},{28,19... | collective-permute-start | bytes 221192 | tf_op jit(solution)/shard_map/while/body/eval_jaxpr/cond/branch_27_fun/ppermute | solution.py:18
  105.5 4.0 %collective-permute-done.26 = bf16[32,1152]{1,0:T(8,128)(2,1)} collective-permute-done((bf16[32,1152]{1,0:T(8,128)(2,1)S(1)}, bf16[32,1152]{1,0:T(8,128)(2,1)}, u32[]{:S(2)}, u32[]{:S(2)}) %collective-permute-start.26) | collective-permute-done | bytes 73760 | tf_op jit(solution)/shard_map/while/body/eval_jaxpr/cond/branch_27_fun/ppermute | solution.py:18
  109.6 0.9 constant_dynamic-update-slice_fusion.2
  110.5 0.6 dynamic_slice.344
  111.7 15.6 %conditional.2 = (bf16[1,32,1152]{2,1,0:T(8,128)(2,1)}) conditional(s32[]{:T(128)} %bitcast.225, (bf16[4,32,1152]{2,1,0:T(8,128)(2,1)S(1)}, s32[]{:T(128)}) %tuple.359, (bf16[4,32,1152]{2,1,0:T(8,128)(2,1)S(1)}, s32[]{:T(128)}) %tuple.359, (bf16[4,32,1152]{2,1,0:T(8,128)(2,1)S(1)}, s32[]{:T(128)}) %tuple.359, ...), branch_computations={%region_1.1_spmd, %region_2.2_spmd, %region_3.3_spmd, %region_4.4_... | conditional | bytes 442420 | solution.py:93
  111.8 11.6 %collective-permute-start.18 = (bf16[32,1152]{1,0:T(8,128)(2,1)S(1)}, bf16[32,1152]{1,0:T(8,128)(2,1)}, u32[]{:S(2)}, u32[]{:S(2)}) collective-permute-start(bf16[32,1152]{1,0:T(8,128)(2,1)S(1)} %dynamic-slice_bitcast_fusion.18), channel_id=1, source_target_pairs={{0,152},{4,156},{8,144},{12,148},{16,136},{20,140},{24,128},{28,13... | collective-permute-start | bytes 221192 | tf_op jit(solution)/shard_map/while/body/eval_jaxpr/cond/branch_19_fun/ppermute | solution.py:18
  123.5 3.9 %collective-permute-done.18 = bf16[32,1152]{1,0:T(8,128)(2,1)} collective-permute-done((bf16[32,1152]{1,0:T(8,128)(2,1)S(1)}, bf16[32,1152]{1,0:T(8,128)(2,1)}, u32[]{:S(2)}, u32[]{:S(2)}) %collective-permute-start.18) | collective-permute-done | bytes 73760 | tf_op jit(solution)/shard_map/while/body/eval_jaxpr/cond/branch_19_fun/ppermute | solution.py:18
  127.3 0.9 constant_dynamic-update-slice_fusion.2
  128.3 0.6 dynamic_slice.344
  129.5 31.9 %conditional.2 = (bf16[1,32,1152]{2,1,0:T(8,128)(2,1)}) conditional(s32[]{:T(128)} %bitcast.225, (bf16[4,32,1152]{2,1,0:T(8,128)(2,1)S(1)}, s32[]{:T(128)}) %tuple.359, (bf16[4,32,1152]{2,1,0:T(8,128)(2,1)S(1)}, s32[]{:T(128)}) %tuple.359, (bf16[4,32,1152]{2,1,0:T(8,128)(2,1)S(1)}, s32[]{:T(128)}) %tuple.359, ...), branch_computations={%region_1.1_spmd, %region_2.2_spmd, %region_3.3_spmd, %region_4.4_... | conditional | bytes 442420 | solution.py:93
  129.6 16.5 %collective-permute-start.58 = (bf16[32,1152]{1,0:T(8,128)(2,1)S(1)}, bf16[32,1152]{1,0:T(8,128)(2,1)}, u32[]{:S(2)}, u32[]{:S(2)}) collective-permute-start(bf16[32,1152]{1,0:T(8,128)(2,1)S(1)} %dynamic-slice_bitcast_fusion.58), channel_id=1, source_target_pairs={{0,472},{4,476},{8,464},{12,468},{16,456},{20,460},{24,448},{28,45... | collective-permute-start | bytes 221192 | tf_op jit(solution)/shard_map/while/body/eval_jaxpr/cond/branch_59_fun/ppermute | solution.py:18
  146.1 15.3 %collective-permute-done.58 = bf16[32,1152]{1,0:T(8,128)(2,1)} collective-permute-done((bf16[32,1152]{1,0:T(8,128)(2,1)S(1)}, bf16[32,1152]{1,0:T(8,128)(2,1)}, u32[]{:S(2)}, u32[]{:S(2)}) %collective-permute-start.58) | collective-permute-done | bytes 73760 | tf_op jit(solution)/shard_map/while/body/eval_jaxpr/cond/branch_59_fun/ppermute | solution.py:18
  161.4 0.9 constant_dynamic-update-slice_fusion.2
  162.3 0.6 dynamic_slice.344
  163.6 26.0 %conditional.2 = (bf16[1,32,1152]{2,1,0:T(8,128)(2,1)}) conditional(s32[]{:T(128)} %bitcast.225, (bf16[4,32,1152]{2,1,0:T(8,128)(2,1)S(1)}, s32[]{:T(128)}) %tuple.359, (bf16[4,32,1152]{2,1,0:T(8,128)(2,1)S(1)}, s32[]{:T(128)}) %tuple.359, (bf16[4,32,1152]{2,1,0:T(8,128)(2,1)S(1)}, s32[]{:T(128)}) %tuple.359, ...), branch_computations={%region_1.1_spmd, %region_2.2_spmd, %region_3.3_spmd, %region_4.4_... | conditional | bytes 442420 | solution.py:93
  163.7 12.8 %collective-permute-start.45 = (bf16[32,1152]{1,0:T(8,128)(2,1)S(1)}, bf16[32,1152]{1,0:T(8,128)(2,1)}, u32[]{:S(2)}, u32[]{:S(2)}) collective-permute-start(bf16[32,1152]{1,0:T(8,128)(2,1)S(1)} %dynamic-slice_bitcast_fusion.45), channel_id=1, source_target_pairs={{0,368},{4,372},{8,376},{12,380},{16,352},{20,356},{24,360},{28,36... | collective-permute-start | bytes 221192 | tf_op jit(solution)/shard_map/while/body/eval_jaxpr/cond/branch_46_fun/ppermute | solution.py:18
  176.5 13.1 %collective-permute-done.45 = bf16[32,1152]{1,0:T(8,128)(2,1)} collective-permute-done((bf16[32,1152]{1,0:T(8,128)(2,1)S(1)}, bf16[32,1152]{1,0:T(8,128)(2,1)}, u32[]{:S(2)}, u32[]{:S(2)}) %collective-permute-start.45) | collective-permute-done | bytes 73760 | tf_op jit(solution)/shard_map/while/body/eval_jaxpr/cond/branch_46_fun/ppermute | solution.py:18
  189.6 0.9 constant_dynamic-update-slice_fusion.2
  190.6 0.2 reshape.182
  190.8 0.6 fusion.26
  191.3 0.0 copy-start.1
  191.3 1.2 copy.19
  192.6 0.0 copy-start.8
  192.6 1.1 add_convert_fusion
  193.7 0.6 convert_add_fusion
  (30 shorter events, 0.2 us)
Async XLA Ops:
  0.6 24.8 %copy-start = (bf16[320,1280]{1,0:T(8,128)(2,1)S(1)}, bf16[320,1280]{1,0:T(8,128)(2,1)}, u32[]{:S(2)}) copy-start(bf16[320,1280]{1,0:T(8,128)(2,1)} %param.77) | copy-start | bytes 2457604
  0.6 24.8 %copy-start.9 = (s32[1,1280]{1,0:T(1,128)S(1)}, s32[1,1280]{1,0:T(1,128)}, u32[]{:S(2)}) copy-start(s32[1,1280]{1,0:T(1,128)} %param.78) | copy-start | bytes 15364
  0.7 16.9 %collective-permute-start.63 = (bf16[1280,256]{1,0:T(8,128)(2,1)}, bf16[1280,256]{1,0:T(8,128)(2,1)S(1)}, u32[]{:S(2)}, u32[]{:S(2)}) collective-permute-start(bf16[1280,256]{1,0:T(8,128)(2,1)} %param.75), channel_id=1, source_target_pairs={{0,2},{1,3},{2,0},{3,1},{4,6},{5,7},{6,4},{7,5},{8,10},{9,11},{10,... | collective-permute-start | bytes 1966088 | tf_op jit(solution)/shard_map/ppermute | solution.py:24
  18.8 9.3 %collective-permute-start.64 = (bf16[2,1280,256]{2,1,0:T(8,128)(2,1)S(1)}, bf16[2,1280,256]{2,1,0:T(8,128)(2,1)}, u32[]{:S(2)}, u32[]{:S(2)}) collective-permute-start(bf16[2,1280,256]{2,1,0:T(8,128)(2,1)S(1)} %pad_maximum_fusion.1), channel_id=1, source_target_pairs={{0,1},{1,0},{2,3},{3,2},{4,5},{5,4},{6,7},{7,6},{8,9},{9,8},{10,11... | collective-permute-start | bytes 3932168 | tf_op jit(solution)/shard_map/ppermute | solution.py:26
  25.5 1.6 copy-start.7
  25.5 2.6 %copy-start.4 = (bf16[1280,256]{1,0:T(8,128)(2,1)S(1)}, bf16[1280,256]{1,0:T(8,128)(2,1)}, u32[]{:S(2)}) copy-start(bf16[1280,256]{1,0:T(8,128)(2,1)} %param.75) | copy-start | bytes 1966084
  27.4 3.8 %copy-start.6 = (bf16[320,128]{1,0:T(8,128)(2,1)}, bf16[320,128]{1,0:T(8,128)(2,1)S(1)}, u32[]{:S(2)}) copy-start(bf16[320,128]{1,0:T(8,128)(2,1)S(1)} %convolution_convert_fusion) | copy-start | bytes 245764
  31.4 26.5 %copy-start.5 = (bf16[256,1280]{1,0:T(8,128)(2,1)S(1)}, bf16[256,1280]{1,0:T(8,128)(2,1)}, u32[]{:S(2)}) copy-start(bf16[256,1280]{1,0:T(8,128)(2,1)} %param.76) | copy-start | bytes 1966084
  31.4 21.2 %collective-permute-start.65 = (bf16[320,1152]{1,0:T(8,128)(2,1)S(1)}, bf16[320,1152]{1,0:T(8,128)(2,1)S(1)}, u32[]{:S(2)}, u32[]{:S(2)}) collective-permute-start(bf16[320,1152]{1,0:T(8,128)(2,1)S(1)} %get-tuple-element.741), channel_id=1, source_target_pairs={{0,2},{1,3},{2,0},{3,1},{4,6},{5,7},{6,4},{7,5},{8,10},{9,11},{10,... | collective-permute-start | bytes 2211848 | tf_op jit(solution)/shard_map/ppermute | solution.py:24
  52.6 0.9 copy-start.2
  53.5 4.7 %copy-start.10 = (s32[4]{0:T(128)S(1)}, s32[4]{0:T(128)}, u32[]{:S(2)}) copy-start(s32[4]{0:T(128)} %constant.265.clone) | copy-start | bytes 52
  54.8 6.3 %collective-permute-start.66 = (bf16[2,320,1152]{2,1,0:T(8,128)(2,1)}, bf16[2,320,1152]{2,1,0:T(8,128)(2,1)}, u32[]{:S(2)}, u32[]{:S(2)}) collective-permute-start(bf16[2,320,1152]{2,1,0:T(8,128)(2,1)} %pad_maximum_fusion), channel_id=1, source_target_pairs={{0,1},{1,0},{2,3},{3,2},{4,5},{5,4},{6,7},{7,6},{8,9},{9,8},{10,11... | collective-permute-start | bytes 4423688 | tf_op jit(solution)/shard_map/ppermute | solution.py:26
  61.1 7.2 %copy-start.11 = (s32[1,4]{1,0:T(1,128)S(1)}, s32[1,4]{1,0:T(1,128)}, u32[]{:S(2)}) copy-start(s32[1,4]{1,0:T(1,128)} %param.80) | copy-start | bytes 52
  63.8 1.0 copy-start.3
  64.9 10.2 %collective-permute-start.67 = (bf16[128,1152]{1,0:T(8,128)(2,1)S(1)}, bf16[128,1152]{1,0:T(8,128)(2,1)S(1)}, u32[]{:S(2)}, u32[]{:S(2)}) collective-permute-start(bf16[128,1152]{1,0:T(8,128)(2,1)S(1)} %dynamic-slice_convert_fusion), channel_id=1, source_target_pairs={{0,4},{4,0},{8,12},{12,8},{16,20},{20,16},{24,28},{28,24},{32,36},... | collective-permute-start | bytes 884744 | tf_op jit(solution)/shard_map/ppermute | solution.py:75
  77.0 12.6 %all-to-all-start = ((bf16[4,32,1152]{2,1,0:T(8,128)(2,1)}), bf16[4,32,1152]{2,1,0:T(8,128)(2,1)S(1)}, u32[]{:S(2)}, u32[]{:S(2)}) async-start(bf16[4,32,1152]{2,1,0:T(8,128)(2,1)} %bitcast.138), calls=%async_computation | async-start | bytes 589824 | tf_op jit(solution)/shard_map/all_to_all | solution.py:81
  90.9 18.7 %collective-permute-start.26 = (bf16[32,1152]{1,0:T(8,128)(2,1)S(1)}, bf16[32,1152]{1,0:T(8,128)(2,1)}, u32[]{:S(2)}, u32[]{:S(2)}) collective-permute-start(bf16[32,1152]{1,0:T(8,128)(2,1)S(1)} %dynamic-slice_bitcast_fusion.26), channel_id=1, source_target_pairs={{0,216},{4,220},{8,208},{12,212},{16,200},{20,204},{24,192},{28,19... | collective-permute-start | bytes 221192 | tf_op jit(solution)/shard_map/while/body/eval_jaxpr/cond/branch_27_fun/ppermute | solution.py:18
  111.8 15.5 %collective-permute-start.18 = (bf16[32,1152]{1,0:T(8,128)(2,1)S(1)}, bf16[32,1152]{1,0:T(8,128)(2,1)}, u32[]{:S(2)}, u32[]{:S(2)}) collective-permute-start(bf16[32,1152]{1,0:T(8,128)(2,1)S(1)} %dynamic-slice_bitcast_fusion.18), channel_id=1, source_target_pairs={{0,152},{4,156},{8,144},{12,148},{16,136},{20,140},{24,128},{28,13... | collective-permute-start | bytes 221192 | tf_op jit(solution)/shard_map/while/body/eval_jaxpr/cond/branch_19_fun/ppermute | solution.py:18
  129.6 31.8 %collective-permute-start.58 = (bf16[32,1152]{1,0:T(8,128)(2,1)S(1)}, bf16[32,1152]{1,0:T(8,128)(2,1)}, u32[]{:S(2)}, u32[]{:S(2)}) collective-permute-start(bf16[32,1152]{1,0:T(8,128)(2,1)S(1)} %dynamic-slice_bitcast_fusion.58), channel_id=1, source_target_pairs={{0,472},{4,476},{8,464},{12,468},{16,456},{20,460},{24,448},{28,45... | collective-permute-start | bytes 221192 | tf_op jit(solution)/shard_map/while/body/eval_jaxpr/cond/branch_59_fun/ppermute | solution.py:18
  163.7 26.0 %collective-permute-start.45 = (bf16[32,1152]{1,0:T(8,128)(2,1)S(1)}, bf16[32,1152]{1,0:T(8,128)(2,1)}, u32[]{:S(2)}, u32[]{:S(2)}) collective-permute-start(bf16[32,1152]{1,0:T(8,128)(2,1)S(1)} %dynamic-slice_bitcast_fusion.45), channel_id=1, source_target_pairs={{0,368},{4,372},{8,376},{12,380},{16,352},{20,356},{24,360},{28,36... | collective-permute-start | bytes 221192 | tf_op jit(solution)/shard_map/while/body/eval_jaxpr/cond/branch_46_fun/ppermute | solution.py:18
  191.3 1.2 copy-start.1
  192.6 1.2 copy-start.8

commit v10 on v6

--- a/solution.py
+++ b/solution.py
@@ -24,7 +24,7 @@
     remote = lax.ppermute(block, COLS, [(c, c ^ 2) for c in range(4)])
     chip = jnp.stack([block, remote])
     partner = lax.ppermute(chip, COLS, [(c, c ^ 1) for c in range(4)])
-    return jnp.concatenate([chip, partner])
+    return chip, partner
 
 
 def relative_order(col_index):
@@ -53,7 +53,12 @@
     )
     canonical = relative_order(col_index)
     eliminated = jnp.take(
-        jnp.einsum("ip,kpn->ikn", inverse_perm, upper_all, preferred_element_type=jnp.float32),
+        jnp.einsum(
+            "ip,kpn->ikn",
+            inverse_perm,
+            jnp.concatenate(upper_all),
+            preferred_element_type=jnp.float32,
+        ),
         canonical,
         axis=1,
     ).astype(jnp.bfloat16)
@@ -62,11 +67,17 @@
     rows_all = col_gather(rows_out)
     lower_rows = lower_block.shape[0]
     source_blocks = jnp.bitwise_xor(jnp.array([0, 2, 1, 3], jnp.int32), col_index)
-    combined = -jnp.einsum(
-        "rkp,kpn->rn",
-        jnp.take(lower_block.reshape(lower_rows, 4, share), source_blocks, axis=1),
-        rows_all,
-        preferred_element_type=jnp.float32,
+    lower_parts = jnp.take(lower_block.reshape(lower_rows, 4, share), source_blocks, axis=1)
+    chip_rows, partner_rows = rows_all
+    chip_part = jnp.einsum(
+        "rkp,kpn->rn", lower_parts[:, :2], chip_rows, preferred_element_type=jnp.float32
+    )
+    chip_part, partner_rows = lax.optimization_barrier((chip_part, partner_rows))
+    combined = -(
+        chip_part
+        + jnp.einsum(
+            "rkp,kpn->rn", lower_parts[:, 2:], partner_rows, preferred_element_type=jnp.float32
+        )
     )
     own_side = leaf_index % 2
     half_rows = lower_rows // 2

time: 185 us -> 151 us (0.82)
  waiting for transfers between devices: 80.2 us -> 49.5 us
  starting transfers between devices: 75.6 us -> 72.1 us
    ppermute x3 -> x4, waiting for transfers between devices: 38 us -> 9.22 us  [branch(): return lambda x: lax.ppermute(x, LEAF, pairs)]
    ppermute x3 -> x4, starting transfers between devices: 41.6 us -> 38.4 us  [branch(): return lambda x: lax.ppermute(x, LEAF, pairs)]
    ppermute x2, waiting for transfers between devices: 2.74 us -> 0.85 us  [col_gather(): partner = lax.ppermute(chip, COLS, [(c, c ^ 1) for c in range(4)])]
    dot_general x2 -> x3, matrix products: 5.03 us -> 6.35 us  [the longest x1 2.34 us: body(): jnp.einsum('ip,kpn->ikn', inverse_perm, jnp.concatenate(upper_all), prefe...]
  transfers between devices with their start and end apart: 11 -> 12, of which waited for: 10 -> 11; matrix products, arithmetic and copies ran while one was open for 2% -> 3% of each run, Pallas kernels for 0% -> 0%
where the time goes in v10:
time: 151 us; the launch traced here: 149 us
  starting transfers between devices  72.1 us (48%)
  waiting for transfers between devices  49.5 us (33%)
  local copies, waits for them, and re-layouts  9.78 us (6%)
  matrix products  8.82 us (6%)
  other arithmetic  5.08 us (3%)
  loops' own time  2.95 us (2%)
    ppermute x4, starting transfers between devices, branch(): return lambda x: lax.ppermute(x, LEAF, pairs)  38.4 us
    ppermute x2, waiting for transfers between devices, col_gather(): remote = lax.ppermute(block, COLS, [(c, c ^ 2) for c in range(4)])  27.5 us
    ppermute x2, starting transfers between devices, col_gather(): remote = lax.ppermute(block, COLS, [(c, c ^ 2) for c in range(4)])  10.5 us
    ppermute x3, starting transfers between devices, body(): lax.ppermute(outgoing, COLS, [(c, c ^ distance) for c in range(col_count)])  10.2 us
    ppermute x2, starting transfers between devices, col_gather(): partner = lax.ppermute(chip, COLS, [(c, c ^ 1) for c in range(4)])  9.61 us
    ppermute x4, waiting for transfers between devices, branch(): return lambda x: lax.ppermute(x, LEAF, pairs)  9.22 us
    ppermute x1, waiting for transfers between devices, body(): lax.ppermute(other_rows.astype(jnp.bfloat16), LEAF, [(s, s ^ 1) for s in...  6.72 us
    ppermute x3, waiting for transfers between devices, body(): lax.ppermute(outgoing, COLS, [(c, c ^ distance) for c in range(col_count)])  5.2 us
  transfers between devices with their start and end apart: 12, of which 11 were waited for; matrix products, arithmetic and copies ran while one was open for 3% of the time, Pallas kernels for 0%

profile of v10, /device:TPU:1, one launch (start us, length us, event | category | flops | bytes accessed | tf_op | source)
XLA Modules:
  0.0 149.4 jit_solution(8986945803577655696)
XLA Ops:
  0.6 0.0 copy-start
  0.7 5.6 %collective-permute-start.63 = (bf16[1280,256]{1,0:T(8,128)(2,1)}, bf16[1280,256]{1,0:T(8,128)(2,1)S(1)}, u32[]{:S(2)}, u32[]{:S(2)}) collective-permute-start(bf16[1280,256]{1,0:T(8,128)(2,1)} %param.75), channel_id=1, source_target_pairs={{0,2},{1,3},{2,0},{3,1},{4,6},{5,7},{6,4},{7,5},{8,10},{9,11},{10,... | collective-permute-start | bytes 1966088 | tf_op jit(solution)/shard_map/ppermute | solution.py:24
  6.3 11.3 %collective-permute-done.63 = bf16[1280,256]{1,0:T(8,128)(2,1)S(1)} collective-permute-done((bf16[1280,256]{1,0:T(8,128)(2,1)}, bf16[1280,256]{1,0:T(8,128)(2,1)S(1)}, u32[]{:S(2)}, u32[]{:S(2)}) %collective-permute-start.63) | collective-permute-done | bytes 655392 | tf_op jit(solution)/shard_map/ppermute | solution.py:24
  17.6 1.2 pad_maximum_fusion.1
  18.8 6.5 %collective-permute-start.64 = (bf16[2,1280,256]{2,1,0:T(8,128)(2,1)S(1)}, bf16[2,1280,256]{2,1,0:T(8,128)(2,1)}, u32[]{:S(2)}, u32[]{:S(2)}) collective-permute-start(bf16[2,1280,256]{2,1,0:T(8,128)(2,1)S(1)} %pad_maximum_fusion.1), channel_id=1, source_target_pairs={{0,1},{1,0},{2,3},{3,2},{4,5},{5,4},{6,7},{7,6},{8,9},{9,8},{10,11... | collective-permute-start | bytes 3932168 | tf_op jit(solution)/shard_map/ppermute | solution.py:26
  25.3 0.1 broadcast_in_dim.247
  25.5 1.5 %fusion.2 = bf16[1280,320]{0,1:T(8,128)(2,1)S(1)} fusion(bf16[320,1280]{1,0:T(8,128)(2,1)S(1)} %copy-done, s32[1280]{0:T(1024)S(1)} %reduce), kind=kOutput, calls=%fused_computation.73 | convolution fusion | flops 1050624000 | bytes 1643520 | tf_op jit(solution)/shard_map/dot_general | solution.py:48
  27.1 0.4 convolution_convert_fusion
  27.4 0.0 copy-start.5
  27.5 0.6 collective-permute-done.64
  28.1 2.3 %fusion.3 = bf16[320,4,256]{2,0,1:T(8,128)(2,1)S(1)} fusion(bf16[2,1280,256]{2,1,0:T(8,128)(2,1)} %collective-permute-done.64, bf16[1,1280,256]{2,1,0:T(8,128)(2,1)S(1)} %bitcast.251, bf16[1,1280,256]{2,1,0:T(8,128)(2,1)S(1)} %bitcast.249, bf16[1280,320]{0,1:T(8,128)(2,1)S(1)} %fusion.2), kind=kOutput, calls=%fused_computation.74 | convolution fusion | flops 846725120 | bytes 4096000 | tf_op jit(solution)/shard_map/ip,kpn->ikn/dot_general | solution.py:56
  30.4 0.6 gather_fusion.1
  31.0 0.1 copy.18
  31.1 0.2 select_convert_fusion
  31.3 0.1 fusion.26
  31.4 4.9 %collective-permute-start.65 = (bf16[320,1152]{1,0:T(8,128)(2,1)S(1)}, bf16[320,1152]{1,0:T(8,128)(2,1)S(1)}, u32[]{:S(2)}, u32[]{:S(2)}) collective-permute-start(bf16[320,1152]{1,0:T(8,128)(2,1)S(1)} %get-tuple-element.745), channel_id=1, source_target_pairs={{0,2},{1,3},{2,0},{3,1},{4,6},{5,7},{6,4},{7,5},{8,10},{9,11},{10,... | collective-permute-start | bytes 2211848 | tf_op jit(solution)/shard_map/ppermute | solution.py:24
  36.3 16.2 %collective-permute-done.65 = bf16[320,1152]{1,0:T(8,128)(2,1)S(1)} collective-permute-done((bf16[320,1152]{1,0:T(8,128)(2,1)S(1)}, bf16[320,1152]{1,0:T(8,128)(2,1)S(1)}, u32[]{:S(2)}, u32[]{:S(2)}) %collective-permute-start.65) | collective-permute-done | bytes 737312 | tf_op jit(solution)/shard_map/ppermute | solution.py:24
  52.5 1.3 pad_maximum_fusion
  53.8 0.1 copy-done.1
  53.8 3.1 %collective-permute-start.66 = (bf16[2,320,1152]{2,1,0:T(8,128)(2,1)}, bf16[2,320,1152]{2,1,0:T(8,128)(2,1)}, u32[]{:S(2)}, u32[]{:S(2)}) collective-permute-start(bf16[2,320,1152]{2,1,0:T(8,128)(2,1)} %pad_maximum_fusion), channel_id=1, source_target_pairs={{0,1},{1,0},{2,3},{3,2},{4,5},{5,4},{6,7},{7,6},{8,9},{9,8},{10,11... | collective-permute-start | bytes 4423688 | tf_op jit(solution)/shard_map/ppermute | solution.py:26
  57.0 0.2 copy.13
  57.3 0.6 gather_fusion
  58.0 0.1 xor_xor_fusion
  58.0 1.9 %convolution_bitcast_fusion.1 = f32[256,1152]{1,0:T(8,128)S(1)} fusion(bf16[4,256,320]{1,2,0:T(8,128)(2,1)S(1)} %gather_fusion, pred[4]{0:T(512)(128)(4,1)S(1)} %get-tuple-element.742, bf16[1,320,1152]{2,1,0:T(8,128)(2,1)} %bitcast.243, bf16[1,320,1152]{2,1,0:T(8,128)(2,1)S(1)} %get-tuple-element.744), kind=kOutput, calls=%fused_computation.72 | convolution fusion | flops 380764160 | bytes 3309572 | tf_op jit(solution)/shard_map/rkp,kpn->rn/dot_general | solution.py:72
  59.9 0.2 collective-permute-done.66
  60.2 2.1 %convolution_bitcast_fusion = f32[256,1152]{1,0:T(8,128)S(1)} fusion(bf16[2,320,1152]{2,1,0:T(8,128)(2,1)} %collective-permute-done.66, bf16[4,256,320]{1,2,0:T(8,128)(2,1)S(1)} %gather_fusion, pred[4]{0:T(512)(128)(4,1)S(1)} %get-tuple-element.742), kind=kOutput, calls=%fused_computation.71 | convolution fusion | flops 377815040 | bytes 3309572 | tf_op jit(solution)/shard_map/rkp,kpn->rn/dot_general | solution.py:78
  62.3 0.1 add_negate_fusion
  62.5 3.4 %collective-permute-start.67 = (bf16[128,1152]{1,0:T(8,128)(2,1)S(1)}, bf16[128,1152]{1,0:T(8,128)(2,1)S(1)}, u32[]{:S(2)}, u32[]{:S(2)}) collective-permute-start(bf16[128,1152]{1,0:T(8,128)(2,1)S(1)} %dynamic-slice_convert_fusion), channel_id=1, source_target_pairs={{0,4},{4,0},{8,12},{12,8},{16,20},{20,16},{24,28},{28,24},{32,36},... | collective-permute-start | bytes 884744 | tf_op jit(solution)/shard_map/ppermute | solution.py:86
  65.9 0.1 fusion.16
  66.0 6.7 %collective-permute-done.67 = bf16[128,1152]{1,0:T(8,128)(2,1)S(1)} collective-permute-done((bf16[128,1152]{1,0:T(8,128)(2,1)S(1)}, bf16[128,1152]{1,0:T(8,128)(2,1)S(1)}, u32[]{:S(2)}, u32[]{:S(2)}) %collective-permute-start.67) | collective-permute-done | bytes 294944 | tf_op jit(solution)/shard_map/ppermute | solution.py:86
  72.7 0.1 add_convert_fusion.1
  72.8 3.0 %collective-permute-start.68 = (bf16[32,1152]{1,0:T(8,128)(2,1)S(1)}, bf16[32,1152]{1,0:T(8,128)(2,1)S(1)}, u32[]{:S(2)}, u32[]{:S(2)}) collective-permute-start(bf16[32,1152]{1,0:T(8,128)(2,1)S(1)} %get-tuple-element.749), channel_id=1, source_target_pairs={{0,1},{1,0},{2,3},{3,2},{4,5},{5,4},{6,7},{7,6},{8,9},{9,8},{10,11... | collective-permute-start | bytes 221192 | tf_op jit(solution)/shard_map/ppermute | solution.py:99
  75.9 4.8 %collective-permute-start.69 = (bf16[32,1152]{1,0:T(8,128)(2,1)S(1)}, bf16[32,1152]{1,0:T(8,128)(2,1)S(1)}, u32[]{:S(2)}, u32[]{:S(2)}) collective-permute-start(bf16[32,1152]{1,0:T(8,128)(2,1)S(1)} %get-tuple-element.748), channel_id=1, source_target_pairs={{0,2},{1,3},{2,0},{3,1},{4,6},{5,7},{6,4},{7,5},{8,10},{9,11},{10,... | collective-permute-start | bytes 221192 | tf_op jit(solution)/shard_map/ppermute | solution.py:99
  80.7 2.3 %collective-permute-start.70 = (bf16[32,1152]{1,0:T(8,128)(2,1)S(1)}, bf16[32,1152]{1,0:T(8,128)(2,1)S(1)}, u32[]{:S(2)}, u32[]{:S(2)}) collective-permute-start(bf16[32,1152]{1,0:T(8,128)(2,1)S(1)} %get-tuple-element.747), channel_id=1, source_target_pairs={{0,3},{1,2},{2,1},{3,0},{4,7},{5,6},{6,5},{7,4},{8,11},{9,10},{10,... | collective-permute-start | bytes 221192 | tf_op jit(solution)/shard_map/ppermute | solution.py:99
  83.1 0.1 collective-permute-done.69
  83.2 5.1 %collective-permute-done.70 = bf16[32,1152]{1,0:T(8,128)(2,1)S(1)} collective-permute-done((bf16[32,1152]{1,0:T(8,128)(2,1)S(1)}, bf16[32,1152]{1,0:T(8,128)(2,1)S(1)}, u32[]{:S(2)}, u32[]{:S(2)}) %collective-permute-start.70) | collective-permute-done | bytes 73760 | tf_op jit(solution)/shard_map/ppermute | solution.py:99
  88.3 0.6 gather_fusion.2
  88.9 0.1 broadcast_select_fusion.1
  89.0 56.6 %while.13 = (s32[]{:T(128)}, bf16[4,32,1152]{2,1,0:T(8,128)(2,1)S(1)}, s32[4]{0:T(128)S(1)}, bf16[4,32,1152]{2,1,0:T(8,128)(2,1)S(1)}, s32[]{:T(128)}, /*index=5*/s32[1]{0:T(128)}, s32[1]{0:T(128)}) while((s32[]{:T(128)}, bf16[4,32,1152]{2,1,0:T(8,128)(2,1)S(1)}, s32[4]{0:T(128)S(1)}, bf16[4,32,1152]{2,1,0:T(8,128)(2,1)S(1)}, s32[]{:T(128)}, ...), condition=%wide.region_65.66_spmd, body=%wide.region_0.65_spmd.sunk | while | flops 3 | bytes 590001 | solution.py:114
  89.0 0.6 dynamic_slice.365
  90.3 17.7 %conditional.2 = (bf16[1,32,1152]{2,1,0:T(8,128)(2,1)}) conditional(s32[]{:T(128)} %bitcast.239, (bf16[4,32,1152]{2,1,0:T(8,128)(2,1)S(1)}, s32[]{:T(128)}) %tuple.365, (bf16[4,32,1152]{2,1,0:T(8,128)(2,1)S(1)}, s32[]{:T(128)}) %tuple.365, (bf16[4,32,1152]{2,1,0:T(8,128)(2,1)S(1)}, s32[]{:T(128)}) %tuple.365, ...), branch_computations={%region_1.1_spmd, %region_2.2_spmd, %region_3.3_spmd, %region_4.4_... | conditional | bytes 442420 | solution.py:111
  90.3 14.6 %collective-permute-start.19 = (bf16[32,1152]{1,0:T(8,128)(2,1)S(1)}, bf16[32,1152]{1,0:T(8,128)(2,1)}, u32[]{:S(2)}, u32[]{:S(2)}) collective-permute-start(bf16[32,1152]{1,0:T(8,128)(2,1)S(1)} %dynamic-slice_bitcast_fusion.19), channel_id=1, source_target_pairs={{0,160},{4,164},{8,168},{12,172},{16,176},{20,180},{24,184},{28,18... | collective-permute-start | bytes 221192 | tf_op jit(solution)/shard_map/while/body/eval_jaxpr/cond/branch_20_fun/ppermute | solution.py:18
  104.9 3.0 %collective-permute-done.19 = bf16[32,1152]{1,0:T(8,128)(2,1)} collective-permute-done((bf16[32,1152]{1,0:T(8,128)(2,1)S(1)}, bf16[32,1152]{1,0:T(8,128)(2,1)}, u32[]{:S(2)}, u32[]{:S(2)}) %collective-permute-start.19) | collective-permute-done | bytes 73760 | tf_op jit(solution)/shard_map/while/body/eval_jaxpr/cond/branch_20_fun/ppermute | solution.py:18
  107.9 0.9 constant_dynamic-update-slice_fusion.2
  108.8 0.6 dynamic_slice.365
  110.1 7.2 %conditional.2 = (bf16[1,32,1152]{2,1,0:T(8,128)(2,1)}) conditional(s32[]{:T(128)} %bitcast.239, (bf16[4,32,1152]{2,1,0:T(8,128)(2,1)S(1)}, s32[]{:T(128)}) %tuple.365, (bf16[4,32,1152]{2,1,0:T(8,128)(2,1)S(1)}, s32[]{:T(128)}) %tuple.365, (bf16[4,32,1152]{2,1,0:T(8,128)(2,1)S(1)}, s32[]{:T(128)}) %tuple.365, ...), branch_computations={%region_1.1_spmd, %region_2.2_spmd, %region_3.3_spmd, %region_4.4_... | conditional | bytes 442420 | solution.py:111
  110.2 4.6 %collective-permute-start.5 = (bf16[32,1152]{1,0:T(8,128)(2,1)S(1)}, bf16[32,1152]{1,0:T(8,128)(2,1)}, u32[]{:S(2)}, u32[]{:S(2)}) collective-permute-start(bf16[32,1152]{1,0:T(8,128)(2,1)S(1)} %dynamic-slice_bitcast_fusion.5), channel_id=1, source_target_pairs={{0,48},{4,52},{8,56},{12,60},{16,32},{20,36},{24,40},{28,44},{32,1... | collective-permute-start | bytes 221192 | tf_op jit(solution)/shard_map/while/body/eval_jaxpr/cond/branch_6_fun/ppermute | solution.py:18
  114.7 2.5 %collective-permute-done.5 = bf16[32,1152]{1,0:T(8,128)(2,1)} collective-permute-done((bf16[32,1152]{1,0:T(8,128)(2,1)S(1)}, bf16[32,1152]{1,0:T(8,128)(2,1)}, u32[]{:S(2)}, u32[]{:S(2)}) %collective-permute-start.5) | collective-permute-done | bytes 73760 | tf_op jit(solution)/shard_map/while/body/eval_jaxpr/cond/branch_6_fun/ppermute | solution.py:18
  117.3 0.9 constant_dynamic-update-slice_fusion.2
  118.2 0.6 dynamic_slice.365
  119.4 12.7 %conditional.2 = (bf16[1,32,1152]{2,1,0:T(8,128)(2,1)}) conditional(s32[]{:T(128)} %bitcast.239, (bf16[4,32,1152]{2,1,0:T(8,128)(2,1)S(1)}, s32[]{:T(128)}) %tuple.365, (bf16[4,32,1152]{2,1,0:T(8,128)(2,1)S(1)}, s32[]{:T(128)}) %tuple.365, (bf16[4,32,1152]{2,1,0:T(8,128)(2,1)S(1)}, s32[]{:T(128)}) %tuple.365, ...), branch_computations={%region_1.1_spmd, %region_2.2_spmd, %region_3.3_spmd, %region_4.4_... | conditional | bytes 442420 | solution.py:111
  119.5 10.7 %collective-permute-start.30 = (bf16[32,1152]{1,0:T(8,128)(2,1)S(1)}, bf16[32,1152]{1,0:T(8,128)(2,1)}, u32[]{:S(2)}, u32[]{:S(2)}) collective-permute-start(bf16[32,1152]{1,0:T(8,128)(2,1)S(1)} %dynamic-slice_bitcast_fusion.30), channel_id=1, source_target_pairs={{0,248},{4,252},{8,240},{12,244},{16,232},{20,236},{24,224},{28,22... | collective-permute-start | bytes 221192 | tf_op jit(solution)/shard_map/while/body/eval_jaxpr/cond/branch_31_fun/ppermute | solution.py:18
  130.3 1.8 %collective-permute-done.30 = bf16[32,1152]{1,0:T(8,128)(2,1)} collective-permute-done((bf16[32,1152]{1,0:T(8,128)(2,1)S(1)}, bf16[32,1152]{1,0:T(8,128)(2,1)}, u32[]{:S(2)}, u32[]{:S(2)}) %collective-permute-start.30) | collective-permute-done | bytes 73760 | tf_op jit(solution)/shard_map/while/body/eval_jaxpr/cond/branch_31_fun/ppermute | solution.py:18
  132.1 0.9 constant_dynamic-update-slice_fusion.2
  133.0 0.6 dynamic_slice.365
  134.2 10.5 %conditional.2 = (bf16[1,32,1152]{2,1,0:T(8,128)(2,1)}) conditional(s32[]{:T(128)} %bitcast.239, (bf16[4,32,1152]{2,1,0:T(8,128)(2,1)S(1)}, s32[]{:T(128)}) %tuple.365, (bf16[4,32,1152]{2,1,0:T(8,128)(2,1)S(1)}, s32[]{:T(128)}) %tuple.365, (bf16[4,32,1152]{2,1,0:T(8,128)(2,1)S(1)}, s32[]{:T(128)}) %tuple.365, ...), branch_computations={%region_1.1_spmd, %region_2.2_spmd, %region_3.3_spmd, %region_4.4_... | conditional | bytes 442420 | solution.py:111
  134.3 8.6 %collective-permute-start.1 = (bf16[32,1152]{1,0:T(8,128)(2,1)S(1)}, bf16[32,1152]{1,0:T(8,128)(2,1)}, u32[]{:S(2)}, u32[]{:S(2)}) collective-permute-start(bf16[32,1152]{1,0:T(8,128)(2,1)S(1)} %dynamic-slice_bitcast_fusion.1), channel_id=1, source_target_pairs={{0,16},{4,20},{8,24},{12,28},{16,0},{20,4},{24,8},{28,12},{32,48},... | collective-permute-start | bytes 221192 | tf_op jit(solution)/shard_map/while/body/eval_jaxpr/cond/branch_2_fun/ppermute | solution.py:18
  142.9 1.8 %collective-permute-done.1 = bf16[32,1152]{1,0:T(8,128)(2,1)} collective-permute-done((bf16[32,1152]{1,0:T(8,128)(2,1)S(1)}, bf16[32,1152]{1,0:T(8,128)(2,1)}, u32[]{:S(2)}, u32[]{:S(2)}) %collective-permute-start.1) | collective-permute-done | bytes 73760 | tf_op jit(solution)/shard_map/while/body/eval_jaxpr/cond/branch_2_fun/ppermute | solution.py:18
  144.7 0.9 constant_dynamic-update-slice_fusion.2
  145.7 0.2 reshape.203
  145.9 0.6 fusion.12
  146.4 1.2 copy.19
  147.7 1.1 add_convert_fusion
  148.8 0.6 convert_add_fusion
  (40 shorter events, 0.4 us)
Async XLA Ops:
  0.6 24.8 %copy-start = (bf16[320,1280]{1,0:T(8,128)(2,1)S(1)}, bf16[320,1280]{1,0:T(8,128)(2,1)}, u32[]{:S(2)}) copy-start(bf16[320,1280]{1,0:T(8,128)(2,1)} %param.77) | copy-start | bytes 2457604
  0.6 24.8 %copy-start.8 = (s32[1,1280]{1,0:T(1,128)S(1)}, s32[1,1280]{1,0:T(1,128)}, u32[]{:S(2)}) copy-start(s32[1,1280]{1,0:T(1,128)} %param.78) | copy-start | bytes 15364
  0.7 16.9 %collective-permute-start.63 = (bf16[1280,256]{1,0:T(8,128)(2,1)}, bf16[1280,256]{1,0:T(8,128)(2,1)S(1)}, u32[]{:S(2)}, u32[]{:S(2)}) collective-permute-start(bf16[1280,256]{1,0:T(8,128)(2,1)} %param.75), channel_id=1, source_target_pairs={{0,2},{1,3},{2,0},{3,1},{4,6},{5,7},{6,4},{7,5},{8,10},{9,11},{10,... | collective-permute-start | bytes 1966088 | tf_op jit(solution)/shard_map/ppermute | solution.py:24
  18.8 9.3 %collective-permute-start.64 = (bf16[2,1280,256]{2,1,0:T(8,128)(2,1)S(1)}, bf16[2,1280,256]{2,1,0:T(8,128)(2,1)}, u32[]{:S(2)}, u32[]{:S(2)}) collective-permute-start(bf16[2,1280,256]{2,1,0:T(8,128)(2,1)S(1)} %pad_maximum_fusion.1), channel_id=1, source_target_pairs={{0,1},{1,0},{2,3},{3,2},{4,5},{5,4},{6,7},{7,6},{8,9},{9,8},{10,11... | collective-permute-start | bytes 3932168 | tf_op jit(solution)/shard_map/ppermute | solution.py:26
  25.5 1.6 %copy-start.6 = (bf16[1280,128]{1,0:T(8,128)(2,1)S(1)}, bf16[1280,128]{1,0:T(8,128)(2,1)}, u32[]{:S(2)}) copy-start(bf16[1280,128]{1,0:T(8,128)(2,1)} %param.79) | copy-start | bytes 983044
  25.5 2.6 %copy-start.3 = (bf16[1280,256]{1,0:T(8,128)(2,1)S(1)}, bf16[1280,256]{1,0:T(8,128)(2,1)}, u32[]{:S(2)}) copy-start(bf16[1280,256]{1,0:T(8,128)(2,1)} %param.75) | copy-start | bytes 1966084
  27.4 3.8 %copy-start.5 = (bf16[320,128]{1,0:T(8,128)(2,1)}, bf16[320,128]{1,0:T(8,128)(2,1)S(1)}, u32[]{:S(2)}) copy-start(bf16[320,128]{1,0:T(8,128)(2,1)S(1)} %convolution_convert_fusion) | copy-start | bytes 245764
  31.4 21.1 %collective-permute-start.65 = (bf16[320,1152]{1,0:T(8,128)(2,1)S(1)}, bf16[320,1152]{1,0:T(8,128)(2,1)S(1)}, u32[]{:S(2)}, u32[]{:S(2)}) collective-permute-start(bf16[320,1152]{1,0:T(8,128)(2,1)S(1)} %get-tuple-element.745), channel_id=1, source_target_pairs={{0,2},{1,3},{2,0},{3,1},{4,6},{5,7},{6,4},{7,5},{8,10},{9,11},{10,... | collective-permute-start | bytes 2211848 | tf_op jit(solution)/shard_map/ppermute | solution.py:24
  52.5 1.3 copy-start.1
  52.5 4.5 %copy-start.4 = (bf16[256,1280]{1,0:T(8,128)(2,1)S(1)}, bf16[256,1280]{1,0:T(8,128)(2,1)}, u32[]{:S(2)}) copy-start(bf16[256,1280]{1,0:T(8,128)(2,1)} %param.76) | copy-start | bytes 1966084
  52.5 4.8 %copy-start.9 = (s32[4]{0:T(128)S(1)}, s32[4]{0:T(128)}, u32[]{:S(2)}) copy-start(s32[4]{0:T(128)} %constant.288.clone) | copy-start | bytes 52
  53.8 6.3 %collective-permute-start.66 = (bf16[2,320,1152]{2,1,0:T(8,128)(2,1)}, bf16[2,320,1152]{2,1,0:T(8,128)(2,1)}, u32[]{:S(2)}, u32[]{:S(2)}) collective-permute-start(bf16[2,320,1152]{2,1,0:T(8,128)(2,1)} %pad_maximum_fusion), channel_id=1, source_target_pairs={{0,1},{1,0},{2,3},{3,2},{4,5},{5,4},{6,7},{7,6},{8,9},{9,8},{10,11... | collective-permute-start | bytes 4423688 | tf_op jit(solution)/shard_map/ppermute | solution.py:26
  57.0 1.0 copy-start.10
  62.5 10.2 %collective-permute-start.67 = (bf16[128,1152]{1,0:T(8,128)(2,1)S(1)}, bf16[128,1152]{1,0:T(8,128)(2,1)S(1)}, u32[]{:S(2)}, u32[]{:S(2)}) collective-permute-start(bf16[128,1152]{1,0:T(8,128)(2,1)S(1)} %dynamic-slice_convert_fusion), channel_id=1, source_target_pairs={{0,4},{4,0},{8,12},{12,8},{16,20},{20,16},{24,28},{28,24},{32,36},... | collective-permute-start | bytes 884744 | tf_op jit(solution)/shard_map/ppermute | solution.py:86
  72.8 10.2 %collective-permute-start.68 = (bf16[32,1152]{1,0:T(8,128)(2,1)S(1)}, bf16[32,1152]{1,0:T(8,128)(2,1)S(1)}, u32[]{:S(2)}, u32[]{:S(2)}) collective-permute-start(bf16[32,1152]{1,0:T(8,128)(2,1)S(1)} %get-tuple-element.749), channel_id=1, source_target_pairs={{0,1},{1,0},{2,3},{3,2},{4,5},{5,4},{6,7},{7,6},{8,9},{9,8},{10,11... | collective-permute-start | bytes 221192 | tf_op jit(solution)/shard_map/ppermute | solution.py:99
  75.9 7.3 %collective-permute-start.69 = (bf16[32,1152]{1,0:T(8,128)(2,1)S(1)}, bf16[32,1152]{1,0:T(8,128)(2,1)S(1)}, u32[]{:S(2)}, u32[]{:S(2)}) collective-permute-start(bf16[32,1152]{1,0:T(8,128)(2,1)S(1)} %get-tuple-element.748), channel_id=1, source_target_pairs={{0,2},{1,3},{2,0},{3,1},{4,6},{5,7},{6,4},{7,5},{8,10},{9,11},{10,... | collective-permute-start | bytes 221192 | tf_op jit(solution)/shard_map/ppermute | solution.py:99
  80.7 7.6 %collective-permute-start.70 = (bf16[32,1152]{1,0:T(8,128)(2,1)S(1)}, bf16[32,1152]{1,0:T(8,128)(2,1)S(1)}, u32[]{:S(2)}, u32[]{:S(2)}) collective-permute-start(bf16[32,1152]{1,0:T(8,128)(2,1)S(1)} %get-tuple-element.747), channel_id=1, source_target_pairs={{0,3},{1,2},{2,1},{3,0},{4,7},{5,6},{6,5},{7,4},{8,11},{9,10},{10,... | collective-permute-start | bytes 221192 | tf_op jit(solution)/shard_map/ppermute | solution.py:99
  90.3 17.6 %collective-permute-start.19 = (bf16[32,1152]{1,0:T(8,128)(2,1)S(1)}, bf16[32,1152]{1,0:T(8,128)(2,1)}, u32[]{:S(2)}, u32[]{:S(2)}) collective-permute-start(bf16[32,1152]{1,0:T(8,128)(2,1)S(1)} %dynamic-slice_bitcast_fusion.19), channel_id=1, source_target_pairs={{0,160},{4,164},{8,168},{12,172},{16,176},{20,180},{24,184},{28,18... | collective-permute-start | bytes 221192 | tf_op jit(solution)/shard_map/while/body/eval_jaxpr/cond/branch_20_fun/ppermute | solution.py:18
  110.2 7.1 %collective-permute-start.5 = (bf16[32,1152]{1,0:T(8,128)(2,1)S(1)}, bf16[32,1152]{1,0:T(8,128)(2,1)}, u32[]{:S(2)}, u32[]{:S(2)}) collective-permute-start(bf16[32,1152]{1,0:T(8,128)(2,1)S(1)} %dynamic-slice_bitcast_fusion.5), channel_id=1, source_target_pairs={{0,48},{4,52},{8,56},{12,60},{16,32},{20,36},{24,40},{28,44},{32,1... | collective-permute-start | bytes 221192 | tf_op jit(solution)/shard_map/while/body/eval_jaxpr/cond/branch_6_fun/ppermute | solution.py:18
  119.5 12.6 %collective-permute-start.30 = (bf16[32,1152]{1,0:T(8,128)(2,1)S(1)}, bf16[32,1152]{1,0:T(8,128)(2,1)}, u32[]{:S(2)}, u32[]{:S(2)}) collective-permute-start(bf16[32,1152]{1,0:T(8,128)(2,1)S(1)} %dynamic-slice_bitcast_fusion.30), channel_id=1, source_target_pairs={{0,248},{4,252},{8,240},{12,244},{16,232},{20,236},{24,224},{28,22... | collective-permute-start | bytes 221192 | tf_op jit(solution)/shard_map/while/body/eval_jaxpr/cond/branch_31_fun/ppermute | solution.py:18
  134.3 10.4 %collective-permute-start.1 = (bf16[32,1152]{1,0:T(8,128)(2,1)S(1)}, bf16[32,1152]{1,0:T(8,128)(2,1)}, u32[]{:S(2)}, u32[]{:S(2)}) collective-permute-start(bf16[32,1152]{1,0:T(8,128)(2,1)S(1)} %dynamic-slice_bitcast_fusion.1), channel_id=1, source_target_pairs={{0,16},{4,20},{8,24},{12,28},{16,0},{20,4},{24,8},{28,12},{32,48},... | collective-permute-start | bytes 221192 | tf_op jit(solution)/shard_map/while/body/eval_jaxpr/cond/branch_2_fun/ppermute | solution.py:18
  146.4 1.2 copy-start.2
  147.7 1.2 copy-start.7

commit v11 on v10

--- a/solution.py
+++ b/solution.py
@@ -64,17 +64,20 @@
     ).astype(jnp.bfloat16)
     coupled_width = eliminated.shape[1] * eliminated.shape[2]
     rows_out = jnp.concatenate([eliminated.reshape(share, coupled_width), forward], axis=1)
-    rows_all = col_gather(rows_out)
     lower_rows = lower_block.shape[0]
     source_blocks = jnp.bitwise_xor(jnp.array([0, 2, 1, 3], jnp.int32), col_index)
     lower_parts = jnp.take(lower_block.reshape(lower_rows, 4, share), source_blocks, axis=1)
-    chip_rows, partner_rows = rows_all
-    chip_part = jnp.einsum(
-        "rkp,kpn->rn", lower_parts[:, :2], chip_rows, preferred_element_type=jnp.float32
+    rows_remote = lax.ppermute(rows_out, COLS, [(c, c ^ 2) for c in range(4)])
+    own_part = jnp.dot(lower_parts[:, 0], rows_out, preferred_element_type=jnp.float32)
+    own_part, rows_remote = lax.optimization_barrier((own_part, rows_remote))
+    partner_rows = lax.ppermute(
+        jnp.stack([rows_out, rows_remote]), COLS, [(c, c ^ 1) for c in range(4)]
     )
-    chip_part, partner_rows = lax.optimization_barrier((chip_part, partner_rows))
+    remote_part = jnp.dot(lower_parts[:, 1], rows_remote, preferred_element_type=jnp.float32)
+    remote_part, partner_rows = lax.optimization_barrier((remote_part, partner_rows))
     combined = -(
-        chip_part
+        own_part
+        + remote_part
         + jnp.einsum(
             "rkp,kpn->rn", lower_parts[:, 2:], partner_rows, preferred_element_type=jnp.float32
         )

time: 151 us -> 194 us (1.28)
  waiting for transfers between devices: 49.5 us -> 88.8 us
  starting transfers between devices: 72.1 us -> 74.9 us
    ppermute x4, waiting for transfers between devices: 9.22 us -> 48.8 us  [branch(): return lambda x: lax.ppermute(x, LEAF, pairs)]
    ppermute x2 -> x1, waiting for transfers between devices: 27.5 us -> 11.3 us  [col_gather(): remote = lax.ppermute(block, COLS, [(c, c ^ 2) for c in range(4)])]
    ppermute x0 -> x2, waiting for transfers between devices: none -> 16.2 us  [the longest x1 13.7 us: body(): rows_remote = lax.ppermute(rows_out, COLS, [(c, c ^ 2) for c in range(4)])]
    ppermute x0 -> x2, starting transfers between devices: none -> 7.95 us  [the longest x1 4.85 us: body(): rows_remote = lax.ppermute(rows_out, COLS, [(c, c ^ 2) for c in range(4)])]
    ppermute x2 -> x1, starting transfers between devices: 10.5 us -> 5.62 us  [col_gather(): remote = lax.ppermute(block, COLS, [(c, c ^ 2) for c in range(4)])]
    ppermute x2 -> x1, starting transfers between devices: 9.61 us -> 6.51 us  [col_gather(): partner = lax.ppermute(chip, COLS, [(c, c ^ 1) for c in range(4)])]
    ppermute x4, starting transfers between devices: 38.4 us -> 41 us  [branch(): return lambda x: lax.ppermute(x, LEAF, pairs)]
    another operation x0 -> x2, other arithmetic: none -> 2.48 us  [body(): jnp.stack([rows_out, rows_remote])]
where the time goes in v11:
time: 194 us; the launch traced here: 193 us
  waiting for transfers between devices  88.8 us (46%)
  starting transfers between devices  74.9 us (39%)
  local copies, waits for them, and re-layouts  9.74 us (5%)
  matrix products  9.09 us (5%)
  other arithmetic  6.18 us (3%)
  loops' own time  2.97 us (2%)
    ppermute x4, waiting for transfers between devices, branch(): return lambda x: lax.ppermute(x, LEAF, pairs)  48.8 us
    ppermute x4, starting transfers between devices, branch(): return lambda x: lax.ppermute(x, LEAF, pairs)  41 us
    ppermute x1, waiting for transfers between devices, body(): rows_remote = lax.ppermute(rows_out, COLS, [(c, c ^ 2) for c in range(4)])  13.7 us
    ppermute x1, waiting for transfers between devices, col_gather(): remote = lax.ppermute(block, COLS, [(c, c ^ 2) for c in range(4)])  11.3 us
    ppermute x3, starting transfers between devices, body(): lax.ppermute(outgoing, COLS, [(c, c ^ distance) for c in range(col_count)])  10.3 us
    ppermute x1, waiting for transfers between devices, body(): lax.ppermute(other_rows.astype(jnp.bfloat16), LEAF, [(s, s ^ 1) for s in...  6.72 us
    ppermute x1, starting transfers between devices, col_gather(): partner = lax.ppermute(chip, COLS, [(c, c ^ 1) for c in range(4)])  6.51 us
    ppermute x1, starting transfers between devices, col_gather(): remote = lax.ppermute(block, COLS, [(c, c ^ 2) for c in range(4)])  5.62 us
  transfers between devices with their start and end apart: 12, of which 11 were waited for; matrix products, arithmetic and copies ran while one was open for 3% of the time, Pallas kernels for 0%

profile of v11, /device:TPU:1, one launch (start us, length us, event | category | flops | bytes accessed | tf_op | source)
XLA Modules:
  0.0 192.8 jit_solution(11532808931564516616)
XLA Ops:
  0.6 0.0 copy-start
  0.6 0.0 copy-start.12
  0.7 5.6 %collective-permute-start.63 = (bf16[1280,256]{1,0:T(8,128)(2,1)}, bf16[1280,256]{1,0:T(8,128)(2,1)S(1)}, u32[]{:S(2)}, u32[]{:S(2)}) collective-permute-start(bf16[1280,256]{1,0:T(8,128)(2,1)} %param.75), channel_id=1, source_target_pairs={{0,2},{1,3},{2,0},{3,1},{4,6},{5,7},{6,4},{7,5},{8,10},{9,11},{10,... | collective-permute-start | bytes 1966088 | tf_op jit(solution)/shard_map/ppermute | solution.py:24
  6.3 11.3 %collective-permute-done.63 = bf16[1280,256]{1,0:T(8,128)(2,1)S(1)} collective-permute-done((bf16[1280,256]{1,0:T(8,128)(2,1)}, bf16[1280,256]{1,0:T(8,128)(2,1)S(1)}, u32[]{:S(2)}, u32[]{:S(2)}) %collective-permute-start.63) | collective-permute-done | bytes 655392 | tf_op jit(solution)/shard_map/ppermute | solution.py:24
  17.6 1.2 pad_maximum_fusion.1
  18.8 6.5 %collective-permute-start.64 = (bf16[2,1280,256]{2,1,0:T(8,128)(2,1)S(1)}, bf16[2,1280,256]{2,1,0:T(8,128)(2,1)}, u32[]{:S(2)}, u32[]{:S(2)}) collective-permute-start(bf16[2,1280,256]{2,1,0:T(8,128)(2,1)S(1)} %pad_maximum_fusion.1), channel_id=1, source_target_pairs={{0,1},{1,0},{2,3},{3,2},{4,5},{5,4},{6,7},{7,6},{8,9},{9,8},{10,11... | collective-permute-start | bytes 3932168 | tf_op jit(solution)/shard_map/ppermute | solution.py:26
  25.3 0.1 broadcast_in_dim.247
  25.5 1.5 fusion.2
  27.1 0.4 convolution_convert_fusion
  27.5 0.6 collective-permute-done.64
  28.1 2.3 %fusion.3 = bf16[320,4,256]{2,0,1:T(8,128)(2,1)S(1)} fusion(bf16[2,1280,256]{2,1,0:T(8,128)(2,1)} %collective-permute-done.64, bf16[1,1280,256]{2,1,0:T(8,128)(2,1)S(1)} %bitcast.253, bf16[1,1280,256]{2,1,0:T(8,128)(2,1)S(1)} %bitcast.251, bf16[1280,320]{0,1:T(8,128)(2,1)S(1)} %fusion.2), kind=kOutput, calls=%fused_computation.73 | convolution fusion | flops 846725120 | bytes 4096000 | tf_op jit(solution)/shard_map/ip,kpn->ikn/dot_general | solution.py:56
  30.4 0.6 gather_fusion.1
  31.0 0.1 copy.18
  31.1 0.1 select_convert_fusion
  31.3 1.2 fusion.24
  32.5 4.9 %collective-permute-start.65 = (bf16[320,1152]{1,0:T(8,128)(2,1)}, bf16[320,1152]{1,0:T(8,128)(2,1)S(1)}, u32[]{:S(2)}, u32[]{:S(2)}) collective-permute-start(bf16[320,1152]{1,0:T(8,128)(2,1)} %get-tuple-element.749), channel_id=1, source_target_pairs={{0,2},{1,3},{2,0},{3,1},{4,6},{5,7},{6,4},{7,5},{8,10},{9,11},{10,... | collective-permute-start | bytes 2211848 | tf_op jit(solution)/shard_map/ppermute | solution.py:70
  37.4 0.2 copy.13
  37.6 0.6 gather_fusion
  38.2 0.1 select_bitcast_fusion
  38.4 1.7 fusion.14
  40.1 13.7 %collective-permute-done.65 = bf16[320,1152]{1,0:T(8,128)(2,1)S(1)} collective-permute-done((bf16[320,1152]{1,0:T(8,128)(2,1)}, bf16[320,1152]{1,0:T(8,128)(2,1)S(1)}, u32[]{:S(2)}, u32[]{:S(2)}) %collective-permute-start.65) | collective-permute-done | bytes 737312 | tf_op jit(solution)/shard_map/ppermute | solution.py:70
  53.8 1.3 pad_maximum_fusion
  55.1 3.1 %collective-permute-start.66 = (bf16[2,320,1152]{2,1,0:T(8,128)(2,1)}, bf16[2,320,1152]{2,1,0:T(8,128)(2,1)}, u32[]{:S(2)}, u32[]{:S(2)}) collective-permute-start(bf16[2,320,1152]{2,1,0:T(8,128)(2,1)} %pad_maximum_fusion), channel_id=1, source_target_pairs={{0,1},{1,0},{2,3},{3,2},{4,5},{5,4},{6,7},{7,6},{8,9},{9,8},{10,11... | collective-permute-start | bytes 4423688 | tf_op jit(solution)/shard_map/ppermute | solution.py:73
  58.3 0.1 xor_xor_fusion
  58.4 0.5 fusion.13
  58.9 2.5 %collective-permute-done.66 = bf16[2,320,1152]{2,1,0:T(8,128)(2,1)} collective-permute-done((bf16[2,320,1152]{2,1,0:T(8,128)(2,1)}, bf16[2,320,1152]{2,1,0:T(8,128)(2,1)}, u32[]{:S(2)}, u32[]{:S(2)}) %collective-permute-start.66) | collective-permute-done | bytes 1474592 | tf_op jit(solution)/shard_map/ppermute | solution.py:73
  61.4 2.1 %add_negate_fusion = f32[256,1152]{1,0:T(8,128)S(1)} fusion(f32[256,1152]{1,0:T(8,128)S(1)} %fusion.14, f32[256,1152]{1,0:T(8,128)S(1)} %fusion.13, bf16[256,4,320]{0,2,1:T(8,128)(2,1)S(1)} %copy-done.3, bf16[2,320,1152]{2,1,0:T(8,128)(2,1)} %collective-permute-done.66), kind=kOutput, calls=%fused_computation.83 | convolution fusion | flops 378372096 | bytes 5668864 | tf_op jit(solution)/shard_map/rkp,kpn->rn/dot_general | solution.py:81
  63.5 3.4 %collective-permute-start.67 = (bf16[128,1152]{1,0:T(8,128)(2,1)S(1)}, bf16[128,1152]{1,0:T(8,128)(2,1)S(1)}, u32[]{:S(2)}, u32[]{:S(2)}) collective-permute-start(bf16[128,1152]{1,0:T(8,128)(2,1)S(1)} %dynamic-slice_convert_fusion), channel_id=1, source_target_pairs={{0,4},{4,0},{8,12},{12,8},{16,20},{20,16},{24,28},{28,24},{32,36},... | collective-permute-start | bytes 884744 | tf_op jit(solution)/shard_map/ppermute | solution.py:89
  67.0 0.1 fusion.16
  67.0 6.7 %collective-permute-done.67 = bf16[128,1152]{1,0:T(8,128)(2,1)S(1)} collective-permute-done((bf16[128,1152]{1,0:T(8,128)(2,1)S(1)}, bf16[128,1152]{1,0:T(8,128)(2,1)S(1)}, u32[]{:S(2)}, u32[]{:S(2)}) %collective-permute-start.67) | collective-permute-done | bytes 294944 | tf_op jit(solution)/shard_map/ppermute | solution.py:89
  73.8 0.1 add_convert_fusion.1
  73.9 3.2 %collective-permute-start.68 = (bf16[32,1152]{1,0:T(8,128)(2,1)S(1)}, bf16[32,1152]{1,0:T(8,128)(2,1)S(1)}, u32[]{:S(2)}, u32[]{:S(2)}) collective-permute-start(bf16[32,1152]{1,0:T(8,128)(2,1)S(1)} %get-tuple-element.753), channel_id=1, source_target_pairs={{0,1},{1,0},{2,3},{3,2},{4,5},{5,4},{6,7},{7,6},{8,9},{9,8},{10,11... | collective-permute-start | bytes 221192 | tf_op jit(solution)/shard_map/ppermute | solution.py:102
  77.1 4.8 %collective-permute-start.69 = (bf16[32,1152]{1,0:T(8,128)(2,1)S(1)}, bf16[32,1152]{1,0:T(8,128)(2,1)S(1)}, u32[]{:S(2)}, u32[]{:S(2)}) collective-permute-start(bf16[32,1152]{1,0:T(8,128)(2,1)S(1)} %get-tuple-element.752), channel_id=1, source_target_pairs={{0,2},{1,3},{2,0},{3,1},{4,6},{5,7},{6,4},{7,5},{8,10},{9,11},{10,... | collective-permute-start | bytes 221192 | tf_op jit(solution)/shard_map/ppermute | solution.py:102
  81.9 2.3 %collective-permute-start.70 = (bf16[32,1152]{1,0:T(8,128)(2,1)S(1)}, bf16[32,1152]{1,0:T(8,128)(2,1)S(1)}, u32[]{:S(2)}, u32[]{:S(2)}) collective-permute-start(bf16[32,1152]{1,0:T(8,128)(2,1)S(1)} %get-tuple-element.751), channel_id=1, source_target_pairs={{0,3},{1,2},{2,1},{3,0},{4,7},{5,6},{6,5},{7,4},{8,11},{9,10},{10,... | collective-permute-start | bytes 221192 | tf_op jit(solution)/shard_map/ppermute | solution.py:102
  84.2 0.1 collective-permute-done.69
  84.3 5.1 %collective-permute-done.70 = bf16[32,1152]{1,0:T(8,128)(2,1)S(1)} collective-permute-done((bf16[32,1152]{1,0:T(8,128)(2,1)S(1)}, bf16[32,1152]{1,0:T(8,128)(2,1)S(1)}, u32[]{:S(2)}, u32[]{:S(2)}) %collective-permute-start.70) | collective-permute-done | bytes 73760 | tf_op jit(solution)/shard_map/ppermute | solution.py:102
  89.5 0.6 gather_fusion.2
  90.1 0.1 broadcast_select_fusion
  90.2 98.8 %while.13 = (s32[]{:T(128)}, bf16[4,32,1152]{2,1,0:T(8,128)(2,1)S(1)}, s32[4]{0:T(128)S(1)}, bf16[4,32,1152]{2,1,0:T(8,128)(2,1)S(1)}, s32[]{:T(128)}, /*index=5*/s32[1]{0:T(128)}, s32[1]{0:T(128)}) while((s32[]{:T(128)}, bf16[4,32,1152]{2,1,0:T(8,128)(2,1)S(1)}, s32[4]{0:T(128)S(1)}, bf16[4,32,1152]{2,1,0:T(8,128)(2,1)S(1)}, s32[]{:T(128)}, ...), condition=%wide.region_65.66_spmd, body=%wide.region_0.65_spmd.sunk | while | flops 3 | bytes 590001 | solution.py:117
  90.2 0.6 dynamic_slice.365
  91.5 35.0 %conditional.2 = (bf16[1,32,1152]{2,1,0:T(8,128)(2,1)}) conditional(s32[]{:T(128)} %bitcast.242, (bf16[4,32,1152]{2,1,0:T(8,128)(2,1)S(1)}, s32[]{:T(128)}) %tuple.367, (bf16[4,32,1152]{2,1,0:T(8,128)(2,1)S(1)}, s32[]{:T(128)}) %tuple.367, (bf16[4,32,1152]{2,1,0:T(8,128)(2,1)S(1)}, s32[]{:T(128)}) %tuple.367, ...), branch_computations={%region_1.1_spmd, %region_2.2_spmd, %region_3.3_spmd, %region_4.4_... | conditional | bytes 442420 | solution.py:114
  91.6 18.7 %collective-permute-start.60 = (bf16[32,1152]{1,0:T(8,128)(2,1)S(1)}, bf16[32,1152]{1,0:T(8,128)(2,1)}, u32[]{:S(2)}, u32[]{:S(2)}) collective-permute-start(bf16[32,1152]{1,0:T(8,128)(2,1)S(1)} %dynamic-slice_bitcast_fusion.60), channel_id=1, source_target_pairs={{0,488},{4,492},{8,480},{12,484},{16,504},{20,508},{24,496},{28,50... | collective-permute-start | bytes 221192 | tf_op jit(solution)/shard_map/while/body/eval_jaxpr/cond/branch_61_fun/ppermute | solution.py:18
  110.3 16.2 %collective-permute-done.60 = bf16[32,1152]{1,0:T(8,128)(2,1)} collective-permute-done((bf16[32,1152]{1,0:T(8,128)(2,1)S(1)}, bf16[32,1152]{1,0:T(8,128)(2,1)}, u32[]{:S(2)}, u32[]{:S(2)}) %collective-permute-start.60) | collective-permute-done | bytes 73760 | tf_op jit(solution)/shard_map/while/body/eval_jaxpr/cond/branch_61_fun/ppermute | solution.py:18
  126.5 0.9 constant_dynamic-update-slice_fusion.2
  127.4 0.6 dynamic_slice.365
  128.6 32.2 %conditional.2 = (bf16[1,32,1152]{2,1,0:T(8,128)(2,1)}) conditional(s32[]{:T(128)} %bitcast.242, (bf16[4,32,1152]{2,1,0:T(8,128)(2,1)S(1)}, s32[]{:T(128)}) %tuple.367, (bf16[4,32,1152]{2,1,0:T(8,128)(2,1)S(1)}, s32[]{:T(128)}) %tuple.367, (bf16[4,32,1152]{2,1,0:T(8,128)(2,1)S(1)}, s32[]{:T(128)}) %tuple.367, ...), branch_computations={%region_1.1_spmd, %region_2.2_spmd, %region_3.3_spmd, %region_4.4_... | conditional | bytes 442420 | solution.py:114
  128.7 11.9 %collective-permute-start.47 = (bf16[32,1152]{1,0:T(8,128)(2,1)S(1)}, bf16[32,1152]{1,0:T(8,128)(2,1)}, u32[]{:S(2)}, u32[]{:S(2)}) collective-permute-start(bf16[32,1152]{1,0:T(8,128)(2,1)S(1)} %dynamic-slice_bitcast_fusion.47), channel_id=1, source_target_pairs={{0,384},{4,388},{8,392},{12,396},{16,400},{20,404},{24,408},{28,41... | collective-permute-start | bytes 221192 | tf_op jit(solution)/shard_map/while/body/eval_jaxpr/cond/branch_48_fun/ppermute | solution.py:18
  140.6 20.2 %collective-permute-done.47 = bf16[32,1152]{1,0:T(8,128)(2,1)} collective-permute-done((bf16[32,1152]{1,0:T(8,128)(2,1)S(1)}, bf16[32,1152]{1,0:T(8,128)(2,1)}, u32[]{:S(2)}, u32[]{:S(2)}) %collective-permute-start.47) | collective-permute-done | bytes 73760 | tf_op jit(solution)/shard_map/while/body/eval_jaxpr/cond/branch_48_fun/ppermute | solution.py:18
  160.8 0.9 constant_dynamic-update-slice_fusion.2
  161.7 0.6 dynamic_slice.365
  162.9 9.6 %conditional.2 = (bf16[1,32,1152]{2,1,0:T(8,128)(2,1)}) conditional(s32[]{:T(128)} %bitcast.242, (bf16[4,32,1152]{2,1,0:T(8,128)(2,1)S(1)}, s32[]{:T(128)}) %tuple.367, (bf16[4,32,1152]{2,1,0:T(8,128)(2,1)S(1)}, s32[]{:T(128)}) %tuple.367, (bf16[4,32,1152]{2,1,0:T(8,128)(2,1)S(1)}, s32[]{:T(128)}) %tuple.367, ...), branch_computations={%region_1.1_spmd, %region_2.2_spmd, %region_3.3_spmd, %region_4.4_... | conditional | bytes 442420 | solution.py:114
  163.0 1.9 collective-permute-start.6
  165.0 7.6 %collective-permute-done.6 = bf16[32,1152]{1,0:T(8,128)(2,1)} collective-permute-done((bf16[32,1152]{1,0:T(8,128)(2,1)S(1)}, bf16[32,1152]{1,0:T(8,128)(2,1)}, u32[]{:S(2)}, u32[]{:S(2)}) %collective-permute-start.6) | collective-permute-done | bytes 73760 | tf_op jit(solution)/shard_map/while/body/eval_jaxpr/cond/branch_7_fun/ppermute | solution.py:18
  172.5 0.9 constant_dynamic-update-slice_fusion.2
  173.4 0.6 dynamic_slice.365
  174.7 13.5 %conditional.2 = (bf16[1,32,1152]{2,1,0:T(8,128)(2,1)}) conditional(s32[]{:T(128)} %bitcast.242, (bf16[4,32,1152]{2,1,0:T(8,128)(2,1)S(1)}, s32[]{:T(128)}) %tuple.367, (bf16[4,32,1152]{2,1,0:T(8,128)(2,1)S(1)}, s32[]{:T(128)}) %tuple.367, (bf16[4,32,1152]{2,1,0:T(8,128)(2,1)S(1)}, s32[]{:T(128)}) %tuple.367, ...), branch_computations={%region_1.1_spmd, %region_2.2_spmd, %region_3.3_spmd, %region_4.4_... | conditional | bytes 442420 | solution.py:114
  174.8 8.5 %collective-permute-start.33 = (bf16[32,1152]{1,0:T(8,128)(2,1)S(1)}, bf16[32,1152]{1,0:T(8,128)(2,1)}, u32[]{:S(2)}, u32[]{:S(2)}) collective-permute-start(bf16[32,1152]{1,0:T(8,128)(2,1)S(1)} %dynamic-slice_bitcast_fusion.33), channel_id=1, source_target_pairs={{0,272},{4,276},{8,280},{12,284},{16,256},{20,260},{24,264},{28,26... | collective-permute-start | bytes 221192 | tf_op jit(solution)/shard_map/while/body/eval_jaxpr/cond/branch_34_fun/ppermute | solution.py:18
  183.3 4.8 %collective-permute-done.33 = bf16[32,1152]{1,0:T(8,128)(2,1)} collective-permute-done((bf16[32,1152]{1,0:T(8,128)(2,1)S(1)}, bf16[32,1152]{1,0:T(8,128)(2,1)}, u32[]{:S(2)}, u32[]{:S(2)}) %collective-permute-start.33) | collective-permute-done | bytes 73760 | tf_op jit(solution)/shard_map/while/body/eval_jaxpr/cond/branch_34_fun/ppermute | solution.py:18
  188.1 0.9 constant_dynamic-update-slice_fusion.2
  189.1 0.2 reshape.202
  189.3 0.6 fusion.10
  189.8 1.2 copy.19
  191.1 1.1 add_convert_fusion
  192.2 0.6 convert_add_fusion
  (47 shorter events, 0.4 us)
Async XLA Ops:
  0.6 24.9 %copy-start = (bf16[320,1280]{1,0:T(8,128)(2,1)S(1)}, bf16[320,1280]{1,0:T(8,128)(2,1)}, u32[]{:S(2)}) copy-start(bf16[320,1280]{1,0:T(8,128)(2,1)} %param.77) | copy-start | bytes 2457604
  0.6 24.7 %copy-start.12 = (s32[4]{0:T(128)S(1)}, s32[4]{0:T(128)}, u32[]{:S(2)}) copy-start(s32[4]{0:T(128)} %constant.288.clone) | copy-start | bytes 52
  0.7 24.8 %copy-start.11 = (s32[1,1280]{1,0:T(1,128)S(1)}, s32[1,1280]{1,0:T(1,128)}, u32[]{:S(2)}) copy-start(s32[1,1280]{1,0:T(1,128)} %param.78) | copy-start | bytes 15364
  0.7 16.9 %collective-permute-start.63 = (bf16[1280,256]{1,0:T(8,128)(2,1)}, bf16[1280,256]{1,0:T(8,128)(2,1)S(1)}, u32[]{:S(2)}, u32[]{:S(2)}) collective-permute-start(bf16[1280,256]{1,0:T(8,128)(2,1)} %param.75), channel_id=1, source_target_pairs={{0,2},{1,3},{2,0},{3,1},{4,6},{5,7},{6,4},{7,5},{8,10},{9,11},{10,... | collective-permute-start | bytes 1966088 | tf_op jit(solution)/shard_map/ppermute | solution.py:24
  18.8 9.3 %collective-permute-start.64 = (bf16[2,1280,256]{2,1,0:T(8,128)(2,1)S(1)}, bf16[2,1280,256]{2,1,0:T(8,128)(2,1)}, u32[]{:S(2)}, u32[]{:S(2)}) collective-permute-start(bf16[2,1280,256]{2,1,0:T(8,128)(2,1)S(1)} %pad_maximum_fusion.1), channel_id=1, source_target_pairs={{0,1},{1,0},{2,3},{3,2},{4,5},{5,4},{6,7},{7,6},{8,9},{9,8},{10,11... | collective-permute-start | bytes 3932168 | tf_op jit(solution)/shard_map/ppermute | solution.py:26
  25.5 1.6 copy-start.8
  25.5 2.6 %copy-start.6 = (bf16[1280,256]{1,0:T(8,128)(2,1)S(1)}, bf16[1280,256]{1,0:T(8,128)(2,1)}, u32[]{:S(2)}) copy-start(bf16[1280,256]{1,0:T(8,128)(2,1)} %param.75) | copy-start | bytes 1966084
  27.5 3.8 %copy-start.5 = (bf16[320,128]{1,0:T(8,128)(2,1)}, bf16[320,128]{1,0:T(8,128)(2,1)S(1)}, u32[]{:S(2)}) copy-start(bf16[320,128]{1,0:T(8,128)(2,1)S(1)} %convolution_convert_fusion) | copy-start | bytes 245764
  31.1 6.3 %copy-start.7 = (bf16[256,1280]{1,0:T(8,128)(2,1)S(1)}, bf16[256,1280]{1,0:T(8,128)(2,1)}, u32[]{:S(2)}) copy-start(bf16[256,1280]{1,0:T(8,128)(2,1)} %param.76) | copy-start | bytes 1966084
  32.5 21.3 %collective-permute-start.65 = (bf16[320,1152]{1,0:T(8,128)(2,1)}, bf16[320,1152]{1,0:T(8,128)(2,1)S(1)}, u32[]{:S(2)}, u32[]{:S(2)}) collective-permute-start(bf16[320,1152]{1,0:T(8,128)(2,1)} %get-tuple-element.749), channel_id=1, source_target_pairs={{0,2},{1,3},{2,0},{3,1},{4,6},{5,7},{6,4},{7,5},{8,10},{9,11},{10,... | collective-permute-start | bytes 2211848 | tf_op jit(solution)/shard_map/ppermute | solution.py:70
  38.2 15.6 %copy-start.1 = (bf16[1,320,1152]{2,1,0:T(8,128)(2,1)S(1)}, bf16[1,320,1152]{2,1,0:T(8,128)(2,1)}, u32[]{:S(2)}) copy-start(bf16[1,320,1152]{2,1,0:T(8,128)(2,1)} %get-tuple-element.748) | copy-start | bytes 2211844
  38.4 15.4 %copy-start.2 = (bf16[256,4,320]{0,2,1:T(8,128)(2,1)}, bf16[256,4,320]{0,2,1:T(8,128)(2,1)S(1)}, u32[]{:S(2)}) copy-start(bf16[256,4,320]{0,2,1:T(8,128)(2,1)S(1)} %select_bitcast_fusion) | copy-start | bytes 1966084
  53.8 4.5 %copy-start.13 = (s32[1,4]{1,0:T(1,128)S(1)}, s32[1,4]{1,0:T(1,128)}, u32[]{:S(2)}) copy-start(s32[1,4]{1,0:T(1,128)} %param.80) | copy-start | bytes 52
  53.8 4.6 %copy-start.3 = (bf16[256,4,320]{0,2,1:T(8,128)(2,1)S(1)}, bf16[256,4,320]{0,2,1:T(8,128)(2,1)}, u32[]{:S(2)}) copy-start(bf16[256,4,320]{0,2,1:T(8,128)(2,1)} %copy-done.2) | copy-start | bytes 1966084
  55.1 6.3 %collective-permute-start.66 = (bf16[2,320,1152]{2,1,0:T(8,128)(2,1)}, bf16[2,320,1152]{2,1,0:T(8,128)(2,1)}, u32[]{:S(2)}, u32[]{:S(2)}) collective-permute-start(bf16[2,320,1152]{2,1,0:T(8,128)(2,1)} %pad_maximum_fusion), channel_id=1, source_target_pairs={{0,1},{1,0},{2,3},{3,2},{4,5},{5,4},{6,7},{7,6},{8,9},{9,8},{10,11... | collective-permute-start | bytes 4423688 | tf_op jit(solution)/shard_map/ppermute | solution.py:73
  63.5 10.2 %collective-permute-start.67 = (bf16[128,1152]{1,0:T(8,128)(2,1)S(1)}, bf16[128,1152]{1,0:T(8,128)(2,1)S(1)}, u32[]{:S(2)}, u32[]{:S(2)}) collective-permute-start(bf16[128,1152]{1,0:T(8,128)(2,1)S(1)} %dynamic-slice_convert_fusion), channel_id=1, source_target_pairs={{0,4},{4,0},{8,12},{12,8},{16,20},{20,16},{24,28},{28,24},{32,36},... | collective-permute-start | bytes 884744 | tf_op jit(solution)/shard_map/ppermute | solution.py:89
  73.8 16.4 %copy-start.9 = (bf16[4,32,1152]{2,1,0:T(8,128)(2,1)S(1)}, bf16[4,32,1152]{2,1,0:T(8,128)(2,1)}, u32[]{:S(2)}) copy-start(bf16[4,32,1152]{2,1,0:T(8,128)(2,1)} %custom-call.6) | copy-start | bytes 884740
  73.9 10.4 %collective-permute-start.68 = (bf16[32,1152]{1,0:T(8,128)(2,1)S(1)}, bf16[32,1152]{1,0:T(8,128)(2,1)S(1)}, u32[]{:S(2)}, u32[]{:S(2)}) collective-permute-start(bf16[32,1152]{1,0:T(8,128)(2,1)S(1)} %get-tuple-element.753), channel_id=1, source_target_pairs={{0,1},{1,0},{2,3},{3,2},{4,5},{5,4},{6,7},{7,6},{8,9},{9,8},{10,11... | collective-permute-start | bytes 221192 | tf_op jit(solution)/shard_map/ppermute | solution.py:102
  77.1 7.3 %collective-permute-start.69 = (bf16[32,1152]{1,0:T(8,128)(2,1)S(1)}, bf16[32,1152]{1,0:T(8,128)(2,1)S(1)}, u32[]{:S(2)}, u32[]{:S(2)}) collective-permute-start(bf16[32,1152]{1,0:T(8,128)(2,1)S(1)} %get-tuple-element.752), channel_id=1, source_target_pairs={{0,2},{1,3},{2,0},{3,1},{4,6},{5,7},{6,4},{7,5},{8,10},{9,11},{10,... | collective-permute-start | bytes 221192 | tf_op jit(solution)/shard_map/ppermute | solution.py:102
  81.9 7.6 %collective-permute-start.70 = (bf16[32,1152]{1,0:T(8,128)(2,1)S(1)}, bf16[32,1152]{1,0:T(8,128)(2,1)S(1)}, u32[]{:S(2)}, u32[]{:S(2)}) collective-permute-start(bf16[32,1152]{1,0:T(8,128)(2,1)S(1)} %get-tuple-element.751), channel_id=1, source_target_pairs={{0,3},{1,2},{2,1},{3,0},{4,7},{5,6},{6,5},{7,4},{8,11},{9,10},{10,... | collective-permute-start | bytes 221192 | tf_op jit(solution)/shard_map/ppermute | solution.py:102
  91.6 34.9 %collective-permute-start.60 = (bf16[32,1152]{1,0:T(8,128)(2,1)S(1)}, bf16[32,1152]{1,0:T(8,128)(2,1)}, u32[]{:S(2)}, u32[]{:S(2)}) collective-permute-start(bf16[32,1152]{1,0:T(8,128)(2,1)S(1)} %dynamic-slice_bitcast_fusion.60), channel_id=1, source_target_pairs={{0,488},{4,492},{8,480},{12,484},{16,504},{20,508},{24,496},{28,50... | collective-permute-start | bytes 221192 | tf_op jit(solution)/shard_map/while/body/eval_jaxpr/cond/branch_61_fun/ppermute | solution.py:18
  128.7 32.1 %collective-permute-start.47 = (bf16[32,1152]{1,0:T(8,128)(2,1)S(1)}, bf16[32,1152]{1,0:T(8,128)(2,1)}, u32[]{:S(2)}, u32[]{:S(2)}) collective-permute-start(bf16[32,1152]{1,0:T(8,128)(2,1)S(1)} %dynamic-slice_bitcast_fusion.47), channel_id=1, source_target_pairs={{0,384},{4,388},{8,392},{12,396},{16,400},{20,404},{24,408},{28,41... | collective-permute-start | bytes 221192 | tf_op jit(solution)/shard_map/while/body/eval_jaxpr/cond/branch_48_fun/ppermute | solution.py:18
  163.0 9.5 %collective-permute-start.6 = (bf16[32,1152]{1,0:T(8,128)(2,1)S(1)}, bf16[32,1152]{1,0:T(8,128)(2,1)}, u32[]{:S(2)}, u32[]{:S(2)}) collective-permute-start(bf16[32,1152]{1,0:T(8,128)(2,1)S(1)} %dynamic-slice_bitcast_fusion.6), channel_id=1, source_target_pairs={{0,56},{4,60},{8,48},{12,52},{16,40},{20,44},{24,32},{28,36},{32,2... | collective-permute-start | bytes 221192 | tf_op jit(solution)/shard_map/while/body/eval_jaxpr/cond/branch_7_fun/ppermute | solution.py:18
  174.8 13.4 %collective-permute-start.33 = (bf16[32,1152]{1,0:T(8,128)(2,1)S(1)}, bf16[32,1152]{1,0:T(8,128)(2,1)}, u32[]{:S(2)}, u32[]{:S(2)}) collective-permute-start(bf16[32,1152]{1,0:T(8,128)(2,1)S(1)} %dynamic-slice_bitcast_fusion.33), channel_id=1, source_target_pairs={{0,272},{4,276},{8,280},{12,284},{16,256},{20,260},{24,264},{28,26... | collective-permute-start | bytes 221192 | tf_op jit(solution)/shard_map/while/body/eval_jaxpr/cond/branch_34_fun/ppermute | solution.py:18
  189.8 1.2 copy-start.4
  191.1 1.2 copy-start.10

commit v12 on v10

--- a/solution.py
+++ b/solution.py
@@ -111,7 +111,7 @@
         sent = lax.switch(column_masks[a], branches, piece)
         return lax.dynamic_update_index_in_dim(routed, sent, a, 0)
 
-    routed = lax.fori_loop(0, col_count, route_piece, jnp.zeros_like(spread))
+    routed = lax.fori_loop(0, col_count, route_piece, spread)
     tile_size = coupled_width // col_count
     front_part = routed[:, :, :coupled_width].reshape(col_count, share_rows, col_count, tile_size)
     target_tiles = jnp.bitwise_xor(

time: 151 us -> 175 us (1.16)
  the two profiles are of different devices: /device:TPU:1 before, /device:TPU:8 now
where the time goes in v12:
time: 175 us; the launch traced here: 174 us
  waiting for transfers between devices  96.3 us (55%)
  starting transfers between devices  49.8 us (28%)
  local copies, waits for them, and re-layouts  9.81 us (6%)
  matrix products  8.83 us (5%)
  other arithmetic  5.08 us (3%)
  loops' own time  2.94 us (2%)
    ppermute x4, waiting for transfers between devices, branch(): return lambda x: lax.ppermute(x, LEAF, pairs)  48.7 us
    ppermute x2, waiting for transfers between devices, col_gather(): remote = lax.ppermute(block, COLS, [(c, c ^ 2) for c in range(4)])  32.1 us
    ppermute x4, starting transfers between devices, branch(): return lambda x: lax.ppermute(x, LEAF, pairs)  24.5 us
    ppermute x2, starting transfers between devices, col_gather(): remote = lax.ppermute(block, COLS, [(c, c ^ 2) for c in range(4)])  10 us
    ppermute x3, starting transfers between devices, body(): lax.ppermute(outgoing, COLS, [(c, c ^ distance) for c in range(col_count)])  9.27 us
    ppermute x1, waiting for transfers between devices, body(): lax.ppermute(other_rows.astype(jnp.bfloat16), LEAF, [(s, s ^ 1) for s in...  8.71 us
    ppermute x3, waiting for transfers between devices, body(): lax.ppermute(outgoing, COLS, [(c, c ^ distance) for c in range(col_count)])  5.21 us
    ppermute x2, starting transfers between devices, col_gather(): partner = lax.ppermute(chip, COLS, [(c, c ^ 1) for c in range(4)])  3.83 us
  transfers between devices with their start and end apart: 12, of which 11 were waited for; matrix products, arithmetic and copies ran while one was open for 3% of the time, Pallas kernels for 0%

profile of v12, /device:TPU:8, one launch (start us, length us, event | category | flops | bytes accessed | tf_op | source)
XLA Modules:
  0.0 173.9 jit_solution(8646502709202276447)
XLA Ops:
  0.6 0.0 copy-start
  0.7 5.1 %collective-permute-start.63 = (bf16[1280,256]{1,0:T(8,128)(2,1)}, bf16[1280,256]{1,0:T(8,128)(2,1)S(1)}, u32[]{:S(2)}, u32[]{:S(2)}) collective-permute-start(bf16[1280,256]{1,0:T(8,128)(2,1)} %param.75), channel_id=1, source_target_pairs={{0,2},{1,3},{2,0},{3,1},{4,6},{5,7},{6,4},{7,5},{8,10},{9,11},{10,... | collective-permute-start | bytes 1966088 | tf_op jit(solution)/shard_map/ppermute | solution.py:24
  5.7 15.1 %collective-permute-done.63 = bf16[1280,256]{1,0:T(8,128)(2,1)S(1)} collective-permute-done((bf16[1280,256]{1,0:T(8,128)(2,1)}, bf16[1280,256]{1,0:T(8,128)(2,1)S(1)}, u32[]{:S(2)}, u32[]{:S(2)}) %collective-permute-start.63) | collective-permute-done | bytes 655392 | tf_op jit(solution)/shard_map/ppermute | solution.py:24
  20.9 1.2 pad_maximum_fusion.1
  22.1 1.9 %collective-permute-start.64 = (bf16[2,1280,256]{2,1,0:T(8,128)(2,1)S(1)}, bf16[2,1280,256]{2,1,0:T(8,128)(2,1)}, u32[]{:S(2)}, u32[]{:S(2)}) collective-permute-start(bf16[2,1280,256]{2,1,0:T(8,128)(2,1)S(1)} %pad_maximum_fusion.1), channel_id=1, source_target_pairs={{0,1},{1,0},{2,3},{3,2},{4,5},{5,4},{6,7},{7,6},{8,9},{9,8},{10,11... | collective-permute-start | bytes 3932168 | tf_op jit(solution)/shard_map/ppermute | solution.py:26
  24.0 0.1 broadcast_in_dim.243
  24.2 1.5 fusion.2
  25.8 0.4 convolution_convert_fusion
  26.2 0.0 copy-start.5
  26.2 1.0 collective-permute-done.64
  27.1 2.3 %fusion.3 = bf16[320,4,256]{2,0,1:T(8,128)(2,1)S(1)} fusion(bf16[2,1280,256]{2,1,0:T(8,128)(2,1)} %collective-permute-done.64, bf16[1,1280,256]{2,1,0:T(8,128)(2,1)S(1)} %bitcast.251, bf16[1,1280,256]{2,1,0:T(8,128)(2,1)S(1)} %bitcast.249, bf16[1280,320]{0,1:T(8,128)(2,1)S(1)} %fusion.2), kind=kOutput, calls=%fused_computation.74 | convolution fusion | flops 846725120 | bytes 4096000 | tf_op jit(solution)/shard_map/ip,kpn->ikn/dot_general | solution.py:56
  29.5 0.6 gather_fusion.1
  30.1 0.1 copy.18
  30.2 0.2 select_convert_fusion
  30.3 0.1 fusion.26
  30.5 4.9 %collective-permute-start.65 = (bf16[320,1152]{1,0:T(8,128)(2,1)S(1)}, bf16[320,1152]{1,0:T(8,128)(2,1)S(1)}, u32[]{:S(2)}, u32[]{:S(2)}) collective-permute-start(bf16[320,1152]{1,0:T(8,128)(2,1)S(1)} %get-tuple-element.745), channel_id=1, source_target_pairs={{0,2},{1,3},{2,0},{3,1},{4,6},{5,7},{6,4},{7,5},{8,10},{9,11},{10,... | collective-permute-start | bytes 2211848 | tf_op jit(solution)/shard_map/ppermute | solution.py:24
  35.4 17.0 %collective-permute-done.65 = bf16[320,1152]{1,0:T(8,128)(2,1)S(1)} collective-permute-done((bf16[320,1152]{1,0:T(8,128)(2,1)S(1)}, bf16[320,1152]{1,0:T(8,128)(2,1)S(1)}, u32[]{:S(2)}, u32[]{:S(2)}) %collective-permute-start.65) | collective-permute-done | bytes 737312 | tf_op jit(solution)/shard_map/ppermute | solution.py:24
  52.4 1.3 pad_maximum_fusion
  53.7 0.1 copy-done.1
  53.7 1.9 %collective-permute-start.66 = (bf16[2,320,1152]{2,1,0:T(8,128)(2,1)}, bf16[2,320,1152]{2,1,0:T(8,128)(2,1)}, u32[]{:S(2)}, u32[]{:S(2)}) collective-permute-start(bf16[2,320,1152]{2,1,0:T(8,128)(2,1)} %pad_maximum_fusion), channel_id=1, source_target_pairs={{0,1},{1,0},{2,3},{3,2},{4,5},{5,4},{6,7},{7,6},{8,9},{9,8},{10,11... | collective-permute-start | bytes 4423688 | tf_op jit(solution)/shard_map/ppermute | solution.py:26
  55.7 0.2 copy.13
  56.0 0.6 gather_fusion
  56.7 0.1 xor_xor_fusion
  56.7 1.9 %convolution_bitcast_fusion.1 = f32[256,1152]{1,0:T(8,128)S(1)} fusion(bf16[4,256,320]{1,2,0:T(8,128)(2,1)S(1)} %gather_fusion, pred[4]{0:T(512)(128)(4,1)S(1)} %get-tuple-element.742, bf16[1,320,1152]{2,1,0:T(8,128)(2,1)} %bitcast.243, bf16[1,320,1152]{2,1,0:T(8,128)(2,1)S(1)} %get-tuple-element.744), kind=kOutput, calls=%fused_computation.72 | convolution fusion | flops 380764160 | bytes 3309572 | tf_op jit(solution)/shard_map/rkp,kpn->rn/dot_general | solution.py:72
  58.6 0.6 collective-permute-done.66
  59.2 2.1 %convolution_bitcast_fusion = f32[256,1152]{1,0:T(8,128)S(1)} fusion(bf16[2,320,1152]{2,1,0:T(8,128)(2,1)} %collective-permute-done.66, bf16[4,256,320]{1,2,0:T(8,128)(2,1)S(1)} %gather_fusion, pred[4]{0:T(512)(128)(4,1)S(1)} %get-tuple-element.742), kind=kOutput, calls=%fused_computation.71 | convolution fusion | flops 377815040 | bytes 3309572 | tf_op jit(solution)/shard_map/rkp,kpn->rn/dot_general | solution.py:78
  61.4 0.1 add_negate_fusion
  61.6 2.1 %collective-permute-start.67 = (bf16[128,1152]{1,0:T(8,128)(2,1)S(1)}, bf16[128,1152]{1,0:T(8,128)(2,1)S(1)}, u32[]{:S(2)}, u32[]{:S(2)}) collective-permute-start(bf16[128,1152]{1,0:T(8,128)(2,1)S(1)} %dynamic-slice_convert_fusion), channel_id=1, source_target_pairs={{0,4},{4,0},{8,12},{12,8},{16,20},{20,16},{24,28},{28,24},{32,36},... | collective-permute-start | bytes 884744 | tf_op jit(solution)/shard_map/ppermute | solution.py:86
  63.7 0.1 fusion.16
  63.8 8.7 %collective-permute-done.67 = bf16[128,1152]{1,0:T(8,128)(2,1)S(1)} collective-permute-done((bf16[128,1152]{1,0:T(8,128)(2,1)S(1)}, bf16[128,1152]{1,0:T(8,128)(2,1)S(1)}, u32[]{:S(2)}, u32[]{:S(2)}) %collective-permute-start.67) | collective-permute-done | bytes 294944 | tf_op jit(solution)/shard_map/ppermute | solution.py:86
  72.5 0.1 add_convert_fusion.1
  72.6 1.9 %collective-permute-start.68 = (bf16[32,1152]{1,0:T(8,128)(2,1)S(1)}, bf16[32,1152]{1,0:T(8,128)(2,1)S(1)}, u32[]{:S(2)}, u32[]{:S(2)}) collective-permute-start(bf16[32,1152]{1,0:T(8,128)(2,1)S(1)} %get-tuple-element.749), channel_id=1, source_target_pairs={{0,1},{1,0},{2,3},{3,2},{4,5},{5,4},{6,7},{7,6},{8,9},{9,8},{10,11... | collective-permute-start | bytes 221192 | tf_op jit(solution)/shard_map/ppermute | solution.py:99
  74.5 4.9 %collective-permute-start.69 = (bf16[32,1152]{1,0:T(8,128)(2,1)S(1)}, bf16[32,1152]{1,0:T(8,128)(2,1)S(1)}, u32[]{:S(2)}, u32[]{:S(2)}) collective-permute-start(bf16[32,1152]{1,0:T(8,128)(2,1)S(1)} %get-tuple-element.748), channel_id=1, source_target_pairs={{0,2},{1,3},{2,0},{3,1},{4,6},{5,7},{6,4},{7,5},{8,10},{9,11},{10,... | collective-permute-start | bytes 221192 | tf_op jit(solution)/shard_map/ppermute | solution.py:99
  79.5 2.4 %collective-permute-start.70 = (bf16[32,1152]{1,0:T(8,128)(2,1)S(1)}, bf16[32,1152]{1,0:T(8,128)(2,1)S(1)}, u32[]{:S(2)}, u32[]{:S(2)}) collective-permute-start(bf16[32,1152]{1,0:T(8,128)(2,1)S(1)} %get-tuple-element.747), channel_id=1, source_target_pairs={{0,3},{1,2},{2,1},{3,0},{4,7},{5,6},{6,5},{7,4},{8,11},{9,10},{10,... | collective-permute-start | bytes 221192 | tf_op jit(solution)/shard_map/ppermute | solution.py:99
  81.9 0.7 collective-permute-done.69
  82.6 4.5 %collective-permute-done.70 = bf16[32,1152]{1,0:T(8,128)(2,1)S(1)} collective-permute-done((bf16[32,1152]{1,0:T(8,128)(2,1)S(1)}, bf16[32,1152]{1,0:T(8,128)(2,1)S(1)}, u32[]{:S(2)}, u32[]{:S(2)}) %collective-permute-start.70) | collective-permute-done | bytes 73760 | tf_op jit(solution)/shard_map/ppermute | solution.py:99
  87.2 0.6 gather_fusion.2
  87.8 0.1 broadcast_select_fusion.1
  87.9 82.1 %while.13 = (s32[]{:T(128)}, bf16[4,32,1152]{2,1,0:T(8,128)(2,1)S(1)}, s32[4]{0:T(128)S(1)}, bf16[4,32,1152]{2,1,0:T(8,128)(2,1)S(1)}, s32[]{:T(128)}, /*index=5*/s32[1]{0:T(128)}, s32[1]{0:T(128)}) while((s32[]{:T(128)}, bf16[4,32,1152]{2,1,0:T(8,128)(2,1)S(1)}, s32[4]{0:T(128)S(1)}, bf16[4,32,1152]{2,1,0:T(8,128)(2,1)S(1)}, s32[]{:T(128)}, ...), condition=%wide.region_65.66_spmd, body=%wide.region_0.65_spmd.sunk | while | flops 3 | bytes 590001 | solution.py:114
  87.9 0.6 dynamic_slice.365
  89.2 38.7 %conditional.2 = (bf16[1,32,1152]{2,1,0:T(8,128)(2,1)}) conditional(s32[]{:T(128)} %bitcast.239, (bf16[4,32,1152]{2,1,0:T(8,128)(2,1)S(1)}, s32[]{:T(128)}) %tuple.365, (bf16[4,32,1152]{2,1,0:T(8,128)(2,1)S(1)}, s32[]{:T(128)}) %tuple.365, (bf16[4,32,1152]{2,1,0:T(8,128)(2,1)S(1)}, s32[]{:T(128)}) %tuple.365, ...), branch_computations={%region_1.1_spmd, %region_2.2_spmd, %region_3.3_spmd, %region_4.4_... | conditional | bytes 442420 | solution.py:111
  89.3 18.8 %collective-permute-start.49 = (bf16[32,1152]{1,0:T(8,128)(2,1)S(1)}, bf16[32,1152]{1,0:T(8,128)(2,1)}, u32[]{:S(2)}, u32[]{:S(2)}) collective-permute-start(bf16[32,1152]{1,0:T(8,128)(2,1)S(1)} %dynamic-slice_bitcast_fusion.49), channel_id=1, source_target_pairs={{0,400},{4,404},{8,408},{12,412},{16,384},{20,388},{24,392},{28,39... | collective-permute-start | bytes 221192 | tf_op jit(solution)/shard_map/while/body/eval_jaxpr/cond/branch_50_fun/ppermute | solution.py:18
  108.0 19.9 %collective-permute-done.49 = bf16[32,1152]{1,0:T(8,128)(2,1)} collective-permute-done((bf16[32,1152]{1,0:T(8,128)(2,1)S(1)}, bf16[32,1152]{1,0:T(8,128)(2,1)}, u32[]{:S(2)}, u32[]{:S(2)}) %collective-permute-start.49) | collective-permute-done | bytes 73760 | tf_op jit(solution)/shard_map/while/body/eval_jaxpr/cond/branch_50_fun/ppermute | solution.py:18
  127.9 0.9 constant_dynamic-update-slice_fusion.2
  128.8 0.6 dynamic_slice.365
  130.0 14.4 %conditional.2 = (bf16[1,32,1152]{2,1,0:T(8,128)(2,1)}) conditional(s32[]{:T(128)} %bitcast.239, (bf16[4,32,1152]{2,1,0:T(8,128)(2,1)S(1)}, s32[]{:T(128)}) %tuple.365, (bf16[4,32,1152]{2,1,0:T(8,128)(2,1)S(1)}, s32[]{:T(128)}) %tuple.365, (bf16[4,32,1152]{2,1,0:T(8,128)(2,1)S(1)}, s32[]{:T(128)}) %tuple.365, ...), branch_computations={%region_1.1_spmd, %region_2.2_spmd, %region_3.3_spmd, %region_4.4_... | conditional | bytes 442420 | solution.py:111
  130.1 1.9 %collective-permute-start.19 = (bf16[32,1152]{1,0:T(8,128)(2,1)S(1)}, bf16[32,1152]{1,0:T(8,128)(2,1)}, u32[]{:S(2)}, u32[]{:S(2)}) collective-permute-start(bf16[32,1152]{1,0:T(8,128)(2,1)S(1)} %dynamic-slice_bitcast_fusion.19), channel_id=1, source_target_pairs={{0,160},{4,164},{8,168},{12,172},{16,176},{20,180},{24,184},{28,18... | collective-permute-start | bytes 221192 | tf_op jit(solution)/shard_map/while/body/eval_jaxpr/cond/branch_20_fun/ppermute | solution.py:18
  132.0 12.4 %collective-permute-done.19 = bf16[32,1152]{1,0:T(8,128)(2,1)} collective-permute-done((bf16[32,1152]{1,0:T(8,128)(2,1)S(1)}, bf16[32,1152]{1,0:T(8,128)(2,1)}, u32[]{:S(2)}, u32[]{:S(2)}) %collective-permute-start.19) | collective-permute-done | bytes 73760 | tf_op jit(solution)/shard_map/while/body/eval_jaxpr/cond/branch_20_fun/ppermute | solution.py:18
  144.4 0.9 constant_dynamic-update-slice_fusion.2
  145.3 0.6 dynamic_slice.365
  146.6 12.2 %conditional.2 = (bf16[1,32,1152]{2,1,0:T(8,128)(2,1)}) conditional(s32[]{:T(128)} %bitcast.239, (bf16[4,32,1152]{2,1,0:T(8,128)(2,1)S(1)}, s32[]{:T(128)}) %tuple.365, (bf16[4,32,1152]{2,1,0:T(8,128)(2,1)S(1)}, s32[]{:T(128)}) %tuple.365, (bf16[4,32,1152]{2,1,0:T(8,128)(2,1)S(1)}, s32[]{:T(128)}) %tuple.365, ...), branch_computations={%region_1.1_spmd, %region_2.2_spmd, %region_3.3_spmd, %region_4.4_... | conditional | bytes 442420 | solution.py:111
  146.6 1.9 %collective-permute-start.7 = (bf16[32,1152]{1,0:T(8,128)(2,1)S(1)}, bf16[32,1152]{1,0:T(8,128)(2,1)}, u32[]{:S(2)}, u32[]{:S(2)}) collective-permute-start(bf16[32,1152]{1,0:T(8,128)(2,1)S(1)} %dynamic-slice_bitcast_fusion.7), channel_id=1, source_target_pairs={{0,64},{4,68},{8,72},{12,76},{16,80},{20,84},{24,88},{28,92},{32,9... | collective-permute-start | bytes 221192 | tf_op jit(solution)/shard_map/while/body/eval_jaxpr/cond/branch_8_fun/ppermute | solution.py:18
  148.6 10.2 %collective-permute-done.7 = bf16[32,1152]{1,0:T(8,128)(2,1)} collective-permute-done((bf16[32,1152]{1,0:T(8,128)(2,1)S(1)}, bf16[32,1152]{1,0:T(8,128)(2,1)}, u32[]{:S(2)}, u32[]{:S(2)}) %collective-permute-start.7) | collective-permute-done | bytes 73760 | tf_op jit(solution)/shard_map/while/body/eval_jaxpr/cond/branch_8_fun/ppermute | solution.py:18
  158.8 0.9 constant_dynamic-update-slice_fusion.2
  159.7 0.6 dynamic_slice.365
  160.9 8.2 %conditional.2 = (bf16[1,32,1152]{2,1,0:T(8,128)(2,1)}) conditional(s32[]{:T(128)} %bitcast.239, (bf16[4,32,1152]{2,1,0:T(8,128)(2,1)S(1)}, s32[]{:T(128)}) %tuple.365, (bf16[4,32,1152]{2,1,0:T(8,128)(2,1)S(1)}, s32[]{:T(128)}) %tuple.365, (bf16[4,32,1152]{2,1,0:T(8,128)(2,1)S(1)}, s32[]{:T(128)}) %tuple.365, ...), branch_computations={%region_1.1_spmd, %region_2.2_spmd, %region_3.3_spmd, %region_4.4_... | conditional | bytes 442420 | solution.py:111
  161.0 1.9 %collective-permute-start.5 = (bf16[32,1152]{1,0:T(8,128)(2,1)S(1)}, bf16[32,1152]{1,0:T(8,128)(2,1)}, u32[]{:S(2)}, u32[]{:S(2)}) collective-permute-start(bf16[32,1152]{1,0:T(8,128)(2,1)S(1)} %dynamic-slice_bitcast_fusion.5), channel_id=1, source_target_pairs={{0,48},{4,52},{8,56},{12,60},{16,32},{20,36},{24,40},{28,44},{32,1... | collective-permute-start | bytes 221192 | tf_op jit(solution)/shard_map/while/body/eval_jaxpr/cond/branch_6_fun/ppermute | solution.py:18
  162.9 6.2 %collective-permute-done.5 = bf16[32,1152]{1,0:T(8,128)(2,1)} collective-permute-done((bf16[32,1152]{1,0:T(8,128)(2,1)S(1)}, bf16[32,1152]{1,0:T(8,128)(2,1)}, u32[]{:S(2)}, u32[]{:S(2)}) %collective-permute-start.5) | collective-permute-done | bytes 73760 | tf_op jit(solution)/shard_map/while/body/eval_jaxpr/cond/branch_6_fun/ppermute | solution.py:18
  169.2 0.9 constant_dynamic-update-slice_fusion.2
  170.1 0.2 reshape.203
  170.3 0.6 fusion.12
  170.9 1.2 copy.19
  172.1 1.1 add_convert_fusion
  173.3 0.6 convert_add_fusion
  (40 shorter events, 0.4 us)
Async XLA Ops:
  0.6 23.6 %copy-start = (bf16[320,1280]{1,0:T(8,128)(2,1)S(1)}, bf16[320,1280]{1,0:T(8,128)(2,1)}, u32[]{:S(2)}) copy-start(bf16[320,1280]{1,0:T(8,128)(2,1)} %param.77) | copy-start | bytes 2457604
  0.6 23.5 %copy-start.8 = (s32[1,1280]{1,0:T(1,128)S(1)}, s32[1,1280]{1,0:T(1,128)}, u32[]{:S(2)}) copy-start(s32[1,1280]{1,0:T(1,128)} %param.78) | copy-start | bytes 15364
  0.7 20.2 %collective-permute-start.63 = (bf16[1280,256]{1,0:T(8,128)(2,1)}, bf16[1280,256]{1,0:T(8,128)(2,1)S(1)}, u32[]{:S(2)}, u32[]{:S(2)}) collective-permute-start(bf16[1280,256]{1,0:T(8,128)(2,1)} %param.75), channel_id=1, source_target_pairs={{0,2},{1,3},{2,0},{3,1},{4,6},{5,7},{6,4},{7,5},{8,10},{9,11},{10,... | collective-permute-start | bytes 1966088 | tf_op jit(solution)/shard_map/ppermute | solution.py:24
  22.1 5.1 %collective-permute-start.64 = (bf16[2,1280,256]{2,1,0:T(8,128)(2,1)S(1)}, bf16[2,1280,256]{2,1,0:T(8,128)(2,1)}, u32[]{:S(2)}, u32[]{:S(2)}) collective-permute-start(bf16[2,1280,256]{2,1,0:T(8,128)(2,1)S(1)} %pad_maximum_fusion.1), channel_id=1, source_target_pairs={{0,1},{1,0},{2,3},{3,2},{4,5},{5,4},{6,7},{7,6},{8,9},{9,8},{10,11... | collective-permute-start | bytes 3932168 | tf_op jit(solution)/shard_map/ppermute | solution.py:26
  24.2 1.6 copy-start.6
  24.2 2.9 %copy-start.3 = (bf16[1280,256]{1,0:T(8,128)(2,1)S(1)}, bf16[1280,256]{1,0:T(8,128)(2,1)}, u32[]{:S(2)}) copy-start(bf16[1280,256]{1,0:T(8,128)(2,1)} %param.75) | copy-start | bytes 1966084
  26.2 4.2 %copy-start.5 = (bf16[320,128]{1,0:T(8,128)(2,1)}, bf16[320,128]{1,0:T(8,128)(2,1)S(1)}, u32[]{:S(2)}) copy-start(bf16[320,128]{1,0:T(8,128)(2,1)S(1)} %convolution_convert_fusion) | copy-start | bytes 245764
  30.5 21.9 %collective-permute-start.65 = (bf16[320,1152]{1,0:T(8,128)(2,1)S(1)}, bf16[320,1152]{1,0:T(8,128)(2,1)S(1)}, u32[]{:S(2)}, u32[]{:S(2)}) collective-permute-start(bf16[320,1152]{1,0:T(8,128)(2,1)S(1)} %get-tuple-element.745), channel_id=1, source_target_pairs={{0,2},{1,3},{2,0},{3,1},{4,6},{5,7},{6,4},{7,5},{8,10},{9,11},{10,... | collective-permute-start | bytes 2211848 | tf_op jit(solution)/shard_map/ppermute | solution.py:24
  52.4 1.3 copy-start.1
  52.4 3.3 %copy-start.4 = (bf16[256,1280]{1,0:T(8,128)(2,1)S(1)}, bf16[256,1280]{1,0:T(8,128)(2,1)}, u32[]{:S(2)}) copy-start(bf16[256,1280]{1,0:T(8,128)(2,1)} %param.76) | copy-start | bytes 1966084
  52.4 3.6 %copy-start.9 = (s32[4]{0:T(128)S(1)}, s32[4]{0:T(128)}, u32[]{:S(2)}) copy-start(s32[4]{0:T(128)} %constant.286.clone) | copy-start | bytes 52
  53.7 5.5 %collective-permute-start.66 = (bf16[2,320,1152]{2,1,0:T(8,128)(2,1)}, bf16[2,320,1152]{2,1,0:T(8,128)(2,1)}, u32[]{:S(2)}, u32[]{:S(2)}) collective-permute-start(bf16[2,320,1152]{2,1,0:T(8,128)(2,1)} %pad_maximum_fusion), channel_id=1, source_target_pairs={{0,1},{1,0},{2,3},{3,2},{4,5},{5,4},{6,7},{7,6},{8,9},{9,8},{10,11... | collective-permute-start | bytes 4423688 | tf_op jit(solution)/shard_map/ppermute | solution.py:26
  55.7 1.0 copy-start.10
  61.6 10.9 %collective-permute-start.67 = (bf16[128,1152]{1,0:T(8,128)(2,1)S(1)}, bf16[128,1152]{1,0:T(8,128)(2,1)S(1)}, u32[]{:S(2)}, u32[]{:S(2)}) collective-permute-start(bf16[128,1152]{1,0:T(8,128)(2,1)S(1)} %dynamic-slice_convert_fusion), channel_id=1, source_target_pairs={{0,4},{4,0},{8,12},{12,8},{16,20},{20,16},{24,28},{28,24},{32,36},... | collective-permute-start | bytes 884744 | tf_op jit(solution)/shard_map/ppermute | solution.py:86
  72.6 9.3 %collective-permute-start.68 = (bf16[32,1152]{1,0:T(8,128)(2,1)S(1)}, bf16[32,1152]{1,0:T(8,128)(2,1)S(1)}, u32[]{:S(2)}, u32[]{:S(2)}) collective-permute-start(bf16[32,1152]{1,0:T(8,128)(2,1)S(1)} %get-tuple-element.749), channel_id=1, source_target_pairs={{0,1},{1,0},{2,3},{3,2},{4,5},{5,4},{6,7},{7,6},{8,9},{9,8},{10,11... | collective-permute-start | bytes 221192 | tf_op jit(solution)/shard_map/ppermute | solution.py:99
  74.5 8.1 %collective-permute-start.69 = (bf16[32,1152]{1,0:T(8,128)(2,1)S(1)}, bf16[32,1152]{1,0:T(8,128)(2,1)S(1)}, u32[]{:S(2)}, u32[]{:S(2)}) collective-permute-start(bf16[32,1152]{1,0:T(8,128)(2,1)S(1)} %get-tuple-element.748), channel_id=1, source_target_pairs={{0,2},{1,3},{2,0},{3,1},{4,6},{5,7},{6,4},{7,5},{8,10},{9,11},{10,... | collective-permute-start | bytes 221192 | tf_op jit(solution)/shard_map/ppermute | solution.py:99
  79.5 7.7 %collective-permute-start.70 = (bf16[32,1152]{1,0:T(8,128)(2,1)S(1)}, bf16[32,1152]{1,0:T(8,128)(2,1)S(1)}, u32[]{:S(2)}, u32[]{:S(2)}) collective-permute-start(bf16[32,1152]{1,0:T(8,128)(2,1)S(1)} %get-tuple-element.747), channel_id=1, source_target_pairs={{0,3},{1,2},{2,1},{3,0},{4,7},{5,6},{6,5},{7,4},{8,11},{9,10},{10,... | collective-permute-start | bytes 221192 | tf_op jit(solution)/shard_map/ppermute | solution.py:99
  89.3 38.6 %collective-permute-start.49 = (bf16[32,1152]{1,0:T(8,128)(2,1)S(1)}, bf16[32,1152]{1,0:T(8,128)(2,1)}, u32[]{:S(2)}, u32[]{:S(2)}) collective-permute-start(bf16[32,1152]{1,0:T(8,128)(2,1)S(1)} %dynamic-slice_bitcast_fusion.49), channel_id=1, source_target_pairs={{0,400},{4,404},{8,408},{12,412},{16,384},{20,388},{24,392},{28,39... | collective-permute-start | bytes 221192 | tf_op jit(solution)/shard_map/while/body/eval_jaxpr/cond/branch_50_fun/ppermute | solution.py:18
  130.1 14.3 %collective-permute-start.19 = (bf16[32,1152]{1,0:T(8,128)(2,1)S(1)}, bf16[32,1152]{1,0:T(8,128)(2,1)}, u32[]{:S(2)}, u32[]{:S(2)}) collective-permute-start(bf16[32,1152]{1,0:T(8,128)(2,1)S(1)} %dynamic-slice_bitcast_fusion.19), channel_id=1, source_target_pairs={{0,160},{4,164},{8,168},{12,172},{16,176},{20,180},{24,184},{28,18... | collective-permute-start | bytes 221192 | tf_op jit(solution)/shard_map/while/body/eval_jaxpr/cond/branch_20_fun/ppermute | solution.py:18
  146.6 12.1 %collective-permute-start.7 = (bf16[32,1152]{1,0:T(8,128)(2,1)S(1)}, bf16[32,1152]{1,0:T(8,128)(2,1)}, u32[]{:S(2)}, u32[]{:S(2)}) collective-permute-start(bf16[32,1152]{1,0:T(8,128)(2,1)S(1)} %dynamic-slice_bitcast_fusion.7), channel_id=1, source_target_pairs={{0,64},{4,68},{8,72},{12,76},{16,80},{20,84},{24,88},{28,92},{32,9... | collective-permute-start | bytes 221192 | tf_op jit(solution)/shard_map/while/body/eval_jaxpr/cond/branch_8_fun/ppermute | solution.py:18
  161.0 8.2 %collective-permute-start.5 = (bf16[32,1152]{1,0:T(8,128)(2,1)S(1)}, bf16[32,1152]{1,0:T(8,128)(2,1)}, u32[]{:S(2)}, u32[]{:S(2)}) collective-permute-start(bf16[32,1152]{1,0:T(8,128)(2,1)S(1)} %dynamic-slice_bitcast_fusion.5), channel_id=1, source_target_pairs={{0,48},{4,52},{8,56},{12,60},{16,32},{20,36},{24,40},{28,44},{32,1... | collective-permute-start | bytes 221192 | tf_op jit(solution)/shard_map/while/body/eval_jaxpr/cond/branch_6_fun/ppermute | solution.py:18
  170.8 1.2 copy-start.2
  172.1 1.2 copy-start.7
